TPU v7x, 32 devices: a whole 2x2x4 slice. The times are simulated.
32 devices in a mesh: grp: 2 (over x), ep: 16 (over z, y, core).
Axes of the slice: x: 2, y: 2, z: 4, core: 2. Of those that a mesh axis runs over, the one named last changes fastest.
Arguments:
- attention: bfloat16 [4096, 1024], P(('grp', 'ep')), may hold values from -6 to 6
- residual: bfloat16 [4096, 1024], P(('grp', 'ep')), may hold values from -6 to 6
- out_proj: bfloat16 [1024, 1024], P(None, 'grp'), may hold values from -0.1875 to 0.1875
- pre_gain: float32 [1024], replicated, may hold values from 0.25 to 1.75
- post_gain: float32 [1024], replicated, may hold values from 0.25 to 1.75
- slot_gate_up: bfloat16 [16, 1024, 1024], P('ep'), may hold values from -0.1875 to 0.1875
- slot_down: bfloat16 [16, 512, 1024], P('ep'), may hold values from -0.25 to 0.25
- expert_ids: int32 [4096, 8], P(('grp', 'ep')), may hold values from 0 to 15, all different within a row
- copy_choice: int32 [4096, 8], P(('grp', 'ep')), may hold values from 0 to 1
- placement: int32 [16], replicated, may hold values from 0 to 15, each once
- request_age: int32 [4096], P(('grp', 'ep')), may hold values from 0 to 1048575
- decode_flag: int32 [4096], P(('grp', 'ep')), may hold values 0 or 1
- capacity: int32 [2, 16], replicated, may hold values from 16 to 32, as said below
- route_weight: float32 [4096, 8], P(('grp', 'ep')), may hold values from 0.05 to 1
Outputs:
- layer_out: bfloat16 [4096, 1024], P(('grp', 'ep'))
Inputs may be any that keep to these rules, and one draw needn't show every extreme that they name: At least one block has capacity 32. `expert_ids`: each row names 8 different experts. `placement`: each slot holds a different expert.
All inputs are finite; a program needn't handle non-finite values. No bound on the sum of `decode_flag` on one device may be relied on, other than what follows from the above.
Results may differ from a plain program's by a relative error of at most 0.01.
Values may be sent and summed in bfloat16 or wider, within the bound.
No kernel may reach another device: no remote copies, remote signals or barrier semaphores. Data moves between devices by JAX's collectives and lax.ppermute only.
A program may use at most 64 MiB of HBM per device.

v0:
```python
import jax
import jax.numpy as jnp
from jax import lax
from jax.sharding import PartitionSpec as P


def rms_scale(values, gain):
    meansq = jnp.mean(values * values, axis=-1, keepdims=True)
    return values * lax.rsqrt(meansq + 1e-06) * gain


def on_device(
    attention,
    residual,
    out_proj,
    pre_gain,
    post_gain,
    slot_gate_up,
    slot_down,
    expert_ids,
    copy_choice,
    placement,
    request_age,
    decode_flag,
    capacity,
    route_weight,
):
    groups = lax.axis_size("grp")
    owners = lax.axis_size("ep")
    devices_all = groups * owners
    rows_here = attention.shape[0]
    features = attention.shape[1]
    picks_row = expert_ids.shape[1]
    cap_size = max(2, rows_here * picks_row // devices_all)
    columns = jnp.dot(
        lax.all_gather(attention, "grp", axis=0, tiled=True),
        out_proj,
        preferred_element_type=jnp.float32,
    )
    attn_proj = lax.all_to_all(columns, "grp", split_axis=0, concat_axis=1, tiled=True)
    hidden_state = (residual.astype(jnp.float32) + attn_proj).astype(jnp.bfloat16)
    normed = rms_scale(hidden_state.astype(jnp.float32), pre_gain).astype(jnp.bfloat16)
    experts_all = placement.shape[0]
    slot_table = jnp.arange(owners, dtype=jnp.int32)
    matches = (placement[None, :] == jnp.arange(experts_all, dtype=jnp.int32)[:, None]).astype(
        jnp.int32
    )
    slot_of = jnp.sum(slot_table[None, :] * matches, axis=1)
    expert_hits = (
        expert_ids[:, :, None] == jnp.arange(experts_all, dtype=jnp.int32)[None, None, :]
    ).astype(jnp.int32)
    target = copy_choice * owners + jnp.sum(expert_hits * slot_of[None, None, :], axis=2)
    priority = decode_flag * 1048576 + request_age
    order = jnp.arange(rows_here, dtype=jnp.int32)
    ahead_mask = (priority[None, :] > priority[:, None]) | (
        priority[None, :] == priority[:, None]
    ) & (order[None, :] < order[:, None])
    target_hits = jnp.sum(
        (target[:, :, None] == jnp.arange(devices_all, dtype=jnp.int32)[None, None, :]).astype(
            jnp.bfloat16
        ),
        axis=1,
    )
    counts = jnp.dot(
        ahead_mask.astype(jnp.bfloat16), target_hits, preferred_element_type=jnp.float32
    )
    position = jnp.take_along_axis(counts, target, axis=1).astype(jnp.int32)
    granted = jnp.take(capacity.reshape(-1), target)
    accepted = position < granted
    total_slots = devices_all * cap_size
    index = jnp.where(accepted, target * cap_size + position, total_slots)
    spread_rows = jnp.broadcast_to(normed[:, None, :], (rows_here, picks_row, features)).reshape(
        rows_here * picks_row, features
    )
    buffer = (
        jnp.zeros((total_slots, features), jnp.bfloat16)
        .at[index.reshape(-1)]
        .set(spread_rows, mode="drop")
    )
    gate_up_local = slot_gate_up[0]
    down_local = slot_down[0]
    hidden_units = down_local.shape[0]
    arrived = lax.all_to_all(
        buffer.reshape(devices_all, cap_size, features),
        ("grp", "ep"),
        split_axis=0,
        concat_axis=0,
        tiled=True,
    )
    flattened = arrived.reshape(-1, features)
    gate_up = jnp.dot(flattened, gate_up_local, preferred_element_type=jnp.float32)
    expert_hidden = (jax.nn.silu(gate_up[:, :hidden_units]) * gate_up[:, hidden_units:]).astype(
        jnp.bfloat16
    )
    produced = jnp.dot(expert_hidden, down_local, preferred_element_type=jnp.float32).astype(
        jnp.bfloat16
    )
    returned = lax.all_to_all(
        produced.reshape(arrived.shape), ("grp", "ep"), split_axis=0, concat_axis=0, tiled=True
    )
    flat_back = returned.reshape(total_slots, features)
    expert_out = flat_back[jnp.minimum(index, total_slots - 1)]
    weights_kept = jnp.where(accepted, route_weight, jnp.float32(0.0))
    mixture = jnp.einsum("rk,rkd->rd", weights_kept, expert_out, preferred_element_type=jnp.float32)
    return rms_scale(hidden_state.astype(jnp.float32) + mixture, post_gain).astype(jnp.bfloat16)


def solution(mesh):
    placed = (
        P(("grp", "ep"), None),
        P(("grp", "ep"), None),
        P(None, "grp"),
        P(),
        P(),
        P("ep", None, None),
        P("ep", None, None),
        P(("grp", "ep"), None),
        P(("grp", "ep"), None),
        P(),
        P(("grp", "ep")),
        P(("grp", "ep")),
        P(),
        P(("grp", "ep"), None),
    )
    return jax.shard_map(
        on_device, mesh=mesh, in_specs=placed, out_specs=P(("grp", "ep"), None), check_vma=False
    )
```

profile of v0, /device:TPU:0, one launch (start us, length us, event | category | flops | bytes accessed | tf_op | source)
XLA Modules:
  0.0 164.9 jit_solution(11830861207387818985)
XLA Ops:
  0.0 0.0 copy-start
  0.0 0.0 copy-start.10
  0.0 0.0 copy-start.11
  0.0 10.3 %all_gather.3 = bf16[256,1024]{1,0:T(8,128)(2,1)S(1)} all-gather(bf16[128,1024]{1,0:T(8,128)(2,1)} %param.14), channel_id=1, replica_groups=mesh['grp'=2,'ep'=16] {'grp'}, dimensions={0}, use_global_device_ids=true | all-gather | bytes 786432 | tf_op jit(solution)/shard_map/all_gather | solution.py:36
  10.4 2.5 %fusion.24 = f32[256,512]{1,0:T(8,128)} fusion(bf16[256,1024]{1,0:T(8,128)(2,1)S(1)} %all_gather.3, bf16[1024,512]{1,0:T(8,128)(2,1)} %param.16), kind=kOutput, calls=%fused_computation.54 | convolution fusion | flops 268435456 | bytes 2097152 | tf_op jit(solution)/shard_map/dot_general | solution.py:35
  12.8 3.5 %all-to-all-start = ((f32[2,128,512]{2,1,0:T(8,128)}), f32[2,128,512]{2,1,0:T(8,128)S(1)}, u32[]{:S(2)}, u32[]{:S(2)}) async-start(f32[2,128,512]{2,1,0:T(8,128)} %bitcast), calls=%async_computation | async-start | bytes 1048576 | tf_op jit(solution)/shard_map/all_to_all | solution.py:40
  16.3 0.0 copy-done.9
  16.3 0.1 select_reduce_fusion.1
  16.5 0.0 copy-done.5
  16.5 0.1 select_reduce_fusion
  16.6 0.0 copy-done.6
  16.6 0.1 copy.24
  16.7 0.1 reshape.110
  16.8 0.0 copy-done.10
  16.8 0.0 copy-done.11
  16.8 0.2 fusion.19
  17.1 7.0 %gather_fusion.2 = f32[1024]{0:T(1024)S(1)} fusion(f32[128,32]{0,1:T(8,128)S(1)} %fusion.19, s32[1024]{0:T(1024)S(1)} %reshape.110), kind=kCustom, calls=%fused_computation.2 | custom fusion | bytes 16384 | tf_op jit(solution)/shard_map/jit(take_along_axis)/gather | solution.py:67
  24.1 0.1 reshape.113
  24.2 0.1 copy.26
  24.3 0.1 reshape.96
  24.5 0.0 copy-done.8
  24.5 0.1 reshape.87
  24.6 6.6 %gather_fusion = s32[1024]{0:T(1024)S(1)} fusion(s32[32]{0:T(128)S(1)} %reshape.87, s32[1024]{0:T(1024)S(1)} %broadcast_clamp_fusion.1), kind=kCustom, calls=%fused_computation | custom fusion | bytes 12288 | tf_op jit(solution)/shard_map/jit(_take)/gather | solution.py:68
  31.1 0.0 copy-start.2
  31.1 0.1 reshape.95
  31.3 0.1 copy.28
  31.4 0.1 reshape.88
  31.5 0.0 all-to-all-done
  31.6 0.0 copy-done.1
  31.6 0.2 fusion.12
  31.8 0.1 copy-done.2
  31.8 0.1 fusion.14
  31.9 6.8 %scatter_custom_fusion = bf16[1024,1024]{1,0:T(8,128)(2,1)} fusion(s32[1024]{0:T(1024)S(1)} %bitcast.43, bf16[128,1024]{1,0:T(8,128)(2,1)S(1)} %fusion.14, bf16[]{:T(256)} %constant.29.clone.1), kind=kCustom, calls=%fused_computation.10 | custom fusion | bytes 2359298 | tf_op jit(solution)/shard_map/scatter | solution.py:78
  38.8 56.2 %all_to_all.29 = bf16[32,32,1024]{2,1,0:T(8,128)(2,1)S(1)} all-to-all(bf16[32,32,1024]{2,1,0:T(8,128)(2,1)} %bitcast.38), channel_id=1, replica_groups=mesh['grp'=2,'ep'=16] {'grp','ep'}, dimensions={0} | all-to-all | bytes 4194304 | tf_op jit(solution)/shard_map/all_to_all | solution.py:83
  95.0 0.0 copy-done
  95.0 2.4 %fusion.3 = f32[1024,1024]{1,0:T(8,128)S(1)} fusion(bf16[1024,1024]{1,0:T(8,128)(2,1)S(1)} %bitcast.40, bf16[1,1024,1024]{2,1,0:T(8,128)(2,1)S(1)} %copy-done), kind=kOutput, calls=%fused_computation.8 | convolution fusion | flops 2147483648 | bytes 8388608 | tf_op jit(solution)/shard_map/dot_general | solution.py:91
  97.3 0.0 copy-done.7
  97.3 2.6 %convolution_convert_fusion = bf16[1024,1024]{1,0:T(8,128)(2,1)} fusion(f32[1024,1024]{1,0:T(8,128)S(1)} %fusion.3, bf16[1,512,1024]{2,1,0:T(8,128)(2,1)S(1)} %copy-done.7), kind=kOutput, calls=%fused_computation.12 | convolution fusion | flops 1077936128 | bytes 7340032 | tf_op jit(solution)/shard_map/dot_general | solution.py:95
  99.9 3.6 %all-to-all-start.2 = ((bf16[32,32,1024]{2,1,0:T(8,128)(2,1)}), bf16[32,32,1024]{2,1,0:T(8,128)(2,1)}, u32[]{:S(2)}, u32[]{:S(2)}) async-start(bf16[32,32,1024]{2,1,0:T(8,128)(2,1)} %bitcast.39), calls=%async_computation.2 | async-start | bytes 4194304 | tf_op jit(solution)/shard_map/all_to_all | solution.py:98
  103.5 0.1 copy.29
  103.6 0.1 reshape.104
  103.7 0.0 copy-done.4
  103.8 0.1 copy.30
  103.9 49.7 %all-to-all-done.2 = bf16[32,32,1024]{2,1,0:T(8,128)(2,1)} async-done(((bf16[32,32,1024]{2,1,0:T(8,128)(2,1)}), bf16[32,32,1024]{2,1,0:T(8,128)(2,1)}, u32[]{:S(2)}, u32[]{:S(2)}) %all-to-all-start.2) | async-done | bytes 2097184 | tf_op jit(solution)/shard_map/all_to_all | solution.py:98
  153.6 7.9 %gather_fusion.1 = bf16[1024,1024]{1,0:T(8,128)(2,1)} fusion(bf16[1024,1024]{1,0:T(8,128)(2,1)} %bitcast.11, s32[1024]{0:T(1024)S(1)} %broadcast_clamp_fusion), kind=kCustom, calls=%fused_computation.1 | custom fusion | bytes 4198400 | tf_op jit(solution)/shard_map/gather | solution.py:102
  161.6 2.3 %fusion.1 = f32[128,1,1024]{2,1,0:T(1,128)S(1)} fusion(bf16[128,8,1]{1,2,0:T(2,128)(2,1)S(1)} %copy.30, bf16[1024,1024]{1,0:T(8,128)(2,1)} %gather_fusion.1), kind=kOutput, calls=%fused_computation.6 | convolution fusion | flops 2097152 | bytes 2623488 | tf_op jit(solution)/shard_map/rk,rkd->rd/dot_general | solution.py:104
  163.9 0.2 multiply_reduce_fusion
  164.0 0.8 multiply_convert_fusion
  (23 shorter events, 0.3 us)
Async XLA Ops:
  0.0 95.0 %copy-start = (bf16[1,1024,1024]{2,1,0:T(8,128)(2,1)S(1)}, bf16[1,1024,1024]{2,1,0:T(8,128)(2,1)}, u32[]{:S(2)}) copy-start(bf16[1,1024,1024]{2,1,0:T(8,128)(2,1)} %param.19) | copy-start | bytes 6291460
  0.0 16.3 %copy-start.9 = (s32[16]{0:T(128)S(1)}, s32[16]{0:T(128)}, u32[]{:S(2)}) copy-start(s32[16]{0:T(128)} %param.23) | copy-start | bytes 196
  0.0 16.5 %copy-start.5 = (s32[128,8]{0,1:T(8,128)S(1)}, s32[128,8]{0,1:T(8,128)}, u32[]{:S(2)}) copy-start(s32[128,8]{0,1:T(8,128)} %param.21) | copy-start | bytes 12292
  0.0 16.5 %copy-start.6 = (s32[128,8]{0,1:T(8,128)S(1)}, s32[128,8]{0,1:T(8,128)}, u32[]{:S(2)}) copy-start(s32[128,8]{0,1:T(8,128)} %param.22) | copy-start | bytes 12292
  0.0 16.8 %copy-start.10 = (s32[128]{0:T(128)S(1)}, s32[128]{0:T(128)}, u32[]{:S(2)}) copy-start(s32[128]{0:T(128)} %param.24) | copy-start | bytes 1540
  0.0 16.8 %copy-start.11 = (s32[128]{0:T(128)S(1)}, s32[128]{0:T(128)}, u32[]{:S(2)}) copy-start(s32[128]{0:T(128)} %param.25) | copy-start | bytes 1540
  12.8 18.7 %all-to-all-start = ((f32[2,128,512]{2,1,0:T(8,128)}), f32[2,128,512]{2,1,0:T(8,128)S(1)}, u32[]{:S(2)}, u32[]{:S(2)}) async-start(f32[2,128,512]{2,1,0:T(8,128)} %bitcast), calls=%async_computation | async-start | bytes 1048576 | tf_op jit(solution)/shard_map/all_to_all | solution.py:40
  17.1 7.4 %copy-start.8 = (s32[2,16]{1,0:T(2,128)S(1)}, s32[2,16]{1,0:T(2,128)}, u32[]{:S(2)}) copy-start(s32[2,16]{1,0:T(2,128)} %param.26) | copy-start | bytes 388
  24.6 7.0 %copy-start.1 = (bf16[128,1024]{1,0:T(8,128)(2,1)S(1)}, bf16[128,1024]{1,0:T(8,128)(2,1)}, u32[]{:S(2)}) copy-start(bf16[128,1024]{1,0:T(8,128)(2,1)} %param.15) | copy-start | bytes 786436
  31.1 0.7 copy-start.2
  95.0 2.4 %copy-start.7 = (bf16[1,512,1024]{2,1,0:T(8,128)(2,1)S(1)}, bf16[1,512,1024]{2,1,0:T(8,128)(2,1)}, u32[]{:S(2)}) copy-start(bf16[1,512,1024]{2,1,0:T(8,128)(2,1)} %param.20) | copy-start | bytes 3145732
  99.9 3.8 %copy-start.4 = (f32[128,8]{0,1:T(8,128)S(1)}, f32[128,8]{0,1:T(8,128)}, u32[]{:S(2)}) copy-start(f32[128,8]{0,1:T(8,128)} %param.27) | copy-start | bytes 12292
  99.9 53.7 %all-to-all-start.2 = ((bf16[32,32,1024]{2,1,0:T(8,128)(2,1)}), bf16[32,32,1024]{2,1,0:T(8,128)(2,1)}, u32[]{:S(2)}, u32[]{:S(2)}) async-start(bf16[32,32,1024]{2,1,0:T(8,128)(2,1)} %bitcast.39), calls=%async_computation.2 | async-start | bytes 4194304 | tf_op jit(solution)/shard_map/all_to_all | solution.py:98
  161.6 2.5 %copy-start.3 = (f32[1024]{0:T(1024)S(1)}, f32[1024]{0:T(1024)}, u32[]{:S(2)}) copy-start(f32[1024]{0:T(1024)} %param.18) | copy-start | bytes 12292
where the time goes:
time: 165 us
  blocking collectives  66.5 us (40%)
  waiting for transfers between devices  49.7 us (30%)
  local copies, waits for them, and re-layouts  29.7 us (18%)
  matrix products  9.92 us (6%)
  starting transfers between devices  7.09 us (4%)
    all_to_all x1, blocking collectives, on_device(): lax.all_to_all(buffer.reshape(devices_all, cap_size, features), ('grp', '...  56.2 us
    all_to_all x1, waiting for transfers between devices, on_device(): lax.all_to_all(produced.reshape(arrived.shape), ('grp', 'ep'), split_axis...  49.7 us
    all_gather x1, blocking collectives, on_device(): lax.all_gather(attention, 'grp', axis=0, tiled=True)  10.3 us
    gather x1, local copies, waits for them, and re-layouts, on_device(): expert_out = flat_back[jnp.minimum(index, total_slots - 1)]  7.93 us
    gather x5, local copies, waits for them, and re-layouts, on_device(): position = jnp.take_along_axis(counts, target, axis=1).astype(jnp.int32)  7.35 us
    scatter x1, local copies, waits for them, and re-layouts, on_device(): buffer = jnp.zeros((total_slots, features), jnp.bfloat16).at[index.reshap...  6.82 us
    gather x3, local copies, waits for them, and re-layouts, on_device(): granted = jnp.take(capacity.reshape(-1), target)  6.69 us
    all_to_all x1, starting transfers between devices, on_device(): lax.all_to_all(produced.reshape(arrived.shape), ('grp', 'ep'), split_axis...  3.6 us
  transfers between devices with their start and end apart: 2, of which 1 were waited for; matrix products, arithmetic and copies ran while one was open for 9% of the time, Pallas kernels for 0%

commit v1 on v0

--- a/solution.py
+++ b/solution.py
@@ -55,28 +55,23 @@
     ahead_mask = (priority[None, :] > priority[:, None]) | (
         priority[None, :] == priority[:, None]
     ) & (order[None, :] < order[:, None])
-    target_hits = jnp.sum(
-        (target[:, :, None] == jnp.arange(devices_all, dtype=jnp.int32)[None, None, :]).astype(
-            jnp.bfloat16
-        ),
-        axis=1,
-    )
+    target_onehot = target[:, :, None] == jnp.arange(devices_all, dtype=jnp.int32)[None, None, :]
+    target_hits = jnp.sum(target_onehot.astype(jnp.bfloat16), axis=1)
     counts = jnp.dot(
         ahead_mask.astype(jnp.bfloat16), target_hits, preferred_element_type=jnp.float32
     )
-    position = jnp.take_along_axis(counts, target, axis=1).astype(jnp.int32)
-    granted = jnp.take(capacity.reshape(-1), target)
+    position = jnp.sum(
+        jnp.where(target_onehot, counts[:, None, :], 0.0), axis=2
+    ).astype(jnp.int32)
+    granted = jnp.sum(
+        jnp.where(target_onehot, capacity.reshape(-1)[None, None, :], 0), axis=2
+    )
     accepted = position < granted
     total_slots = devices_all * cap_size
     index = jnp.where(accepted, target * cap_size + position, total_slots)
-    spread_rows = jnp.broadcast_to(normed[:, None, :], (rows_here, picks_row, features)).reshape(
-        rows_here * picks_row, features
-    )
-    buffer = (
-        jnp.zeros((total_slots, features), jnp.bfloat16)
-        .at[index.reshape(-1)]
-        .set(spread_rows, mode="drop")
-    )
+    slot_ids = jnp.arange(total_slots, dtype=jnp.int32)
+    dispatch = jnp.any(index[None, :, :] == slot_ids[:, None, None], axis=2).astype(jnp.bfloat16)
+    buffer = jnp.dot(dispatch, normed, preferred_element_type=jnp.float32).astype(jnp.bfloat16)
     gate_up_local = slot_gate_up[0]
     down_local = slot_down[0]
     hidden_units = down_local.shape[0]
@@ -99,9 +94,17 @@
         produced.reshape(arrived.shape), ("grp", "ep"), split_axis=0, concat_axis=0, tiled=True
     )
     flat_back = returned.reshape(total_slots, features)
-    expert_out = flat_back[jnp.minimum(index, total_slots - 1)]
     weights_kept = jnp.where(accepted, route_weight, jnp.float32(0.0))
-    mixture = jnp.einsum("rk,rkd->rd", weights_kept, expert_out, preferred_element_type=jnp.float32)
+    combine = jnp.sum(
+        jnp.where(index[:, :, None] == slot_ids[None, None, :], weights_kept[:, :, None], 0.0),
+        axis=1,
+    )
+    mixture = jnp.dot(
+        combine,
+        flat_back.astype(jnp.float32),
+        precision=lax.Precision.HIGHEST,
+        preferred_element_type=jnp.float32,
+    )
     return rms_scale(hidden_state.astype(jnp.float32) + mixture, post_gain).astype(jnp.bfloat16)
 
 

time: 165 us -> 142 us (0.86)
  local copies, waits for them, and re-layouts: 29.7 us -> 0.37 us
  waiting for transfers between devices: 49.7 us -> 53.5 us
  other arithmetic: 1.6 us -> 4.62 us
  blocking collectives: 66.5 us -> 64.6 us
    gather x9 -> x0, local copies, waits for them, and re-layouts: 22 us -> none  [the longest x1 7.93 us: on_device(): expert_out = flat_back[jnp.minimum(index, total_slots - 1)]]
    scatter x1 -> x0, local copies, waits for them, and re-layouts: 6.82 us -> none  [on_device(): buffer = jnp.zeros((total_slots, features), jnp.bfloat16).at[index.reshap...]
    all_to_all x1, waiting for transfers between devices: 0.01 us -> 4.99 us  [on_device(): lax.all_to_all(columns, 'grp', split_axis=0, concat_axis=1, tiled=True)]
    all_to_all x1, blocking collectives: 56.2 us -> 54.3 us  [on_device(): lax.all_to_all(buffer.reshape(devices_all, cap_size, features), ('grp', '...]
    reduce_or x0 -> x1, other arithmetic: none -> 1.92 us  [on_device(): jnp.any(index[None, :, :] == slot_ids[:, None, None], axis=2)]
    dot_general x1 -> x2, matrix products: 2.29 us -> 3.49 us  [the longest x1 2.71 us: on_device(): jnp.dot(combine, flat_back.astype(jnp.float32), precision=lax.Precision.H...]
  transfers between devices with their start and end apart: 2 -> 2, of which waited for: 1 -> 2; matrix products, arithmetic and copies ran while one was open for 9% -> 3% of each run, Pallas kernels for 0% -> 0%
where the time goes in v1:
time: 142 us
  blocking collectives  64.6 us (45%)
  waiting for transfers between devices  53.5 us (38%)
  matrix products  11.1 us (8%)
  starting transfers between devices  7.23 us (5%)
  other arithmetic  4.62 us (3%)
    all_to_all x1, blocking collectives, on_device(): lax.all_to_all(buffer.reshape(devices_all, cap_size, features), ('grp', '...  54.3 us
    all_to_all x1, waiting for transfers between devices, on_device(): lax.all_to_all(produced.reshape(arrived.shape), ('grp', 'ep'), split_axis...  48.5 us
    all_gather x1, blocking collectives, on_device(): lax.all_gather(attention, 'grp', axis=0, tiled=True)  10.3 us
    all_to_all x1, waiting for transfers between devices, on_device(): lax.all_to_all(columns, 'grp', split_axis=0, concat_axis=1, tiled=True)  4.99 us
    all_to_all x1, starting transfers between devices, on_device(): lax.all_to_all(columns, 'grp', split_axis=0, concat_axis=1, tiled=True)  3.62 us
    all_to_all x1, starting transfers between devices, on_device(): lax.all_to_all(produced.reshape(arrived.shape), ('grp', 'ep'), split_axis...  3.61 us
  transfers between devices with their start and end apart: 2, of which 2 were waited for; matrix products, arithmetic and copies ran while one was open for 3% of the time, Pallas kernels for 0%

profile of v1, /device:TPU:0, one launch (start us, length us, event | category | flops | bytes accessed | tf_op | source)
XLA Modules:
  0.0 141.7 jit_solution(11151042143079868038)
XLA Ops:
  0.0 0.0 copy-start
  0.0 0.0 copy-start.9
  0.0 0.0 copy-start.8
  0.0 0.0 copy-start.5
  0.0 0.0 copy-start.4
  0.0 0.0 copy-start.11
  0.0 0.0 copy-start.10
  0.0 10.3 %all_gather.3 = bf16[256,1024]{1,0:T(8,128)(2,1)S(1)} all-gather(bf16[128,1024]{1,0:T(8,128)(2,1)} %param.14), channel_id=1, replica_groups=mesh['grp'=2,'ep'=16] {'grp'}, dimensions={0}, use_global_device_ids=true | all-gather | bytes 786432 | tf_op jit(solution)/shard_map/all_gather | solution.py:36
  10.4 0.0 copy-start.1
  10.4 2.5 %fusion.22 = f32[256,512]{1,0:T(8,128)} fusion(bf16[256,1024]{1,0:T(8,128)(2,1)S(1)} %all_gather.3, bf16[1024,512]{1,0:T(8,128)(2,1)} %param.16), kind=kOutput, calls=%fused_computation.46 | convolution fusion | flops 268435456 | bytes 2097152 | tf_op jit(solution)/shard_map/dot_general | solution.py:35
  12.9 0.0 copy-start.2
  12.9 3.6 %all-to-all-start = ((f32[2,128,512]{2,1,0:T(8,128)}), f32[2,128,512]{2,1,0:T(8,128)S(1)}, u32[]{:S(2)}, u32[]{:S(2)}) async-start(f32[2,128,512]{2,1,0:T(8,128)} %bitcast), calls=%async_computation | async-start | bytes 1048576 | tf_op jit(solution)/shard_map/all_to_all | solution.py:40
  16.5 0.0 copy-done.9
  16.5 0.1 select_reduce_fusion.4
  16.6 0.0 copy-done.8
  16.6 0.1 broadcast_in_dim.44
  16.7 0.0 copy-done.5
  16.7 0.1 select_reduce_fusion.3
  16.8 0.0 copy-done.4
  16.9 0.1 select_reduce_fusion.1
  17.0 0.0 copy-done.11
  17.0 0.0 copy-done.10
  17.0 0.2 fusion.17
  17.3 1.9 %fusion = pred[1024,128]{1,0:T(8,128)(4,1)S(1)} fusion(s32[128,8]{0,1:T(8,128)S(1)} %get-tuple-element.7), kind=kLoop, calls=%fused_computation.3 | loop fusion | flops 1966080 | bytes 135168 | tf_op jit(solution)/shard_map/reduce_or | solution.py:73
  19.2 5.0 %all-to-all-done = f32[2,128,512]{2,1,0:T(8,128)S(1)} async-done(((f32[2,128,512]{2,1,0:T(8,128)}), f32[2,128,512]{2,1,0:T(8,128)S(1)}, u32[]{:S(2)}, u32[]{:S(2)}) %all-to-all-start) | async-done | bytes 524320 | tf_op jit(solution)/shard_map/all_to_all | solution.py:40
  24.2 0.0 copy-done.1
  24.2 0.2 fusion.7
  24.4 0.0 copy-done.2
  24.4 0.8 convolution_convert_fusion.1
  25.2 54.3 %all_to_all.29 = bf16[32,32,1024]{2,1,0:T(8,128)(2,1)S(1)} all-to-all(bf16[32,32,1024]{2,1,0:T(8,128)(2,1)S(1)} %bitcast.21), channel_id=1, replica_groups=mesh['grp'=2,'ep'=16] {'grp','ep'}, dimensions={0} | all-to-all | bytes 4194304 | tf_op jit(solution)/shard_map/all_to_all | solution.py:78
  79.5 0.0 copy-done
  79.5 0.0 copy-start.7
  79.5 2.4 %fusion.2 = f32[1024,1024]{1,0:T(8,128)S(1)} fusion(bf16[1024,1024]{1,0:T(8,128)(2,1)S(1)} %bitcast.23, bf16[1,1024,1024]{2,1,0:T(8,128)(2,1)S(1)} %copy-done), kind=kOutput, calls=%fused_computation.6 | convolution fusion | flops 2147483648 | bytes 8388608 | tf_op jit(solution)/shard_map/dot_general | solution.py:86
  81.8 0.0 copy-done.7
  81.8 2.6 %convolution_convert_fusion = bf16[1024,1024]{1,0:T(8,128)(2,1)} fusion(f32[1024,1024]{1,0:T(8,128)S(1)} %fusion.2, bf16[1,512,1024]{2,1,0:T(8,128)(2,1)S(1)} %copy-done.7), kind=kOutput, calls=%fused_computation.8 | convolution fusion | flops 1077936128 | bytes 7340032 | tf_op jit(solution)/shard_map/dot_general | solution.py:90
  84.4 0.0 copy-start.6
  84.4 3.6 %all-to-all-start.2 = ((bf16[32,32,1024]{2,1,0:T(8,128)(2,1)}), bf16[32,32,1024]{2,1,0:T(8,128)(2,1)}, u32[]{:S(2)}, u32[]{:S(2)}) async-start(bf16[32,32,1024]{2,1,0:T(8,128)(2,1)} %bitcast.22), calls=%async_computation.2 | async-start | bytes 4194304 | tf_op jit(solution)/shard_map/all_to_all | solution.py:93
  88.0 0.0 copy-start.3
  88.1 0.1 copy.23
  88.2 0.0 copy-done.6
  88.2 0.1 copy.24
  88.3 1.3 select_reduce_fusion
  89.6 48.5 %all-to-all-done.2 = bf16[32,32,1024]{2,1,0:T(8,128)(2,1)} async-done(((bf16[32,32,1024]{2,1,0:T(8,128)(2,1)}), bf16[32,32,1024]{2,1,0:T(8,128)(2,1)}, u32[]{:S(2)}, u32[]{:S(2)}) %all-to-all-start.2) | async-done | bytes 2097184 | tf_op jit(solution)/shard_map/all_to_all | solution.py:93
  138.1 2.7 %multiply_reduce_fusion = (f32[128]{0:T(128)S(1)}, f32[128,1024]{1,0:T(8,128)S(1)}) fusion(f32[128,1024]{1,0:T(8,128)S(1)} %select_reduce_fusion, bf16[1024,1024]{1,0:T(8,128)(2,1)} %bitcast.7, bf16[128,1024]{1,0:T(8,128)(2,1)S(1)} %get-tuple-element.6), kind=kOutput, calls=%fused_computation.19 | convolution fusion | flops 1611136896 | bytes 3408384 | tf_op jit(solution)/shard_map/dot_general | solution.py:102
  140.9 0.0 copy-done.3
  140.9 0.8 multiply_convert_fusion
  (9 shorter events, 0.1 us)
Async XLA Ops:
  0.0 79.5 %copy-start = (bf16[1,1024,1024]{2,1,0:T(8,128)(2,1)S(1)}, bf16[1,1024,1024]{2,1,0:T(8,128)(2,1)}, u32[]{:S(2)}) copy-start(bf16[1,1024,1024]{2,1,0:T(8,128)(2,1)} %param.19) | copy-start | bytes 6291460
  0.0 16.5 %copy-start.9 = (s32[16]{0:T(128)S(1)}, s32[16]{0:T(128)}, u32[]{:S(2)}) copy-start(s32[16]{0:T(128)} %param.23) | copy-start | bytes 196
  0.0 16.6 %copy-start.8 = (s32[2,16]{1,0:T(2,128)S(1)}, s32[2,16]{1,0:T(2,128)}, u32[]{:S(2)}) copy-start(s32[2,16]{1,0:T(2,128)} %param.26) | copy-start | bytes 388
  0.0 16.7 %copy-start.5 = (s32[128,8]{0,1:T(8,128)S(1)}, s32[128,8]{0,1:T(8,128)}, u32[]{:S(2)}) copy-start(s32[128,8]{0,1:T(8,128)} %param.21) | copy-start | bytes 12292
  0.0 16.8 %copy-start.4 = (s32[128,8]{0,1:T(8,128)S(1)}, s32[128,8]{0,1:T(8,128)}, u32[]{:S(2)}) copy-start(s32[128,8]{0,1:T(8,128)} %param.22) | copy-start | bytes 12292
  0.0 16.9 %copy-start.11 = (s32[128]{0:T(128)S(1)}, s32[128]{0:T(128)}, u32[]{:S(2)}) copy-start(s32[128]{0:T(128)} %param.25) | copy-start | bytes 1540
  0.0 16.9 %copy-start.10 = (s32[128]{0:T(128)S(1)}, s32[128]{0:T(128)}, u32[]{:S(2)}) copy-start(s32[128]{0:T(128)} %param.24) | copy-start | bytes 1540
  10.4 13.8 %copy-start.1 = (bf16[128,1024]{1,0:T(8,128)(2,1)S(1)}, bf16[128,1024]{1,0:T(8,128)(2,1)}, u32[]{:S(2)}) copy-start(bf16[128,1024]{1,0:T(8,128)(2,1)} %param.15) | copy-start | bytes 786436
  12.9 11.5 %copy-start.2 = (f32[1024]{0:T(1024)S(1)}, f32[1024]{0:T(1024)}, u32[]{:S(2)}) copy-start(f32[1024]{0:T(1024)} %param.17) | copy-start | bytes 12292
  12.9 11.3 %all-to-all-start = ((f32[2,128,512]{2,1,0:T(8,128)}), f32[2,128,512]{2,1,0:T(8,128)S(1)}, u32[]{:S(2)}, u32[]{:S(2)}) async-start(f32[2,128,512]{2,1,0:T(8,128)} %bitcast), calls=%async_computation | async-start | bytes 1048576 | tf_op jit(solution)/shard_map/all_to_all | solution.py:40
  79.5 2.4 %copy-start.7 = (bf16[1,512,1024]{2,1,0:T(8,128)(2,1)S(1)}, bf16[1,512,1024]{2,1,0:T(8,128)(2,1)}, u32[]{:S(2)}) copy-start(bf16[1,512,1024]{2,1,0:T(8,128)(2,1)} %param.20) | copy-start | bytes 3145732
  84.4 3.7 %copy-start.6 = (f32[128,8]{0,1:T(8,128)S(1)}, f32[128,8]{0,1:T(8,128)}, u32[]{:S(2)}) copy-start(f32[128,8]{0,1:T(8,128)} %param.27) | copy-start | bytes 12292
  84.4 53.7 %all-to-all-start.2 = ((bf16[32,32,1024]{2,1,0:T(8,128)(2,1)}), bf16[32,32,1024]{2,1,0:T(8,128)(2,1)}, u32[]{:S(2)}, u32[]{:S(2)}) async-start(bf16[32,32,1024]{2,1,0:T(8,128)(2,1)} %bitcast.22), calls=%async_computation.2 | async-start | bytes 4194304 | tf_op jit(solution)/shard_map/all_to_all | solution.py:93
  88.0 52.8 %copy-start.3 = (f32[1024]{0:T(1024)S(1)}, f32[1024]{0:T(1024)}, u32[]{:S(2)}) copy-start(f32[1024]{0:T(1024)} %param.18) | copy-start | bytes 12292

commit v2 on v1

v2 whole, which is shorter than its diff:
```python
import jax
import jax.numpy as jnp
import numpy as np
from jax import lax
from jax.sharding import Mesh
from jax.sharding import PartitionSpec as P

ROWS_AXES = ("grp", "eh", "el")
SLOT_AXES = ("eh", "el")
PLANE_AXES = ("grp", "el")


def rms_scale(values, gain):
    meansq = jnp.mean(values * values, axis=-1, keepdims=True)
    return values * lax.rsqrt(meansq + 1e-06) * gain


def on_device(
    attention,
    residual,
    out_proj,
    pre_gain,
    post_gain,
    slot_gate_up,
    slot_down,
    expert_ids,
    copy_choice,
    placement,
    request_age,
    decode_flag,
    capacity,
    route_weight,
):
    groups = lax.axis_size("grp")
    planes = lax.axis_size("eh")
    lanes = lax.axis_size("el")
    owners = planes * lanes
    devices_all = groups * owners
    rows_here = attention.shape[0]
    features = attention.shape[1]
    picks_row = expert_ids.shape[1]
    cap_size = max(2, rows_here * picks_row // devices_all)
    plane_slots = groups * lanes * cap_size
    my_plane = lax.axis_index("eh")

    columns = jnp.dot(
        lax.all_gather(attention, "grp", axis=0, tiled=True),
        out_proj,
        preferred_element_type=jnp.float32,
    )
    attn_proj = lax.all_to_all(columns, "grp", split_axis=0, concat_axis=1, tiled=True)
    hidden_state = (residual.astype(jnp.float32) + attn_proj).astype(jnp.bfloat16)
    normed = rms_scale(hidden_state.astype(jnp.float32), pre_gain).astype(jnp.bfloat16)

    experts_all = placement.shape[0]
    slot_table = jnp.arange(owners, dtype=jnp.int32)
    matches = (placement[None, :] == jnp.arange(experts_all, dtype=jnp.int32)[:, None]).astype(
        jnp.int32
    )
    slot_of = jnp.sum(slot_table[None, :] * matches, axis=1)
    expert_hits = (
        expert_ids[:, :, None] == jnp.arange(experts_all, dtype=jnp.int32)[None, None, :]
    ).astype(jnp.int32)
    slot = jnp.sum(expert_hits * slot_of[None, None, :], axis=2)
    target = copy_choice * owners + slot
    priority = decode_flag * 1048576 + request_age
    order = jnp.arange(rows_here, dtype=jnp.int32)
    ahead_mask = (priority[None, :] > priority[:, None]) | (
        priority[None, :] == priority[:, None]
    ) & (order[None, :] < order[:, None])
    target_onehot = target[:, :, None] == jnp.arange(devices_all, dtype=jnp.int32)[None, None, :]
    target_hits = jnp.sum(target_onehot.astype(jnp.bfloat16), axis=1)
    counts = jnp.dot(
        ahead_mask.astype(jnp.bfloat16), target_hits, preferred_element_type=jnp.float32
    )
    position = jnp.sum(
        jnp.where(target_onehot, counts[:, None, :], 0.0), axis=2
    ).astype(jnp.int32)
    granted = jnp.sum(
        jnp.where(target_onehot, capacity.reshape(-1)[None, None, :], 0), axis=2
    )
    accepted = position < granted
    in_plane = (copy_choice * lanes + slot % lanes) * cap_size + position
    code = jnp.where(accepted, (slot // lanes) * plane_slots + in_plane, planes * plane_slots)
    weights_kept = jnp.where(accepted, route_weight, jnp.float32(0.0))
    meta = jnp.concatenate([code.astype(jnp.float32), weights_kept], axis=1)

    meta_all = lax.all_gather(meta, "eh", axis=0)
    normed_all = lax.all_gather(normed, "eh", axis=0)
    local = meta_all[:, :, :picks_row].astype(jnp.int32) - my_plane * plane_slots
    weights_all = meta_all[:, :, picks_row:]
    slot_ids = jnp.arange(plane_slots, dtype=jnp.int32)
    hit = local[:, None, :, :] == slot_ids[None, :, None, None]
    dispatch = jnp.any(hit, axis=3).astype(jnp.bfloat16)
    buffer = jnp.einsum(
        "hcr,hrd->hcd", dispatch, normed_all, preferred_element_type=jnp.float32
    ).astype(jnp.bfloat16)

    gate_up_local = slot_gate_up[0]
    down_local = slot_down[0]
    hidden_units = down_local.shape[0]
    arrived = lax.all_to_all(
        buffer.reshape(planes, groups * lanes, cap_size, features),
        PLANE_AXES,
        split_axis=1,
        concat_axis=1,
        tiled=True,
    )
    flattened = arrived.reshape(-1, features)
    gate_up = jnp.dot(flattened, gate_up_local, preferred_element_type=jnp.float32)
    expert_hidden = (jax.nn.silu(gate_up[:, :hidden_units]) * gate_up[:, hidden_units:]).astype(
        jnp.bfloat16
    )
    produced = jnp.dot(expert_hidden, down_local, preferred_element_type=jnp.float32).astype(
        jnp.bfloat16
    )
    returned = lax.all_to_all(
        produced.reshape(arrived.shape), PLANE_AXES, split_axis=1, concat_axis=1, tiled=True
    )
    combine = jnp.sum(jnp.where(hit, weights_all[:, None, :, :], 0.0), axis=3)
    partial = jnp.einsum(
        "hcr,hcd->hrd",
        combine,
        returned.reshape(planes, plane_slots, features).astype(jnp.float32),
        precision=lax.Precision.HIGHEST,
        preferred_element_type=jnp.float32,
    )
    mixture = lax.psum_scatter(partial, "eh", scatter_dimension=0, tiled=True)[0]
    return rms_scale(hidden_state.astype(jnp.float32) + mixture, post_gain).astype(jnp.bfloat16)


def plane_split(devices):
    row = devices[0]
    try:
        coords = [tuple(d.coords) for d in row]
    except AttributeError:
        return 1, len(row)
    best = 0
    for axis in range(len(coords[0])):
        changes = [e for e in range(len(row)) if coords[e][axis] != coords[0][axis]]
        if changes:
            best = max(best, changes[0])
    if best == 0 or len(row) % best:
        return 1, len(row)
    return len(row) // best, best


def solution(mesh):
    devices = np.asarray(mesh.devices)
    planes, lanes = plane_split(devices)
    fine = Mesh(devices.reshape(devices.shape[0], planes, lanes), ROWS_AXES)
    rows = P(ROWS_AXES, None)
    placed = (
        rows,
        rows,
        P(None, "grp"),
        P(),
        P(),
        P(SLOT_AXES, None, None),
        P(SLOT_AXES, None, None),
        rows,
        rows,
        P(),
        P(ROWS_AXES),
        P(ROWS_AXES),
        P(),
        rows,
    )
    return jax.shard_map(on_device, mesh=fine, in_specs=placed, out_specs=rows, check_vma=False)
```

time: 142 us -> 184 us (1.30)
  waiting for transfers between devices: 53.5 us -> 86.5 us
  between operations: 0.21 us -> 13.7 us
  blocking collectives: 64.6 us -> 53.2 us
  local copies, waits for them, and re-layouts: 0.37 us -> 3.96 us
  other arithmetic: 4.62 us -> 7.79 us
    reduce_scatter x0 -> x1, waiting for transfers between devices: none -> 42.2 us  [on_device(): lax.psum_scatter(partial, 'eh', scatter_dimension=0, tiled=True)[0]]
    all_to_all x1, blocking collectives: 54.3 us -> 29.5 us  [on_device(): lax.all_to_all(buffer.reshape(planes, groups * lanes, cap_size, features)...]
    all_to_all x1, waiting for transfers between devices: 48.5 us -> 24.2 us  [on_device(): lax.all_to_all(produced.reshape(arrived.shape), PLANE_AXES, split_axis=1,...]
    all_gather x0 -> x1, blocking collectives: none -> 13.4 us  [on_device(): meta_all = lax.all_gather(meta, 'eh', axis=0)]
    all_gather x0 -> x1, waiting for transfers between devices: none -> 12.8 us  [on_device(): normed_all = lax.all_gather(normed, 'eh', axis=0)]
    all_to_all x1, waiting for transfers between devices: 4.99 us -> 7.17 us  [on_device(): lax.all_to_all(columns, 'grp', split_axis=0, concat_axis=1, tiled=True)]
    all_to_all x0 -> x2, local copies, waits for them, and re-layouts: none -> 2.03 us  [the longest x1 1.76 us: on_device(): lax.all_to_all(produced.reshape(arrived.shape), PLANE_AXES, split_axis=1,...]
  transfers between devices with their start and end apart: 2 -> 4, of which waited for: 2 -> 4; matrix products, arithmetic and copies ran while one was open for 3% -> 2% of each run, Pallas kernels for 0% -> 0%
where the time goes in v2:
time: 184 us
  waiting for transfers between devices  86.5 us (47%)
  blocking collectives  53.2 us (29%)
  between operations  13.7 us (7%)
  matrix products  10.8 us (6%)
  starting transfers between devices  8.04 us (4%)
  other arithmetic  7.79 us (4%)
  local copies, waits for them, and re-layouts  3.96 us (2%)
    reduce_scatter x1, waiting for transfers between devices, on_device(): lax.psum_scatter(partial, 'eh', scatter_dimension=0, tiled=True)[0]  42.2 us
    all_to_all x1, blocking collectives, on_device(): lax.all_to_all(buffer.reshape(planes, groups * lanes, cap_size, features)...  29.5 us
    all_to_all x1, waiting for transfers between devices, on_device(): lax.all_to_all(produced.reshape(arrived.shape), PLANE_AXES, split_axis=1,...  24.2 us
    all_gather x1, blocking collectives, on_device(): meta_all = lax.all_gather(meta, 'eh', axis=0)  13.4 us
    all_gather x1, waiting for transfers between devices, on_device(): normed_all = lax.all_gather(normed, 'eh', axis=0)  12.8 us
    all_gather x1, blocking collectives, on_device(): lax.all_gather(attention, 'grp', axis=0, tiled=True)  10.3 us
    all_to_all x1, waiting for transfers between devices, on_device(): lax.all_to_all(columns, 'grp', split_axis=0, concat_axis=1, tiled=True)  7.17 us
    all_to_all x1, starting transfers between devices, on_device(): lax.all_to_all(produced.reshape(arrived.shape), PLANE_AXES, split_axis=1,...  4.34 us
  transfers between devices with their start and end apart: 4, of which 4 were waited for; matrix products, arithmetic and copies ran while one was open for 2% of the time, Pallas kernels for 0%

profile of v2, /device:TPU:0, one launch (start us, length us, event | category | flops | bytes accessed | tf_op | source)
XLA Modules:
  0.0 183.9 jit_solution(9227596970296101772)
XLA Ops:
  6.5 0.0 copy-start
  6.5 0.0 copy-start.11
  6.6 0.0 copy-start.10
  6.6 10.3 %all_gather.15 = bf16[256,1024]{1,0:T(8,128)(2,1)S(1)} all-gather(bf16[128,1024]{1,0:T(8,128)(2,1)} %param.14), channel_id=1, replica_groups=mesh['grp'=2,'eh'=4,'el'=4] {'grp'}, dimensions={0}, use_global_device_ids=true | all-gather | bytes 786432 | tf_op jit(solution)/shard_map/all_gather | solution.py:47
  16.9 2.5 %fusion.32 = f32[256,512]{1,0:T(8,128)} fusion(bf16[256,1024]{1,0:T(8,128)(2,1)S(1)} %all_gather.15, bf16[1024,512]{1,0:T(8,128)(2,1)} %param.16), kind=kOutput, calls=%fused_computation.63 | convolution fusion | flops 268435456 | bytes 2097152 | tf_op jit(solution)/shard_map/dot_general | solution.py:46
  19.4 3.6 %all-to-all-start = ((f32[2,128,512]{2,1,0:T(8,128)}), f32[2,128,512]{2,1,0:T(8,128)S(1)}, u32[]{:S(2)}, u32[]{:S(2)}) async-start(f32[2,128,512]{2,1,0:T(8,128)} %bitcast), calls=%async_computation | async-start | bytes 1048576 | tf_op jit(solution)/shard_map/all_to_all | solution.py:51
  23.0 0.0 all-gather.4.cloned.1.call-start
  23.1 0.0 copy-done.9
  23.1 0.1 select_reduce_fusion.4
  23.2 0.0 copy-done.8
  23.2 0.1 broadcast_in_dim.48
  23.3 0.0 copy-done.5
  23.3 0.1 select_reduce_fusion.3
  23.4 0.0 copy-done.2
  23.4 0.1 select_reduce_fusion.1
  23.5 0.0 copy-done.11
  23.5 0.0 copy-done.10
  23.5 7.2 %all-to-all-done = f32[2,128,512]{2,1,0:T(8,128)S(1)} async-done(((f32[2,128,512]{2,1,0:T(8,128)}), f32[2,128,512]{2,1,0:T(8,128)S(1)}, u32[]{:S(2)}, u32[]{:S(2)}) %all-to-all-start) | async-done | bytes 524320 | tf_op jit(solution)/shard_map/all_to_all | solution.py:51
  30.8 0.0 copy-done.1
  30.8 0.2 fusion.7
  30.9 0.0 copy-done.3
  30.9 0.8 fusion.9
  31.8 0.0 all-gather.4.cloned.1.call-update
  31.8 0.2 fusion.14
  32.1 0.0 copy-done.6
  32.2 13.4 %all-gather = f32[512,16]{0,1:T(8,128)S(1)} all-gather(f32[128,16]{0,1:T(8,128)S(1)} %pad_maximum_fusion), channel_id=2, replica_groups=mesh['grp'=2,'eh'=4,'el'=4] {'eh'}, dimensions={0}, use_global_device_ids=true | all-gather | bytes 40960 | tf_op jit(solution)/shard_map/all_gather | solution.py:88
  45.6 1.9 %fusion = pred[4,256,128]{2,1,0:T(8,128)(4,1)S(1)} fusion(s32[4,128,8]{1,2,0:T(8,128)S(1)} %fusion.18), kind=kLoop, calls=%fused_computation.2 | loop fusion | flops 1966080 | bytes 147456 | tf_op jit(solution)/shard_map/reduce_or | solution.py:94
  47.4 12.8 %all-gather.4.cloned.1.call-done = bf16[512,1024]{1,0:T(8,128)(2,1)} async-done(((bf16[128,1024]{1,0:T(8,128)(2,1)}), bf16[512,1024]{1,0:T(8,128)(2,1)}) %all-gather.4.cloned.1.call-update) | async-done | bytes 1048592 | tf_op jit(solution)/shard_map/all_gather | solution.py:89
  60.3 1.9 %convolution_convert_fusion.1 = bf16[4,256,1024]{2,1,0:T(8,128)(2,1)S(1)} fusion(pred[4,256,128]{2,1,0:T(8,128)(4,1)S(1)} %fusion, bf16[4,128,1024]{2,1,0:T(8,128)(2,1)} %bitcast.37), kind=kOutput, calls=%fused_computation.8 | convolution fusion | flops 269484032 | bytes 3276800 | tf_op jit(solution)/shard_map/hcr,hrd->hcd/dot_general | solution.py:95
  62.2 0.3 copy.57
  62.5 29.5 %all_to_all.29 = bf16[4,8,32,1024]{3,2,0,1:T(8,128)(2,1)S(1)} all-to-all(bf16[4,8,32,1024]{3,2,0,1:T(8,128)(2,1)S(1)} %copy.57), channel_id=1, replica_groups=mesh['grp'=2,'eh'=4,'el'=4] {'grp','el'}, dimensions={1} | all-to-all | bytes 4194304 | tf_op jit(solution)/shard_map/all_to_all | solution.py:102
  91.9 0.3 copy.58
  92.2 0.0 copy-done
  92.2 0.0 copy-start.7
  92.2 2.3 %fusion.2 = f32[1024,1024]{1,0:T(8,128)S(1)} fusion(bf16[1024,1024]{1,0:T(8,128)(2,1)S(1)} %bitcast.33, bf16[1,1024,1024]{2,1,0:T(8,128)(2,1)S(1)} %copy-done), kind=kOutput, calls=%fused_computation.5 | convolution fusion | flops 2147483648 | bytes 8388608 | tf_op jit(solution)/shard_map/dot_general | solution.py:110
  94.6 0.0 copy-done.7
  94.6 1.3 convolution_convert_fusion
  95.9 1.5 copy.59
  97.4 4.3 %all-to-all-start.2 = ((bf16[4,8,32,1024]{3,2,0,1:T(8,128)(2,1)}), bf16[4,8,32,1024]{3,2,0,1:T(8,128)(2,1)}, u32[]{:S(2)}, u32[]{:S(2)}) async-start(bf16[4,8,32,1024]{3,2,0,1:T(8,128)(2,1)} %copy.59), calls=%async_computation.2 | async-start | bytes 4194304 | tf_op jit(solution)/shard_map/all_to_all | solution.py:117
  101.7 0.0 reduce-scatter.2.cloned.1.call-start
  101.8 1.4 select_reduce_fusion
  103.2 24.2 %all-to-all-done.2 = bf16[4,8,32,1024]{3,2,0,1:T(8,128)(2,1)} async-done(((bf16[4,8,32,1024]{3,2,0,1:T(8,128)(2,1)}), bf16[4,8,32,1024]{3,2,0,1:T(8,128)(2,1)}, u32[]{:S(2)}, u32[]{:S(2)}) %all-to-all-start.2) | async-done | bytes 2097184 | tf_op jit(solution)/shard_map/all_to_all | solution.py:117
  127.4 1.8 copy.60
  129.2 2.5 %fusion.33 = f32[4,128,1024]{2,1,0:T(8,128)} fusion(f32[4,256,128]{2,1,0:T(8,128)S(1)} %select_reduce_fusion, bf16[4,256,1024]{2,1,0:T(8,128)(2,1)S(1)} %bitcast.32), kind=kOutput, calls=%fused_computation.64 | convolution fusion | flops 1610612736 | bytes 4718592 | tf_op jit(solution)/shard_map/hcr,hcd->hrd/dot_general | solution.py:121
  131.7 0.0 reduce-scatter.2.cloned.1.call-update
  131.7 42.2 %reduce-scatter.2.cloned.1.call-done = f32[1,128,1024]{2,1,0:T(8,128)} async-done(((f32[4,128,1024]{2,1,0:T(8,128)}), f32[1,128,1024]{2,1,0:T(8,128)}) %reduce-scatter.2.cloned.1.call-update) | async-done | bytes 524304 | tf_op jit(solution)/shard_map/reduce_scatter | solution.py:128
  173.9 1.2 multiply_reduce_fusion
  175.2 1.9 %multiply_convert_fusion = bf16[128,1024]{1,0:T(8,128)(2,1)} fusion(f32[1,128,1024]{2,1,0:T(8,128)} %reduce-scatter.2.cloned.1.call-done, bf16[128,1024]{1,0:T(8,128)(2,1)S(1)} %get-tuple-element.6, f32[1024]{0:T(1024)S(1)} %copy-done.4, f32[128]{0:T(128)S(1)} %add_rsqrt_fusion), kind=kLoop, calls=%fused_computation.17 | loop fusion | flops 655360 | bytes 1053184 | tf_op jit(solution)/shard_map/convert_element_type | solution.py:129
  (23 shorter events, 0.2 us)
Async XLA Ops:
  6.5 85.7 %copy-start = (bf16[1,1024,1024]{2,1,0:T(8,128)(2,1)S(1)}, bf16[1,1024,1024]{2,1,0:T(8,128)(2,1)}, u32[]{:S(2)}) copy-start(bf16[1,1024,1024]{2,1,0:T(8,128)(2,1)} %param.19) | copy-start | bytes 6291460
  6.5 16.6 %copy-start.9 = (s32[16]{0:T(128)S(1)}, s32[16]{0:T(128)}, u32[]{:S(2)}) copy-start(s32[16]{0:T(128)} %param.23) | copy-start | bytes 196
  6.5 16.7 %copy-start.8 = (s32[2,16]{1,0:T(2,128)S(1)}, s32[2,16]{1,0:T(2,128)}, u32[]{:S(2)}) copy-start(s32[2,16]{1,0:T(2,128)} %param.26) | copy-start | bytes 388
  6.5 16.8 %copy-start.5 = (s32[128,8]{0,1:T(8,128)S(1)}, s32[128,8]{0,1:T(8,128)}, u32[]{:S(2)}) copy-start(s32[128,8]{0,1:T(8,128)} %param.21) | copy-start | bytes 12292
  6.5 16.8 %copy-start.2 = (s32[128,8]{0,1:T(8,128)S(1)}, s32[128,8]{0,1:T(8,128)}, u32[]{:S(2)}) copy-start(s32[128,8]{0,1:T(8,128)} %param.22) | copy-start | bytes 12292
  6.5 17.0 %copy-start.11 = (s32[128]{0:T(128)S(1)}, s32[128]{0:T(128)}, u32[]{:S(2)}) copy-start(s32[128]{0:T(128)} %param.25) | copy-start | bytes 1540
  6.6 17.0 %copy-start.10 = (s32[128]{0:T(128)S(1)}, s32[128]{0:T(128)}, u32[]{:S(2)}) copy-start(s32[128]{0:T(128)} %param.24) | copy-start | bytes 1540
  16.9 13.8 %copy-start.1 = (bf16[128,1024]{1,0:T(8,128)(2,1)S(1)}, bf16[128,1024]{1,0:T(8,128)(2,1)}, u32[]{:S(2)}) copy-start(bf16[128,1024]{1,0:T(8,128)(2,1)} %param.15) | copy-start | bytes 786436
  19.4 11.5 %copy-start.3 = (f32[1024]{0:T(1024)S(1)}, f32[1024]{0:T(1024)}, u32[]{:S(2)}) copy-start(f32[1024]{0:T(1024)} %param.17) | copy-start | bytes 12292
  19.4 12.7 %copy-start.6 = (f32[128,8]{0,1:T(8,128)S(1)}, f32[128,8]{0,1:T(8,128)}, u32[]{:S(2)}) copy-start(f32[128,8]{0,1:T(8,128)} %param.27) | copy-start | bytes 12292
  19.4 11.3 %all-to-all-start = ((f32[2,128,512]{2,1,0:T(8,128)}), f32[2,128,512]{2,1,0:T(8,128)S(1)}, u32[]{:S(2)}, u32[]{:S(2)}) async-start(f32[2,128,512]{2,1,0:T(8,128)} %bitcast), calls=%async_computation | async-start | bytes 1048576 | tf_op jit(solution)/shard_map/all_to_all | solution.py:51
  23.0 37.2 %all-gather.4.cloned.1.call-start = ((), (), s32[]{:S(2)}) async-start(), calls=%async_computation.5 | async-start | bytes 1310720 | tf_op jit(solution)/shard_map/all_gather | solution.py:89
  92.2 2.4 %copy-start.7 = (bf16[1,512,1024]{2,1,0:T(8,128)(2,1)S(1)}, bf16[1,512,1024]{2,1,0:T(8,128)(2,1)}, u32[]{:S(2)}) copy-start(bf16[1,512,1024]{2,1,0:T(8,128)(2,1)} %param.20) | copy-start | bytes 3145732
  97.4 30.1 %all-to-all-start.2 = ((bf16[4,8,32,1024]{3,2,0,1:T(8,128)(2,1)}), bf16[4,8,32,1024]{3,2,0,1:T(8,128)(2,1)}, u32[]{:S(2)}, u32[]{:S(2)}) async-start(bf16[4,8,32,1024]{3,2,0,1:T(8,128)(2,1)} %copy.59), calls=%async_computation.2 | async-start | bytes 4194304 | tf_op jit(solution)/shard_map/all_to_all | solution.py:117
  101.7 72.2 %reduce-scatter.2.cloned.1.call-start = ((), (), s32[]{:S(2)}) async-start(), calls=%async_computation.4 | async-start | bytes 2621440 | tf_op jit(solution)/shard_map/reduce_scatter | solution.py:128
  131.7 43.5 %copy-start.4 = (f32[1024]{0:T(1024)S(1)}, f32[1024]{0:T(1024)}, u32[]{:S(2)}) copy-start(f32[1024]{0:T(1024)} %param.18) | copy-start | bytes 12292
Sparse Core Ops, SparseCore 0:
  31.9 28.2 all-gather.3
  131.8 42.0 reduce-scatter.1

commit v3 on v2

--- a/solution.py
+++ b/solution.py
@@ -83,12 +83,35 @@
     in_plane = (copy_choice * lanes + slot % lanes) * cap_size + position
     code = jnp.where(accepted, (slot // lanes) * plane_slots + in_plane, planes * plane_slots)
     weights_kept = jnp.where(accepted, route_weight, jnp.float32(0.0))
-    meta = jnp.concatenate([code.astype(jnp.float32), weights_kept], axis=1)
-
-    meta_all = lax.all_gather(meta, "eh", axis=0)
-    normed_all = lax.all_gather(normed, "eh", axis=0)
-    local = meta_all[:, :, :picks_row].astype(jnp.int32) - my_plane * plane_slots
-    weights_all = meta_all[:, :, picks_row:]
+    code_hi = (code // 128).astype(jnp.bfloat16)
+    code_lo = (code % 128).astype(jnp.bfloat16)
+    w_first = lax.reduce_precision(weights_kept, exponent_bits=8, mantissa_bits=7)
+    w_rest = weights_kept - w_first
+    w_second = lax.reduce_precision(w_rest, exponent_bits=8, mantissa_bits=7)
+    w_third = w_rest - w_second
+    meta = jnp.concatenate(
+        [code_hi, code_lo]
+        + [part.astype(jnp.bfloat16) for part in (w_first, w_second, w_third)],
+        axis=1,
+    )
+    meta_size = rows_here * meta.shape[1]
+    meta_rows = -(-meta_size // (8 * features)) * 8
+    meta_block = jnp.pad(meta.reshape(-1), (0, meta_rows * features - meta_size))
+    packed = jnp.concatenate([normed, meta_block.reshape(meta_rows, features)], axis=0)
+    packed_all = lax.all_gather(packed, "eh", axis=0)
+    normed_all = packed_all[:, :rows_here]
+    meta_all = (
+        packed_all[:, rows_here:]
+        .reshape(planes, -1)[:, :meta_size]
+        .reshape(planes, rows_here, meta.shape[1])
+        .astype(jnp.float32)
+    )
+    code_all = meta_all[:, :, :picks_row] * 128 + meta_all[:, :, picks_row : 2 * picks_row]
+    local = code_all.astype(jnp.int32) - my_plane * plane_slots
+    weights_all = (
+        meta_all[:, :, 2 * picks_row : 3 * picks_row]
+        + meta_all[:, :, 3 * picks_row : 4 * picks_row]
+    ) + meta_all[:, :, 4 * picks_row :]
     slot_ids = jnp.arange(plane_slots, dtype=jnp.int32)
     hit = local[:, None, :, :] == slot_ids[None, :, None, None]
     dispatch = jnp.any(hit, axis=3).astype(jnp.bfloat16)
@@ -125,7 +148,9 @@
         precision=lax.Precision.HIGHEST,
         preferred_element_type=jnp.float32,
     )
-    mixture = lax.psum_scatter(partial, "eh", scatter_dimension=0, tiled=True)[0]
+    mixture = lax.psum_scatter(
+        partial.astype(jnp.bfloat16), "eh", scatter_dimension=0, tiled=True
+    )[0].astype(jnp.float32)
     return rms_scale(hidden_state.astype(jnp.float32) + mixture, post_gain).astype(jnp.bfloat16)
 
 

time: 184 us -> 172 us (0.935)
  blocking collectives: 53.2 us -> 39.8 us
    all_gather x1, waiting for transfers between devices: 12.8 us -> 29.4 us  [on_device(): packed_all = lax.all_gather(packed, 'eh', axis=0)]
    reduce_scatter x1, waiting for transfers between devices: 42.2 us -> 25.9 us  [on_device(): lax.psum_scatter(partial.astype(jnp.bfloat16), 'eh', scatter_dimension=0,...]
    all_gather x1 -> x0, blocking collectives: 13.4 us -> none  [on_device(): meta_all = lax.all_gather(meta, 'eh', axis=0)]
  transfers between devices with their start and end apart: 4 -> 4, of which waited for: 4 -> 4; matrix products, arithmetic and copies ran while one was open for 2% -> 1% of each run, Pallas kernels for 0% -> 0%
where the time goes in v3:
time: 172 us
  waiting for transfers between devices  85.9 us (50%)
  blocking collectives  39.8 us (23%)
  between operations  13.7 us (8%)
  matrix products  10.4 us (6%)
  other arithmetic  8.07 us (5%)
  starting transfers between devices  8.04 us (5%)
  local copies, waits for them, and re-layouts  5.58 us (3%)
    all_to_all x1, blocking collectives, on_device(): lax.all_to_all(buffer.reshape(planes, groups * lanes, cap_size, features)...  29.5 us
    all_gather x1, waiting for transfers between devices, on_device(): packed_all = lax.all_gather(packed, 'eh', axis=0)  29.4 us
    reduce_scatter x1, waiting for transfers between devices, on_device(): lax.psum_scatter(partial.astype(jnp.bfloat16), 'eh', scatter_dimension=0,...  25.9 us
    all_to_all x1, waiting for transfers between devices, on_device(): lax.all_to_all(produced.reshape(arrived.shape), PLANE_AXES, split_axis=1,...  24.1 us
    all_gather x1, blocking collectives, on_device(): lax.all_gather(attention, 'grp', axis=0, tiled=True)  10.3 us
    all_to_all x1, waiting for transfers between devices, on_device(): lax.all_to_all(columns, 'grp', split_axis=0, concat_axis=1, tiled=True)  6.49 us
    all_to_all x1, starting transfers between devices, on_device(): lax.all_to_all(produced.reshape(arrived.shape), PLANE_AXES, split_axis=1,...  4.34 us
    all_to_all x1, starting transfers between devices, on_device(): lax.all_to_all(columns, 'grp', split_axis=0, concat_axis=1, tiled=True)  3.62 us
  transfers between devices with their start and end apart: 4, of which 4 were waited for; matrix products, arithmetic and copies ran while one was open for 1% of the time, Pallas kernels for 0%

profile of v3, /device:TPU:0, one launch (start us, length us, event | category | flops | bytes accessed | tf_op | source)
XLA Modules:
  0.0 171.6 jit_solution(14408575570016139125)
XLA Ops:
  6.5 0.0 copy-start.11
  6.6 0.0 copy-start.8
  6.6 0.0 copy-start.2
  6.6 10.3 %all_gather.9 = bf16[256,1024]{1,0:T(8,128)(2,1)S(1)} all-gather(bf16[128,1024]{1,0:T(8,128)(2,1)} %param.14), channel_id=1, replica_groups=mesh['grp'=2,'eh'=4,'el'=4] {'grp'}, dimensions={0}, use_global_device_ids=true | all-gather | bytes 786432 | tf_op jit(solution)/shard_map/all_gather | solution.py:47
  16.9 2.5 %fusion.37 = f32[256,512]{1,0:T(8,128)} fusion(bf16[256,1024]{1,0:T(8,128)(2,1)S(1)} %all_gather.9, bf16[1024,512]{1,0:T(8,128)(2,1)} %param.16), kind=kOutput, calls=%fused_computation.86 | convolution fusion | flops 268435456 | bytes 2097152 | tf_op jit(solution)/shard_map/dot_general | solution.py:46
  19.4 3.6 %all-to-all-start = ((f32[2,128,512]{2,1,0:T(8,128)}), f32[2,128,512]{2,1,0:T(8,128)S(1)}, u32[]{:S(2)}, u32[]{:S(2)}) async-start(f32[2,128,512]{2,1,0:T(8,128)} %bitcast), calls=%async_computation | async-start | bytes 1048576 | tf_op jit(solution)/shard_map/all_to_all | solution.py:51
  23.0 0.0 all-gather.3.cloned.1.call-start
  23.1 0.0 copy-done.9
  23.1 0.1 select_reduce_fusion.4
  23.2 0.1 select_reduce_fusion.3
  23.4 0.2 fusion.15
  23.7 0.1 broadcast_in_dim.48
  23.7 0.1 select_reduce_fusion.1
  23.9 0.1 copy.51
  24.1 0.1 reshape.57
  24.2 6.5 %all-to-all-done = f32[2,128,512]{2,1,0:T(8,128)S(1)} async-done(((f32[2,128,512]{2,1,0:T(8,128)}), f32[2,128,512]{2,1,0:T(8,128)S(1)}, u32[]{:S(2)}, u32[]{:S(2)}) %all-to-all-start) | async-done | bytes 524320 | tf_op jit(solution)/shard_map/all_to_all | solution.py:51
  30.8 0.2 fusion.8
  30.9 0.1 fusion.10
  31.1 0.7 pad_maximum_fusion
  31.8 0.0 all-gather.3.cloned.1.call-update
  31.8 29.4 %all-gather.3.cloned.1.call-done = bf16[544,1024]{1,0:T(8,128)(2,1)} async-done(((bf16[136,1024]{1,0:T(8,128)(2,1)}), bf16[544,1024]{1,0:T(8,128)(2,1)}) %all-gather.3.cloned.1.call-update) | async-done | bytes 1114128 | tf_op jit(solution)/shard_map/all_gather | solution.py:101
  61.3 0.8 slice_bitcast_fusion
  62.1 0.1 copy.64
  62.2 0.2 reshape.64
  62.4 0.3 fusion.36
  62.7 0.1 copy.61
  62.8 0.1 copy.62
  63.0 1.9 %fusion = pred[4,256,128]{2,1,0:T(8,128)(4,1)S(1)} fusion(s32[4,128,8]{1,2,0:T(8,128)S(1)} %convert_subtract_fusion), kind=kLoop, calls=%fused_computation.2 | loop fusion | flops 1966080 | bytes 147456 | tf_op jit(solution)/shard_map/reduce_or | solution.py:117
  64.8 1.9 %convolution_convert_fusion.1 = bf16[4,256,1024]{2,1,0:T(8,128)(2,1)S(1)} fusion(pred[4,256,128]{2,1,0:T(8,128)(4,1)S(1)} %fusion, bf16[4,136,1024]{2,1,0:T(8,128)(2,1)} %bitcast.36), kind=kOutput, calls=%fused_computation.8 | convolution fusion | flops 269484032 | bytes 3276800 | tf_op jit(solution)/shard_map/hcr,hrd->hcd/dot_general | solution.py:118
  66.8 0.3 copy.55
  67.1 29.5 %all_to_all.29 = bf16[4,8,32,1024]{3,2,0,1:T(8,128)(2,1)S(1)} all-to-all(bf16[4,8,32,1024]{3,2,0,1:T(8,128)(2,1)S(1)} %copy.55), channel_id=1, replica_groups=mesh['grp'=2,'eh'=4,'el'=4] {'grp','el'}, dimensions={1} | all-to-all | bytes 4194304 | tf_op jit(solution)/shard_map/all_to_all | solution.py:125
  96.5 0.3 copy.56
  96.8 0.0 copy-start.7
  96.8 2.3 %fusion.2 = f32[1024,1024]{1,0:T(8,128)S(1)} fusion(bf16[1024,1024]{1,0:T(8,128)(2,1)S(1)} %bitcast.31, bf16[1,1024,1024]{2,1,0:T(8,128)(2,1)S(1)} %copy-done), kind=kOutput, calls=%fused_computation.5 | convolution fusion | flops 2147483648 | bytes 8388608 | tf_op jit(solution)/shard_map/dot_general | solution.py:133
  99.2 1.3 convolution_convert_fusion
  100.5 1.5 copy.57
  102.0 4.3 %all-to-all-start.2 = ((bf16[4,8,32,1024]{3,2,0,1:T(8,128)(2,1)}), bf16[4,8,32,1024]{3,2,0,1:T(8,128)(2,1)}, u32[]{:S(2)}, u32[]{:S(2)}) async-start(bf16[4,8,32,1024]{3,2,0,1:T(8,128)(2,1)} %copy.57), calls=%async_computation.2 | async-start | bytes 4194304 | tf_op jit(solution)/shard_map/all_to_all | solution.py:140
  106.3 0.0 reduce-scatter.2.cloned.1.call-start
  106.4 0.1 copy.54
  106.4 1.5 select_reduce_fusion
  107.9 24.1 %all-to-all-done.2 = bf16[4,8,32,1024]{3,2,0,1:T(8,128)(2,1)} async-done(((bf16[4,8,32,1024]{3,2,0,1:T(8,128)(2,1)}), bf16[4,8,32,1024]{3,2,0,1:T(8,128)(2,1)}, u32[]{:S(2)}, u32[]{:S(2)}) %all-to-all-start.2) | async-done | bytes 2097184 | tf_op jit(solution)/shard_map/all_to_all | solution.py:140
  132.0 1.8 %copy.58 = bf16[4,8,32,1024]{3,2,1,0:T(8,128)(2,1)S(1)} copy(bf16[4,8,32,1024]{3,2,0,1:T(8,128)(2,1)} %all-to-all-done.2) | data formatting | bytes 4194304 | tf_op jit(solution)/shard_map/all_to_all | solution.py:140
  133.8 0.0 copy-start.5
  133.8 2.1 %convolution_convert_fusion.2 = bf16[4,128,1024]{2,1,0:T(8,128)(2,1)} fusion(f32[4,256,128]{2,1,0:T(8,128)S(1)} %select_reduce_fusion, bf16[4,256,1024]{2,1,0:T(8,128)(2,1)S(1)} %bitcast.29), kind=kOutput, calls=%fused_computation.9 | convolution fusion | flops 1611137024 | bytes 3670016 | tf_op jit(solution)/shard_map/hcr,hcd->hrd/dot_general | solution.py:144
  135.9 0.0 reduce-scatter.2.cloned.1.call-update
  135.9 25.9 %reduce-scatter.2.cloned.1.call-done = bf16[1,128,1024]{2,1,0:T(8,128)(2,1)} async-done(((bf16[4,128,1024]{2,1,0:T(8,128)(2,1)}), bf16[1,128,1024]{2,1,0:T(8,128)(2,1)}) %reduce-scatter.2.cloned.1.call-update) | async-done | bytes 262160 | tf_op jit(solution)/shard_map/reduce_scatter | solution.py:151
  161.8 1.1 multiply_reduce_fusion
  162.9 1.8 %multiply_convert_fusion = bf16[128,1024]{1,0:T(8,128)(2,1)} fusion(bf16[128,1024]{1,0:T(8,128)(2,1)S(1)} %get-tuple-element.6, bf16[1,128,1024]{2,1,0:T(8,128)(2,1)} %reduce-scatter.2.cloned.1.call-done, f32[1024]{0:T(1024)S(1)} %copy-done.5, f32[128]{0:T(128)S(1)} %add_rsqrt_fusion), kind=kLoop, calls=%fused_computation.19 | loop fusion | flops 786432 | bytes 791040 | tf_op jit(solution)/shard_map/convert_element_type | solution.py:154
  (34 shorter events, 0.3 us)
Async XLA Ops:
  6.5 90.3 %copy-start = (bf16[1,1024,1024]{2,1,0:T(8,128)(2,1)S(1)}, bf16[1,1024,1024]{2,1,0:T(8,128)(2,1)}, u32[]{:S(2)}) copy-start(bf16[1,1024,1024]{2,1,0:T(8,128)(2,1)} %param.19) | copy-start | bytes 6291460
  6.5 16.6 %copy-start.9 = (s32[16]{0:T(128)S(1)}, s32[16]{0:T(128)}, u32[]{:S(2)}) copy-start(s32[16]{0:T(128)} %param.23) | copy-start | bytes 196
  6.5 16.7 %copy-start.6 = (s32[128,8]{0,1:T(8,128)S(1)}, s32[128,8]{0,1:T(8,128)}, u32[]{:S(2)}) copy-start(s32[128,8]{0,1:T(8,128)} %param.21) | copy-start | bytes 12292
  6.5 16.8 %copy-start.3 = (s32[128,8]{0,1:T(8,128)S(1)}, s32[128,8]{0,1:T(8,128)}, u32[]{:S(2)}) copy-start(s32[128,8]{0,1:T(8,128)} %param.22) | copy-start | bytes 12292
  6.5 16.8 %copy-start.10 = (s32[128]{0:T(128)S(1)}, s32[128]{0:T(128)}, u32[]{:S(2)}) copy-start(s32[128]{0:T(128)} %param.24) | copy-start | bytes 1540
  6.5 16.8 %copy-start.11 = (s32[128]{0:T(128)S(1)}, s32[128]{0:T(128)}, u32[]{:S(2)}) copy-start(s32[128]{0:T(128)} %param.25) | copy-start | bytes 1540
  6.6 17.1 %copy-start.8 = (s32[2,16]{1,0:T(2,128)S(1)}, s32[2,16]{1,0:T(2,128)}, u32[]{:S(2)}) copy-start(s32[2,16]{1,0:T(2,128)} %param.26) | copy-start | bytes 388
  6.6 17.3 %copy-start.2 = (f32[128,8]{0,1:T(8,128)S(1)}, f32[128,8]{0,1:T(8,128)}, u32[]{:S(2)}) copy-start(f32[128,8]{0,1:T(8,128)} %param.27) | copy-start | bytes 12292
  16.9 13.8 %copy-start.1 = (bf16[128,1024]{1,0:T(8,128)(2,1)S(1)}, bf16[128,1024]{1,0:T(8,128)(2,1)}, u32[]{:S(2)}) copy-start(bf16[128,1024]{1,0:T(8,128)(2,1)} %param.15) | copy-start | bytes 786436
  19.4 11.5 %copy-start.4 = (f32[1024]{0:T(1024)S(1)}, f32[1024]{0:T(1024)}, u32[]{:S(2)}) copy-start(f32[1024]{0:T(1024)} %param.17) | copy-start | bytes 12292
  19.4 11.3 %all-to-all-start = ((f32[2,128,512]{2,1,0:T(8,128)}), f32[2,128,512]{2,1,0:T(8,128)S(1)}, u32[]{:S(2)}, u32[]{:S(2)}) async-start(f32[2,128,512]{2,1,0:T(8,128)} %bitcast), calls=%async_computation | async-start | bytes 1048576 | tf_op jit(solution)/shard_map/all_to_all | solution.py:51
  23.0 38.2 %all-gather.3.cloned.1.call-start = ((), (), s32[]{:S(2)}) async-start(), calls=%async_computation.5 | async-start | bytes 1392640 | tf_op jit(solution)/shard_map/all_gather | solution.py:101
  96.8 2.4 %copy-start.7 = (bf16[1,512,1024]{2,1,0:T(8,128)(2,1)S(1)}, bf16[1,512,1024]{2,1,0:T(8,128)(2,1)}, u32[]{:S(2)}) copy-start(bf16[1,512,1024]{2,1,0:T(8,128)(2,1)} %param.20) | copy-start | bytes 3145732
  102.0 30.1 %all-to-all-start.2 = ((bf16[4,8,32,1024]{3,2,0,1:T(8,128)(2,1)}), bf16[4,8,32,1024]{3,2,0,1:T(8,128)(2,1)}, u32[]{:S(2)}, u32[]{:S(2)}) async-start(bf16[4,8,32,1024]{3,2,0,1:T(8,128)(2,1)} %copy.57), calls=%async_computation.2 | async-start | bytes 4194304 | tf_op jit(solution)/shard_map/all_to_all | solution.py:140
  106.3 55.5 %reduce-scatter.2.cloned.1.call-start = ((), (), s32[]{:S(2)}) async-start(), calls=%async_computation.4 | async-start | bytes 1310720 | tf_op jit(solution)/shard_map/reduce_scatter | solution.py:151
  133.8 29.2 %copy-start.5 = (f32[1024]{0:T(1024)S(1)}, f32[1024]{0:T(1024)}, u32[]{:S(2)}) copy-start(f32[1024]{0:T(1024)} %param.18) | copy-start | bytes 12292
Sparse Core Ops, SparseCore 0:
  32.0 29.2 all-gather.2
  136.1 25.7 reduce-scatter.1

commit v4 on v3

--- a/solution.py
+++ b/solution.py
@@ -98,7 +98,9 @@
     meta_rows = -(-meta_size // (8 * features)) * 8
     meta_block = jnp.pad(meta.reshape(-1), (0, meta_rows * features - meta_size))
     packed = jnp.concatenate([normed, meta_block.reshape(meta_rows, features)], axis=0)
-    packed_all = lax.all_gather(packed, "eh", axis=0)
+    packed_all = lax.all_to_all(
+        jnp.broadcast_to(packed[None], (planes,) + packed.shape), "eh", 0, 0, tiled=True
+    )
     normed_all = packed_all[:, :rows_here]
     meta_all = (
         packed_all[:, rows_here:]
@@ -148,9 +150,10 @@
         precision=lax.Precision.HIGHEST,
         preferred_element_type=jnp.float32,
     )
-    mixture = lax.psum_scatter(
-        partial.astype(jnp.bfloat16), "eh", scatter_dimension=0, tiled=True
-    )[0].astype(jnp.float32)
+    mixture = jnp.sum(
+        lax.all_to_all(partial.astype(jnp.bfloat16), "eh", 0, 0, tiled=True).astype(jnp.float32),
+        axis=0,
+    )
     return rms_scale(hidden_state.astype(jnp.float32) + mixture, post_gain).astype(jnp.bfloat16)
 
 

time: 172 us -> 160 us (0.930)
  waiting for transfers between devices: 85.9 us -> 56.1 us
  blocking collectives: 39.8 us -> 67.2 us
  between operations: 13.7 us -> 0.35 us
  starting transfers between devices: 8.04 us -> 12.9 us
  local copies, waits for them, and re-layouts: 5.58 us -> 8.44 us
  matrix products: 10.4 us -> 8.17 us
    all_gather x1 -> x0, waiting for transfers between devices: 29.4 us -> none  [on_device(): packed_all = lax.all_gather(packed, 'eh', axis=0)]
    all_to_all x0 -> x1, blocking collectives: none -> 28.3 us  [on_device(): lax.all_to_all(partial.astype(jnp.bfloat16), 'eh', 0, 0, tiled=True)]
    reduce_scatter x1 -> x0, waiting for transfers between devices: 25.9 us -> none  [on_device(): lax.psum_scatter(partial.astype(jnp.bfloat16), 'eh', scatter_dimension=0,...]
    all_to_all x0 -> x1, waiting for transfers between devices: none -> 25.4 us  [on_device(): lax.all_to_all(jnp.broadcast_to(packed[None], (planes,) + packed.shape),...]
    all_to_all x0 -> x1, starting transfers between devices: none -> 4.78 us  [on_device(): lax.all_to_all(jnp.broadcast_to(packed[None], (planes,) + packed.shape),...]
    unnamed x28 -> x34, local copies, waits for them, and re-layouts: 1.15 us -> 2.89 us
  transfers between devices with their start and end apart: 4 -> 3, of which waited for: 4 -> 3; matrix products, arithmetic and copies ran while one was open for 1% -> 2% of each run, Pallas kernels for 0% -> 0%
where the time goes in v4:
time: 160 us
  blocking collectives  67.2 us (42%)
  waiting for transfers between devices  56.1 us (35%)
  starting transfers between devices  12.9 us (8%)
  local copies, waits for them, and re-layouts  8.44 us (5%)
  matrix products  8.17 us (5%)
  other arithmetic  6.44 us (4%)
    all_to_all x1, blocking collectives, on_device(): lax.all_to_all(buffer.reshape(planes, groups * lanes, cap_size, features)...  28.6 us
    all_to_all x1, blocking collectives, on_device(): lax.all_to_all(partial.astype(jnp.bfloat16), 'eh', 0, 0, tiled=True)  28.3 us
    all_to_all x1, waiting for transfers between devices, on_device(): lax.all_to_all(jnp.broadcast_to(packed[None], (planes,) + packed.shape),...  25.4 us
    all_to_all x1, waiting for transfers between devices, on_device(): lax.all_to_all(produced.reshape(arrived.shape), PLANE_AXES, split_axis=1,...  24.1 us
    all_gather x1, blocking collectives, on_device(): lax.all_gather(attention, 'grp', axis=0, tiled=True)  10.3 us
    all_to_all x1, waiting for transfers between devices, on_device(): lax.all_to_all(columns, 'grp', split_axis=0, concat_axis=1, tiled=True)  6.54 us
    all_to_all x1, starting transfers between devices, on_device(): lax.all_to_all(jnp.broadcast_to(packed[None], (planes,) + packed.shape),...  4.78 us
    all_to_all x1, starting transfers between devices, on_device(): lax.all_to_all(produced.reshape(arrived.shape), PLANE_AXES, split_axis=1,...  4.47 us
  transfers between devices with their start and end apart: 3, of which 3 were waited for; matrix products, arithmetic and copies ran while one was open for 2% of the time, Pallas kernels for 0%

profile of v4, /device:TPU:0, one launch (start us, length us, event | category | flops | bytes accessed | tf_op | source)
XLA Modules:
  0.0 159.6 jit_solution(7039064132969043733)
XLA Ops:
  0.0 0.0 copy-start.13
  0.0 0.0 copy-start.14
  0.0 0.0 copy-start.11
  0.0 0.0 copy-start.5
  0.1 10.3 %all_gather.3 = bf16[256,1024]{1,0:T(8,128)(2,1)S(1)} all-gather(bf16[128,1024]{1,0:T(8,128)(2,1)} %param.14), channel_id=1, replica_groups=mesh['grp'=2,'eh'=4,'el'=4] {'grp'}, dimensions={0}, use_global_device_ids=true | all-gather | bytes 786432 | tf_op jit(solution)/shard_map/all_gather | solution.py:47
  10.4 2.5 %fusion.37 = f32[256,512]{1,0:T(8,128)} fusion(bf16[256,1024]{1,0:T(8,128)(2,1)S(1)} %all_gather.3, bf16[1024,512]{1,0:T(8,128)(2,1)} %param.16), kind=kOutput, calls=%fused_computation.87 | convolution fusion | flops 268435456 | bytes 2097152 | tf_op jit(solution)/shard_map/dot_general | solution.py:46
  12.9 3.6 %all-to-all-start = ((f32[2,128,512]{2,1,0:T(8,128)}), f32[2,128,512]{2,1,0:T(8,128)S(1)}, u32[]{:S(2)}, u32[]{:S(2)}) async-start(f32[2,128,512]{2,1,0:T(8,128)} %bitcast), calls=%async_computation | async-start | bytes 1048576 | tf_op jit(solution)/shard_map/all_to_all | solution.py:51
  16.5 0.1 select_reduce_fusion.4
  16.7 0.0 copy-done.9
  16.7 0.1 select_reduce_fusion.3
  16.8 0.0 copy-done.13
  16.8 0.2 fusion.15
  17.1 0.1 broadcast_in_dim.46
  17.2 0.1 select_reduce_fusion.1
  17.4 0.1 copy.51
  17.5 0.1 reshape.56
  17.7 6.5 %all-to-all-done = f32[2,128,512]{2,1,0:T(8,128)S(1)} async-done(((f32[2,128,512]{2,1,0:T(8,128)}), f32[2,128,512]{2,1,0:T(8,128)S(1)}, u32[]{:S(2)}, u32[]{:S(2)}) %all-to-all-start) | async-done | bytes 524320 | tf_op jit(solution)/shard_map/all_to_all | solution.py:51
  24.2 0.2 fusion.8
  24.4 0.7 copy-done.1
  25.1 0.1 fusion.10
  25.3 1.1 broadcast_in_dim.81
  26.4 4.8 %all-to-all-start.1 = ((bf16[4,136,1024]{2,1,0:T(8,128)(2,1)}), bf16[4,136,1024]{2,1,0:T(8,128)(2,1)S(1)}, u32[]{:S(2)}, u32[]{:S(2)}) async-start(bf16[4,136,1024]{2,1,0:T(8,128)(2,1)} %broadcast_in_dim.81), calls=%async_computation.1 | async-start | bytes 2228224 | tf_op jit(solution)/shard_map/all_to_all | solution.py:101
  31.2 25.4 %all-to-all-done.1 = bf16[4,136,1024]{2,1,0:T(8,128)(2,1)S(1)} async-done(((bf16[4,136,1024]{2,1,0:T(8,128)(2,1)}), bf16[4,136,1024]{2,1,0:T(8,128)(2,1)S(1)}, u32[]{:S(2)}, u32[]{:S(2)}) %all-to-all-start.1) | async-done | bytes 1114144 | tf_op jit(solution)/shard_map/all_to_all | solution.py:101
  56.6 0.1 copy.64
  56.7 0.2 reshape.63
  56.9 1.1 fusion.36
  58.0 1.0 copy.61
  59.1 1.1 copy.62
  60.1 1.9 %fusion = pred[4,256,128]{2,1,0:T(8,128)(4,1)S(1)} fusion(s32[4,128,8]{1,2,0:T(8,128)S(1)} %convert_subtract_fusion), kind=kLoop, calls=%fused_computation.2 | loop fusion | flops 1966080 | bytes 147456 | tf_op jit(solution)/shard_map/reduce_or | solution.py:119
  62.0 0.7 convolution_convert_fusion.1
  62.7 0.3 copy.55
  63.0 28.6 %all_to_all.39 = bf16[4,8,32,1024]{3,2,0,1:T(8,128)(2,1)S(1)} all-to-all(bf16[4,8,32,1024]{3,2,0,1:T(8,128)(2,1)S(1)} %copy.55), channel_id=1, replica_groups=mesh['grp'=2,'eh'=4,'el'=4] {'grp','el'}, dimensions={1} | all-to-all | bytes 4194304 | tf_op jit(solution)/shard_map/all_to_all | solution.py:127
  91.6 0.3 copy.56
  91.9 0.0 copy-start.10
  91.9 2.3 %fusion.2 = f32[1024,1024]{1,0:T(8,128)S(1)} fusion(bf16[1024,1024]{1,0:T(8,128)(2,1)S(1)} %bitcast.26, bf16[1,1024,1024]{2,1,0:T(8,128)(2,1)S(1)} %copy-done), kind=kOutput, calls=%fused_computation.5 | convolution fusion | flops 2147483648 | bytes 8388608 | tf_op jit(solution)/shard_map/dot_general | solution.py:135
  94.2 1.3 convolution_convert_fusion
  95.5 1.5 copy.57
  97.0 4.5 %all-to-all-start.3 = ((bf16[4,8,32,1024]{3,2,0,1:T(8,128)(2,1)}), bf16[4,8,32,1024]{3,2,0,1:T(8,128)(2,1)}, u32[]{:S(2)}, u32[]{:S(2)}) async-start(bf16[4,8,32,1024]{3,2,0,1:T(8,128)(2,1)} %copy.57), calls=%async_computation.3 | async-start | bytes 4194304 | tf_op jit(solution)/shard_map/all_to_all | solution.py:142
  101.5 0.1 copy.54
  101.6 1.5 select_reduce_fusion
  103.1 24.1 %all-to-all-done.3 = bf16[4,8,32,1024]{3,2,0,1:T(8,128)(2,1)} async-done(((bf16[4,8,32,1024]{3,2,0,1:T(8,128)(2,1)}), bf16[4,8,32,1024]{3,2,0,1:T(8,128)(2,1)}, u32[]{:S(2)}, u32[]{:S(2)}) %all-to-all-start.3) | async-done | bytes 2097184 | tf_op jit(solution)/shard_map/all_to_all | solution.py:142
  127.2 1.8 %copy.58 = bf16[4,8,32,1024]{3,2,1,0:T(8,128)(2,1)S(1)} copy(bf16[4,8,32,1024]{3,2,0,1:T(8,128)(2,1)} %all-to-all-done.3) | data formatting | bytes 4194304 | tf_op jit(solution)/shard_map/all_to_all | solution.py:142
  129.0 1.1 convolution_convert_fusion.2
  130.1 0.0 copy-start.8
  130.1 28.3 %all_to_all.40 = bf16[4,128,1024]{2,1,0:T(8,128)(2,1)S(1)} all-to-all(bf16[4,128,1024]{2,1,0:T(8,128)(2,1)S(1)} %convolution_convert_fusion.2), channel_id=1, replica_groups=mesh['grp'=2,'eh'=4,'el'=4] {'eh'}, dimensions={0} | all-to-all | bytes 2097152 | tf_op jit(solution)/shard_map/all_to_all | solution.py:154
  158.4 0.2 convert_reduce_fusion
  158.6 0.2 multiply_reduce_fusion
  158.8 0.8 multiply_convert_fusion
  (39 shorter events, 0.3 us)
Async XLA Ops:
  0.0 91.9 %copy-start = (bf16[1,1024,1024]{2,1,0:T(8,128)(2,1)S(1)}, bf16[1,1024,1024]{2,1,0:T(8,128)(2,1)}, u32[]{:S(2)}) copy-start(bf16[1,1024,1024]{2,1,0:T(8,128)(2,1)} %param.19) | copy-start | bytes 6291460
  0.0 16.5 %copy-start.12 = (s32[16]{0:T(128)S(1)}, s32[16]{0:T(128)}, u32[]{:S(2)}) copy-start(s32[16]{0:T(128)} %param.23) | copy-start | bytes 196
  0.0 16.7 %copy-start.9 = (s32[128,8]{0,1:T(8,128)S(1)}, s32[128,8]{0,1:T(8,128)}, u32[]{:S(2)}) copy-start(s32[128,8]{0,1:T(8,128)} %param.21) | copy-start | bytes 12292
  0.0 16.7 %copy-start.6 = (s32[128,8]{0,1:T(8,128)S(1)}, s32[128,8]{0,1:T(8,128)}, u32[]{:S(2)}) copy-start(s32[128,8]{0,1:T(8,128)} %param.22) | copy-start | bytes 12292
  0.0 16.8 %copy-start.13 = (s32[128]{0:T(128)S(1)}, s32[128]{0:T(128)}, u32[]{:S(2)}) copy-start(s32[128]{0:T(128)} %param.24) | copy-start | bytes 1540
  0.0 16.8 %copy-start.14 = (s32[128]{0:T(128)S(1)}, s32[128]{0:T(128)}, u32[]{:S(2)}) copy-start(s32[128]{0:T(128)} %param.25) | copy-start | bytes 1540
  0.0 17.1 %copy-start.11 = (s32[2,16]{1,0:T(2,128)S(1)}, s32[2,16]{1,0:T(2,128)}, u32[]{:S(2)}) copy-start(s32[2,16]{1,0:T(2,128)} %param.26) | copy-start | bytes 388
  0.0 17.3 %copy-start.5 = (f32[128,8]{0,1:T(8,128)S(1)}, f32[128,8]{0,1:T(8,128)}, u32[]{:S(2)}) copy-start(f32[128,8]{0,1:T(8,128)} %param.27) | copy-start | bytes 12292
  10.4 13.8 %copy-start.4 = (bf16[128,1024]{1,0:T(8,128)(2,1)S(1)}, bf16[128,1024]{1,0:T(8,128)(2,1)}, u32[]{:S(2)}) copy-start(bf16[128,1024]{1,0:T(8,128)(2,1)} %param.15) | copy-start | bytes 786436
  12.9 12.2 %copy-start.7 = (f32[1024]{0:T(1024)S(1)}, f32[1024]{0:T(1024)}, u32[]{:S(2)}) copy-start(f32[1024]{0:T(1024)} %param.17) | copy-start | bytes 12292
  12.9 11.3 %all-to-all-start = ((f32[2,128,512]{2,1,0:T(8,128)}), f32[2,128,512]{2,1,0:T(8,128)S(1)}, u32[]{:S(2)}, u32[]{:S(2)}) async-start(f32[2,128,512]{2,1,0:T(8,128)} %bitcast), calls=%async_computation | async-start | bytes 1048576 | tf_op jit(solution)/shard_map/all_to_all | solution.py:51
  24.4 0.7 copy-start.1
  26.4 30.2 %all-to-all-start.1 = ((bf16[4,136,1024]{2,1,0:T(8,128)(2,1)}), bf16[4,136,1024]{2,1,0:T(8,128)(2,1)S(1)}, u32[]{:S(2)}, u32[]{:S(2)}) async-start(bf16[4,136,1024]{2,1,0:T(8,128)(2,1)} %broadcast_in_dim.81), calls=%async_computation.1 | async-start | bytes 2228224 | tf_op jit(solution)/shard_map/all_to_all | solution.py:101
  91.9 2.4 %copy-start.10 = (bf16[1,512,1024]{2,1,0:T(8,128)(2,1)S(1)}, bf16[1,512,1024]{2,1,0:T(8,128)(2,1)}, u32[]{:S(2)}) copy-start(bf16[1,512,1024]{2,1,0:T(8,128)(2,1)} %param.20) | copy-start | bytes 3145732
  97.0 4.5 %copy-start.3 = (f32[4,128,8]{2,1,0:T(8,128)S(1)}, f32[4,128,8]{2,1,0:T(8,128)}, u32[]{:S(2)}) copy-start(f32[4,128,8]{2,1,0:T(8,128)} %get-tuple-element.11) | copy-start | bytes 49156
  97.0 30.2 %all-to-all-start.3 = ((bf16[4,8,32,1024]{3,2,0,1:T(8,128)(2,1)}), bf16[4,8,32,1024]{3,2,0,1:T(8,128)(2,1)}, u32[]{:S(2)}, u32[]{:S(2)}) async-start(bf16[4,8,32,1024]{3,2,0,1:T(8,128)(2,1)} %copy.57), calls=%async_computation.3 | async-start | bytes 4194304 | tf_op jit(solution)/shard_map/all_to_all | solution.py:142
  130.1 28.5 %copy-start.2 = (bf16[128,1024]{1,0:T(8,128)(2,1)S(1)}, bf16[128,1024]{1,0:T(8,128)(2,1)}, u32[]{:S(2)}) copy-start(bf16[128,1024]{1,0:T(8,128)(2,1)} %copy-done.1) | copy-start | bytes 786436
  130.1 28.6 %copy-start.8 = (f32[1024]{0:T(1024)S(1)}, f32[1024]{0:T(1024)}, u32[]{:S(2)}) copy-start(f32[1024]{0:T(1024)} %param.18) | copy-start | bytes 12292

commit v5 on v1

--- a/solution.py
+++ b/solution.py
@@ -32,12 +32,20 @@
     features = attention.shape[1]
     picks_row = expert_ids.shape[1]
     cap_size = max(2, rows_here * picks_row // devices_all)
-    columns = jnp.dot(
-        lax.all_gather(attention, "grp", axis=0, tiled=True),
-        out_proj,
-        preferred_element_type=jnp.float32,
+    me_grp = lax.axis_index("grp")
+    blocks = [None] * groups
+    blocks[0] = jnp.dot(attention, out_proj, preferred_element_type=jnp.float32)
+    for shift in range(1, groups):
+        ahead = [(g, (g + shift) % groups) for g in range(groups)]
+        back = [(b, a) for a, b in ahead]
+        visiting = lax.ppermute(attention, "grp", ahead)
+        done = jnp.dot(visiting, out_proj, preferred_element_type=jnp.float32)
+        blocks[shift] = lax.ppermute(done, "grp", back)
+    stacked = jnp.stack(blocks, axis=0)
+    order_cols = (jnp.arange(groups, dtype=jnp.int32) - me_grp) % groups
+    attn_proj = jnp.concatenate(
+        [jnp.take(stacked, order_cols[j], axis=0) for j in range(groups)], axis=1
     )
-    attn_proj = lax.all_to_all(columns, "grp", split_axis=0, concat_axis=1, tiled=True)
     hidden_state = (residual.astype(jnp.float32) + attn_proj).astype(jnp.bfloat16)
     normed = rms_scale(hidden_state.astype(jnp.float32), pre_gain).astype(jnp.bfloat16)
     experts_all = placement.shape[0]

time: 142 us -> 139 us (0.979)
  blocking collectives: 64.6 us -> 54.5 us
  between operations: 0.21 us -> 3.99 us
  other arithmetic: 4.62 us -> 7.47 us
    all_gather x1 -> x0, blocking collectives: 10.3 us -> none  [on_device(): lax.all_gather(attention, 'grp', axis=0, tiled=True)]
    ppermute x0 -> x2, waiting for transfers between devices: none -> 5.31 us  [the longest x1 5.31 us: on_device(): blocks[shift] = lax.ppermute(done, 'grp', back)]
    all_to_all x1 -> x0, waiting for transfers between devices: 4.99 us -> none  [on_device(): lax.all_to_all(columns, 'grp', split_axis=0, concat_axis=1, tiled=True)]
    all_to_all x1 -> x0, starting transfers between devices: 3.62 us -> none  [on_device(): lax.all_to_all(columns, 'grp', split_axis=0, concat_axis=1, tiled=True)]
    ppermute x0 -> x2, starting transfers between devices: none -> 3.31 us  [the longest x1 3.04 us: on_device(): visiting = lax.ppermute(attention, 'grp', ahead)]
  transfers between devices with their start and end apart: 2 -> 3, of which waited for: 2 -> 2; matrix products, arithmetic and copies ran while one was open for 3% -> 6% of each run, Pallas kernels for 0% -> 0%
where the time goes in v5:
time: 139 us
  blocking collectives  54.5 us (39%)
  waiting for transfers between devices  53.8 us (39%)
  matrix products  10.6 us (8%)
  other arithmetic  7.47 us (5%)
  starting transfers between devices  6.92 us (5%)
  between operations  3.99 us (3%)
  local copies, waits for them, and re-layouts  1.65 us (1%)
    all_to_all x1, blocking collectives, on_device(): lax.all_to_all(buffer.reshape(devices_all, cap_size, features), ('grp', '...  54.5 us
    all_to_all x1, waiting for transfers between devices, on_device(): lax.all_to_all(produced.reshape(arrived.shape), ('grp', 'ep'), split_axis...  48.5 us
    ppermute x1, waiting for transfers between devices, on_device(): blocks[shift] = lax.ppermute(done, 'grp', back)  5.31 us
    all_to_all x1, starting transfers between devices, on_device(): lax.all_to_all(produced.reshape(arrived.shape), ('grp', 'ep'), split_axis...  3.61 us
    ppermute x1, starting transfers between devices, on_device(): visiting = lax.ppermute(attention, 'grp', ahead)  3.04 us
  transfers between devices with their start and end apart: 3, of which 2 were waited for; matrix products, arithmetic and copies ran while one was open for 6% of the time, Pallas kernels for 0%

profile of v5, /device:TPU:0, one launch (start us, length us, event | category | flops | bytes accessed | tf_op | source)
XLA Modules:
  0.0 139.0 jit_solution(2351785440625254884)
XLA Ops:
  0.0 0.0 copy-start
  0.0 0.0 copy-start.2
  0.0 0.0 copy-start.1
  0.0 3.0 %collective-permute-start = (bf16[128,1024]{1,0:T(8,128)(2,1)}, bf16[128,1024]{1,0:T(8,128)(2,1)}, u32[]{:S(2)}, u32[]{:S(2)}) collective-permute-start(bf16[128,1024]{1,0:T(8,128)(2,1)} %param.16), channel_id=1, source_target_pairs={{0,16},{16,0},{1,17},{17,1},{2,18},{18,2},{3,19},{19,3},{4,20},{20... | collective-permute-start | bytes 786440 | tf_op jit(solution)/shard_map/ppermute | solution.py:41
  3.1 0.8 select_reduce_fusion.4
  3.8 0.8 select_reduce_fusion.3
  4.6 0.7 multiply_add_fusion
  5.3 0.7 multiply_add_fusion.1
  6.0 0.2 fusion.24
  6.3 0.8 broadcast_in_dim.57
  7.0 0.1 select_reduce_fusion.1
  7.1 0.6 fusion.31
  11.6 0.0 copy-start.3
  11.6 0.0 collective-permute-done
  11.6 1.6 %fusion.32 = f32[128,512]{1,0:T(8,128)S(1)} fusion(bf16[128,1024]{1,0:T(8,128)(2,1)} %collective-permute-done, bf16[1024,512]{1,0:T(8,128)(2,1)} %param.18), kind=kOutput, calls=%fused_computation.63 | convolution fusion | flops 134217728 | bytes 1572864 | tf_op jit(solution)/shard_map/dot_general | solution.py:42
  13.3 0.0 copy-start.4
  13.3 0.3 collective-permute-start.1
  13.5 1.9 %fusion = pred[1024,128]{1,0:T(8,128)(4,1)S(1)} fusion(s32[128,8]{0,1:T(8,128)S(1)} %get-tuple-element.19), kind=kLoop, calls=%fused_computation.3 | loop fusion | flops 1966080 | bytes 135168 | tf_op jit(solution)/shard_map/reduce_or | solution.py:81
  15.5 0.0 copy-done.2
  15.5 0.0 copy-done.1
  15.5 0.3 convolution_bitcast_fusion
  15.8 5.3 %collective-permute-done.1 = f32[128,512]{1,0:T(8,128)S(1)} collective-permute-done((f32[128,512]{1,0:T(8,128)S(1)}, f32[128,512]{1,0:T(8,128)S(1)}, u32[]{:S(2)}, u32[]{:S(2)}) %collective-permute-start.1) | collective-permute-done | bytes 262176 | tf_op jit(solution)/shard_map/ppermute | solution.py:43
  21.1 0.1 fusion.17
  21.2 0.0 copy-done.3
  21.3 0.2 fusion.7
  21.4 0.0 copy-done.4
  21.4 0.8 convolution_convert_fusion.1
  22.2 54.5 %all_to_all.10 = bf16[32,32,1024]{2,1,0:T(8,128)(2,1)S(1)} all-to-all(bf16[32,32,1024]{2,1,0:T(8,128)(2,1)S(1)} %bitcast.28), channel_id=1, replica_groups=mesh['grp'=2,'ep'=16] {'grp','ep'}, dimensions={0} | all-to-all | bytes 4194304 | tf_op jit(solution)/shard_map/all_to_all | solution.py:86
  76.7 0.0 copy-done
  76.7 0.0 copy-start.7
  76.7 2.4 %fusion.2 = f32[1024,1024]{1,0:T(8,128)S(1)} fusion(bf16[1024,1024]{1,0:T(8,128)(2,1)S(1)} %bitcast.30, bf16[1,1024,1024]{2,1,0:T(8,128)(2,1)S(1)} %copy-done), kind=kOutput, calls=%fused_computation.6 | convolution fusion | flops 2147483648 | bytes 8388608 | tf_op jit(solution)/shard_map/dot_general | solution.py:94
  79.1 0.0 copy-done.7
  79.1 2.6 %convolution_convert_fusion = bf16[1024,1024]{1,0:T(8,128)(2,1)} fusion(f32[1024,1024]{1,0:T(8,128)S(1)} %fusion.2, bf16[1,512,1024]{2,1,0:T(8,128)(2,1)S(1)} %copy-done.7), kind=kOutput, calls=%fused_computation.8 | convolution fusion | flops 1077936128 | bytes 7340032 | tf_op jit(solution)/shard_map/dot_general | solution.py:98
  81.7 0.0 copy-start.6
  81.7 3.6 %all-to-all-start.1 = ((bf16[32,32,1024]{2,1,0:T(8,128)(2,1)}), bf16[32,32,1024]{2,1,0:T(8,128)(2,1)}, u32[]{:S(2)}, u32[]{:S(2)}) async-start(bf16[32,32,1024]{2,1,0:T(8,128)(2,1)} %bitcast.29), calls=%async_computation.1 | async-start | bytes 4194304 | tf_op jit(solution)/shard_map/all_to_all | solution.py:101
  85.3 0.0 copy-start.5
  85.4 0.1 copy.21
  85.5 0.0 copy-done.6
  85.5 0.1 copy.22
  85.6 1.3 select_reduce_fusion
  86.9 48.5 %all-to-all-done.1 = bf16[32,32,1024]{2,1,0:T(8,128)(2,1)} async-done(((bf16[32,32,1024]{2,1,0:T(8,128)(2,1)}), bf16[32,32,1024]{2,1,0:T(8,128)(2,1)}, u32[]{:S(2)}, u32[]{:S(2)}) %all-to-all-start.1) | async-done | bytes 2097184 | tf_op jit(solution)/shard_map/all_to_all | solution.py:101
  135.4 2.7 %multiply_reduce_fusion = (f32[128]{0:T(128)S(1)}, f32[128,1024]{1,0:T(8,128)S(1)}) fusion(f32[128,1024]{1,0:T(8,128)S(1)} %select_reduce_fusion, bf16[1024,1024]{1,0:T(8,128)(2,1)} %bitcast.11, bf16[128,1024]{1,0:T(8,128)(2,1)S(1)} %get-tuple-element.18), kind=kOutput, calls=%fused_computation.26 | convolution fusion | flops 1611136896 | bytes 3408384 | tf_op jit(solution)/shard_map/dot_general | solution.py:110
  138.2 0.0 copy-done.5
  138.2 0.8 multiply_convert_fusion
  (7 shorter events, 0.1 us)
Async XLA Ops:
  0.0 76.7 %copy-start = (bf16[1,1024,1024]{2,1,0:T(8,128)(2,1)S(1)}, bf16[1,1024,1024]{2,1,0:T(8,128)(2,1)}, u32[]{:S(2)}) copy-start(bf16[1,1024,1024]{2,1,0:T(8,128)(2,1)} %param.21) | copy-start | bytes 6291460
  0.0 15.5 %copy-start.2 = (bf16[128,1024]{1,0:T(8,128)(2,1)S(1)}, bf16[128,1024]{1,0:T(8,128)(2,1)}, u32[]{:S(2)}) copy-start(bf16[128,1024]{1,0:T(8,128)(2,1)} %param.16) | copy-start | bytes 786436
  0.0 15.5 %copy-start.1 = (bf16[1024,512]{1,0:T(8,128)(2,1)S(1)}, bf16[1024,512]{1,0:T(8,128)(2,1)}, u32[]{:S(2)}) copy-start(bf16[1024,512]{1,0:T(8,128)(2,1)} %param.18) | copy-start | bytes 3145732
  0.0 11.6 %collective-permute-start = (bf16[128,1024]{1,0:T(8,128)(2,1)}, bf16[128,1024]{1,0:T(8,128)(2,1)}, u32[]{:S(2)}, u32[]{:S(2)}) collective-permute-start(bf16[128,1024]{1,0:T(8,128)(2,1)} %param.16), channel_id=1, source_target_pairs={{0,16},{16,0},{1,17},{17,1},{2,18},{18,2},{3,19},{19,3},{4,20},{20... | collective-permute-start | bytes 786440 | tf_op jit(solution)/shard_map/ppermute | solution.py:41
  11.6 9.7 %copy-start.3 = (bf16[128,1024]{1,0:T(8,128)(2,1)S(1)}, bf16[128,1024]{1,0:T(8,128)(2,1)}, u32[]{:S(2)}) copy-start(bf16[128,1024]{1,0:T(8,128)(2,1)} %param.17) | copy-start | bytes 786436
  13.3 8.2 %copy-start.4 = (f32[1024]{0:T(1024)S(1)}, f32[1024]{0:T(1024)}, u32[]{:S(2)}) copy-start(f32[1024]{0:T(1024)} %param.19) | copy-start | bytes 12292
  13.3 7.8 %collective-permute-start.1 = (f32[128,512]{1,0:T(8,128)S(1)}, f32[128,512]{1,0:T(8,128)S(1)}, u32[]{:S(2)}, u32[]{:S(2)}) collective-permute-start(f32[128,512]{1,0:T(8,128)S(1)} %fusion.32), channel_id=1, source_target_pairs={{16,0},{0,16},{17,1},{1,17},{18,2},{2,18},{19,3},{3,19},{20,4},{4,... | collective-permute-start | bytes 786440 | tf_op jit(solution)/shard_map/ppermute | solution.py:43
  76.7 2.4 %copy-start.7 = (bf16[1,512,1024]{2,1,0:T(8,128)(2,1)S(1)}, bf16[1,512,1024]{2,1,0:T(8,128)(2,1)}, u32[]{:S(2)}) copy-start(bf16[1,512,1024]{2,1,0:T(8,128)(2,1)} %param.22) | copy-start | bytes 3145732
  81.7 3.7 %copy-start.6 = (f32[128,8]{0,1:T(8,128)S(1)}, f32[128,8]{0,1:T(8,128)}, u32[]{:S(2)}) copy-start(f32[128,8]{0,1:T(8,128)} %param.29) | copy-start | bytes 12292
  81.7 53.7 %all-to-all-start.1 = ((bf16[32,32,1024]{2,1,0:T(8,128)(2,1)}), bf16[32,32,1024]{2,1,0:T(8,128)(2,1)}, u32[]{:S(2)}, u32[]{:S(2)}) async-start(bf16[32,32,1024]{2,1,0:T(8,128)(2,1)} %bitcast.29), calls=%async_computation.1 | async-start | bytes 4194304 | tf_op jit(solution)/shard_map/all_to_all | solution.py:101
  85.3 52.8 %copy-start.5 = (f32[1024]{0:T(1024)S(1)}, f32[1024]{0:T(1024)}, u32[]{:S(2)}) copy-start(f32[1024]{0:T(1024)} %param.20) | copy-start | bytes 12292

commit v6 on v5

--- a/solution.py
+++ b/solution.py
@@ -76,19 +76,28 @@
     )
     accepted = position < granted
     total_slots = devices_all * cap_size
-    index = jnp.where(accepted, target * cap_size + position, total_slots)
+    me_all = lax.axis_index(("grp", "ep"))
+    index = jnp.where(
+        accepted, ((target - me_all) % devices_all) * cap_size + position, total_slots
+    )
     slot_ids = jnp.arange(total_slots, dtype=jnp.int32)
     dispatch = jnp.any(index[None, :, :] == slot_ids[:, None, None], axis=2).astype(jnp.bfloat16)
     buffer = jnp.dot(dispatch, normed, preferred_element_type=jnp.float32).astype(jnp.bfloat16)
     gate_up_local = slot_gate_up[0]
     down_local = slot_down[0]
     hidden_units = down_local.shape[0]
-    arrived = lax.all_to_all(
-        buffer.reshape(devices_all, cap_size, features),
-        ("grp", "ep"),
-        split_axis=0,
-        concat_axis=0,
-        tiled=True,
+    chunks = buffer.reshape(devices_all, cap_size, features)
+    arrived = jnp.stack(
+        [chunks[0]]
+        + [
+            lax.ppermute(
+                chunks[shift],
+                ("grp", "ep"),
+                [(i, (i + shift) % devices_all) for i in range(devices_all)],
+            )
+            for shift in range(1, devices_all)
+        ],
+        axis=0,
     )
     flattened = arrived.reshape(-1, features)
     gate_up = jnp.dot(flattened, gate_up_local, preferred_element_type=jnp.float32)
@@ -98,8 +107,18 @@
     produced = jnp.dot(expert_hidden, down_local, preferred_element_type=jnp.float32).astype(
         jnp.bfloat16
     )
-    returned = lax.all_to_all(
-        produced.reshape(arrived.shape), ("grp", "ep"), split_axis=0, concat_axis=0, tiled=True
+    outs = produced.reshape(arrived.shape)
+    returned = jnp.stack(
+        [outs[0]]
+        + [
+            lax.ppermute(
+                outs[shift],
+                ("grp", "ep"),
+                [(i, (i - shift) % devices_all) for i in range(devices_all)],
+            )
+            for shift in range(1, devices_all)
+        ],
+        axis=0,
     )
     flat_back = returned.reshape(total_slots, features)
     weights_kept = jnp.where(accepted, route_weight, jnp.float32(0.0))

time: 139 us -> 322 us (2.32); the launches traced: 139 us -> 318 us
  waiting for transfers between devices: 53.8 us -> 189 us
  starting transfers between devices: 6.92 us -> 103 us
  blocking collectives: 54.5 us -> 0 us
    ppermute x0 -> x62, waiting for transfers between devices: none -> 188 us  [the longest x31 112 us: on_device(): lax.ppermute(chunks[shift], ('grp', 'ep'), [(i, (i + shift) % devices_all...]
    ppermute x0 -> x62, starting transfers between devices: none -> 99.9 us  [the longest x31 73.2 us: on_device(): lax.ppermute(outs[shift], ('grp', 'ep'), [(i, (i - shift) % devices_all)...]
    all_to_all x1 -> x0, blocking collectives: 54.5 us -> none  [on_device(): lax.all_to_all(buffer.reshape(devices_all, cap_size, features), ('grp', '...]
    all_to_all x1 -> x0, waiting for transfers between devices: 48.5 us -> none  [on_device(): lax.all_to_all(produced.reshape(arrived.shape), ('grp', 'ep'), split_axis...]
    all_to_all x1 -> x0, starting transfers between devices: 3.61 us -> none  [on_device(): lax.all_to_all(produced.reshape(arrived.shape), ('grp', 'ep'), split_axis...]
    ppermute x1, waiting for transfers between devices: 5.31 us -> 1.84 us  [on_device(): blocks[shift] = lax.ppermute(done, 'grp', back)]
  transfers between devices with their start and end apart: 3 -> 64, of which waited for: 2 -> 45; matrix products, arithmetic and copies ran while one was open for 6% -> 3% of each run, Pallas kernels for 0% -> 0%
where the time goes in v6:
time: 322 us; the launch traced here: 318 us
  waiting for transfers between devices  189 us (59%)
  starting transfers between devices  103 us (32%)
  matrix products  9.37 us (3%)
  other arithmetic  9.1 us (3%)
  between operations  4.29 us (1%)
    ppermute x31, waiting for transfers between devices, on_device(): lax.ppermute(chunks[shift], ('grp', 'ep'), [(i, (i + shift) % devices_all...  112 us
    ppermute x31, waiting for transfers between devices, on_device(): lax.ppermute(outs[shift], ('grp', 'ep'), [(i, (i - shift) % devices_all)...  75.9 us
    ppermute x31, starting transfers between devices, on_device(): lax.ppermute(outs[shift], ('grp', 'ep'), [(i, (i - shift) % devices_all)...  73.2 us
    ppermute x31, starting transfers between devices, on_device(): lax.ppermute(chunks[shift], ('grp', 'ep'), [(i, (i + shift) % devices_all...  26.8 us
  transfers between devices with their start and end apart: 64, of which 45 were waited for; matrix products, arithmetic and copies ran while one was open for 3% of the time, Pallas kernels for 0%

profile of v6, /device:TPU:0, one launch (start us, length us, event | category | flops | bytes accessed | tf_op | source)
XLA Modules:
  0.0 317.7 jit_solution(1283807095049487503)
XLA Ops:
  0.0 3.0 collective-permute-start
  23.6 3.7 %collective-permute-start.13 = (bf16[32,1024]{1,0:T(8,128)(2,1)S(1)}, bf16[32,1024]{1,0:T(8,128)(2,1)S(1)}, u32[]{:S(2)}, u32[]{:S(2)}) collective-permute-start(bf16[32,1024]{1,0:T(8,128)(2,1)S(1)} %get-tuple-element.71), channel_id=1, source_target_pairs={{0,12},{1,13},{2,14},{3,15},{4,16},{5,17},{6,18},{7,19},{8,20},{9,... | collective-permute-start | bytes 196616 | tf_op jit(solution)/shard_map/ppermute | solution.py:93
  32.5 7.3 %collective-permute-done.3 = bf16[32,1024]{1,0:T(8,128)(2,1)S(1)} collective-permute-done((bf16[32,1024]{1,0:T(8,128)(2,1)S(1)}, bf16[32,1024]{1,0:T(8,128)(2,1)S(1)}, u32[]{:S(2)}, u32[]{:S(2)}) %collective-permute-start.3) | collective-permute-done | bytes 65568 | tf_op jit(solution)/shard_map/ppermute | solution.py:93
  39.9 6.4 %collective-permute-done.4 = bf16[32,1024]{1,0:T(8,128)(2,1)S(1)} collective-permute-done((bf16[32,1024]{1,0:T(8,128)(2,1)S(1)}, bf16[32,1024]{1,0:T(8,128)(2,1)S(1)}, u32[]{:S(2)}, u32[]{:S(2)}) %collective-permute-start.4) | collective-permute-done | bytes 65568 | tf_op jit(solution)/shard_map/ppermute | solution.py:93
  46.3 7.3 %collective-permute-done.5 = bf16[32,1024]{1,0:T(8,128)(2,1)S(1)} collective-permute-done((bf16[32,1024]{1,0:T(8,128)(2,1)S(1)}, bf16[32,1024]{1,0:T(8,128)(2,1)S(1)}, u32[]{:S(2)}, u32[]{:S(2)}) %collective-permute-start.5) | collective-permute-done | bytes 65568 | tf_op jit(solution)/shard_map/ppermute | solution.py:93
  53.6 6.4 %collective-permute-done.6 = bf16[32,1024]{1,0:T(8,128)(2,1)S(1)} collective-permute-done((bf16[32,1024]{1,0:T(8,128)(2,1)S(1)}, bf16[32,1024]{1,0:T(8,128)(2,1)S(1)}, u32[]{:S(2)}, u32[]{:S(2)}) %collective-permute-start.6) | collective-permute-done | bytes 65568 | tf_op jit(solution)/shard_map/ppermute | solution.py:93
  60.0 7.0 %collective-permute-done.7 = bf16[32,1024]{1,0:T(8,128)(2,1)S(1)} collective-permute-done((bf16[32,1024]{1,0:T(8,128)(2,1)S(1)}, bf16[32,1024]{1,0:T(8,128)(2,1)S(1)}, u32[]{:S(2)}, u32[]{:S(2)}) %collective-permute-start.7) | collective-permute-done | bytes 65568 | tf_op jit(solution)/shard_map/ppermute | solution.py:93
  66.9 5.5 %collective-permute-done.8 = bf16[32,1024]{1,0:T(8,128)(2,1)S(1)} collective-permute-done((bf16[32,1024]{1,0:T(8,128)(2,1)S(1)}, bf16[32,1024]{1,0:T(8,128)(2,1)S(1)}, u32[]{:S(2)}, u32[]{:S(2)}) %collective-permute-start.8) | collective-permute-done | bytes 65568 | tf_op jit(solution)/shard_map/ppermute | solution.py:93
  72.4 6.1 %collective-permute-done.9 = bf16[32,1024]{1,0:T(8,128)(2,1)S(1)} collective-permute-done((bf16[32,1024]{1,0:T(8,128)(2,1)S(1)}, bf16[32,1024]{1,0:T(8,128)(2,1)S(1)}, u32[]{:S(2)}, u32[]{:S(2)}) %collective-permute-start.9) | collective-permute-done | bytes 65568 | tf_op jit(solution)/shard_map/ppermute | solution.py:93
  81.3 5.0 %collective-permute-done.14 = bf16[32,1024]{1,0:T(8,128)(2,1)S(1)} collective-permute-done((bf16[32,1024]{1,0:T(8,128)(2,1)S(1)}, bf16[32,1024]{1,0:T(8,128)(2,1)S(1)}, u32[]{:S(2)}, u32[]{:S(2)}) %collective-permute-start.14) | collective-permute-done | bytes 65568 | tf_op jit(solution)/shard_map/ppermute | solution.py:93
  86.3 3.8 %collective-permute-start.15 = (bf16[32,1024]{1,0:T(8,128)(2,1)S(1)}, bf16[32,1024]{1,0:T(8,128)(2,1)S(1)}, u32[]{:S(2)}, u32[]{:S(2)}) collective-permute-start(bf16[32,1024]{1,0:T(8,128)(2,1)S(1)} %get-tuple-element.69), channel_id=1, source_target_pairs={{0,14},{1,15},{2,16},{3,17},{4,18},{5,19},{6,20},{7,21},{8,22},{9,... | collective-permute-start | bytes 196616 | tf_op jit(solution)/shard_map/ppermute | solution.py:93
  93.6 2.7 collective-permute-done.16
  97.5 3.6 %collective-permute-done.17 = bf16[32,1024]{1,0:T(8,128)(2,1)S(1)} collective-permute-done((bf16[32,1024]{1,0:T(8,128)(2,1)S(1)}, bf16[32,1024]{1,0:T(8,128)(2,1)S(1)}, u32[]{:S(2)}, u32[]{:S(2)}) %collective-permute-start.17) | collective-permute-done | bytes 65568 | tf_op jit(solution)/shard_map/ppermute | solution.py:93
  102.0 5.5 %collective-permute-done.18 = bf16[32,1024]{1,0:T(8,128)(2,1)S(1)} collective-permute-done((bf16[32,1024]{1,0:T(8,128)(2,1)S(1)}, bf16[32,1024]{1,0:T(8,128)(2,1)S(1)}, u32[]{:S(2)}, u32[]{:S(2)}) %collective-permute-start.18) | collective-permute-done | bytes 65568 | tf_op jit(solution)/shard_map/ppermute | solution.py:93
  108.1 6.3 %collective-permute-done.19 = bf16[32,1024]{1,0:T(8,128)(2,1)S(1)} collective-permute-done((bf16[32,1024]{1,0:T(8,128)(2,1)S(1)}, bf16[32,1024]{1,0:T(8,128)(2,1)S(1)}, u32[]{:S(2)}, u32[]{:S(2)}) %collective-permute-start.19) | collective-permute-done | bytes 65568 | tf_op jit(solution)/shard_map/ppermute | solution.py:93
  114.4 5.5 %collective-permute-done.20 = bf16[32,1024]{1,0:T(8,128)(2,1)S(1)} collective-permute-done((bf16[32,1024]{1,0:T(8,128)(2,1)S(1)}, bf16[32,1024]{1,0:T(8,128)(2,1)S(1)}, u32[]{:S(2)}, u32[]{:S(2)}) %collective-permute-start.20) | collective-permute-done | bytes 65568 | tf_op jit(solution)/shard_map/ppermute | solution.py:93
  119.9 6.1 %collective-permute-done.21 = bf16[32,1024]{1,0:T(8,128)(2,1)S(1)} collective-permute-done((bf16[32,1024]{1,0:T(8,128)(2,1)S(1)}, bf16[32,1024]{1,0:T(8,128)(2,1)S(1)}, u32[]{:S(2)}, u32[]{:S(2)}) %collective-permute-start.21) | collective-permute-done | bytes 65568 | tf_op jit(solution)/shard_map/ppermute | solution.py:93
  126.0 5.5 %collective-permute-done.22 = bf16[32,1024]{1,0:T(8,128)(2,1)S(1)} collective-permute-done((bf16[32,1024]{1,0:T(8,128)(2,1)S(1)}, bf16[32,1024]{1,0:T(8,128)(2,1)S(1)}, u32[]{:S(2)}, u32[]{:S(2)}) %collective-permute-start.22) | collective-permute-done | bytes 65568 | tf_op jit(solution)/shard_map/ppermute | solution.py:93
  131.5 6.1 %collective-permute-done.23 = bf16[32,1024]{1,0:T(8,128)(2,1)S(1)} collective-permute-done((bf16[32,1024]{1,0:T(8,128)(2,1)S(1)}, bf16[32,1024]{1,0:T(8,128)(2,1)S(1)}, u32[]{:S(2)}, u32[]{:S(2)}) %collective-permute-start.23) | collective-permute-done | bytes 65568 | tf_op jit(solution)/shard_map/ppermute | solution.py:93
  137.5 5.1 %collective-permute-done.24 = bf16[32,1024]{1,0:T(8,128)(2,1)S(1)} collective-permute-done((bf16[32,1024]{1,0:T(8,128)(2,1)S(1)}, bf16[32,1024]{1,0:T(8,128)(2,1)S(1)}, u32[]{:S(2)}, u32[]{:S(2)}) %collective-permute-start.24) | collective-permute-done | bytes 65568 | tf_op jit(solution)/shard_map/ppermute | solution.py:93
  142.6 5.2 %collective-permute-done.25 = bf16[32,1024]{1,0:T(8,128)(2,1)S(1)} collective-permute-done((bf16[32,1024]{1,0:T(8,128)(2,1)S(1)}, bf16[32,1024]{1,0:T(8,128)(2,1)S(1)}, u32[]{:S(2)}, u32[]{:S(2)}) %collective-permute-start.25) | collective-permute-done | bytes 65568 | tf_op jit(solution)/shard_map/ppermute | solution.py:93
  148.9 3.5 %collective-permute-done.26 = bf16[32,1024]{1,0:T(8,128)(2,1)S(1)} collective-permute-done((bf16[32,1024]{1,0:T(8,128)(2,1)S(1)}, bf16[32,1024]{1,0:T(8,128)(2,1)S(1)}, u32[]{:S(2)}, u32[]{:S(2)}) %collective-permute-start.26) | collective-permute-done | bytes 65568 | tf_op jit(solution)/shard_map/ppermute | solution.py:93
  152.4 4.3 %collective-permute-start.27 = (bf16[32,1024]{1,0:T(8,128)(2,1)S(1)}, bf16[32,1024]{1,0:T(8,128)(2,1)S(1)}, u32[]{:S(2)}, u32[]{:S(2)}) collective-permute-start(bf16[32,1024]{1,0:T(8,128)(2,1)S(1)} %get-tuple-element.57), channel_id=1, source_target_pairs={{0,26},{1,27},{2,28},{3,29},{4,30},{5,31},{6,0},{7,1},{8,2},{9,3},... | collective-permute-start | bytes 196616 | tf_op jit(solution)/shard_map/ppermute | solution.py:93
  166.3 4.4 %collective-permute-start.33 = (bf16[32,1024]{1,0:T(8,128)(2,1)S(1)}, bf16[32,1024]{1,0:T(8,128)(2,1)S(1)}, u32[]{:S(2)}, u32[]{:S(2)}) collective-permute-start(bf16[32,1024]{1,0:T(8,128)(2,1)S(1)} %get-tuple-element.51), channel_id=1, source_target_pairs={{0,31},{1,0},{2,1},{3,2},{4,3},{5,4},{6,5},{7,6},{8,7},{9,8},{10,9... | collective-permute-start | bytes 196616 | tf_op jit(solution)/shard_map/ppermute | solution.py:114
  170.8 6.9 %collective-permute-start.42 = (bf16[32,1024]{1,0:T(8,128)(2,1)S(1)}, bf16[32,1024]{1,0:T(8,128)(2,1)S(1)}, u32[]{:S(2)}, u32[]{:S(2)}) collective-permute-start(bf16[32,1024]{1,0:T(8,128)(2,1)S(1)} %get-tuple-element.42), channel_id=1, source_target_pairs={{0,22},{1,23},{2,24},{3,25},{4,26},{5,27},{6,28},{7,29},{8,30},{9,... | collective-permute-start | bytes 196616 | tf_op jit(solution)/shard_map/ppermute | solution.py:114
  178.8 3.3 %collective-permute-start.34 = (bf16[32,1024]{1,0:T(8,128)(2,1)S(1)}, bf16[32,1024]{1,0:T(8,128)(2,1)S(1)}, u32[]{:S(2)}, u32[]{:S(2)}) collective-permute-start(bf16[32,1024]{1,0:T(8,128)(2,1)S(1)} %get-tuple-element.50), channel_id=1, source_target_pairs={{0,30},{1,31},{2,0},{3,1},{4,2},{5,3},{6,4},{7,5},{8,6},{9,7},{10,... | collective-permute-start | bytes 196616 | tf_op jit(solution)/shard_map/ppermute | solution.py:114
  184.0 2.7 collective-permute-start.35
  192.9 3.3 %collective-permute-start.37 = (bf16[32,1024]{1,0:T(8,128)(2,1)S(1)}, bf16[32,1024]{1,0:T(8,128)(2,1)S(1)}, u32[]{:S(2)}, u32[]{:S(2)}) collective-permute-start(bf16[32,1024]{1,0:T(8,128)(2,1)S(1)} %get-tuple-element.47), channel_id=1, source_target_pairs={{0,27},{1,28},{2,29},{3,30},{4,31},{5,0},{6,1},{7,2},{8,3},{9,4},{... | collective-permute-start | bytes 196616 | tf_op jit(solution)/shard_map/ppermute | solution.py:114
  198.1 5.7 %collective-permute-start.38 = (bf16[32,1024]{1,0:T(8,128)(2,1)S(1)}, bf16[32,1024]{1,0:T(8,128)(2,1)S(1)}, u32[]{:S(2)}, u32[]{:S(2)}) collective-permute-start(bf16[32,1024]{1,0:T(8,128)(2,1)S(1)} %get-tuple-element.46), channel_id=1, source_target_pairs={{0,26},{1,27},{2,28},{3,29},{4,30},{5,31},{6,0},{7,1},{8,2},{9,3},... | collective-permute-start | bytes 196616 | tf_op jit(solution)/shard_map/ppermute | solution.py:114
  205.6 4.8 %collective-permute-start.39 = (bf16[32,1024]{1,0:T(8,128)(2,1)S(1)}, bf16[32,1024]{1,0:T(8,128)(2,1)S(1)}, u32[]{:S(2)}, u32[]{:S(2)}) collective-permute-start(bf16[32,1024]{1,0:T(8,128)(2,1)S(1)} %get-tuple-element.45), channel_id=1, source_target_pairs={{0,25},{1,26},{2,27},{3,28},{4,29},{5,30},{6,31},{7,0},{8,1},{9,2}... | collective-permute-start | bytes 196616 | tf_op jit(solution)/shard_map/ppermute | solution.py:114
  212.7 5.3 %collective-permute-start.40 = (bf16[32,1024]{1,0:T(8,128)(2,1)S(1)}, bf16[32,1024]{1,0:T(8,128)(2,1)S(1)}, u32[]{:S(2)}, u32[]{:S(2)}) collective-permute-start(bf16[32,1024]{1,0:T(8,128)(2,1)S(1)} %get-tuple-element.44), channel_id=1, source_target_pairs={{0,24},{1,25},{2,26},{3,27},{4,28},{5,29},{6,30},{7,31},{8,0},{9,1... | collective-permute-start | bytes 196616 | tf_op jit(solution)/shard_map/ppermute | solution.py:114
  222.0 8.2 %collective-permute-start.61 = (bf16[32,1024]{1,0:T(8,128)(2,1)S(1)}, bf16[32,1024]{1,0:T(8,128)(2,1)S(1)}, u32[]{:S(2)}, u32[]{:S(2)}) collective-permute-start(bf16[32,1024]{1,0:T(8,128)(2,1)S(1)} %get-tuple-element.23), channel_id=1, source_target_pairs={{0,3},{1,4},{2,5},{3,6},{4,7},{5,8},{6,9},{7,10},{8,11},{9,12},{10... | collective-permute-start | bytes 196616 | tf_op jit(solution)/shard_map/ppermute | solution.py:114
  230.9 5.0 %collective-permute-done.45 = bf16[32,1024]{1,0:T(8,128)(2,1)S(1)} collective-permute-done((bf16[32,1024]{1,0:T(8,128)(2,1)S(1)}, bf16[32,1024]{1,0:T(8,128)(2,1)S(1)}, u32[]{:S(2)}, u32[]{:S(2)}) %collective-permute-start.45) | collective-permute-done | bytes 65568 | tf_op jit(solution)/shard_map/ppermute | solution.py:114
  237.9 6.4 %collective-permute-done.46 = bf16[32,1024]{1,0:T(8,128)(2,1)S(1)} collective-permute-done((bf16[32,1024]{1,0:T(8,128)(2,1)S(1)}, bf16[32,1024]{1,0:T(8,128)(2,1)S(1)}, u32[]{:S(2)}, u32[]{:S(2)}) %collective-permute-start.46) | collective-permute-done | bytes 65568 | tf_op jit(solution)/shard_map/ppermute | solution.py:114
  244.9 5.8 %collective-permute-done.47 = bf16[32,1024]{1,0:T(8,128)(2,1)S(1)} collective-permute-done((bf16[32,1024]{1,0:T(8,128)(2,1)S(1)}, bf16[32,1024]{1,0:T(8,128)(2,1)S(1)}, u32[]{:S(2)}, u32[]{:S(2)}) %collective-permute-start.47) | collective-permute-done | bytes 65568 | tf_op jit(solution)/shard_map/ppermute | solution.py:114
  251.6 3.4 %collective-permute-done.48 = bf16[32,1024]{1,0:T(8,128)(2,1)S(1)} collective-permute-done((bf16[32,1024]{1,0:T(8,128)(2,1)S(1)}, bf16[32,1024]{1,0:T(8,128)(2,1)S(1)}, u32[]{:S(2)}, u32[]{:S(2)}) %collective-permute-start.48) | collective-permute-done | bytes 65568 | tf_op jit(solution)/shard_map/ppermute | solution.py:114
  255.0 3.7 %collective-permute-done.49 = bf16[32,1024]{1,0:T(8,128)(2,1)S(1)} collective-permute-done((bf16[32,1024]{1,0:T(8,128)(2,1)S(1)}, bf16[32,1024]{1,0:T(8,128)(2,1)S(1)}, u32[]{:S(2)}, u32[]{:S(2)}) %collective-permute-start.49) | collective-permute-done | bytes 65568 | tf_op jit(solution)/shard_map/ppermute | solution.py:114
  259.7 4.1 %collective-permute-done.50 = bf16[32,1024]{1,0:T(8,128)(2,1)S(1)} collective-permute-done((bf16[32,1024]{1,0:T(8,128)(2,1)S(1)}, bf16[32,1024]{1,0:T(8,128)(2,1)S(1)}, u32[]{:S(2)}, u32[]{:S(2)}) %collective-permute-start.50) | collective-permute-done | bytes 65568 | tf_op jit(solution)/shard_map/ppermute | solution.py:114
  264.1 4.9 %collective-permute-done.51 = bf16[32,1024]{1,0:T(8,128)(2,1)S(1)} collective-permute-done((bf16[32,1024]{1,0:T(8,128)(2,1)S(1)}, bf16[32,1024]{1,0:T(8,128)(2,1)S(1)}, u32[]{:S(2)}, u32[]{:S(2)}) %collective-permute-start.51) | collective-permute-done | bytes 65568 | tf_op jit(solution)/shard_map/ppermute | solution.py:114
  270.0 4.1 %collective-permute-done.52 = bf16[32,1024]{1,0:T(8,128)(2,1)S(1)} collective-permute-done((bf16[32,1024]{1,0:T(8,128)(2,1)S(1)}, bf16[32,1024]{1,0:T(8,128)(2,1)S(1)}, u32[]{:S(2)}, u32[]{:S(2)}) %collective-permute-start.52) | collective-permute-done | bytes 65568 | tf_op jit(solution)/shard_map/ppermute | solution.py:114
  275.5 3.2 %collective-permute-done.53 = bf16[32,1024]{1,0:T(8,128)(2,1)S(1)} collective-permute-done((bf16[32,1024]{1,0:T(8,128)(2,1)S(1)}, bf16[32,1024]{1,0:T(8,128)(2,1)S(1)}, u32[]{:S(2)}, u32[]{:S(2)}) %collective-permute-start.53) | collective-permute-done | bytes 65568 | tf_op jit(solution)/shard_map/ppermute | solution.py:114
  281.1 3.7 %collective-permute-done.54 = bf16[32,1024]{1,0:T(8,128)(2,1)S(1)} collective-permute-done((bf16[32,1024]{1,0:T(8,128)(2,1)S(1)}, bf16[32,1024]{1,0:T(8,128)(2,1)S(1)}, u32[]{:S(2)}, u32[]{:S(2)}) %collective-permute-start.54) | collective-permute-done | bytes 65568 | tf_op jit(solution)/shard_map/ppermute | solution.py:114
  287.3 2.9 collective-permute-done.55
  290.2 3.7 %collective-permute-start.56 = (bf16[32,1024]{1,0:T(8,128)(2,1)S(1)}, bf16[32,1024]{1,0:T(8,128)(2,1)S(1)}, u32[]{:S(2)}, u32[]{:S(2)}) collective-permute-start(bf16[32,1024]{1,0:T(8,128)(2,1)S(1)} %get-tuple-element.28), channel_id=1, source_target_pairs={{0,8},{1,9},{2,10},{3,11},{4,12},{5,13},{6,14},{7,15},{8,16},{9,17... | collective-permute-start | bytes 196616 | tf_op jit(solution)/shard_map/ppermute | solution.py:114
  298.8 3.1 collective-permute-done.57
  301.9 3.8 %collective-permute-start.58 = (bf16[32,1024]{1,0:T(8,128)(2,1)S(1)}, bf16[32,1024]{1,0:T(8,128)(2,1)S(1)}, u32[]{:S(2)}, u32[]{:S(2)}) collective-permute-start(bf16[32,1024]{1,0:T(8,128)(2,1)S(1)} %get-tuple-element.26), channel_id=1, source_target_pairs={{0,6},{1,7},{2,8},{3,9},{4,10},{5,11},{6,12},{7,13},{8,14},{9,15},... | collective-permute-start | bytes 196616 | tf_op jit(solution)/shard_map/ppermute | solution.py:114
  305.7 3.5 %collective-permute-done.58 = bf16[32,1024]{1,0:T(8,128)(2,1)S(1)} collective-permute-done((bf16[32,1024]{1,0:T(8,128)(2,1)S(1)}, bf16[32,1024]{1,0:T(8,128)(2,1)S(1)}, u32[]{:S(2)}, u32[]{:S(2)}) %collective-permute-start.58) | collective-permute-done | bytes 65568 | tf_op jit(solution)/shard_map/ppermute | solution.py:114
  310.0 5.6 %collective-permute-done.59 = bf16[32,1024]{1,0:T(8,128)(2,1)S(1)} collective-permute-done((bf16[32,1024]{1,0:T(8,128)(2,1)S(1)}, bf16[32,1024]{1,0:T(8,128)(2,1)S(1)}, u32[]{:S(2)}, u32[]{:S(2)}) %collective-permute-start.59) | collective-permute-done | bytes 65568 | tf_op jit(solution)/shard_map/ppermute | solution.py:114
  (186 shorter events, 81.3 us)
Async XLA Ops:
  0.0 11.3 %collective-permute-start = (bf16[128,1024]{1,0:T(8,128)(2,1)}, bf16[128,1024]{1,0:T(8,128)(2,1)}, u32[]{:S(2)}, u32[]{:S(2)}) collective-permute-start(bf16[128,1024]{1,0:T(8,128)(2,1)} %param.16), channel_id=1, source_target_pairs={{0,16},{16,0},{1,17},{17,1},{2,18},{18,2},{3,19},{19,3},{4,20},{20... | collective-permute-start | bytes 786440 | tf_op jit(solution)/shard_map/ppermute | solution.py:41
  13.3 8.0 %collective-permute-start.1 = (f32[128,512]{1,0:T(8,128)}, f32[128,512]{1,0:T(8,128)S(1)}, u32[]{:S(2)}, u32[]{:S(2)}) collective-permute-start(f32[128,512]{1,0:T(8,128)} %fusion.40), channel_id=1, source_target_pairs={{16,0},{0,16},{17,1},{1,17},{18,2},{2,18},{19,3},{3,19},{20,4},{4,... | collective-permute-start | bytes 786440 | tf_op jit(solution)/shard_map/ppermute | solution.py:43
  23.5 8.4 %collective-permute-start.2 = (bf16[32,1024]{1,0:T(8,128)(2,1)S(1)}, bf16[32,1024]{1,0:T(8,128)(2,1)S(1)}, u32[]{:S(2)}, u32[]{:S(2)}) collective-permute-start(bf16[32,1024]{1,0:T(8,128)(2,1)S(1)} %get-tuple-element.82), channel_id=1, source_target_pairs={{0,1},{1,2},{2,3},{3,4},{4,5},{5,6},{6,7},{7,8},{8,9},{9,10},{10,1... | collective-permute-start | bytes 196616 | tf_op jit(solution)/shard_map/ppermute | solution.py:93
  23.6 57.4 %collective-permute-start.13 = (bf16[32,1024]{1,0:T(8,128)(2,1)S(1)}, bf16[32,1024]{1,0:T(8,128)(2,1)S(1)}, u32[]{:S(2)}, u32[]{:S(2)}) collective-permute-start(bf16[32,1024]{1,0:T(8,128)(2,1)S(1)} %get-tuple-element.71), channel_id=1, source_target_pairs={{0,12},{1,13},{2,14},{3,15},{4,16},{5,17},{6,18},{7,19},{8,20},{9,... | collective-permute-start | bytes 196616 | tf_op jit(solution)/shard_map/ppermute | solution.py:93
  27.2 51.6 %collective-permute-start.12 = (bf16[32,1024]{1,0:T(8,128)(2,1)S(1)}, bf16[32,1024]{1,0:T(8,128)(2,1)S(1)}, u32[]{:S(2)}, u32[]{:S(2)}) collective-permute-start(bf16[32,1024]{1,0:T(8,128)(2,1)S(1)} %get-tuple-element.72), channel_id=1, source_target_pairs={{0,11},{1,12},{2,13},{3,14},{4,15},{5,16},{6,17},{7,18},{8,19},{9,... | collective-permute-start | bytes 196616 | tf_op jit(solution)/shard_map/ppermute | solution.py:93
  28.7 49.9 %collective-permute-start.11 = (bf16[32,1024]{1,0:T(8,128)(2,1)S(1)}, bf16[32,1024]{1,0:T(8,128)(2,1)S(1)}, u32[]{:S(2)}, u32[]{:S(2)}) collective-permute-start(bf16[32,1024]{1,0:T(8,128)(2,1)S(1)} %get-tuple-element.73), channel_id=1, source_target_pairs={{0,10},{1,11},{2,12},{3,13},{4,14},{5,15},{6,16},{7,17},{8,18},{9,... | collective-permute-start | bytes 196616 | tf_op jit(solution)/shard_map/ppermute | solution.py:93
  29.8 48.7 %collective-permute-start.10 = (bf16[32,1024]{1,0:T(8,128)(2,1)S(1)}, bf16[32,1024]{1,0:T(8,128)(2,1)S(1)}, u32[]{:S(2)}, u32[]{:S(2)}) collective-permute-start(bf16[32,1024]{1,0:T(8,128)(2,1)S(1)} %get-tuple-element.74), channel_id=1, source_target_pairs={{0,9},{1,10},{2,11},{3,12},{4,13},{5,14},{6,15},{7,16},{8,17},{9,1... | collective-permute-start | bytes 196616 | tf_op jit(solution)/shard_map/ppermute | solution.py:93
  31.9 8.0 %collective-permute-start.3 = (bf16[32,1024]{1,0:T(8,128)(2,1)S(1)}, bf16[32,1024]{1,0:T(8,128)(2,1)S(1)}, u32[]{:S(2)}, u32[]{:S(2)}) collective-permute-start(bf16[32,1024]{1,0:T(8,128)(2,1)S(1)} %get-tuple-element.81), channel_id=1, source_target_pairs={{0,2},{1,3},{2,4},{3,5},{4,6},{5,7},{6,8},{7,9},{8,10},{9,11},{10,... | collective-permute-start | bytes 196616 | tf_op jit(solution)/shard_map/ppermute | solution.py:93
  39.9 6.4 %collective-permute-start.4 = (bf16[32,1024]{1,0:T(8,128)(2,1)S(1)}, bf16[32,1024]{1,0:T(8,128)(2,1)S(1)}, u32[]{:S(2)}, u32[]{:S(2)}) collective-permute-start(bf16[32,1024]{1,0:T(8,128)(2,1)S(1)} %get-tuple-element.80), channel_id=1, source_target_pairs={{0,3},{1,4},{2,5},{3,6},{4,7},{5,8},{6,9},{7,10},{8,11},{9,12},{10... | collective-permute-start | bytes 196616 | tf_op jit(solution)/shard_map/ppermute | solution.py:93
  46.3 7.3 %collective-permute-start.5 = (bf16[32,1024]{1,0:T(8,128)(2,1)S(1)}, bf16[32,1024]{1,0:T(8,128)(2,1)S(1)}, u32[]{:S(2)}, u32[]{:S(2)}) collective-permute-start(bf16[32,1024]{1,0:T(8,128)(2,1)S(1)} %get-tuple-element.79), channel_id=1, source_target_pairs={{0,4},{1,5},{2,6},{3,7},{4,8},{5,9},{6,10},{7,11},{8,12},{9,13},{1... | collective-permute-start | bytes 196616 | tf_op jit(solution)/shard_map/ppermute | solution.py:93
  53.6 6.4 %collective-permute-start.6 = (bf16[32,1024]{1,0:T(8,128)(2,1)S(1)}, bf16[32,1024]{1,0:T(8,128)(2,1)S(1)}, u32[]{:S(2)}, u32[]{:S(2)}) collective-permute-start(bf16[32,1024]{1,0:T(8,128)(2,1)S(1)} %get-tuple-element.78), channel_id=1, source_target_pairs={{0,5},{1,6},{2,7},{3,8},{4,9},{5,10},{6,11},{7,12},{8,13},{9,14},{... | collective-permute-start | bytes 196616 | tf_op jit(solution)/shard_map/ppermute | solution.py:93
  60.0 7.0 %collective-permute-start.7 = (bf16[32,1024]{1,0:T(8,128)(2,1)S(1)}, bf16[32,1024]{1,0:T(8,128)(2,1)S(1)}, u32[]{:S(2)}, u32[]{:S(2)}) collective-permute-start(bf16[32,1024]{1,0:T(8,128)(2,1)S(1)} %get-tuple-element.77), channel_id=1, source_target_pairs={{0,6},{1,7},{2,8},{3,9},{4,10},{5,11},{6,12},{7,13},{8,14},{9,15},... | collective-permute-start | bytes 196616 | tf_op jit(solution)/shard_map/ppermute | solution.py:93
  66.9 5.5 %collective-permute-start.8 = (bf16[32,1024]{1,0:T(8,128)(2,1)S(1)}, bf16[32,1024]{1,0:T(8,128)(2,1)S(1)}, u32[]{:S(2)}, u32[]{:S(2)}) collective-permute-start(bf16[32,1024]{1,0:T(8,128)(2,1)S(1)} %get-tuple-element.76), channel_id=1, source_target_pairs={{0,7},{1,8},{2,9},{3,10},{4,11},{5,12},{6,13},{7,14},{8,15},{9,16}... | collective-permute-start | bytes 196616 | tf_op jit(solution)/shard_map/ppermute | solution.py:93
  72.4 6.1 %collective-permute-start.9 = (bf16[32,1024]{1,0:T(8,128)(2,1)S(1)}, bf16[32,1024]{1,0:T(8,128)(2,1)S(1)}, u32[]{:S(2)}, u32[]{:S(2)}) collective-permute-start(bf16[32,1024]{1,0:T(8,128)(2,1)S(1)} %get-tuple-element.75), channel_id=1, source_target_pairs={{0,8},{1,9},{2,10},{3,11},{4,12},{5,13},{6,14},{7,15},{8,16},{9,17... | collective-permute-start | bytes 196616 | tf_op jit(solution)/shard_map/ppermute | solution.py:93
  78.5 83.9 %collective-permute-start.32 = (bf16[32,1024]{1,0:T(8,128)(2,1)S(1)}, bf16[32,1024]{1,0:T(8,128)(2,1)S(1)}, u32[]{:S(2)}, u32[]{:S(2)}) collective-permute-start(bf16[32,1024]{1,0:T(8,128)(2,1)S(1)} %get-tuple-element.52), channel_id=1, source_target_pairs={{0,31},{1,0},{2,1},{3,2},{4,3},{5,4},{6,5},{7,6},{8,7},{9,8},{10,9... | collective-permute-start | bytes 196616 | tf_op jit(solution)/shard_map/ppermute | solution.py:93
  78.5 83.8 %collective-permute-start.31 = (bf16[32,1024]{1,0:T(8,128)(2,1)S(1)}, bf16[32,1024]{1,0:T(8,128)(2,1)S(1)}, u32[]{:S(2)}, u32[]{:S(2)}) collective-permute-start(bf16[32,1024]{1,0:T(8,128)(2,1)S(1)} %get-tuple-element.53), channel_id=1, source_target_pairs={{0,30},{1,31},{2,0},{3,1},{4,2},{5,3},{6,4},{7,5},{8,6},{9,7},{10,... | collective-permute-start | bytes 196616 | tf_op jit(solution)/shard_map/ppermute | solution.py:93
  78.6 83.7 %collective-permute-start.30 = (bf16[32,1024]{1,0:T(8,128)(2,1)S(1)}, bf16[32,1024]{1,0:T(8,128)(2,1)S(1)}, u32[]{:S(2)}, u32[]{:S(2)}) collective-permute-start(bf16[32,1024]{1,0:T(8,128)(2,1)S(1)} %get-tuple-element.54), channel_id=1, source_target_pairs={{0,29},{1,30},{2,31},{3,0},{4,1},{5,2},{6,3},{7,4},{8,5},{9,6},{10... | collective-permute-start | bytes 196616 | tf_op jit(solution)/shard_map/ppermute | solution.py:93
  78.8 83.4 %collective-permute-start.29 = (bf16[32,1024]{1,0:T(8,128)(2,1)S(1)}, bf16[32,1024]{1,0:T(8,128)(2,1)S(1)}, u32[]{:S(2)}, u32[]{:S(2)}) collective-permute-start(bf16[32,1024]{1,0:T(8,128)(2,1)S(1)} %get-tuple-element.55), channel_id=1, source_target_pairs={{0,28},{1,29},{2,30},{3,31},{4,0},{5,1},{6,2},{7,3},{8,4},{9,5},{1... | collective-permute-start | bytes 196616 | tf_op jit(solution)/shard_map/ppermute | solution.py:93
  81.0 5.3 %collective-permute-start.14 = (bf16[32,1024]{1,0:T(8,128)(2,1)S(1)}, bf16[32,1024]{1,0:T(8,128)(2,1)S(1)}, u32[]{:S(2)}, u32[]{:S(2)}) collective-permute-start(bf16[32,1024]{1,0:T(8,128)(2,1)S(1)} %get-tuple-element.70), channel_id=1, source_target_pairs={{0,13},{1,14},{2,15},{3,16},{4,17},{5,18},{6,19},{7,20},{8,21},{9,... | collective-permute-start | bytes 196616 | tf_op jit(solution)/shard_map/ppermute | solution.py:93
  86.3 5.7 %collective-permute-start.15 = (bf16[32,1024]{1,0:T(8,128)(2,1)S(1)}, bf16[32,1024]{1,0:T(8,128)(2,1)S(1)}, u32[]{:S(2)}, u32[]{:S(2)}) collective-permute-start(bf16[32,1024]{1,0:T(8,128)(2,1)S(1)} %get-tuple-element.69), channel_id=1, source_target_pairs={{0,14},{1,15},{2,16},{3,17},{4,18},{5,19},{6,20},{7,21},{8,22},{9,... | collective-permute-start | bytes 196616 | tf_op jit(solution)/shard_map/ppermute | solution.py:93
  101.1 6.4 %collective-permute-start.18 = (bf16[32,1024]{1,0:T(8,128)(2,1)S(1)}, bf16[32,1024]{1,0:T(8,128)(2,1)S(1)}, u32[]{:S(2)}, u32[]{:S(2)}) collective-permute-start(bf16[32,1024]{1,0:T(8,128)(2,1)S(1)} %get-tuple-element.66), channel_id=1, source_target_pairs={{0,17},{1,18},{2,19},{3,20},{4,21},{5,22},{6,23},{7,24},{8,25},{9,... | collective-permute-start | bytes 196616 | tf_op jit(solution)/shard_map/ppermute | solution.py:93
  107.5 7.0 %collective-permute-start.19 = (bf16[32,1024]{1,0:T(8,128)(2,1)S(1)}, bf16[32,1024]{1,0:T(8,128)(2,1)S(1)}, u32[]{:S(2)}, u32[]{:S(2)}) collective-permute-start(bf16[32,1024]{1,0:T(8,128)(2,1)S(1)} %get-tuple-element.65), channel_id=1, source_target_pairs={{0,18},{1,19},{2,20},{3,21},{4,22},{5,23},{6,24},{7,25},{8,26},{9,... | collective-permute-start | bytes 196616 | tf_op jit(solution)/shard_map/ppermute | solution.py:93
  114.4 5.5 %collective-permute-start.20 = (bf16[32,1024]{1,0:T(8,128)(2,1)S(1)}, bf16[32,1024]{1,0:T(8,128)(2,1)S(1)}, u32[]{:S(2)}, u32[]{:S(2)}) collective-permute-start(bf16[32,1024]{1,0:T(8,128)(2,1)S(1)} %get-tuple-element.64), channel_id=1, source_target_pairs={{0,19},{1,20},{2,21},{3,22},{4,23},{5,24},{6,25},{7,26},{8,27},{9,... | collective-permute-start | bytes 196616 | tf_op jit(solution)/shard_map/ppermute | solution.py:93
  119.9 6.1 %collective-permute-start.21 = (bf16[32,1024]{1,0:T(8,128)(2,1)S(1)}, bf16[32,1024]{1,0:T(8,128)(2,1)S(1)}, u32[]{:S(2)}, u32[]{:S(2)}) collective-permute-start(bf16[32,1024]{1,0:T(8,128)(2,1)S(1)} %get-tuple-element.63), channel_id=1, source_target_pairs={{0,20},{1,21},{2,22},{3,23},{4,24},{5,25},{6,26},{7,27},{8,28},{9,... | collective-permute-start | bytes 196616 | tf_op jit(solution)/shard_map/ppermute | solution.py:93
  126.0 5.5 %collective-permute-start.22 = (bf16[32,1024]{1,0:T(8,128)(2,1)S(1)}, bf16[32,1024]{1,0:T(8,128)(2,1)S(1)}, u32[]{:S(2)}, u32[]{:S(2)}) collective-permute-start(bf16[32,1024]{1,0:T(8,128)(2,1)S(1)} %get-tuple-element.62), channel_id=1, source_target_pairs={{0,21},{1,22},{2,23},{3,24},{4,25},{5,26},{6,27},{7,28},{8,29},{9,... | collective-permute-start | bytes 196616 | tf_op jit(solution)/shard_map/ppermute | solution.py:93
  131.5 6.1 %collective-permute-start.23 = (bf16[32,1024]{1,0:T(8,128)(2,1)S(1)}, bf16[32,1024]{1,0:T(8,128)(2,1)S(1)}, u32[]{:S(2)}, u32[]{:S(2)}) collective-permute-start(bf16[32,1024]{1,0:T(8,128)(2,1)S(1)} %get-tuple-element.61), channel_id=1, source_target_pairs={{0,22},{1,23},{2,24},{3,25},{4,26},{5,27},{6,28},{7,29},{8,30},{9,... | collective-permute-start | bytes 196616 | tf_op jit(solution)/shard_map/ppermute | solution.py:93
  152.4 6.2 %collective-permute-start.27 = (bf16[32,1024]{1,0:T(8,128)(2,1)S(1)}, bf16[32,1024]{1,0:T(8,128)(2,1)S(1)}, u32[]{:S(2)}, u32[]{:S(2)}) collective-permute-start(bf16[32,1024]{1,0:T(8,128)(2,1)S(1)} %get-tuple-element.57), channel_id=1, source_target_pairs={{0,26},{1,27},{2,28},{3,29},{4,30},{5,31},{6,0},{7,1},{8,2},{9,3},... | collective-permute-start | bytes 196616 | tf_op jit(solution)/shard_map/ppermute | solution.py:93
  166.3 12.5 %collective-permute-start.33 = (bf16[32,1024]{1,0:T(8,128)(2,1)S(1)}, bf16[32,1024]{1,0:T(8,128)(2,1)S(1)}, u32[]{:S(2)}, u32[]{:S(2)}) collective-permute-start(bf16[32,1024]{1,0:T(8,128)(2,1)S(1)} %get-tuple-element.51), channel_id=1, source_target_pairs={{0,31},{1,0},{2,1},{3,2},{4,3},{5,4},{6,5},{7,6},{8,7},{9,8},{10,9... | collective-permute-start | bytes 196616 | tf_op jit(solution)/shard_map/ppermute | solution.py:114
  170.7 59.6 %collective-permute-start.44 = (bf16[32,1024]{1,0:T(8,128)(2,1)S(1)}, bf16[32,1024]{1,0:T(8,128)(2,1)S(1)}, u32[]{:S(2)}, u32[]{:S(2)}) collective-permute-start(bf16[32,1024]{1,0:T(8,128)(2,1)S(1)} %get-tuple-element.40), channel_id=1, source_target_pairs={{0,20},{1,21},{2,22},{3,23},{4,24},{5,25},{6,26},{7,27},{8,28},{9,... | collective-permute-start | bytes 196616 | tf_op jit(solution)/shard_map/ppermute | solution.py:114
  170.7 59.5 %collective-permute-start.43 = (bf16[32,1024]{1,0:T(8,128)(2,1)S(1)}, bf16[32,1024]{1,0:T(8,128)(2,1)S(1)}, u32[]{:S(2)}, u32[]{:S(2)}) collective-permute-start(bf16[32,1024]{1,0:T(8,128)(2,1)S(1)} %get-tuple-element.41), channel_id=1, source_target_pairs={{0,21},{1,22},{2,23},{3,24},{4,25},{5,26},{6,27},{7,28},{8,29},{9,... | collective-permute-start | bytes 196616 | tf_op jit(solution)/shard_map/ppermute | solution.py:114
  170.8 51.2 %collective-permute-start.42 = (bf16[32,1024]{1,0:T(8,128)(2,1)S(1)}, bf16[32,1024]{1,0:T(8,128)(2,1)S(1)}, u32[]{:S(2)}, u32[]{:S(2)}) collective-permute-start(bf16[32,1024]{1,0:T(8,128)(2,1)S(1)} %get-tuple-element.42), channel_id=1, source_target_pairs={{0,22},{1,23},{2,24},{3,25},{4,26},{5,27},{6,28},{7,29},{8,30},{9,... | collective-permute-start | bytes 196616 | tf_op jit(solution)/shard_map/ppermute | solution.py:114
  177.7 42.6 %collective-permute-start.41 = (bf16[32,1024]{1,0:T(8,128)(2,1)S(1)}, bf16[32,1024]{1,0:T(8,128)(2,1)S(1)}, u32[]{:S(2)}, u32[]{:S(2)}) collective-permute-start(bf16[32,1024]{1,0:T(8,128)(2,1)S(1)} %get-tuple-element.43), channel_id=1, source_target_pairs={{0,23},{1,24},{2,25},{3,26},{4,27},{5,28},{6,29},{7,30},{8,31},{9,... | collective-permute-start | bytes 196616 | tf_op jit(solution)/shard_map/ppermute | solution.py:114
  198.1 7.6 %collective-permute-start.38 = (bf16[32,1024]{1,0:T(8,128)(2,1)S(1)}, bf16[32,1024]{1,0:T(8,128)(2,1)S(1)}, u32[]{:S(2)}, u32[]{:S(2)}) collective-permute-start(bf16[32,1024]{1,0:T(8,128)(2,1)S(1)} %get-tuple-element.46), channel_id=1, source_target_pairs={{0,26},{1,27},{2,28},{3,29},{4,30},{5,31},{6,0},{7,1},{8,2},{9,3},... | collective-permute-start | bytes 196616 | tf_op jit(solution)/shard_map/ppermute | solution.py:114
  205.6 7.0 %collective-permute-start.39 = (bf16[32,1024]{1,0:T(8,128)(2,1)S(1)}, bf16[32,1024]{1,0:T(8,128)(2,1)S(1)}, u32[]{:S(2)}, u32[]{:S(2)}) collective-permute-start(bf16[32,1024]{1,0:T(8,128)(2,1)S(1)} %get-tuple-element.45), channel_id=1, source_target_pairs={{0,25},{1,26},{2,27},{3,28},{4,29},{5,30},{6,31},{7,0},{8,1},{9,2}... | collective-permute-start | bytes 196616 | tf_op jit(solution)/shard_map/ppermute | solution.py:114
  212.7 7.5 %collective-permute-start.40 = (bf16[32,1024]{1,0:T(8,128)(2,1)S(1)}, bf16[32,1024]{1,0:T(8,128)(2,1)S(1)}, u32[]{:S(2)}, u32[]{:S(2)}) collective-permute-start(bf16[32,1024]{1,0:T(8,128)(2,1)S(1)} %get-tuple-element.44), channel_id=1, source_target_pairs={{0,24},{1,25},{2,26},{3,27},{4,28},{5,29},{6,30},{7,31},{8,0},{9,1... | collective-permute-start | bytes 196616 | tf_op jit(solution)/shard_map/ppermute | solution.py:114
  220.2 95.5 %collective-permute-start.63 = (bf16[32,1024]{1,0:T(8,128)(2,1)S(1)}, bf16[32,1024]{1,0:T(8,128)(2,1)S(1)}, u32[]{:S(2)}, u32[]{:S(2)}) collective-permute-start(bf16[32,1024]{1,0:T(8,128)(2,1)S(1)} %get-tuple-element.21), channel_id=1, source_target_pairs={{0,1},{1,2},{2,3},{3,4},{4,5},{5,6},{6,7},{7,8},{8,9},{9,10},{10,1... | collective-permute-start | bytes 196616 | tf_op jit(solution)/shard_map/ppermute | solution.py:114
  220.3 95.3 %collective-permute-start.62 = (bf16[32,1024]{1,0:T(8,128)(2,1)S(1)}, bf16[32,1024]{1,0:T(8,128)(2,1)S(1)}, u32[]{:S(2)}, u32[]{:S(2)}) collective-permute-start(bf16[32,1024]{1,0:T(8,128)(2,1)S(1)} %get-tuple-element.22), channel_id=1, source_target_pairs={{0,2},{1,3},{2,4},{3,5},{4,6},{5,7},{6,8},{7,9},{8,10},{9,11},{10,... | collective-permute-start | bytes 196616 | tf_op jit(solution)/shard_map/ppermute | solution.py:114
  222.0 93.6 %collective-permute-start.61 = (bf16[32,1024]{1,0:T(8,128)(2,1)S(1)}, bf16[32,1024]{1,0:T(8,128)(2,1)S(1)}, u32[]{:S(2)}, u32[]{:S(2)}) collective-permute-start(bf16[32,1024]{1,0:T(8,128)(2,1)S(1)} %get-tuple-element.23), channel_id=1, source_target_pairs={{0,3},{1,4},{2,5},{3,6},{4,7},{5,8},{6,9},{7,10},{8,11},{9,12},{10... | collective-permute-start | bytes 196616 | tf_op jit(solution)/shard_map/ppermute | solution.py:114
  230.2 85.4 %collective-permute-start.60 = (bf16[32,1024]{1,0:T(8,128)(2,1)S(1)}, bf16[32,1024]{1,0:T(8,128)(2,1)S(1)}, u32[]{:S(2)}, u32[]{:S(2)}) collective-permute-start(bf16[32,1024]{1,0:T(8,128)(2,1)S(1)} %get-tuple-element.24), channel_id=1, source_target_pairs={{0,4},{1,5},{2,6},{3,7},{4,8},{5,9},{6,10},{7,11},{8,12},{9,13},{1... | collective-permute-start | bytes 196616 | tf_op jit(solution)/shard_map/ppermute | solution.py:114
  230.3 5.5 %collective-permute-start.45 = (bf16[32,1024]{1,0:T(8,128)(2,1)S(1)}, bf16[32,1024]{1,0:T(8,128)(2,1)S(1)}, u32[]{:S(2)}, u32[]{:S(2)}) collective-permute-start(bf16[32,1024]{1,0:T(8,128)(2,1)S(1)} %get-tuple-element.39), channel_id=1, source_target_pairs={{0,19},{1,20},{2,21},{3,22},{4,23},{5,24},{6,25},{7,26},{8,27},{9,... | collective-permute-start | bytes 196616 | tf_op jit(solution)/shard_map/ppermute | solution.py:114
  235.9 8.5 %collective-permute-start.46 = (bf16[32,1024]{1,0:T(8,128)(2,1)S(1)}, bf16[32,1024]{1,0:T(8,128)(2,1)S(1)}, u32[]{:S(2)}, u32[]{:S(2)}) collective-permute-start(bf16[32,1024]{1,0:T(8,128)(2,1)S(1)} %get-tuple-element.38), channel_id=1, source_target_pairs={{0,18},{1,19},{2,20},{3,21},{4,22},{5,23},{6,24},{7,25},{8,26},{9,... | collective-permute-start | bytes 196616 | tf_op jit(solution)/shard_map/ppermute | solution.py:114
  244.3 6.4 %collective-permute-start.47 = (bf16[32,1024]{1,0:T(8,128)(2,1)S(1)}, bf16[32,1024]{1,0:T(8,128)(2,1)S(1)}, u32[]{:S(2)}, u32[]{:S(2)}) collective-permute-start(bf16[32,1024]{1,0:T(8,128)(2,1)S(1)} %get-tuple-element.37), channel_id=1, source_target_pairs={{0,17},{1,18},{2,19},{3,20},{4,21},{5,22},{6,23},{7,24},{8,25},{9,... | collective-permute-start | bytes 196616 | tf_op jit(solution)/shard_map/ppermute | solution.py:114
  278.7 6.1 %collective-permute-start.54 = (bf16[32,1024]{1,0:T(8,128)(2,1)S(1)}, bf16[32,1024]{1,0:T(8,128)(2,1)S(1)}, u32[]{:S(2)}, u32[]{:S(2)}) collective-permute-start(bf16[32,1024]{1,0:T(8,128)(2,1)S(1)} %get-tuple-element.30), channel_id=1, source_target_pairs={{0,10},{1,11},{2,12},{3,13},{4,14},{5,15},{6,16},{7,17},{8,18},{9,... | collective-permute-start | bytes 196616 | tf_op jit(solution)/shard_map/ppermute | solution.py:114
  284.7 5.5 %collective-permute-start.55 = (bf16[32,1024]{1,0:T(8,128)(2,1)S(1)}, bf16[32,1024]{1,0:T(8,128)(2,1)S(1)}, u32[]{:S(2)}, u32[]{:S(2)}) collective-permute-start(bf16[32,1024]{1,0:T(8,128)(2,1)S(1)} %get-tuple-element.29), channel_id=1, source_target_pairs={{0,9},{1,10},{2,11},{3,12},{4,13},{5,14},{6,15},{7,16},{8,17},{9,1... | collective-permute-start | bytes 196616 | tf_op jit(solution)/shard_map/ppermute | solution.py:114
  290.2 6.2 %collective-permute-start.56 = (bf16[32,1024]{1,0:T(8,128)(2,1)S(1)}, bf16[32,1024]{1,0:T(8,128)(2,1)S(1)}, u32[]{:S(2)}, u32[]{:S(2)}) collective-permute-start(bf16[32,1024]{1,0:T(8,128)(2,1)S(1)} %get-tuple-element.28), channel_id=1, source_target_pairs={{0,8},{1,9},{2,10},{3,11},{4,12},{5,13},{6,14},{7,15},{8,16},{9,17... | collective-permute-start | bytes 196616 | tf_op jit(solution)/shard_map/ppermute | solution.py:114
  296.4 5.5 %collective-permute-start.57 = (bf16[32,1024]{1,0:T(8,128)(2,1)S(1)}, bf16[32,1024]{1,0:T(8,128)(2,1)S(1)}, u32[]{:S(2)}, u32[]{:S(2)}) collective-permute-start(bf16[32,1024]{1,0:T(8,128)(2,1)S(1)} %get-tuple-element.27), channel_id=1, source_target_pairs={{0,7},{1,8},{2,9},{3,10},{4,11},{5,12},{6,13},{7,14},{8,15},{9,16}... | collective-permute-start | bytes 196616 | tf_op jit(solution)/shard_map/ppermute | solution.py:114
  301.9 7.3 %collective-permute-start.58 = (bf16[32,1024]{1,0:T(8,128)(2,1)S(1)}, bf16[32,1024]{1,0:T(8,128)(2,1)S(1)}, u32[]{:S(2)}, u32[]{:S(2)}) collective-permute-start(bf16[32,1024]{1,0:T(8,128)(2,1)S(1)} %get-tuple-element.26), channel_id=1, source_target_pairs={{0,6},{1,7},{2,8},{3,9},{4,10},{5,11},{6,12},{7,13},{8,14},{9,15},... | collective-permute-start | bytes 196616 | tf_op jit(solution)/shard_map/ppermute | solution.py:114
  309.2 6.4 %collective-permute-start.59 = (bf16[32,1024]{1,0:T(8,128)(2,1)S(1)}, bf16[32,1024]{1,0:T(8,128)(2,1)S(1)}, u32[]{:S(2)}, u32[]{:S(2)}) collective-permute-start(bf16[32,1024]{1,0:T(8,128)(2,1)S(1)} %get-tuple-element.25), channel_id=1, source_target_pairs={{0,5},{1,6},{2,7},{3,8},{4,9},{5,10},{6,11},{7,12},{8,13},{9,14},{... | collective-permute-start | bytes 196616 | tf_op jit(solution)/shard_map/ppermute | solution.py:114
  (21 other events, 269.8 us)

commit v7 on v4

--- a/solution.py
+++ b/solution.py
@@ -43,12 +43,20 @@
     plane_slots = groups * lanes * cap_size
     my_plane = lax.axis_index("eh")
 
-    columns = jnp.dot(
-        lax.all_gather(attention, "grp", axis=0, tiled=True),
-        out_proj,
-        preferred_element_type=jnp.float32,
-    )
-    attn_proj = lax.all_to_all(columns, "grp", split_axis=0, concat_axis=1, tiled=True)
+    me_grp = lax.axis_index("grp")
+    blocks = [None] * groups
+    blocks[0] = jnp.dot(attention, out_proj, preferred_element_type=jnp.float32)
+    for shift in range(1, groups):
+        ahead = [(g, (g + shift) % groups) for g in range(groups)]
+        back = [(b, a) for a, b in ahead]
+        visiting = lax.ppermute(attention, "grp", ahead)
+        done = jnp.dot(visiting, out_proj, preferred_element_type=jnp.float32)
+        blocks[shift] = lax.ppermute(done, "grp", back)
+    stacked = jnp.stack(blocks, axis=0)
+    order_cols = (jnp.arange(groups, dtype=jnp.int32) - me_grp) % groups
+    attn_proj = jnp.concatenate(
+        [jnp.take(stacked, order_cols[j], axis=0) for j in range(groups)], axis=1
+    )
     hidden_state = (residual.astype(jnp.float32) + attn_proj).astype(jnp.bfloat16)
     normed = rms_scale(hidden_state.astype(jnp.float32), pre_gain).astype(jnp.bfloat16)
 
@@ -168,9 +176,9 @@
         changes = [e for e in range(len(row)) if coords[e][axis] != coords[0][axis]]
         if changes:
             best = max(best, changes[0])
-    if best == 0 or len(row) % best:
+    if best == 0 or len(row) % best or (len(row) // best) % 2:
         return 1, len(row)
-    return len(row) // best, best
+    return 2, len(row) // 2
 
 
 def solution(mesh):

time: 160 us -> 133 us (0.83)
  blocking collectives: 67.2 us -> 45.1 us
  waiting for transfers between devices: 56.1 us -> 42.8 us
  other arithmetic: 6.44 us -> 12 us
  between operations: 0.35 us -> 4.04 us
  local copies, waits for them, and re-layouts: 8.44 us -> 6.63 us
    all_to_all x1, blocking collectives: 28.3 us -> 15.1 us  [on_device(): lax.all_to_all(partial.astype(jnp.bfloat16), 'eh', 0, 0, tiled=True)]
    all_to_all x1, waiting for transfers between devices: 25.4 us -> 14.1 us  [on_device(): lax.all_to_all(jnp.broadcast_to(packed[None], (planes,) + packed.shape),...]
    all_gather x1 -> x0, blocking collectives: 10.3 us -> none  [on_device(): lax.all_gather(attention, 'grp', axis=0, tiled=True)]
    all_to_all x1 -> x0, waiting for transfers between devices: 6.54 us -> none  [on_device(): lax.all_to_all(columns, 'grp', split_axis=0, concat_axis=1, tiled=True)]
    ppermute x0 -> x2, starting transfers between devices: none -> 4.5 us  [the longest x1 3.04 us: on_device(): visiting = lax.ppermute(attention, 'grp', ahead)]
    all_to_all x1 -> x0, starting transfers between devices: 3.62 us -> none  [on_device(): lax.all_to_all(columns, 'grp', split_axis=0, concat_axis=1, tiled=True)]
    all_to_all x1, waiting for transfers between devices: 24.1 us -> 27.1 us  [on_device(): lax.all_to_all(produced.reshape(arrived.shape), PLANE_AXES, split_axis=1,...]
    unnamed x34 -> x18, local copies, waits for them, and re-layouts: 2.89 us -> 0.2 us
  transfers between devices with their start and end apart: 3 -> 4, of which waited for: 3 -> 3; matrix products, arithmetic and copies ran while one was open for 2% -> 7% of each run, Pallas kernels for 0% -> 0%
where the time goes in v7:
time: 133 us; the launch traced here: 132 us
  blocking collectives  45.1 us (34%)
  waiting for transfers between devices  42.8 us (32%)
  starting transfers between devices  12.8 us (10%)
  other arithmetic  12 us (9%)
  matrix products  8.31 us (6%)
  local copies, waits for them, and re-layouts  6.63 us (5%)
  between operations  4.04 us (3%)
    all_to_all x1, blocking collectives, on_device(): lax.all_to_all(buffer.reshape(planes, groups * lanes, cap_size, features)...  30.1 us
    all_to_all x1, waiting for transfers between devices, on_device(): lax.all_to_all(produced.reshape(arrived.shape), PLANE_AXES, split_axis=1,...  27.1 us
    all_to_all x1, blocking collectives, on_device(): lax.all_to_all(partial.astype(jnp.bfloat16), 'eh', 0, 0, tiled=True)  15.1 us
    all_to_all x1, waiting for transfers between devices, on_device(): lax.all_to_all(jnp.broadcast_to(packed[None], (planes,) + packed.shape),...  14.1 us
    all_to_all x1, starting transfers between devices, on_device(): lax.all_to_all(produced.reshape(arrived.shape), PLANE_AXES, split_axis=1,...  4.42 us
    all_to_all x1, starting transfers between devices, on_device(): lax.all_to_all(jnp.broadcast_to(packed[None], (planes,) + packed.shape),...  3.86 us
    ppermute x1, starting transfers between devices, on_device(): visiting = lax.ppermute(attention, 'grp', ahead)  3.04 us
  transfers between devices with their start and end apart: 4, of which 3 were waited for; matrix products, arithmetic and copies ran while one was open for 7% of the time, Pallas kernels for 0%

profile of v7, /device:TPU:0, one launch (start us, length us, event | category | flops | bytes accessed | tf_op | source)
XLA Modules:
  0.0 131.7 jit_solution(7379661317519692153)
XLA Ops:
  0.0 3.0 %collective-permute-start = (bf16[128,1024]{1,0:T(8,128)(2,1)}, bf16[128,1024]{1,0:T(8,128)(2,1)}, u32[]{:S(2)}, u32[]{:S(2)}) collective-permute-start(bf16[128,1024]{1,0:T(8,128)(2,1)} %param.16), channel_id=1, source_target_pairs={{0,16},{16,0},{1,17},{17,1},{2,18},{18,2},{3,19},{19,3},{4,20},{20... | collective-permute-start | bytes 786440 | tf_op jit(solution)/shard_map/ppermute | solution.py:52
  3.0 0.8 select_reduce_fusion.4
  3.8 0.8 select_reduce_fusion.3
  4.6 0.7 multiply_add_fusion
  5.3 0.7 multiply_add_fusion.1
  6.0 0.2 fusion.22
  6.2 0.8 broadcast_in_dim.59
  7.0 0.1 select_reduce_fusion.1
  7.1 0.7 constant_dynamic-update-slice_fusion.4
  7.8 0.7 constant_dynamic-update-slice_fusion.2
  8.5 0.7 constant_dynamic-update-slice_fusion.1
  9.2 0.7 constant_dynamic-update-slice_fusion
  9.9 2.3 %fusion.47 = f32[128,512]{1,0:T(8,128)} fusion(bf16[128,1024]{1,0:T(8,128)(2,1)} %collective-permute-done, bf16[1024,512]{1,0:T(8,128)(2,1)} %param.18), kind=kOutput, calls=%fused_computation.104 | convolution fusion | flops 134217728 | bytes 1572864 | tf_op jit(solution)/shard_map/dot_general | solution.py:53
  12.3 1.5 %collective-permute-start.1 = (f32[128,512]{1,0:T(8,128)}, f32[128,512]{1,0:T(8,128)}, u32[]{:S(2)}, u32[]{:S(2)}) collective-permute-start(f32[128,512]{1,0:T(8,128)} %fusion.47), channel_id=1, source_target_pairs={{16,0},{0,16},{17,1},{1,17},{18,2},{2,18},{19,3},{3,19},{20,4},{4,... | collective-permute-start | bytes 786440 | tf_op jit(solution)/shard_map/ppermute | solution.py:54
  13.7 0.6 fusion.46
  18.1 0.1 copy.45
  18.2 0.1 reshape.54
  18.4 0.0 copy-start.3
  18.4 0.3 convolution_bitcast_fusion
  18.8 1.6 %collective-permute-done.1 = f32[128,512]{1,0:T(8,128)} collective-permute-done((f32[128,512]{1,0:T(8,128)}, f32[128,512]{1,0:T(8,128)}, u32[]{:S(2)}, u32[]{:S(2)}) %collective-permute-start.1) | collective-permute-done | bytes 262176 | tf_op jit(solution)/shard_map/ppermute | solution.py:54
  20.4 1.1 fusion.17
  21.4 0.2 fusion.7
  21.6 0.1 fusion.9
  21.8 0.9 broadcast_in_dim.90
  22.6 3.9 %all-to-all-start = ((bf16[2,136,1024]{2,1,0:T(8,128)(2,1)}), bf16[2,136,1024]{2,1,0:T(8,128)(2,1)S(1)}, u32[]{:S(2)}, u32[]{:S(2)}) async-start(bf16[2,136,1024]{2,1,0:T(8,128)(2,1)} %broadcast_in_dim.90), calls=%async_computation | async-start | bytes 1114112 | tf_op jit(solution)/shard_map/all_to_all | solution.py:109
  26.5 14.1 %all-to-all-done = bf16[2,136,1024]{2,1,0:T(8,128)(2,1)S(1)} async-done(((bf16[2,136,1024]{2,1,0:T(8,128)(2,1)}), bf16[2,136,1024]{2,1,0:T(8,128)(2,1)S(1)}, u32[]{:S(2)}, u32[]{:S(2)}) %all-to-all-start) | async-done | bytes 557088 | tf_op jit(solution)/shard_map/all_to_all | solution.py:109
  40.6 0.1 reshape.100
  40.8 0.2 fusion.45
  41.0 0.1 copy.55
  41.0 0.1 copy.56
  41.1 1.9 %fusion = pred[2,512,128]{2,1,0:T(8,128)(4,1)S(1)} fusion(s32[2,128,8]{1,2,0:T(8,128)S(1)} %convert_subtract_fusion), kind=kLoop, calls=%fused_computation.2 | loop fusion | flops 1966080 | bytes 139264 | tf_op jit(solution)/shard_map/reduce_or | solution.py:127
  43.0 0.7 convolution_convert_fusion.1
  43.7 0.3 copy.49
  44.0 30.1 %all_to_all.20 = bf16[2,16,32,1024]{3,2,0,1:T(8,128)(2,1)S(1)} all-to-all(bf16[2,16,32,1024]{3,2,0,1:T(8,128)(2,1)S(1)} %copy.49), channel_id=1, replica_groups=mesh['grp'=2,'eh'=2,'el'=8] {'grp','el'}, dimensions={1} | all-to-all | bytes 4194304 | tf_op jit(solution)/shard_map/all_to_all | solution.py:135
  74.1 0.3 copy.50
  74.4 2.3 %fusion.2 = f32[1024,1024]{1,0:T(8,128)S(1)} fusion(bf16[1024,1024]{1,0:T(8,128)(2,1)S(1)} %bitcast.33, bf16[1,1024,1024]{2,1,0:T(8,128)(2,1)S(1)} %copy-done), kind=kOutput, calls=%fused_computation.5 | convolution fusion | flops 2147483648 | bytes 8388608 | tf_op jit(solution)/shard_map/dot_general | solution.py:143
  76.7 1.3 convolution_convert_fusion
  78.0 1.5 %copy.51 = bf16[2,16,32,1024]{3,2,0,1:T(8,128)(2,1)} copy(bf16[2,16,32,1024]{3,2,1,0:T(8,128)(2,1)S(1)} %bitcast.34) | data formatting | bytes 4194304 | tf_op jit(solution)/shard_map/reshape | solution.py:151
  79.5 4.4 %all-to-all-start.2 = ((bf16[2,16,32,1024]{3,2,0,1:T(8,128)(2,1)}), bf16[2,16,32,1024]{3,2,0,1:T(8,128)(2,1)}, u32[]{:S(2)}, u32[]{:S(2)}) async-start(bf16[2,16,32,1024]{3,2,0,1:T(8,128)(2,1)} %copy.51), calls=%async_computation.2 | async-start | bytes 4194304 | tf_op jit(solution)/shard_map/all_to_all | solution.py:150
  84.0 0.1 copy.48
  84.0 1.5 %select_reduce_fusion = f32[2,512,128]{2,1,0:T(8,128)S(1)} fusion(f32[2,128,8]{1,2,0:T(8,128)S(1)} %copy.48, s32[2,128,8]{1,2,0:T(8,128)S(1)} %convert_subtract_fusion), kind=kLoop, calls=%fused_computation | loop fusion | flops 3014656 | bytes 540672 | tf_op jit(solution)/shard_map/reduce_sum | solution.py:153
  85.5 27.1 %all-to-all-done.2 = bf16[2,16,32,1024]{3,2,0,1:T(8,128)(2,1)} async-done(((bf16[2,16,32,1024]{3,2,0,1:T(8,128)(2,1)}), bf16[2,16,32,1024]{3,2,0,1:T(8,128)(2,1)}, u32[]{:S(2)}, u32[]{:S(2)}) %all-to-all-start.2) | async-done | bytes 2097184 | tf_op jit(solution)/shard_map/all_to_all | solution.py:150
  112.6 1.8 %copy.52 = bf16[2,16,32,1024]{3,2,1,0:T(8,128)(2,1)S(1)} copy(bf16[2,16,32,1024]{3,2,0,1:T(8,128)(2,1)} %all-to-all-done.2) | data formatting | bytes 4194304 | tf_op jit(solution)/shard_map/all_to_all | solution.py:150
  114.4 1.1 convolution_convert_fusion.2
  115.5 15.1 %all_to_all.21 = bf16[2,128,1024]{2,1,0:T(8,128)(2,1)S(1)} all-to-all(bf16[2,128,1024]{2,1,0:T(8,128)(2,1)S(1)} %convolution_convert_fusion.2), channel_id=1, replica_groups=mesh['grp'=2,'eh'=2,'el'=8] {'eh'}, dimensions={0} | all-to-all | bytes 1048576 | tf_op jit(solution)/shard_map/all_to_all | solution.py:162
  130.6 0.1 convert_reduce_fusion
  130.7 0.2 multiply_reduce_fusion
  130.9 0.8 multiply_convert_fusion
  (27 shorter events, 0.2 us)
Async XLA Ops:
  0.0 74.3 %copy-start = (bf16[1,1024,1024]{2,1,0:T(8,128)(2,1)S(1)}, bf16[1,1024,1024]{2,1,0:T(8,128)(2,1)}, u32[]{:S(2)}) copy-start(bf16[1,1024,1024]{2,1,0:T(8,128)(2,1)} %param.21) | copy-start | bytes 6291460
  0.0 18.4 %copy-start.2 = (bf16[128,1024]{1,0:T(8,128)(2,1)S(1)}, bf16[128,1024]{1,0:T(8,128)(2,1)}, u32[]{:S(2)}) copy-start(bf16[128,1024]{1,0:T(8,128)(2,1)} %param.16) | copy-start | bytes 786436
  0.0 18.4 %copy-start.1 = (bf16[1024,512]{1,0:T(8,128)(2,1)S(1)}, bf16[1024,512]{1,0:T(8,128)(2,1)}, u32[]{:S(2)}) copy-start(bf16[1024,512]{1,0:T(8,128)(2,1)} %param.18) | copy-start | bytes 3145732
  0.0 9.9 %collective-permute-start = (bf16[128,1024]{1,0:T(8,128)(2,1)}, bf16[128,1024]{1,0:T(8,128)(2,1)}, u32[]{:S(2)}, u32[]{:S(2)}) collective-permute-start(bf16[128,1024]{1,0:T(8,128)(2,1)} %param.16), channel_id=1, source_target_pairs={{0,16},{16,0},{1,17},{17,1},{2,18},{18,2},{3,19},{19,3},{4,20},{20... | collective-permute-start | bytes 786440 | tf_op jit(solution)/shard_map/ppermute | solution.py:52
  12.3 9.3 %copy-start.4 = (f32[1024]{0:T(1024)S(1)}, f32[1024]{0:T(1024)}, u32[]{:S(2)}) copy-start(f32[1024]{0:T(1024)} %param.19) | copy-start | bytes 12292
  12.3 8.1 %collective-permute-start.1 = (f32[128,512]{1,0:T(8,128)}, f32[128,512]{1,0:T(8,128)}, u32[]{:S(2)}, u32[]{:S(2)}) collective-permute-start(f32[128,512]{1,0:T(8,128)} %fusion.47), channel_id=1, source_target_pairs={{16,0},{0,16},{17,1},{1,17},{18,2},{2,18},{19,3},{3,19},{20,4},{4,... | collective-permute-start | bytes 786440 | tf_op jit(solution)/shard_map/ppermute | solution.py:54
  18.4 3.0 %copy-start.3 = (bf16[128,1024]{1,0:T(8,128)(2,1)S(1)}, bf16[128,1024]{1,0:T(8,128)(2,1)}, u32[]{:S(2)}) copy-start(bf16[128,1024]{1,0:T(8,128)(2,1)} %param.17) | copy-start | bytes 786436
  22.6 17.9 %all-to-all-start = ((bf16[2,136,1024]{2,1,0:T(8,128)(2,1)}), bf16[2,136,1024]{2,1,0:T(8,128)(2,1)S(1)}, u32[]{:S(2)}, u32[]{:S(2)}) async-start(bf16[2,136,1024]{2,1,0:T(8,128)(2,1)} %broadcast_in_dim.90), calls=%async_computation | async-start | bytes 1114112 | tf_op jit(solution)/shard_map/all_to_all | solution.py:109
  74.4 2.4 %copy-start.6 = (bf16[1,512,1024]{2,1,0:T(8,128)(2,1)S(1)}, bf16[1,512,1024]{2,1,0:T(8,128)(2,1)}, u32[]{:S(2)}) copy-start(bf16[1,512,1024]{2,1,0:T(8,128)(2,1)} %param.22) | copy-start | bytes 3145732
  79.5 33.1 %all-to-all-start.2 = ((bf16[2,16,32,1024]{3,2,0,1:T(8,128)(2,1)}), bf16[2,16,32,1024]{3,2,0,1:T(8,128)(2,1)}, u32[]{:S(2)}, u32[]{:S(2)}) async-start(bf16[2,16,32,1024]{3,2,0,1:T(8,128)(2,1)} %copy.51), calls=%async_computation.2 | async-start | bytes 4194304 | tf_op jit(solution)/shard_map/all_to_all | solution.py:150
  115.5 15.3 %copy-start.5 = (f32[1024]{0:T(1024)S(1)}, f32[1024]{0:T(1024)}, u32[]{:S(2)}) copy-start(f32[1024]{0:T(1024)} %param.20) | copy-start | bytes 12292

commit v8 on v7

--- a/solution.py
+++ b/solution.py
@@ -106,62 +106,68 @@
     meta_rows = -(-meta_size // (8 * features)) * 8
     meta_block = jnp.pad(meta.reshape(-1), (0, meta_rows * features - meta_size))
     packed = jnp.concatenate([normed, meta_block.reshape(meta_rows, features)], axis=0)
-    packed_all = lax.all_to_all(
-        jnp.broadcast_to(packed[None], (planes,) + packed.shape), "eh", 0, 0, tiled=True
-    )
-    normed_all = packed_all[:, :rows_here]
-    meta_all = (
-        packed_all[:, rows_here:]
-        .reshape(planes, -1)[:, :meta_size]
-        .reshape(planes, rows_here, meta.shape[1])
-        .astype(jnp.float32)
-    )
-    code_all = meta_all[:, :, :picks_row] * 128 + meta_all[:, :, picks_row : 2 * picks_row]
-    local = code_all.astype(jnp.int32) - my_plane * plane_slots
-    weights_all = (
-        meta_all[:, :, 2 * picks_row : 3 * picks_row]
-        + meta_all[:, :, 3 * picks_row : 4 * picks_row]
-    ) + meta_all[:, :, 4 * picks_row :]
-    slot_ids = jnp.arange(plane_slots, dtype=jnp.int32)
-    hit = local[:, None, :, :] == slot_ids[None, :, None, None]
-    dispatch = jnp.any(hit, axis=3).astype(jnp.bfloat16)
-    buffer = jnp.einsum(
-        "hcr,hrd->hcd", dispatch, normed_all, preferred_element_type=jnp.float32
-    ).astype(jnp.bfloat16)
-
     gate_up_local = slot_gate_up[0]
     down_local = slot_down[0]
     hidden_units = down_local.shape[0]
-    arrived = lax.all_to_all(
-        buffer.reshape(planes, groups * lanes, cap_size, features),
-        PLANE_AXES,
-        split_axis=1,
-        concat_axis=1,
-        tiled=True,
-    )
-    flattened = arrived.reshape(-1, features)
-    gate_up = jnp.dot(flattened, gate_up_local, preferred_element_type=jnp.float32)
-    expert_hidden = (jax.nn.silu(gate_up[:, :hidden_units]) * gate_up[:, hidden_units:]).astype(
-        jnp.bfloat16
-    )
-    produced = jnp.dot(expert_hidden, down_local, preferred_element_type=jnp.float32).astype(
-        jnp.bfloat16
-    )
-    returned = lax.all_to_all(
-        produced.reshape(arrived.shape), PLANE_AXES, split_axis=1, concat_axis=1, tiled=True
-    )
-    combine = jnp.sum(jnp.where(hit, weights_all[:, None, :, :], 0.0), axis=3)
-    partial = jnp.einsum(
-        "hcr,hcd->hrd",
-        combine,
-        returned.reshape(planes, plane_slots, features).astype(jnp.float32),
-        precision=lax.Precision.HIGHEST,
-        preferred_element_type=jnp.float32,
-    )
-    mixture = jnp.sum(
-        lax.all_to_all(partial.astype(jnp.bfloat16), "eh", 0, 0, tiled=True).astype(jnp.float32),
-        axis=0,
-    )
+    slot_ids = jnp.arange(plane_slots, dtype=jnp.int32)
+
+    def expert(rows_in):
+        gate_up = jnp.dot(rows_in, gate_up_local, preferred_element_type=jnp.float32)
+        expert_hidden = (
+            jax.nn.silu(gate_up[:, :hidden_units]) * gate_up[:, hidden_units:]
+        ).astype(jnp.bfloat16)
+        return jnp.dot(expert_hidden, down_local, preferred_element_type=jnp.float32).astype(
+            jnp.bfloat16
+        )
+
+    received = [packed] + [
+        lax.ppermute(packed, "eh", [(i, (i + shift) % planes) for i in range(planes)])
+        for shift in range(1, planes)
+    ]
+    partials = []
+    for shift, block in enumerate(received):
+        normed_s = block[:rows_here]
+        meta_s = (
+            block[rows_here:]
+            .reshape(-1)[:meta_size]
+            .reshape(rows_here, meta.shape[1])
+            .astype(jnp.float32)
+        )
+        code_s = meta_s[:, :picks_row] * 128 + meta_s[:, picks_row : 2 * picks_row]
+        local = code_s.astype(jnp.int32) - my_plane * plane_slots
+        weights_s = (
+            meta_s[:, 2 * picks_row : 3 * picks_row] + meta_s[:, 3 * picks_row : 4 * picks_row]
+        ) + meta_s[:, 4 * picks_row :]
+        hit = local[None, :, :] == slot_ids[:, None, None]
+        dispatch = jnp.any(hit, axis=2).astype(jnp.bfloat16)
+        buffer = jnp.dot(dispatch, normed_s, preferred_element_type=jnp.float32).astype(
+            jnp.bfloat16
+        )
+        arrived = lax.all_to_all(
+            buffer.reshape(groups * lanes, cap_size, features),
+            PLANE_AXES,
+            split_axis=0,
+            concat_axis=0,
+            tiled=True,
+        )
+        produced = expert(arrived.reshape(-1, features))
+        returned = lax.all_to_all(
+            produced.reshape(arrived.shape), PLANE_AXES, split_axis=0, concat_axis=0, tiled=True
+        )
+        combine = jnp.sum(jnp.where(hit, weights_s[None, :, :], 0.0), axis=2)
+        partial = jnp.dot(
+            combine.T,
+            returned.reshape(plane_slots, features).astype(jnp.float32),
+            precision=lax.Precision.HIGHEST,
+            preferred_element_type=jnp.float32,
+        )
+        if shift:
+            back = [((i + shift) % planes, i) for i in range(planes)]
+            partial = lax.ppermute(partial.astype(jnp.bfloat16), "eh", back).astype(jnp.float32)
+        partials.append(partial)
+    mixture = partials[0]
+    for partial in partials[1:]:
+        mixture = mixture + partial
     return rms_scale(hidden_state.astype(jnp.float32) + mixture, post_gain).astype(jnp.bfloat16)
 
 

time: 133 us -> 131 us (0.985)
  blocking collectives: 45.1 us -> 0 us
  waiting for transfers between devices: 42.8 us -> 65.3 us
  starting transfers between devices: 12.8 us -> 24.6 us
  matrix products: 8.31 us -> 18.7 us
  local copies, waits for them, and re-layouts: 6.63 us -> 3.94 us
    all_to_all x2 -> x0, blocking collectives: 45.1 us -> none  [the longest x1 30.1 us: on_device(): lax.all_to_all(buffer.reshape(planes, groups * lanes, cap_size, features)...]
    ppermute x0 -> x2, waiting for transfers between devices: none -> 11.5 us  [the longest x1 11.5 us: on_device(): lax.ppermute(packed, 'eh', [(i, (i + shift) % planes) for i in range(plan...]
    all_to_all x2 -> x4, waiting for transfers between devices: 41.2 us -> 52.2 us  [the longest x2 26.5 us: on_device(): lax.all_to_all(produced.reshape(arrived.shape), PLANE_AXES, split_axis=0,...]
    dot_general x4 -> x8, matrix products: 5.47 us -> 15.9 us  [the longest x2 5.12 us: expert(): jnp.dot(rows_in, gate_up_local, preferred_element_type=jnp.float32)]
    all_to_all x2 -> x4, starting transfers between devices: 8.28 us -> 15.3 us  [the longest x2 7.99 us: on_device(): lax.all_to_all(buffer.reshape(groups * lanes, cap_size, features), PLANE_...]
    ppermute x0 -> x2, starting transfers between devices: none -> 4.8 us  [the longest x1 2.65 us: on_device(): lax.ppermute(packed, 'eh', [(i, (i + shift) % planes) for i in range(plan...]
    all_to_all x2 -> x0, local copies, waits for them, and re-layouts: 2.03 us -> none  [the longest x1 1.76 us: on_device(): lax.all_to_all(produced.reshape(arrived.shape), PLANE_AXES, split_axis=1,...]
    unnamed x18 -> x22, local copies, waits for them, and re-layouts: 0.2 us -> 2.18 us
  transfers between devices with their start and end apart: 4 -> 8, of which waited for: 3 -> 6; matrix products, arithmetic and copies ran while one was open for 7% -> 18% of each run, Pallas kernels for 0% -> 0%
where the time goes in v8:
time: 131 us; the launch traced here: 130 us
  waiting for transfers between devices  65.3 us (50%)
  starting transfers between devices  24.6 us (19%)
  matrix products  18.7 us (14%)
  other arithmetic  13.2 us (10%)
  between operations  4.07 us (3%)
  local copies, waits for them, and re-layouts  3.94 us (3%)
    all_to_all x2, waiting for transfers between devices, on_device(): lax.all_to_all(produced.reshape(arrived.shape), PLANE_AXES, split_axis=0,...  26.5 us
    all_to_all x2, waiting for transfers between devices, on_device(): lax.all_to_all(buffer.reshape(groups * lanes, cap_size, features), PLANE_...  25.6 us
    ppermute x1, waiting for transfers between devices, on_device(): lax.ppermute(packed, 'eh', [(i, (i + shift) % planes) for i in range(plan...  11.5 us
    all_to_all x2, starting transfers between devices, on_device(): lax.all_to_all(buffer.reshape(groups * lanes, cap_size, features), PLANE_...  7.99 us
    all_to_all x2, starting transfers between devices, on_device(): lax.all_to_all(produced.reshape(arrived.shape), PLANE_AXES, split_axis=0,...  7.31 us
    dot_general x2, matrix products, expert(): jnp.dot(rows_in, gate_up_local, preferred_element_type=jnp.float32)  5.12 us
    dot_general x2, matrix products, on_device(): jnp.dot(combine.T, returned.reshape(plane_slots, features).astype(jnp.flo...  4.39 us
    dot_general x2, matrix products, expert(): jnp.dot(expert_hidden, down_local, preferred_element_type=jnp.float32)  3.51 us
  transfers between devices with their start and end apart: 8, of which 6 were waited for; matrix products, arithmetic and copies ran while one was open for 18% of the time, Pallas kernels for 0%

profile of v8, /device:TPU:0, one launch (start us, length us, event | category | flops | bytes accessed | tf_op | source)
XLA Modules:
  0.0 129.8 jit_solution(5309330862122627051)
XLA Ops:
  0.0 3.0 %collective-permute-start = (bf16[128,1024]{1,0:T(8,128)(2,1)}, bf16[128,1024]{1,0:T(8,128)(2,1)}, u32[]{:S(2)}, u32[]{:S(2)}) collective-permute-start(bf16[128,1024]{1,0:T(8,128)(2,1)} %param.16), channel_id=1, source_target_pairs={{0,16},{16,0},{1,17},{17,1},{2,18},{18,2},{3,19},{19,3},{4,20},{20... | collective-permute-start | bytes 786440 | tf_op jit(solution)/shard_map/ppermute | solution.py:52
  3.0 0.8 select_reduce_fusion.5
  3.8 0.8 select_reduce_fusion.4
  4.6 0.7 multiply_add_fusion
  5.3 0.7 multiply_add_fusion.1
  6.0 0.2 fusion.29
  6.2 0.8 broadcast_in_dim.88
  7.1 0.7 constant_dynamic-update-slice_fusion.4
  7.8 0.7 constant_dynamic-update-slice_fusion.2
  8.5 0.7 constant_dynamic-update-slice_fusion.1
  9.2 0.7 constant_dynamic-update-slice_fusion
  9.9 2.3 %fusion.57 = f32[128,512]{1,0:T(8,128)} fusion(bf16[128,1024]{1,0:T(8,128)(2,1)} %collective-permute-done, bf16[1024,512]{1,0:T(8,128)(2,1)} %param.18), kind=kOutput, calls=%fused_computation.120 | convolution fusion | flops 134217728 | bytes 1572864 | tf_op jit(solution)/shard_map/dot_general | solution.py:53
  12.3 1.5 %collective-permute-start.1 = (f32[128,512]{1,0:T(8,128)}, f32[128,512]{1,0:T(8,128)}, u32[]{:S(2)}, u32[]{:S(2)}) collective-permute-start(f32[128,512]{1,0:T(8,128)} %fusion.57), channel_id=1, source_target_pairs={{16,0},{0,16},{17,1},{1,17},{18,2},{2,18},{19,3},{3,19},{20,4},{4,... | collective-permute-start | bytes 786440 | tf_op jit(solution)/shard_map/ppermute | solution.py:54
  13.7 0.6 fusion.56
  18.1 0.1 copy.43
  18.2 0.1 reshape.73
  18.4 0.3 convolution_bitcast_fusion
  18.8 1.6 %collective-permute-done.1 = f32[128,512]{1,0:T(8,128)} collective-permute-done((f32[128,512]{1,0:T(8,128)}, f32[128,512]{1,0:T(8,128)}, u32[]{:S(2)}, u32[]{:S(2)}) %collective-permute-start.1) | collective-permute-done | bytes 262176 | tf_op jit(solution)/shard_map/ppermute | solution.py:54
  20.4 1.1 fusion.23
  21.4 0.2 fusion.10
  21.6 0.1 fusion.12
  21.8 2.7 %collective-permute-start.2 = (bf16[136,1024]{1,0:T(8,128)(2,1)S(1)}, bf16[136,1024]{1,0:T(8,128)(2,1)S(1)}, u32[]{:S(2)}, u32[]{:S(2)}) collective-permute-start(bf16[136,1024]{1,0:T(8,128)(2,1)S(1)} %pad_maximum_fusion), channel_id=1, source_target_pairs={{0,8},{8,0},{1,9},{9,1},{2,10},{10,2},{3,11},{11,3},{4,12},{12,4},... | collective-permute-start | bytes 835592 | tf_op jit(solution)/shard_map/ppermute | solution.py:124
  24.4 11.5 %collective-permute-done.2 = bf16[136,1024]{1,0:T(8,128)(2,1)S(1)} collective-permute-done((bf16[136,1024]{1,0:T(8,128)(2,1)S(1)}, bf16[136,1024]{1,0:T(8,128)(2,1)S(1)}, u32[]{:S(2)}, u32[]{:S(2)}) %collective-permute-start.2) | collective-permute-done | bytes 278560 | tf_op jit(solution)/shard_map/ppermute | solution.py:124
  36.1 0.1 fusion.55
  36.3 0.9 fusion.4
  37.3 1.4 %convolution_convert_fusion = bf16[512,1024]{1,0:T(8,128)(2,1)} fusion(pred[512,128]{1,0:T(8,128)(4,1)S(1)} %fusion.4, bf16[136,1024]{1,0:T(8,128)(2,1)S(1)} %collective-permute-done.2), kind=kOutput, calls=%fused_computation.10 | convolution fusion | flops 134742016 | bytes 1376256 | tf_op jit(solution)/shard_map/dot_general | solution.py:143
  38.7 4.3 %all-to-all-start.2 = ((bf16[16,32,1024]{2,1,0:T(8,128)(2,1)}), bf16[16,32,1024]{2,1,0:T(8,128)(2,1)}, u32[]{:S(2)}, u32[]{:S(2)}) async-start(bf16[16,32,1024]{2,1,0:T(8,128)(2,1)} %bitcast.12), calls=%async_computation.2 | async-start | bytes 2097152 | tf_op jit(solution)/shard_map/all_to_all | solution.py:146
  43.0 0.9 fusion.5
  43.9 1.4 %convolution_convert_fusion.1 = bf16[512,1024]{1,0:T(8,128)(2,1)} fusion(pred[512,128]{1,0:T(8,128)(4,1)S(1)} %fusion.5, bf16[128,1024]{1,0:T(8,128)(2,1)S(1)} %fusion.12), kind=kOutput, calls=%fused_computation.11 | convolution fusion | flops 134742016 | bytes 1376256 | tf_op jit(solution)/shard_map/dot_general | solution.py:143
  45.3 13.9 %all-to-all-done.2 = bf16[16,32,1024]{2,1,0:T(8,128)(2,1)} async-done(((bf16[16,32,1024]{2,1,0:T(8,128)(2,1)}), bf16[16,32,1024]{2,1,0:T(8,128)(2,1)}, u32[]{:S(2)}, u32[]{:S(2)}) %all-to-all-start.2) | async-done | bytes 1048608 | tf_op jit(solution)/shard_map/all_to_all | solution.py:146
  59.2 3.7 %all-to-all-start = ((bf16[16,32,1024]{2,1,0:T(8,128)(2,1)}), bf16[16,32,1024]{2,1,0:T(8,128)(2,1)S(1)}, u32[]{:S(2)}, u32[]{:S(2)}) async-start(bf16[16,32,1024]{2,1,0:T(8,128)(2,1)} %bitcast.6), calls=%async_computation | async-start | bytes 2097152 | tf_op jit(solution)/shard_map/all_to_all | solution.py:146
  62.9 2.6 %fusion = f32[512,1024]{1,0:T(8,128)S(1)} fusion(bf16[512,1024]{1,0:T(8,128)(2,1)} %bitcast.13, bf16[1,1024,1024]{2,1,0:T(8,128)(2,1)S(1)} %copy-done), kind=kOutput, calls=%fused_computation | convolution fusion | flops 1073741824 | bytes 5242880 | tf_op jit(solution)/shard_map/dot_general | solution.py:115
  65.5 1.8 %convolution_convert_fusion.2 = bf16[512,1024]{1,0:T(8,128)(2,1)} fusion(bf16[1,512,1024]{2,1,0:T(8,128)(2,1)S(1)} %copy-done.8, f32[512,1024]{1,0:T(8,128)S(1)} %fusion), kind=kOutput, calls=%fused_computation.12 | convolution fusion | flops 538968064 | bytes 4194304 | tf_op jit(solution)/shard_map/dot_general | solution.py:119
  67.2 11.8 %all-to-all-done = bf16[16,32,1024]{2,1,0:T(8,128)(2,1)S(1)} async-done(((bf16[16,32,1024]{2,1,0:T(8,128)(2,1)}), bf16[16,32,1024]{2,1,0:T(8,128)(2,1)S(1)}, u32[]{:S(2)}, u32[]{:S(2)}) %all-to-all-start) | async-done | bytes 1048608 | tf_op jit(solution)/shard_map/all_to_all | solution.py:146
  79.0 1.0 copy-done.3
  80.0 3.7 %all-to-all-start.3 = ((bf16[16,32,1024]{2,1,0:T(8,128)(2,1)}), bf16[16,32,1024]{2,1,0:T(8,128)(2,1)S(1)}, u32[]{:S(2)}, u32[]{:S(2)}) async-start(bf16[16,32,1024]{2,1,0:T(8,128)(2,1)} %bitcast.45), calls=%async_computation.3 | async-start | bytes 2097152 | tf_op jit(solution)/shard_map/all_to_all | solution.py:154
  83.7 2.6 %fusion.2 = f32[512,1024]{1,0:T(8,128)S(1)} fusion(bf16[512,1024]{1,0:T(8,128)(2,1)} %bitcast.44, bf16[1,1024,1024]{2,1,0:T(8,128)(2,1)S(1)} %copy-done), kind=kOutput, calls=%fused_computation.2 | convolution fusion | flops 1073741824 | bytes 5242880 | tf_op jit(solution)/shard_map/dot_general | solution.py:115
  86.2 1.7 %convolution_convert_fusion.3 = bf16[512,1024]{1,0:T(8,128)(2,1)} fusion(bf16[1,512,1024]{2,1,0:T(8,128)(2,1)S(1)} %copy-done.9, f32[512,1024]{1,0:T(8,128)S(1)} %fusion.2), kind=kOutput, calls=%fused_computation.13 | convolution fusion | flops 538968064 | bytes 4194304 | tf_op jit(solution)/shard_map/dot_general | solution.py:119
  88.0 11.8 %all-to-all-done.3 = bf16[16,32,1024]{2,1,0:T(8,128)(2,1)S(1)} async-done(((bf16[16,32,1024]{2,1,0:T(8,128)(2,1)}), bf16[16,32,1024]{2,1,0:T(8,128)(2,1)S(1)}, u32[]{:S(2)}, u32[]{:S(2)}) %all-to-all-start.3) | async-done | bytes 1048608 | tf_op jit(solution)/shard_map/all_to_all | solution.py:154
  99.8 1.0 copy-done.2
  100.8 3.7 %all-to-all-start.1 = ((bf16[16,32,1024]{2,1,0:T(8,128)(2,1)}), bf16[16,32,1024]{2,1,0:T(8,128)(2,1)S(1)}, u32[]{:S(2)}, u32[]{:S(2)}) async-start(bf16[16,32,1024]{2,1,0:T(8,128)(2,1)} %bitcast.43), calls=%async_computation.1 | async-start | bytes 2097152 | tf_op jit(solution)/shard_map/all_to_all | solution.py:154
  104.5 0.7 select_reduce_fusion
  105.3 2.6 %convolution_convert_fusion.4 = bf16[128,1024]{1,0:T(8,128)(2,1)} fusion(f32[512,128]{1,0:T(8,128)S(1)} %select_reduce_fusion, bf16[512,1024]{1,0:T(8,128)(2,1)} %bitcast.42), kind=kOutput, calls=%fused_computation.14 | convolution fusion | flops 805437440 | bytes 1572864 | tf_op jit(solution)/shard_map/dot_general | solution.py:158
  107.9 2.1 %collective-permute-start.3 = (bf16[128,1024]{1,0:T(8,128)(2,1)}, bf16[128,1024]{1,0:T(8,128)(2,1)}, u32[]{:S(2)}, u32[]{:S(2)}) collective-permute-start(bf16[128,1024]{1,0:T(8,128)(2,1)} %convolution_convert_fusion.4), channel_id=1, source_target_pairs={{8,0},{0,8},{9,1},{1,9},{10,2},{2,10},{11,3},{3,11},{12,4},{4,12},... | collective-permute-start | bytes 786440 | tf_op jit(solution)/shard_map/ppermute | solution.py:166
  110.0 1.4 %select_reduce_fusion.1 = f32[512,128]{1,0:T(8,128)} fusion(f32[128,8]{0,1:T(8,128)S(1)} %slice_add_fusion.2, s32[128,8]{0,1:T(8,128)S(1)} %fusion.43), kind=kLoop, calls=%fused_computation.7 | loop fusion | flops 1507328 | bytes 270336 | tf_op jit(solution)/shard_map/reduce_sum | solution.py:157
  111.5 14.7 %all-to-all-done.1 = bf16[16,32,1024]{2,1,0:T(8,128)(2,1)S(1)} async-done(((bf16[16,32,1024]{2,1,0:T(8,128)(2,1)}), bf16[16,32,1024]{2,1,0:T(8,128)(2,1)S(1)}, u32[]{:S(2)}, u32[]{:S(2)}) %all-to-all-start.1) | async-done | bytes 1048608 | tf_op jit(solution)/shard_map/all_to_all | solution.py:154
  126.2 1.8 %multiply_reduce_fusion = (f32[128]{0:T(128)S(1)}, f32[128,1024]{1,0:T(8,128)S(1)}) fusion(bf16[128,1024]{1,0:T(8,128)(2,1)} %collective-permute-done.3, bf16[128,1024]{1,0:T(8,128)(2,1)S(1)} %get-tuple-element.18, f32[512,128]{1,0:T(8,128)} %select_reduce_fusion.1, bf16[512,1024]{1,0:T(8,128)(2,1)S(1)} %bitcast.41), kind=kOutput, calls=%fused_computation.35 | convolution fusion | flops 806092672 | bytes 2359808 | tf_op jit(solution)/shard_map/dot_general | solution.py:158
  128.1 1.8 %multiply_convert_fusion = bf16[128,1024]{1,0:T(8,128)(2,1)} fusion(f32[1024]{0:T(1024)S(1)} %copy-done.7, f32[128]{0:T(128)S(1)} %add_rsqrt_fusion, f32[128,1024]{1,0:T(8,128)S(1)} %get-tuple-element.30, bf16[128,1024]{1,0:T(8,128)(2,1)} %collective-permute-done.3, bf16[128,1024]{1,0:T(8,128)(2,1)S(1)} %get-tuple-element.18), kind=kLoop, calls=%fused_computation.34 | loop fusion | flops 917504 | bytes 1315328 | tf_op jit(solution)/shard_map/convert_element_type | solution.py:171
  (39 shorter events, 0.6 us)
Async XLA Ops:
  0.0 62.9 %copy-start = (bf16[1,1024,1024]{2,1,0:T(8,128)(2,1)S(1)}, bf16[1,1024,1024]{2,1,0:T(8,128)(2,1)}, u32[]{:S(2)}) copy-start(bf16[1,1024,1024]{2,1,0:T(8,128)(2,1)} %param.21) | copy-start | bytes 6291460
  0.0 18.4 %copy-start.4 = (bf16[128,1024]{1,0:T(8,128)(2,1)S(1)}, bf16[128,1024]{1,0:T(8,128)(2,1)}, u32[]{:S(2)}) copy-start(bf16[128,1024]{1,0:T(8,128)(2,1)} %param.16) | copy-start | bytes 786436
  0.0 18.4 %copy-start.1 = (bf16[1024,512]{1,0:T(8,128)(2,1)S(1)}, bf16[1024,512]{1,0:T(8,128)(2,1)}, u32[]{:S(2)}) copy-start(bf16[1024,512]{1,0:T(8,128)(2,1)} %param.18) | copy-start | bytes 3145732
  0.0 9.9 %collective-permute-start = (bf16[128,1024]{1,0:T(8,128)(2,1)}, bf16[128,1024]{1,0:T(8,128)(2,1)}, u32[]{:S(2)}, u32[]{:S(2)}) collective-permute-start(bf16[128,1024]{1,0:T(8,128)(2,1)} %param.16), channel_id=1, source_target_pairs={{0,16},{16,0},{1,17},{17,1},{2,18},{18,2},{3,19},{19,3},{4,20},{20... | collective-permute-start | bytes 786440 | tf_op jit(solution)/shard_map/ppermute | solution.py:52
  12.3 9.3 %copy-start.6 = (f32[1024]{0:T(1024)S(1)}, f32[1024]{0:T(1024)}, u32[]{:S(2)}) copy-start(f32[1024]{0:T(1024)} %param.19) | copy-start | bytes 12292
  12.3 8.1 %collective-permute-start.1 = (f32[128,512]{1,0:T(8,128)}, f32[128,512]{1,0:T(8,128)}, u32[]{:S(2)}, u32[]{:S(2)}) collective-permute-start(f32[128,512]{1,0:T(8,128)} %fusion.57), channel_id=1, source_target_pairs={{16,0},{0,16},{17,1},{1,17},{18,2},{2,18},{19,3},{3,19},{20,4},{4,... | collective-permute-start | bytes 786440 | tf_op jit(solution)/shard_map/ppermute | solution.py:54
  18.4 3.0 %copy-start.5 = (bf16[128,1024]{1,0:T(8,128)(2,1)S(1)}, bf16[128,1024]{1,0:T(8,128)(2,1)}, u32[]{:S(2)}) copy-start(bf16[128,1024]{1,0:T(8,128)(2,1)} %param.17) | copy-start | bytes 786436
  21.8 14.2 %collective-permute-start.2 = (bf16[136,1024]{1,0:T(8,128)(2,1)S(1)}, bf16[136,1024]{1,0:T(8,128)(2,1)S(1)}, u32[]{:S(2)}, u32[]{:S(2)}) collective-permute-start(bf16[136,1024]{1,0:T(8,128)(2,1)S(1)} %pad_maximum_fusion), channel_id=1, source_target_pairs={{0,8},{8,0},{1,9},{9,1},{2,10},{10,2},{3,11},{11,3},{4,12},{12,4},... | collective-permute-start | bytes 835592 | tf_op jit(solution)/shard_map/ppermute | solution.py:124
  38.7 20.5 %all-to-all-start.2 = ((bf16[16,32,1024]{2,1,0:T(8,128)(2,1)}), bf16[16,32,1024]{2,1,0:T(8,128)(2,1)}, u32[]{:S(2)}, u32[]{:S(2)}) async-start(bf16[16,32,1024]{2,1,0:T(8,128)(2,1)} %bitcast.12), calls=%async_computation.2 | async-start | bytes 2097152 | tf_op jit(solution)/shard_map/all_to_all | solution.py:146
  59.2 19.8 %all-to-all-start = ((bf16[16,32,1024]{2,1,0:T(8,128)(2,1)}), bf16[16,32,1024]{2,1,0:T(8,128)(2,1)S(1)}, u32[]{:S(2)}, u32[]{:S(2)}) async-start(bf16[16,32,1024]{2,1,0:T(8,128)(2,1)} %bitcast.6), calls=%async_computation | async-start | bytes 2097152 | tf_op jit(solution)/shard_map/all_to_all | solution.py:146
  62.9 2.6 %copy-start.8 = (bf16[1,512,1024]{2,1,0:T(8,128)(2,1)S(1)}, bf16[1,512,1024]{2,1,0:T(8,128)(2,1)}, u32[]{:S(2)}) copy-start(bf16[1,512,1024]{2,1,0:T(8,128)(2,1)} %param.22) | copy-start | bytes 3145732
  79.0 1.0 copy-start.3
  80.0 19.8 %all-to-all-start.3 = ((bf16[16,32,1024]{2,1,0:T(8,128)(2,1)}), bf16[16,32,1024]{2,1,0:T(8,128)(2,1)S(1)}, u32[]{:S(2)}, u32[]{:S(2)}) async-start(bf16[16,32,1024]{2,1,0:T(8,128)(2,1)} %bitcast.45), calls=%async_computation.3 | async-start | bytes 2097152 | tf_op jit(solution)/shard_map/all_to_all | solution.py:154
  83.7 2.6 %copy-start.9 = (bf16[1,512,1024]{2,1,0:T(8,128)(2,1)S(1)}, bf16[1,512,1024]{2,1,0:T(8,128)(2,1)}, u32[]{:S(2)}) copy-start(bf16[1,512,1024]{2,1,0:T(8,128)(2,1)} %param.22) | copy-start | bytes 3145732
  99.8 1.0 copy-start.2
  100.8 25.4 %all-to-all-start.1 = ((bf16[16,32,1024]{2,1,0:T(8,128)(2,1)}), bf16[16,32,1024]{2,1,0:T(8,128)(2,1)S(1)}, u32[]{:S(2)}, u32[]{:S(2)}) async-start(bf16[16,32,1024]{2,1,0:T(8,128)(2,1)} %bitcast.43), calls=%async_computation.1 | async-start | bytes 2097152 | tf_op jit(solution)/shard_map/all_to_all | solution.py:154
  105.3 22.7 %copy-start.7 = (f32[1024]{0:T(1024)S(1)}, f32[1024]{0:T(1024)}, u32[]{:S(2)}) copy-start(f32[1024]{0:T(1024)} %param.20) | copy-start | bytes 12292
  107.9 18.3 %collective-permute-start.3 = (bf16[128,1024]{1,0:T(8,128)(2,1)}, bf16[128,1024]{1,0:T(8,128)(2,1)}, u32[]{:S(2)}, u32[]{:S(2)}) collective-permute-start(bf16[128,1024]{1,0:T(8,128)(2,1)} %convolution_convert_fusion.4), channel_id=1, source_target_pairs={{8,0},{0,8},{9,1},{1,9},{10,2},{2,10},{11,3},{3,11},{12,4},{4,12},... | collective-permute-start | bytes 786440 | tf_op jit(solution)/shard_map/ppermute | solution.py:166

commit v9 on v8

--- a/solution.py
+++ b/solution.py
@@ -126,6 +126,8 @@
     ]
     partials = []
     for shift, block in enumerate(received):
+        if shift:
+            block = block + jnp.zeros_like(block) * first_arrived
         normed_s = block[:rows_here]
         meta_s = (
             block[rows_here:]
@@ -150,6 +152,8 @@
             concat_axis=0,
             tiled=True,
         )
+        if shift == 0:
+            first_arrived = arrived[:1, 0, :1]
         produced = expert(arrived.reshape(-1, features))
         returned = lax.all_to_all(
             produced.reshape(arrived.shape), PLANE_AXES, split_axis=0, concat_axis=0, tiled=True

time: 131 us -> 128 us (0.977)
  blocking collectives: 0 us -> 18.8 us
  waiting for transfers between devices: 65.3 us -> 52.5 us
  starting transfers between devices: 24.6 us -> 19.3 us
  matrix products: 18.7 us -> 15.8 us
    all_to_all x0 -> x1, blocking collectives: none -> 18.8 us  [on_device(): lax.all_to_all(buffer.reshape(groups * lanes, cap_size, features), PLANE_...]
    ppermute x1, waiting for transfers between devices: 11.5 us -> 0.01 us  [on_device(): lax.ppermute(packed, 'eh', [(i, (i + shift) % planes) for i in range(plan...]
    all_to_all x2 -> x1, waiting for transfers between devices: 25.6 us -> 19.2 us  [on_device(): lax.all_to_all(buffer.reshape(groups * lanes, cap_size, features), PLANE_...]
    ppermute x1, waiting for transfers between devices: 1.6 us -> 6.35 us  [on_device(): blocks[shift] = lax.ppermute(done, 'grp', back)]
    all_to_all x2 -> x1, starting transfers between devices: 7.99 us -> 4.34 us  [on_device(): lax.all_to_all(buffer.reshape(groups * lanes, cap_size, features), PLANE_...]
    dot_general x2, matrix products: 5.12 us -> 3.81 us  [expert(): jnp.dot(rows_in, gate_up_local, preferred_element_type=jnp.float32)]
  transfers between devices with their start and end apart: 8 -> 7, of which waited for: 6 -> 4; matrix products, arithmetic and copies ran while one was open for 18% -> 15% of each run, Pallas kernels for 0% -> 0%
where the time goes in v9:
time: 128 us
  waiting for transfers between devices  52.5 us (41%)
  starting transfers between devices  19.3 us (15%)
  blocking collectives  18.8 us (15%)
  matrix products  15.8 us (12%)
  other arithmetic  12.3 us (10%)
  between operations  4.79 us (4%)
  local copies, waits for them, and re-layouts  4.18 us (3%)
    all_to_all x2, waiting for transfers between devices, on_device(): lax.all_to_all(produced.reshape(arrived.shape), PLANE_AXES, split_axis=0,...  27 us
    all_to_all x1, waiting for transfers between devices, on_device(): lax.all_to_all(buffer.reshape(groups * lanes, cap_size, features), PLANE_...  19.2 us
    all_to_all x1, blocking collectives, on_device(): lax.all_to_all(buffer.reshape(groups * lanes, cap_size, features), PLANE_...  18.8 us
    all_to_all x2, starting transfers between devices, on_device(): lax.all_to_all(produced.reshape(arrived.shape), PLANE_AXES, split_axis=0,...  7.31 us
    ppermute x1, waiting for transfers between devices, on_device(): blocks[shift] = lax.ppermute(done, 'grp', back)  6.35 us
    dot_general x2, matrix products, on_device(): jnp.dot(combine.T, returned.reshape(plane_slots, features).astype(jnp.flo...  4.39 us
    all_to_all x1, starting transfers between devices, on_device(): lax.all_to_all(buffer.reshape(groups * lanes, cap_size, features), PLANE_...  4.34 us
    dot_general x2, matrix products, expert(): jnp.dot(rows_in, gate_up_local, preferred_element_type=jnp.float32)  3.81 us
  transfers between devices with their start and end apart: 7, of which 4 were waited for; matrix products, arithmetic and copies ran while one was open for 15% of the time, Pallas kernels for 0%

profile of v9, /device:TPU:0, one launch (start us, length us, event | category | flops | bytes accessed | tf_op | source)
XLA Modules:
  0.0 127.6 jit_solution(14024532953780830300)
XLA Ops:
  0.0 3.0 %collective-permute-start = (bf16[128,1024]{1,0:T(8,128)(2,1)}, bf16[128,1024]{1,0:T(8,128)(2,1)}, u32[]{:S(2)}, u32[]{:S(2)}) collective-permute-start(bf16[128,1024]{1,0:T(8,128)(2,1)} %param.16), channel_id=1, source_target_pairs={{0,16},{16,0},{1,17},{17,1},{2,18},{18,2},{3,19},{19,3},{4,20},{20... | collective-permute-start | bytes 786440 | tf_op jit(solution)/shard_map/ppermute | solution.py:52
  3.1 0.8 select_reduce_fusion.5
  3.8 0.8 select_reduce_fusion.4
  4.6 0.7 multiply_add_fusion
  5.3 0.7 multiply_add_fusion.1
  6.0 0.2 fusion.29
  6.3 0.8 broadcast_in_dim.89
  7.0 0.1 select_reduce_fusion.2
  7.1 0.7 constant_dynamic-update-slice_fusion.4
  7.8 0.7 constant_dynamic-update-slice_fusion.2
  8.5 0.7 constant_dynamic-update-slice_fusion.1
  9.2 0.7 constant_dynamic-update-slice_fusion
  9.9 0.6 fusion.56
  14.5 1.6 %fusion.57 = f32[128,512]{1,0:T(8,128)S(1)} fusion(bf16[128,1024]{1,0:T(8,128)(2,1)} %collective-permute-done, bf16[1024,512]{1,0:T(8,128)(2,1)} %param.18), kind=kOutput, calls=%fused_computation.121 | convolution fusion | flops 134217728 | bytes 1572864 | tf_op jit(solution)/shard_map/dot_general | solution.py:53
  16.1 0.3 collective-permute-start.1
  16.4 0.9 fusion.5
  17.3 0.3 convolution_bitcast_fusion
  17.6 6.3 %collective-permute-done.1 = f32[128,512]{1,0:T(8,128)S(1)} collective-permute-done((f32[128,512]{1,0:T(8,128)S(1)}, f32[128,512]{1,0:T(8,128)S(1)}, u32[]{:S(2)}, u32[]{:S(2)}) %collective-permute-start.1) | collective-permute-done | bytes 262176 | tf_op jit(solution)/shard_map/ppermute | solution.py:54
  24.0 0.1 fusion.23
  24.1 0.2 fusion.10
  24.3 0.1 fusion.12
  24.4 1.5 %convolution_convert_fusion.1 = bf16[512,1024]{1,0:T(8,128)(2,1)} fusion(pred[512,128]{1,0:T(8,128)(4,1)S(1)} %fusion.5, bf16[128,1024]{1,0:T(8,128)(2,1)S(1)} %fusion.12), kind=kOutput, calls=%fused_computation.11 | convolution fusion | flops 134742016 | bytes 1376256 | tf_op jit(solution)/shard_map/dot_general | solution.py:145
  25.9 4.3 %all-to-all-start = ((bf16[16,32,1024]{2,1,0:T(8,128)(2,1)}), bf16[16,32,1024]{2,1,0:T(8,128)(2,1)}, u32[]{:S(2)}, u32[]{:S(2)}) async-start(bf16[16,32,1024]{2,1,0:T(8,128)(2,1)} %bitcast.6), calls=%async_computation | async-start | bytes 2097152 | tf_op jit(solution)/shard_map/all_to_all | solution.py:148
  30.2 0.1 copy.43
  30.3 0.1 reshape.76
  30.5 2.7 %collective-permute-start.2 = (bf16[136,1024]{1,0:T(8,128)(2,1)S(1)}, bf16[136,1024]{1,0:T(8,128)(2,1)S(1)}, u32[]{:S(2)}, u32[]{:S(2)}) collective-permute-start(bf16[136,1024]{1,0:T(8,128)(2,1)S(1)} %pad_maximum_fusion), channel_id=1, source_target_pairs={{0,8},{8,0},{1,9},{9,1},{2,10},{10,2},{3,11},{11,3},{4,12},{12,4},... | collective-permute-start | bytes 835592 | tf_op jit(solution)/shard_map/ppermute | solution.py:124
  33.2 19.2 %all-to-all-done = bf16[16,32,1024]{2,1,0:T(8,128)(2,1)} async-done(((bf16[16,32,1024]{2,1,0:T(8,128)(2,1)}), bf16[16,32,1024]{2,1,0:T(8,128)(2,1)}, u32[]{:S(2)}, u32[]{:S(2)}) %all-to-all-start) | async-done | bytes 1048608 | tf_op jit(solution)/shard_map/all_to_all | solution.py:148
  52.3 1.2 slice.96
  54.2 0.1 reshape.121
  54.3 0.1 fusion.55
  54.6 0.9 fusion.4
  55.5 0.4 convolution_convert_fusion
  55.9 18.8 %all_to_all.20 = bf16[16,32,1024]{2,1,0:T(8,128)(2,1)S(1)} all-to-all(bf16[16,32,1024]{2,1,0:T(8,128)(2,1)S(1)} %bitcast.44), channel_id=1, replica_groups=mesh['grp'=2,'eh'=2,'el'=8] {'grp','el'}, dimensions={0} | all-to-all | bytes 2097152 | tf_op jit(solution)/shard_map/all_to_all | solution.py:148
  74.7 1.2 fusion
  76.0 1.8 %convolution_convert_fusion.2 = bf16[512,1024]{1,0:T(8,128)(2,1)} fusion(bf16[1,512,1024]{2,1,0:T(8,128)(2,1)S(1)} %copy-done.7, f32[512,1024]{1,0:T(8,128)S(1)} %fusion), kind=kOutput, calls=%fused_computation.12 | convolution fusion | flops 538968064 | bytes 4194304 | tf_op jit(solution)/shard_map/dot_general | solution.py:119
  77.8 3.7 %all-to-all-start.3 = ((bf16[16,32,1024]{2,1,0:T(8,128)(2,1)}), bf16[16,32,1024]{2,1,0:T(8,128)(2,1)S(1)}, u32[]{:S(2)}, u32[]{:S(2)}) async-start(bf16[16,32,1024]{2,1,0:T(8,128)(2,1)} %bitcast.46), calls=%async_computation.3 | async-start | bytes 2097152 | tf_op jit(solution)/shard_map/all_to_all | solution.py:158
  81.4 2.6 %fusion.2 = f32[512,1024]{1,0:T(8,128)S(1)} fusion(bf16[512,1024]{1,0:T(8,128)(2,1)} %bitcast.7, bf16[1,1024,1024]{2,1,0:T(8,128)(2,1)S(1)} %copy-done), kind=kOutput, calls=%fused_computation.2 | convolution fusion | flops 1073741824 | bytes 5242880 | tf_op jit(solution)/shard_map/dot_general | solution.py:115
  84.0 1.7 %convolution_convert_fusion.3 = bf16[512,1024]{1,0:T(8,128)(2,1)} fusion(bf16[1,512,1024]{2,1,0:T(8,128)(2,1)S(1)} %copy-done.8, f32[512,1024]{1,0:T(8,128)S(1)} %fusion.2), kind=kOutput, calls=%fused_computation.13 | convolution fusion | flops 538968064 | bytes 4194304 | tf_op jit(solution)/shard_map/dot_general | solution.py:119
  85.7 11.8 %all-to-all-done.3 = bf16[16,32,1024]{2,1,0:T(8,128)(2,1)S(1)} async-done(((bf16[16,32,1024]{2,1,0:T(8,128)(2,1)}), bf16[16,32,1024]{2,1,0:T(8,128)(2,1)S(1)}, u32[]{:S(2)}, u32[]{:S(2)}) %all-to-all-start.3) | async-done | bytes 1048608 | tf_op jit(solution)/shard_map/all_to_all | solution.py:158
  97.6 1.0 copy-done.2
  98.6 3.7 %all-to-all-start.1 = ((bf16[16,32,1024]{2,1,0:T(8,128)(2,1)}), bf16[16,32,1024]{2,1,0:T(8,128)(2,1)S(1)}, u32[]{:S(2)}, u32[]{:S(2)}) async-start(bf16[16,32,1024]{2,1,0:T(8,128)(2,1)} %bitcast.45), calls=%async_computation.1 | async-start | bytes 2097152 | tf_op jit(solution)/shard_map/all_to_all | solution.py:158
  102.3 0.7 select_reduce_fusion
  103.1 2.6 %convolution_convert_fusion.4 = bf16[128,1024]{1,0:T(8,128)(2,1)} fusion(f32[512,128]{1,0:T(8,128)S(1)} %select_reduce_fusion, bf16[512,1024]{1,0:T(8,128)(2,1)} %bitcast.43), kind=kOutput, calls=%fused_computation.14 | convolution fusion | flops 805437440 | bytes 1572864 | tf_op jit(solution)/shard_map/dot_general | solution.py:162
  105.7 1.7 %collective-permute-start.3 = (bf16[128,1024]{1,0:T(8,128)(2,1)}, bf16[128,1024]{1,0:T(8,128)(2,1)}, u32[]{:S(2)}, u32[]{:S(2)}) collective-permute-start(bf16[128,1024]{1,0:T(8,128)(2,1)} %convolution_convert_fusion.4), channel_id=1, source_target_pairs={{8,0},{0,8},{9,1},{1,9},{10,2},{2,10},{11,3},{3,11},{12,4},{4,12},... | collective-permute-start | bytes 786440 | tf_op jit(solution)/shard_map/ppermute | solution.py:170
  107.3 1.4 %select_reduce_fusion.1 = f32[512,128]{1,0:T(8,128)} fusion(f32[128,8]{0,1:T(8,128)S(1)} %slice_add_fusion.2, s32[128,8]{0,1:T(8,128)S(1)} %fusion.43), kind=kLoop, calls=%fused_computation.7 | loop fusion | flops 1507328 | bytes 270336 | tf_op jit(solution)/shard_map/reduce_sum | solution.py:161
  108.8 15.2 %all-to-all-done.1 = bf16[16,32,1024]{2,1,0:T(8,128)(2,1)S(1)} async-done(((bf16[16,32,1024]{2,1,0:T(8,128)(2,1)}), bf16[16,32,1024]{2,1,0:T(8,128)(2,1)S(1)}, u32[]{:S(2)}, u32[]{:S(2)}) %all-to-all-start.1) | async-done | bytes 1048608 | tf_op jit(solution)/shard_map/all_to_all | solution.py:158
  124.0 1.8 %multiply_reduce_fusion = (f32[128]{0:T(128)S(1)}, f32[128,1024]{1,0:T(8,128)S(1)}) fusion(bf16[128,1024]{1,0:T(8,128)(2,1)} %collective-permute-done.3, bf16[128,1024]{1,0:T(8,128)(2,1)S(1)} %get-tuple-element.18, f32[512,128]{1,0:T(8,128)} %select_reduce_fusion.1, bf16[512,1024]{1,0:T(8,128)(2,1)S(1)} %bitcast.42), kind=kOutput, calls=%fused_computation.35 | convolution fusion | flops 806092672 | bytes 2359808 | tf_op jit(solution)/shard_map/dot_general | solution.py:162
  125.8 1.8 %multiply_convert_fusion = bf16[128,1024]{1,0:T(8,128)(2,1)} fusion(f32[1024]{0:T(1024)S(1)} %copy-done.6, f32[128]{0:T(128)S(1)} %add_rsqrt_fusion, f32[128,1024]{1,0:T(8,128)S(1)} %get-tuple-element.30, bf16[128,1024]{1,0:T(8,128)(2,1)} %collective-permute-done.3, bf16[128,1024]{1,0:T(8,128)(2,1)S(1)} %get-tuple-element.18), kind=kLoop, calls=%fused_computation.34 | loop fusion | flops 917504 | bytes 1315328 | tf_op jit(solution)/shard_map/convert_element_type | solution.py:175
  (38 shorter events, 0.4 us)
Async XLA Ops:
  0.0 74.7 %copy-start = (bf16[1,1024,1024]{2,1,0:T(8,128)(2,1)S(1)}, bf16[1,1024,1024]{2,1,0:T(8,128)(2,1)}, u32[]{:S(2)}) copy-start(bf16[1,1024,1024]{2,1,0:T(8,128)(2,1)} %param.21) | copy-start | bytes 6291460
  0.0 17.3 %copy-start.3 = (bf16[128,1024]{1,0:T(8,128)(2,1)S(1)}, bf16[128,1024]{1,0:T(8,128)(2,1)}, u32[]{:S(2)}) copy-start(bf16[128,1024]{1,0:T(8,128)(2,1)} %param.16) | copy-start | bytes 786436
  0.0 17.3 %copy-start.1 = (bf16[1024,512]{1,0:T(8,128)(2,1)S(1)}, bf16[1024,512]{1,0:T(8,128)(2,1)}, u32[]{:S(2)}) copy-start(bf16[1024,512]{1,0:T(8,128)(2,1)} %param.18) | copy-start | bytes 3145732
  0.0 14.4 %collective-permute-start = (bf16[128,1024]{1,0:T(8,128)(2,1)}, bf16[128,1024]{1,0:T(8,128)(2,1)}, u32[]{:S(2)}, u32[]{:S(2)}) collective-permute-start(bf16[128,1024]{1,0:T(8,128)(2,1)} %param.16), channel_id=1, source_target_pairs={{0,16},{16,0},{1,17},{17,1},{2,18},{18,2},{3,19},{19,3},{4,20},{20... | collective-permute-start | bytes 786440 | tf_op jit(solution)/shard_map/ppermute | solution.py:52
  14.4 9.7 %copy-start.4 = (bf16[128,1024]{1,0:T(8,128)(2,1)S(1)}, bf16[128,1024]{1,0:T(8,128)(2,1)}, u32[]{:S(2)}) copy-start(bf16[128,1024]{1,0:T(8,128)(2,1)} %param.17) | copy-start | bytes 786436
  16.1 8.2 %copy-start.5 = (f32[1024]{0:T(1024)S(1)}, f32[1024]{0:T(1024)}, u32[]{:S(2)}) copy-start(f32[1024]{0:T(1024)} %param.19) | copy-start | bytes 12292
  16.1 7.8 %collective-permute-start.1 = (f32[128,512]{1,0:T(8,128)S(1)}, f32[128,512]{1,0:T(8,128)S(1)}, u32[]{:S(2)}, u32[]{:S(2)}) collective-permute-start(f32[128,512]{1,0:T(8,128)S(1)} %fusion.57), channel_id=1, source_target_pairs={{16,0},{0,16},{17,1},{1,17},{18,2},{2,18},{19,3},{3,19},{20,4},{4,... | collective-permute-start | bytes 786440 | tf_op jit(solution)/shard_map/ppermute | solution.py:54
  25.9 26.5 %all-to-all-start = ((bf16[16,32,1024]{2,1,0:T(8,128)(2,1)}), bf16[16,32,1024]{2,1,0:T(8,128)(2,1)}, u32[]{:S(2)}, u32[]{:S(2)}) async-start(bf16[16,32,1024]{2,1,0:T(8,128)(2,1)} %bitcast.6), calls=%async_computation | async-start | bytes 2097152 | tf_op jit(solution)/shard_map/all_to_all | solution.py:148
  30.5 23.7 %collective-permute-start.2 = (bf16[136,1024]{1,0:T(8,128)(2,1)S(1)}, bf16[136,1024]{1,0:T(8,128)(2,1)S(1)}, u32[]{:S(2)}, u32[]{:S(2)}) collective-permute-start(bf16[136,1024]{1,0:T(8,128)(2,1)S(1)} %pad_maximum_fusion), channel_id=1, source_target_pairs={{0,8},{8,0},{1,9},{9,1},{2,10},{10,2},{3,11},{11,3},{4,12},{12,4},... | collective-permute-start | bytes 835592 | tf_op jit(solution)/shard_map/ppermute | solution.py:124
  74.7 1.3 copy-start.7
  77.8 19.8 %all-to-all-start.3 = ((bf16[16,32,1024]{2,1,0:T(8,128)(2,1)}), bf16[16,32,1024]{2,1,0:T(8,128)(2,1)S(1)}, u32[]{:S(2)}, u32[]{:S(2)}) async-start(bf16[16,32,1024]{2,1,0:T(8,128)(2,1)} %bitcast.46), calls=%async_computation.3 | async-start | bytes 2097152 | tf_op jit(solution)/shard_map/all_to_all | solution.py:158
  81.4 2.6 %copy-start.8 = (bf16[1,512,1024]{2,1,0:T(8,128)(2,1)S(1)}, bf16[1,512,1024]{2,1,0:T(8,128)(2,1)}, u32[]{:S(2)}) copy-start(bf16[1,512,1024]{2,1,0:T(8,128)(2,1)} %param.22) | copy-start | bytes 3145732
  97.6 1.0 copy-start.2
  98.6 25.4 %all-to-all-start.1 = ((bf16[16,32,1024]{2,1,0:T(8,128)(2,1)}), bf16[16,32,1024]{2,1,0:T(8,128)(2,1)S(1)}, u32[]{:S(2)}, u32[]{:S(2)}) async-start(bf16[16,32,1024]{2,1,0:T(8,128)(2,1)} %bitcast.45), calls=%async_computation.1 | async-start | bytes 2097152 | tf_op jit(solution)/shard_map/all_to_all | solution.py:158
  103.1 22.7 %copy-start.6 = (f32[1024]{0:T(1024)S(1)}, f32[1024]{0:T(1024)}, u32[]{:S(2)}) copy-start(f32[1024]{0:T(1024)} %param.20) | copy-start | bytes 12292
  105.7 18.3 %collective-permute-start.3 = (bf16[128,1024]{1,0:T(8,128)(2,1)}, bf16[128,1024]{1,0:T(8,128)(2,1)}, u32[]{:S(2)}, u32[]{:S(2)}) collective-permute-start(bf16[128,1024]{1,0:T(8,128)(2,1)} %convolution_convert_fusion.4), channel_id=1, source_target_pairs={{8,0},{0,8},{9,1},{1,9},{10,2},{2,10},{11,3},{3,11},{12,4},{4,12},... | collective-permute-start | bytes 786440 | tf_op jit(solution)/shard_map/ppermute | solution.py:170

commit v10 on v9

--- a/solution.py
+++ b/solution.py
@@ -137,9 +137,6 @@
         )
         code_s = meta_s[:, :picks_row] * 128 + meta_s[:, picks_row : 2 * picks_row]
         local = code_s.astype(jnp.int32) - my_plane * plane_slots
-        weights_s = (
-            meta_s[:, 2 * picks_row : 3 * picks_row] + meta_s[:, 3 * picks_row : 4 * picks_row]
-        ) + meta_s[:, 4 * picks_row :]
         hit = local[None, :, :] == slot_ids[:, None, None]
         dispatch = jnp.any(hit, axis=2).astype(jnp.bfloat16)
         buffer = jnp.dot(dispatch, normed_s, preferred_element_type=jnp.float32).astype(
@@ -158,13 +155,19 @@
         returned = lax.all_to_all(
             produced.reshape(arrived.shape), PLANE_AXES, split_axis=0, concat_axis=0, tiled=True
         )
-        combine = jnp.sum(jnp.where(hit, weights_s[None, :, :], 0.0), axis=2)
-        partial = jnp.dot(
-            combine.T,
-            returned.reshape(plane_slots, features).astype(jnp.float32),
-            precision=lax.Precision.HIGHEST,
+        parts = [
+            jnp.sum(jnp.where(hit, meta_s[None, :, k0 : k0 + picks_row], 0.0), axis=2)
+            for k0 in range(2 * picks_row, 5 * picks_row, picks_row)
+        ]
+        stacked = jnp.concatenate([p.T for p in parts], axis=0).astype(jnp.bfloat16)
+        products = jnp.dot(
+            stacked,
+            returned.reshape(plane_slots, features),
             preferred_element_type=jnp.float32,
         )
+        partial = (
+            products[:rows_here] + products[rows_here : 2 * rows_here]
+        ) + products[2 * rows_here :]
         if shift:
             back = [((i + shift) % planes, i) for i in range(planes)]
             partial = lax.ppermute(partial.astype(jnp.bfloat16), "eh", back).astype(jnp.float32)

time: 128 us -> 132 us (1.031)
  other arithmetic: 12.3 us -> 16.2 us
  local copies, waits for them, and re-layouts: 4.18 us -> 7.61 us
  waiting for transfers between devices: 52.5 us -> 49.2 us
    all_to_all x2, waiting for transfers between devices: 27 us -> 15.5 us  [on_device(): lax.all_to_all(produced.reshape(arrived.shape), PLANE_AXES, split_axis=0,...]
    ppermute x1, waiting for transfers between devices: 0.01 us -> 8.19 us  [on_device(): lax.ppermute(partial.astype(jnp.bfloat16), 'eh', back).astype(jnp.float32)]
    slice x0 -> x5, local copies, waits for them, and re-layouts: none -> 3.48 us  [on_device(): meta_s[None, :, k0:k0 + picks_row]]
    reduce_sum x2, other arithmetic: 2.19 us -> 5.23 us  [on_device(): jnp.sum(jnp.where(hit, meta_s[None, :, k0:k0 + picks_row], 0.0), axis=2)]
  transfers between devices with their start and end apart: 7 -> 7, of which waited for: 4 -> 5; matrix products, arithmetic and copies ran while one was open for 15% -> 20% of each run, Pallas kernels for 0% -> 0%
where the time goes in v10:
time: 132 us; the launch traced here: 131 us
  waiting for transfers between devices  49.2 us (37%)
  starting transfers between devices  19.5 us (15%)
  blocking collectives  18.8 us (14%)
  other arithmetic  16.2 us (12%)
  matrix products  14.8 us (11%)
  local copies, waits for them, and re-layouts  7.61 us (6%)
  between operations  4.78 us (4%)
    all_to_all x1, waiting for transfers between devices, on_device(): lax.all_to_all(buffer.reshape(groups * lanes, cap_size, features), PLANE_...  19.2 us
    all_to_all x1, blocking collectives, on_device(): lax.all_to_all(buffer.reshape(groups * lanes, cap_size, features), PLANE_...  18.8 us
    all_to_all x2, waiting for transfers between devices, on_device(): lax.all_to_all(produced.reshape(arrived.shape), PLANE_AXES, split_axis=0,...  15.5 us
    ppermute x1, waiting for transfers between devices, on_device(): lax.ppermute(partial.astype(jnp.bfloat16), 'eh', back).astype(jnp.float32)  8.19 us
    all_to_all x2, starting transfers between devices, on_device(): lax.all_to_all(produced.reshape(arrived.shape), PLANE_AXES, split_axis=0,...  7.49 us
    ppermute x1, waiting for transfers between devices, on_device(): blocks[shift] = lax.ppermute(done, 'grp', back)  6.35 us
    reduce_sum x2, other arithmetic, on_device(): jnp.sum(jnp.where(hit, meta_s[None, :, k0:k0 + picks_row], 0.0), axis=2)  5.23 us
    all_to_all x1, starting transfers between devices, on_device(): lax.all_to_all(buffer.reshape(groups * lanes, cap_size, features), PLANE_...  4.34 us
  transfers between devices with their start and end apart: 7, of which 5 were waited for; matrix products, arithmetic and copies ran while one was open for 20% of the time, Pallas kernels for 0%

profile of v10, /device:TPU:0, one launch (start us, length us, event | category | flops | bytes accessed | tf_op | source)
XLA Modules:
  0.0 130.8 jit_solution(4739657722348749204)
XLA Ops:
  0.0 3.0 %collective-permute-start = (bf16[128,1024]{1,0:T(8,128)(2,1)}, bf16[128,1024]{1,0:T(8,128)(2,1)}, u32[]{:S(2)}, u32[]{:S(2)}) collective-permute-start(bf16[128,1024]{1,0:T(8,128)(2,1)} %param.16), channel_id=1, source_target_pairs={{0,16},{16,0},{1,17},{17,1},{2,18},{18,2},{3,19},{19,3},{4,20},{20... | collective-permute-start | bytes 786440 | tf_op jit(solution)/shard_map/ppermute | solution.py:52
  3.0 0.8 select_reduce_fusion.9
  3.8 0.8 select_reduce_fusion.8
  4.6 0.7 multiply_add_fusion
  5.3 0.7 multiply_add_fusion.1
  6.0 0.2 fusion.43
  6.2 0.8 broadcast_in_dim.117
  7.1 0.7 constant_dynamic-update-slice_fusion.4
  7.8 0.7 constant_dynamic-update-slice_fusion.2
  8.5 0.7 constant_dynamic-update-slice_fusion.1
  9.2 0.7 constant_dynamic-update-slice_fusion
  9.9 0.6 fusion.73
  14.5 1.6 %fusion.74 = f32[128,512]{1,0:T(8,128)S(1)} fusion(bf16[128,1024]{1,0:T(8,128)(2,1)} %collective-permute-done, bf16[1024,512]{1,0:T(8,128)(2,1)} %param.18), kind=kOutput, calls=%fused_computation.147 | convolution fusion | flops 134217728 | bytes 1572864 | tf_op jit(solution)/shard_map/dot_general | solution.py:53
  16.1 0.3 collective-permute-start.1
  16.4 0.9 fusion.5
  17.3 0.3 convolution_bitcast_fusion
  17.6 6.3 %collective-permute-done.1 = f32[128,512]{1,0:T(8,128)S(1)} collective-permute-done((f32[128,512]{1,0:T(8,128)S(1)}, f32[128,512]{1,0:T(8,128)S(1)}, u32[]{:S(2)}, u32[]{:S(2)}) %collective-permute-start.1) | collective-permute-done | bytes 262176 | tf_op jit(solution)/shard_map/ppermute | solution.py:54
  24.1 0.2 fusion.10
  24.4 1.5 %convolution_convert_fusion.1 = bf16[512,1024]{1,0:T(8,128)(2,1)} fusion(pred[512,128]{1,0:T(8,128)(4,1)S(1)} %fusion.5, bf16[128,1024]{1,0:T(8,128)(2,1)S(1)} %fusion.12), kind=kOutput, calls=%fused_computation.15 | convolution fusion | flops 134742016 | bytes 1376256 | tf_op jit(solution)/shard_map/dot_general | solution.py:142
  25.9 4.3 %all-to-all-start = ((bf16[16,32,1024]{2,1,0:T(8,128)(2,1)}), bf16[16,32,1024]{2,1,0:T(8,128)(2,1)}, u32[]{:S(2)}, u32[]{:S(2)}) async-start(bf16[16,32,1024]{2,1,0:T(8,128)(2,1)} %bitcast.9), calls=%async_computation | async-start | bytes 2097152 | tf_op jit(solution)/shard_map/all_to_all | solution.py:145
  30.5 2.7 %collective-permute-start.2 = (bf16[136,1024]{1,0:T(8,128)(2,1)S(1)}, bf16[136,1024]{1,0:T(8,128)(2,1)S(1)}, u32[]{:S(2)}, u32[]{:S(2)}) collective-permute-start(bf16[136,1024]{1,0:T(8,128)(2,1)S(1)} %pad_maximum_fusion), channel_id=1, source_target_pairs={{0,8},{8,0},{1,9},{9,1},{2,10},{10,2},{3,11},{11,3},{4,12},{12,4},... | collective-permute-start | bytes 835592 | tf_op jit(solution)/shard_map/ppermute | solution.py:124
  33.2 19.2 %all-to-all-done = bf16[16,32,1024]{2,1,0:T(8,128)(2,1)} async-done(((bf16[16,32,1024]{2,1,0:T(8,128)(2,1)}), bf16[16,32,1024]{2,1,0:T(8,128)(2,1)}, u32[]{:S(2)}, u32[]{:S(2)}) %all-to-all-start) | async-done | bytes 1048608 | tf_op jit(solution)/shard_map/all_to_all | solution.py:145
  52.3 1.2 slice.123
  54.3 0.8 fusion.71
  55.2 0.9 fusion.4
  56.2 0.4 convolution_convert_fusion
  56.6 18.8 %all_to_all.20 = bf16[16,32,1024]{2,1,0:T(8,128)(2,1)S(1)} all-to-all(bf16[16,32,1024]{2,1,0:T(8,128)(2,1)S(1)} %bitcast.60), channel_id=1, replica_groups=mesh['grp'=2,'eh'=2,'el'=8] {'grp','el'}, dimensions={0} | all-to-all | bytes 2097152 | tf_op jit(solution)/shard_map/all_to_all | solution.py:145
  75.4 1.2 fusion
  76.6 1.8 %convolution_convert_fusion.2 = bf16[512,1024]{1,0:T(8,128)(2,1)} fusion(bf16[1,512,1024]{2,1,0:T(8,128)(2,1)S(1)} %copy-done.7, f32[512,1024]{1,0:T(8,128)S(1)} %fusion), kind=kOutput, calls=%fused_computation.16 | convolution fusion | flops 538968064 | bytes 4194304 | tf_op jit(solution)/shard_map/dot_general | solution.py:119
  78.4 3.7 %all-to-all-start.3 = ((bf16[16,32,1024]{2,1,0:T(8,128)(2,1)}), bf16[16,32,1024]{2,1,0:T(8,128)(2,1)S(1)}, u32[]{:S(2)}, u32[]{:S(2)}) async-start(bf16[16,32,1024]{2,1,0:T(8,128)(2,1)} %bitcast.62), calls=%async_computation.3 | async-start | bytes 2097152 | tf_op jit(solution)/shard_map/all_to_all | solution.py:155
  82.1 2.6 %fusion.2 = f32[512,1024]{1,0:T(8,128)S(1)} fusion(bf16[512,1024]{1,0:T(8,128)(2,1)} %bitcast.10, bf16[1,1024,1024]{2,1,0:T(8,128)(2,1)S(1)} %copy-done), kind=kOutput, calls=%fused_computation.2 | convolution fusion | flops 1073741824 | bytes 5242880 | tf_op jit(solution)/shard_map/dot_general | solution.py:115
  84.7 1.7 %convolution_convert_fusion.3 = bf16[512,1024]{1,0:T(8,128)(2,1)} fusion(bf16[1,512,1024]{2,1,0:T(8,128)(2,1)S(1)} %copy-done.8, f32[512,1024]{1,0:T(8,128)S(1)} %fusion.2), kind=kOutput, calls=%fused_computation.17 | convolution fusion | flops 538968064 | bytes 4194304 | tf_op jit(solution)/shard_map/dot_general | solution.py:119
  86.4 11.8 %all-to-all-done.3 = bf16[16,32,1024]{2,1,0:T(8,128)(2,1)S(1)} async-done(((bf16[16,32,1024]{2,1,0:T(8,128)(2,1)}), bf16[16,32,1024]{2,1,0:T(8,128)(2,1)S(1)}, u32[]{:S(2)}, u32[]{:S(2)}) %all-to-all-start.3) | async-done | bytes 1048608 | tf_op jit(solution)/shard_map/all_to_all | solution.py:155
  98.2 1.0 copy-done.1
  99.2 3.8 %all-to-all-start.1 = ((bf16[16,32,1024]{2,1,0:T(8,128)(2,1)}), bf16[16,32,1024]{2,1,0:T(8,128)(2,1)S(1)}, u32[]{:S(2)}, u32[]{:S(2)}) async-start(bf16[16,32,1024]{2,1,0:T(8,128)(2,1)} %bitcast.61), calls=%async_computation.1 | async-start | bytes 2097152 | tf_op jit(solution)/shard_map/all_to_all | solution.py:155
  103.1 3.0 %select_reduce_fusion.5 = (bf16[512,128]{1,0:T(8,128)(2,1)S(1)}, bf16[512,128]{1,0:T(8,128)(2,1)}, bf16[512,128]{1,0:T(8,128)(2,1)}) fusion(f32[128,8]{0,1:T(8,128)S(1)} %get-tuple-element.39, s32[128,8]{0,1:T(8,128)S(1)} %fusion.57, f32[128,8]{0,1:T(8,128)S(1)} %get-tuple-element.38, f32[128,8]{0,1:T(8,128)S(1)} %get-tuple-element.37), kind=kLoop, calls=%fused_computation.11 | loop fusion | flops 3473408 | bytes 409600 | tf_op jit(solution)/shard_map/reduce_sum | solution.py:159
  106.1 0.9 copy.52
  107.0 0.9 copy.54
  107.9 0.9 copy.53
  108.8 2.3 %select_reduce_fusion.2 = (bf16[512,128]{1,0:T(8,128)(2,1)S(1)}, bf16[512,128]{1,0:T(8,128)(2,1)S(1)}, bf16[512,128]{1,0:T(8,128)(2,1)S(1)}) fusion(f32[128,8]{0,1:T(8,128)S(1)} %copy.52, s32[128,8]{0,1:T(8,128)S(1)} %convert_subtract_fusion, f32[128,8]{0,1:T(8,128)S(1)} %copy.54, f32[128,8]{0,1:T(8,128)S(1)} %copy.53), kind=kLoop, calls=%fused_computation.6 | loop fusion | flops 3473408 | bytes 409600 | tf_op jit(solution)/shard_map/reduce_sum | solution.py:159
  111.0 1.8 %fusion.26 = f32[384,1024]{1,0:T(8,128)S(1)} fusion(bf16[512,1024]{1,0:T(8,128)(2,1)} %bitcast.59, bf16[128,512]{0,1:T(8,128)(2,1)S(1)} %bitcast.68, bf16[128,512]{0,1:T(8,128)(2,1)S(1)} %bitcast.69, bf16[128,512]{0,1:T(8,128)(2,1)S(1)} %bitcast.67), kind=kOutput, calls=%fused_computation.53 | convolution fusion | flops 403832832 | bytes 3014656 | tf_op jit(solution)/shard_map/dot_general | solution.py:163
  112.9 0.8 fusion.15
  113.7 1.7 %collective-permute-start.3 = (bf16[128,1024]{1,0:T(8,128)(2,1)}, bf16[128,1024]{1,0:T(8,128)(2,1)}, u32[]{:S(2)}, u32[]{:S(2)}) collective-permute-start(bf16[128,1024]{1,0:T(8,128)(2,1)} %fusion.15), channel_id=1, source_target_pairs={{8,0},{0,8},{9,1},{1,9},{10,2},{2,10},{11,3},{3,11},{12,4},{4,12},... | collective-permute-start | bytes 786440 | tf_op jit(solution)/shard_map/ppermute | solution.py:173
  115.4 3.7 %all-to-all-done.1 = bf16[16,32,1024]{2,1,0:T(8,128)(2,1)S(1)} async-done(((bf16[16,32,1024]{2,1,0:T(8,128)(2,1)}), bf16[16,32,1024]{2,1,0:T(8,128)(2,1)S(1)}, u32[]{:S(2)}, u32[]{:S(2)}) %all-to-all-start.1) | async-done | bytes 1048608 | tf_op jit(solution)/shard_map/all_to_all | solution.py:155
  119.1 1.6 %fusion.20 = f32[384,1024]{1,0:T(8,128)S(1)} fusion(bf16[512,1024]{1,0:T(8,128)(2,1)S(1)} %bitcast.58, bf16[128,512]{0,1:T(8,128)(2,1)} %bitcast.65, bf16[128,512]{0,1:T(8,128)(2,1)} %bitcast.66, bf16[128,512]{0,1:T(8,128)(2,1)S(1)} %bitcast.64), kind=kOutput, calls=%fused_computation.47 | convolution fusion | flops 403832832 | bytes 3014656 | tf_op jit(solution)/shard_map/dot_general | solution.py:163
  120.6 8.2 %collective-permute-done.3 = bf16[128,1024]{1,0:T(8,128)(2,1)} collective-permute-done((bf16[128,1024]{1,0:T(8,128)(2,1)}, bf16[128,1024]{1,0:T(8,128)(2,1)}, u32[]{:S(2)}, u32[]{:S(2)}) %collective-permute-start.3) | collective-permute-done | bytes 262176 | tf_op jit(solution)/shard_map/ppermute | solution.py:173
  128.8 1.2 multiply_reduce_fusion
  130.0 0.8 multiply_convert_fusion
  (42 shorter events, 1.0 us)
Async XLA Ops:
  0.0 75.3 %copy-start = (bf16[1,1024,1024]{2,1,0:T(8,128)(2,1)S(1)}, bf16[1,1024,1024]{2,1,0:T(8,128)(2,1)}, u32[]{:S(2)}) copy-start(bf16[1,1024,1024]{2,1,0:T(8,128)(2,1)} %param.21) | copy-start | bytes 6291460
  0.0 17.3 %copy-start.3 = (bf16[128,1024]{1,0:T(8,128)(2,1)S(1)}, bf16[128,1024]{1,0:T(8,128)(2,1)}, u32[]{:S(2)}) copy-start(bf16[128,1024]{1,0:T(8,128)(2,1)} %param.16) | copy-start | bytes 786436
  0.0 17.3 %copy-start.2 = (bf16[1024,512]{1,0:T(8,128)(2,1)S(1)}, bf16[1024,512]{1,0:T(8,128)(2,1)}, u32[]{:S(2)}) copy-start(bf16[1024,512]{1,0:T(8,128)(2,1)} %param.18) | copy-start | bytes 3145732
  0.0 14.4 %collective-permute-start = (bf16[128,1024]{1,0:T(8,128)(2,1)}, bf16[128,1024]{1,0:T(8,128)(2,1)}, u32[]{:S(2)}, u32[]{:S(2)}) collective-permute-start(bf16[128,1024]{1,0:T(8,128)(2,1)} %param.16), channel_id=1, source_target_pairs={{0,16},{16,0},{1,17},{17,1},{2,18},{18,2},{3,19},{19,3},{4,20},{20... | collective-permute-start | bytes 786440 | tf_op jit(solution)/shard_map/ppermute | solution.py:52
  14.4 9.7 %copy-start.4 = (bf16[128,1024]{1,0:T(8,128)(2,1)S(1)}, bf16[128,1024]{1,0:T(8,128)(2,1)}, u32[]{:S(2)}) copy-start(bf16[128,1024]{1,0:T(8,128)(2,1)} %param.17) | copy-start | bytes 786436
  16.1 8.2 %copy-start.5 = (f32[1024]{0:T(1024)S(1)}, f32[1024]{0:T(1024)}, u32[]{:S(2)}) copy-start(f32[1024]{0:T(1024)} %param.19) | copy-start | bytes 12292
  16.1 7.8 %collective-permute-start.1 = (f32[128,512]{1,0:T(8,128)S(1)}, f32[128,512]{1,0:T(8,128)S(1)}, u32[]{:S(2)}, u32[]{:S(2)}) collective-permute-start(f32[128,512]{1,0:T(8,128)S(1)} %fusion.74), channel_id=1, source_target_pairs={{16,0},{0,16},{17,1},{1,17},{18,2},{2,18},{19,3},{3,19},{20,4},{4,... | collective-permute-start | bytes 786440 | tf_op jit(solution)/shard_map/ppermute | solution.py:54
  25.9 26.5 %all-to-all-start = ((bf16[16,32,1024]{2,1,0:T(8,128)(2,1)}), bf16[16,32,1024]{2,1,0:T(8,128)(2,1)}, u32[]{:S(2)}, u32[]{:S(2)}) async-start(bf16[16,32,1024]{2,1,0:T(8,128)(2,1)} %bitcast.9), calls=%async_computation | async-start | bytes 2097152 | tf_op jit(solution)/shard_map/all_to_all | solution.py:145
  30.5 23.7 %collective-permute-start.2 = (bf16[136,1024]{1,0:T(8,128)(2,1)S(1)}, bf16[136,1024]{1,0:T(8,128)(2,1)S(1)}, u32[]{:S(2)}, u32[]{:S(2)}) collective-permute-start(bf16[136,1024]{1,0:T(8,128)(2,1)S(1)} %pad_maximum_fusion), channel_id=1, source_target_pairs={{0,8},{8,0},{1,9},{9,1},{2,10},{10,2},{3,11},{11,3},{4,12},{12,4},... | collective-permute-start | bytes 835592 | tf_op jit(solution)/shard_map/ppermute | solution.py:124
  75.3 1.3 copy-start.7
  78.4 19.8 %all-to-all-start.3 = ((bf16[16,32,1024]{2,1,0:T(8,128)(2,1)}), bf16[16,32,1024]{2,1,0:T(8,128)(2,1)S(1)}, u32[]{:S(2)}, u32[]{:S(2)}) async-start(bf16[16,32,1024]{2,1,0:T(8,128)(2,1)} %bitcast.62), calls=%async_computation.3 | async-start | bytes 2097152 | tf_op jit(solution)/shard_map/all_to_all | solution.py:155
  82.1 2.6 %copy-start.8 = (bf16[1,512,1024]{2,1,0:T(8,128)(2,1)S(1)}, bf16[1,512,1024]{2,1,0:T(8,128)(2,1)}, u32[]{:S(2)}) copy-start(bf16[1,512,1024]{2,1,0:T(8,128)(2,1)} %param.22) | copy-start | bytes 3145732
  98.2 1.0 copy-start.1
  99.2 19.8 %all-to-all-start.1 = ((bf16[16,32,1024]{2,1,0:T(8,128)(2,1)}), bf16[16,32,1024]{2,1,0:T(8,128)(2,1)S(1)}, u32[]{:S(2)}, u32[]{:S(2)}) async-start(bf16[16,32,1024]{2,1,0:T(8,128)(2,1)} %bitcast.61), calls=%async_computation.1 | async-start | bytes 2097152 | tf_op jit(solution)/shard_map/all_to_all | solution.py:155
  113.7 15.1 %collective-permute-start.3 = (bf16[128,1024]{1,0:T(8,128)(2,1)}, bf16[128,1024]{1,0:T(8,128)(2,1)}, u32[]{:S(2)}, u32[]{:S(2)}) collective-permute-start(bf16[128,1024]{1,0:T(8,128)(2,1)} %fusion.15), channel_id=1, source_target_pairs={{8,0},{0,8},{9,1},{1,9},{10,2},{2,10},{11,3},{3,11},{12,4},{4,12},... | collective-permute-start | bytes 786440 | tf_op jit(solution)/shard_map/ppermute | solution.py:173
  119.1 10.9 %copy-start.6 = (f32[1024]{0:T(1024)S(1)}, f32[1024]{0:T(1024)}, u32[]{:S(2)}) copy-start(f32[1024]{0:T(1024)} %param.20) | copy-start | bytes 12292

commit v11 on v8

--- a/solution.py
+++ b/solution.py
@@ -44,21 +44,41 @@
     my_plane = lax.axis_index("eh")
 
     me_grp = lax.axis_index("grp")
-    blocks = [None] * groups
-    blocks[0] = jnp.dot(attention, out_proj, preferred_element_type=jnp.float32)
+    pair = jnp.concatenate([attention, residual], axis=0)
+    pairs_in = [pair] + [
+        lax.ppermute(pair, "eh", [(i, (i + shift) % planes) for i in range(planes)])
+        for shift in range(1, planes)
+    ]
+    cols = [[jnp.dot(p[:rows_here], out_proj, preferred_element_type=jnp.float32)]
+            for p in pairs_in]
     for shift in range(1, groups):
         ahead = [(g, (g + shift) % groups) for g in range(groups)]
-        back = [(b, a) for a, b in ahead]
         visiting = lax.ppermute(attention, "grp", ahead)
         done = jnp.dot(visiting, out_proj, preferred_element_type=jnp.float32)
-        blocks[shift] = lax.ppermute(done, "grp", back)
-    stacked = jnp.stack(blocks, axis=0)
+        for plane_shift in range(planes):
+            sends = [
+                (
+                    g * planes + h,
+                    ((g - shift) % groups) * planes + (h + plane_shift) % planes,
+                )
+                for g in range(groups)
+                for h in range(planes)
+            ]
+            cols[plane_shift].append(lax.ppermute(done, ("grp", "eh"), sends))
     order_cols = (jnp.arange(groups, dtype=jnp.int32) - me_grp) % groups
-    attn_proj = jnp.concatenate(
-        [jnp.take(stacked, order_cols[j], axis=0) for j in range(groups)], axis=1
-    )
-    hidden_state = (residual.astype(jnp.float32) + attn_proj).astype(jnp.bfloat16)
-    normed = rms_scale(hidden_state.astype(jnp.float32), pre_gain).astype(jnp.bfloat16)
+    normed_in = []
+    for plane_shift in range(planes):
+        stacked = jnp.stack(cols[plane_shift], axis=0)
+        attn_proj = jnp.concatenate(
+            [jnp.take(stacked, order_cols[j], axis=0) for j in range(groups)], axis=1
+        )
+        residual_s = pairs_in[plane_shift][rows_here:]
+        hidden_s = (residual_s.astype(jnp.float32) + attn_proj).astype(jnp.bfloat16)
+        if plane_shift == 0:
+            hidden_state = hidden_s
+        normed_in.append(
+            rms_scale(hidden_s.astype(jnp.float32), pre_gain).astype(jnp.bfloat16)
+        )
 
     experts_all = placement.shape[0]
     slot_table = jnp.arange(owners, dtype=jnp.int32)
@@ -105,7 +125,11 @@
     meta_size = rows_here * meta.shape[1]
     meta_rows = -(-meta_size // (8 * features)) * 8
     meta_block = jnp.pad(meta.reshape(-1), (0, meta_rows * features - meta_size))
-    packed = jnp.concatenate([normed, meta_block.reshape(meta_rows, features)], axis=0)
+    meta_block = meta_block.reshape(meta_rows, features)
+    meta_in = [meta_block] + [
+        lax.ppermute(meta_block, "eh", [(i, (i + shift) % planes) for i in range(planes)])
+        for shift in range(1, planes)
+    ]
     gate_up_local = slot_gate_up[0]
     down_local = slot_down[0]
     hidden_units = down_local.shape[0]
@@ -120,41 +144,37 @@
             jnp.bfloat16
         )
 
-    received = [packed] + [
-        lax.ppermute(packed, "eh", [(i, (i + shift) % planes) for i in range(planes)])
-        for shift in range(1, planes)
-    ]
-    partials = []
-    for shift, block in enumerate(received):
-        normed_s = block[:rows_here]
+    hits = []
+    weights_in = []
+    buffers = []
+    for shift in range(planes):
         meta_s = (
-            block[rows_here:]
+            meta_in[shift]
             .reshape(-1)[:meta_size]
             .reshape(rows_here, meta.shape[1])
             .astype(jnp.float32)
         )
         code_s = meta_s[:, :picks_row] * 128 + meta_s[:, picks_row : 2 * picks_row]
         local = code_s.astype(jnp.int32) - my_plane * plane_slots
-        weights_s = (
-            meta_s[:, 2 * picks_row : 3 * picks_row] + meta_s[:, 3 * picks_row : 4 * picks_row]
-        ) + meta_s[:, 4 * picks_row :]
+        weights_in.append(
+            (meta_s[:, 2 * picks_row : 3 * picks_row] + meta_s[:, 3 * picks_row : 4 * picks_row])
+            + meta_s[:, 4 * picks_row :]
+        )
         hit = local[None, :, :] == slot_ids[:, None, None]
+        hits.append(hit)
         dispatch = jnp.any(hit, axis=2).astype(jnp.bfloat16)
-        buffer = jnp.dot(dispatch, normed_s, preferred_element_type=jnp.float32).astype(
-            jnp.bfloat16
-        )
-        arrived = lax.all_to_all(
-            buffer.reshape(groups * lanes, cap_size, features),
-            PLANE_AXES,
-            split_axis=0,
-            concat_axis=0,
-            tiled=True,
-        )
-        produced = expert(arrived.reshape(-1, features))
+        buffer = jnp.dot(dispatch, normed_in[shift], preferred_element_type=jnp.float32)
+        buffers.append(buffer.astype(jnp.bfloat16).reshape(groups * lanes, cap_size, features))
+    arrived = lax.all_to_all(
+        jnp.stack(buffers, axis=1), PLANE_AXES, split_axis=0, concat_axis=0, tiled=True
+    )
+    produced = expert(arrived.reshape(-1, features)).reshape(arrived.shape)
+    partials = [None] * planes
+    for shift in list(range(1, planes)) + [0]:
         returned = lax.all_to_all(
-            produced.reshape(arrived.shape), PLANE_AXES, split_axis=0, concat_axis=0, tiled=True
-        )
-        combine = jnp.sum(jnp.where(hit, weights_s[None, :, :], 0.0), axis=2)
+            produced[:, shift], PLANE_AXES, split_axis=0, concat_axis=0, tiled=True
+        )
+        combine = jnp.sum(jnp.where(hits[shift], weights_in[shift][None, :, :], 0.0), axis=2)
         partial = jnp.dot(
             combine.T,
             returned.reshape(plane_slots, features).astype(jnp.float32),
@@ -164,7 +184,7 @@
         if shift:
             back = [((i + shift) % planes, i) for i in range(planes)]
             partial = lax.ppermute(partial.astype(jnp.bfloat16), "eh", back).astype(jnp.float32)
-        partials.append(partial)
+        partials[shift] = partial
     mixture = partials[0]
     for partial in partials[1:]:
         mixture = mixture + partial

time: 131 us -> 141 us (1.076)
  blocking collectives: 0 us -> 50.2 us
  waiting for transfers between devices: 65.3 us -> 34.3 us
  starting transfers between devices: 24.6 us -> 14 us
  matrix products: 18.7 us -> 13.4 us
  other arithmetic: 13.2 us -> 17.6 us
  local copies, waits for them, and re-layouts: 3.94 us -> 6.11 us
    all_to_all x0 -> x2, blocking collectives: none -> 50.2 us  [the longest x1 30.7 us: on_device(): lax.all_to_all(jnp.stack(buffers, axis=1), PLANE_AXES, split_axis=0, conc...]
    all_to_all x4 -> x1, waiting for transfers between devices: 52.2 us -> 13.7 us  [on_device(): lax.all_to_all(produced[:, shift], PLANE_AXES, split_axis=0, concat_axis=...]
    all_to_all x4 -> x1, starting transfers between devices: 15.3 us -> 3.78 us  [on_device(): lax.all_to_all(produced[:, shift], PLANE_AXES, split_axis=0, concat_axis=...]
    ppermute x2 -> x4, waiting for transfers between devices: 13.1 us -> 20.6 us  [the longest x2 11.8 us: on_device(): cols[plane_shift].append(lax.ppermute(done, ('grp', 'eh'), sends))]
    dot_general x2 -> x1, matrix products: 5.12 us -> 2.35 us  [expert(): jnp.dot(rows_in, gate_up_local, preferred_element_type=jnp.float32)]
    dot_general x2 -> x1, matrix products: 3.51 us -> 1.31 us  [expert(): jnp.dot(expert_hidden, down_local, preferred_element_type=jnp.float32)]
    reduce_sum x1 -> x2, other arithmetic: 0.16 us -> 2.22 us  [rms_scale(): meansq = jnp.mean(values * values, axis=-1, keepdims=True)]
    concatenate x1, other arithmetic: 0.02 us -> 1.85 us  [on_device(): pair = jnp.concatenate([attention, residual], axis=0)]
  transfers between devices with their start and end apart: 8 -> 7, of which waited for: 6 -> 4; matrix products, arithmetic and copies ran while one was open for 18% -> 19% of each run, Pallas kernels for 0% -> 0%
where the time goes in v11:
time: 141 us; the launch traced here: 140 us
  blocking collectives  50.2 us (36%)
  waiting for transfers between devices  34.3 us (24%)
  other arithmetic  17.6 us (12%)
  starting transfers between devices  14 us (10%)
  matrix products  13.4 us (10%)
  local copies, waits for them, and re-layouts  6.11 us (4%)
  between operations  4 us (3%)
    all_to_all x1, blocking collectives, on_device(): lax.all_to_all(jnp.stack(buffers, axis=1), PLANE_AXES, split_axis=0, conc...  30.7 us
    all_to_all x1, blocking collectives, on_device(): lax.all_to_all(produced[:, shift], PLANE_AXES, split_axis=0, concat_axis=...  19.5 us
    all_to_all x1, waiting for transfers between devices, on_device(): lax.all_to_all(produced[:, shift], PLANE_AXES, split_axis=0, concat_axis=...  13.7 us
    ppermute x2, waiting for transfers between devices, on_device(): cols[plane_shift].append(lax.ppermute(done, ('grp', 'eh'), sends))  11.8 us
    ppermute x1, waiting for transfers between devices, on_device(): lax.ppermute(meta_block, 'eh', [(i, (i + shift) % planes) for i in range(...  8.83 us
    dot_general x2, matrix products, on_device(): jnp.dot(combine.T, returned.reshape(plane_slots, features).astype(jnp.flo...  4.38 us
    all_to_all x1, starting transfers between devices, on_device(): lax.all_to_all(produced[:, shift], PLANE_AXES, split_axis=0, concat_axis=...  3.78 us
    ppermute x1, starting transfers between devices, on_device(): lax.ppermute(partial.astype(jnp.bfloat16), 'eh', back).astype(jnp.float32)  3.2 us
  transfers between devices with their start and end apart: 7, of which 4 were waited for; matrix products, arithmetic and copies ran while one was open for 19% of the time, Pallas kernels for 0%

profile of v11, /device:TPU:0, one launch (start us, length us, event | category | flops | bytes accessed | tf_op | source)
XLA Modules:
  0.0 139.6 jit_solution(3316678769057352557)
XLA Ops:
  0.0 3.0 %collective-permute-start = (bf16[128,1024]{1,0:T(8,128)(2,1)}, bf16[128,1024]{1,0:T(8,128)(2,1)}, u32[]{:S(2)}, u32[]{:S(2)}) collective-permute-start(bf16[128,1024]{1,0:T(8,128)(2,1)} %param.16), channel_id=1, source_target_pairs={{0,16},{16,0},{1,17},{17,1},{2,18},{18,2},{3,19},{19,3},{4,20},{20... | collective-permute-start | bytes 786440 | tf_op jit(solution)/shard_map/ppermute | solution.py:56
  3.0 1.9 %pad_maximum_fusion.1 = bf16[256,1024]{1,0:T(8,128)(2,1)} fusion(bf16[128,1024]{1,0:T(8,128)(2,1)} %param.17, bf16[128,1024]{1,0:T(8,128)(2,1)} %param.16), kind=kLoop, calls=%fused_computation.42 | loop fusion | flops 1048576 | bytes 1048576 | tf_op jit(solution)/shard_map/concatenate | solution.py:47
  4.8 2.6 %collective-permute-start.3 = (bf16[256,1024]{1,0:T(8,128)(2,1)}, bf16[256,1024]{1,0:T(8,128)(2,1)}, u32[]{:S(2)}, u32[]{:S(2)}) collective-permute-start(bf16[256,1024]{1,0:T(8,128)(2,1)} %pad_maximum_fusion.1), channel_id=1, source_target_pairs={{0,8},{8,0},{1,9},{9,1},{2,10},{10,2},{3,11},{11,3},{4,12},{12,4},... | collective-permute-start | bytes 1572872 | tf_op jit(solution)/shard_map/ppermute | solution.py:49
  7.4 0.8 select_reduce_fusion.5
  8.2 0.8 select_reduce_fusion.4
  9.0 0.7 multiply_add_fusion
  9.7 0.7 multiply_add_fusion.1
  10.4 0.2 fusion.39
  10.6 0.8 broadcast_in_dim.90
  11.5 0.7 constant_dynamic-update-slice_fusion.4
  12.2 0.7 constant_dynamic-update-slice_fusion.2
  12.9 0.7 constant_dynamic-update-slice_fusion.1
  13.6 0.7 constant_dynamic-update-slice_fusion
  14.6 0.6 reshape.66
  15.2 0.3 collective-permute-start.2
  15.5 1.6 %convolution_bitcast_fusion.1 = f32[1,128,512]{2,1,0:T(8,128)S(1)} fusion(bf16[128,1024]{1,0:T(8,128)(2,1)} %param.16, bf16[1024,512]{1,0:T(8,128)(2,1)} %param.18), kind=kOutput, calls=%fused_computation.16 | convolution fusion | flops 134217728 | bytes 1572864 | tf_op jit(solution)/shard_map/dot_general | solution.py:52
  17.2 0.9 fusion.4
  18.1 0.6 fusion.65
  22.4 8.8 %collective-permute-done.2 = bf16[8,1024]{1,0:T(8,128)(2,1)S(1)} collective-permute-done((bf16[8,1024]{1,0:T(8,128)(2,1)}, bf16[8,1024]{1,0:T(8,128)(2,1)S(1)}, u32[]{:S(2)}, u32[]{:S(2)}) %collective-permute-start.2) | collective-permute-done | bytes 16416 | tf_op jit(solution)/shard_map/ppermute | solution.py:130
  31.3 0.6 slice_convert_fusion
  31.9 0.8 reshape.130
  32.7 0.8 slice_add_fusion
  33.5 0.9 copy.54
  34.4 0.9 copy.55
  35.3 1.3 fusion.66
  36.6 0.8 collective-permute-start.1
  37.3 0.9 fusion.3
  38.2 0.4 collective-permute-start.4
  38.6 6.9 %collective-permute-done.1 = f32[128,512]{1,0:T(8,128)S(1)} collective-permute-done((f32[128,512]{1,0:T(8,128)S(1)}, f32[128,512]{1,0:T(8,128)S(1)}, u32[]{:S(2)}, u32[]{:S(2)}) %collective-permute-start.1) | collective-permute-done | bytes 262176 | tf_op jit(solution)/shard_map/ppermute | solution.py:67
  45.7 1.1 fusion.11
  46.8 1.3 convolution_bitcast_fusion
  48.1 4.9 %collective-permute-done.4 = f32[128,512]{1,0:T(8,128)S(1)} collective-permute-done((f32[128,512]{1,0:T(8,128)S(1)}, f32[128,512]{1,0:T(8,128)S(1)}, u32[]{:S(2)}, u32[]{:S(2)}) %collective-permute-start.4) | collective-permute-done | bytes 262176 | tf_op jit(solution)/shard_map/ppermute | solution.py:67
  53.1 1.1 fusion.8
  54.2 0.5 convolution_convert_fusion.2
  54.7 0.5 convolution_convert_fusion.1
  55.4 30.7 %all_to_all.15 = bf16[16,2,32,1024]{3,2,1,0:T(8,128)(2,1)S(1)} all-to-all(bf16[16,2,32,1024]{3,2,1,0:T(8,128)(2,1)S(1)} %pad_maximum_fusion), channel_id=1, replica_groups=mesh['grp'=2,'eh'=2,'el'=8] {'grp','el'}, dimensions={0} | all-to-all | bytes 4194304 | tf_op jit(solution)/shard_map/all_to_all | solution.py:168
  86.1 2.4 %fusion.1 = f32[1024,1024]{1,0:T(8,128)S(1)} fusion(bf16[1024,1024]{1,0:T(8,128)(2,1)S(1)} %bitcast.54, bf16[1,1024,1024]{2,1,0:T(8,128)(2,1)S(1)} %copy-done), kind=kOutput, calls=%fused_computation.3 | convolution fusion | flops 2147483648 | bytes 8388608 | tf_op jit(solution)/shard_map/dot_general | solution.py:139
  88.5 1.3 convolution_convert_fusion
  89.8 1.2 slice_bitcast_fusion
  90.9 19.5 %all_to_all.16 = bf16[16,32,1024]{2,1,0:T(8,128)(2,1)} all-to-all(bf16[16,32,1024]{2,1,0:T(8,128)(2,1)S(1)} %get-tuple-element.24), channel_id=1, replica_groups=mesh['grp'=2,'eh'=2,'el'=8] {'grp','el'}, dimensions={0} | all-to-all | bytes 2097152 | tf_op jit(solution)/shard_map/all_to_all | solution.py:174
  110.5 3.8 %all-to-all-start.1 = ((bf16[16,32,1024]{2,1,0:T(8,128)(2,1)}), bf16[16,32,1024]{2,1,0:T(8,128)(2,1)S(1)}, u32[]{:S(2)}, u32[]{:S(2)}) async-start(bf16[16,32,1024]{2,1,0:T(8,128)(2,1)} %get-tuple-element.25), calls=%async_computation.1 | async-start | bytes 2097152 | tf_op jit(solution)/shard_map/all_to_all | solution.py:174
  114.3 0.7 select_reduce_fusion
  115.1 2.6 %convolution_convert_fusion.3 = bf16[128,1024]{1,0:T(8,128)(2,1)} fusion(f32[512,128]{1,0:T(8,128)S(1)} %select_reduce_fusion, bf16[512,1024]{1,0:T(8,128)(2,1)} %bitcast.50), kind=kOutput, calls=%fused_computation.14 | convolution fusion | flops 805437440 | bytes 1572864 | tf_op jit(solution)/shard_map/dot_general | solution.py:178
  117.7 3.2 %collective-permute-start.5 = (bf16[128,1024]{1,0:T(8,128)(2,1)}, bf16[128,1024]{1,0:T(8,128)(2,1)}, u32[]{:S(2)}, u32[]{:S(2)}) collective-permute-start(bf16[128,1024]{1,0:T(8,128)(2,1)} %convolution_convert_fusion.3), channel_id=1, source_target_pairs={{8,0},{0,8},{9,1},{1,9},{10,2},{2,10},{11,3},{3,11},{12,4},{4,12},... | collective-permute-start | bytes 786440 | tf_op jit(solution)/shard_map/ppermute | solution.py:186
  120.9 1.4 %select_reduce_fusion.1 = f32[512,128]{1,0:T(8,128)} fusion(f32[128,8]{0,1:T(8,128)S(1)} %slice_add_fusion.2, s32[128,8]{0,1:T(8,128)S(1)} %fusion.53), kind=kLoop, calls=%fused_computation.8 | loop fusion | flops 1507328 | bytes 270336 | tf_op jit(solution)/shard_map/reduce_sum | solution.py:177
  122.3 13.7 %all-to-all-done.1 = bf16[16,32,1024]{2,1,0:T(8,128)(2,1)S(1)} async-done(((bf16[16,32,1024]{2,1,0:T(8,128)(2,1)}), bf16[16,32,1024]{2,1,0:T(8,128)(2,1)S(1)}, u32[]{:S(2)}, u32[]{:S(2)}) %all-to-all-start.1) | async-done | bytes 1048608 | tf_op jit(solution)/shard_map/all_to_all | solution.py:174
  136.0 1.8 %multiply_reduce_fusion = (f32[128]{0:T(128)S(1)}, f32[128,1024]{1,0:T(8,128)S(1)}) fusion(bf16[128,1024]{1,0:T(8,128)(2,1)} %collective-permute-done.5, bf16[128,1024]{1,0:T(8,128)(2,1)S(1)} %get-tuple-element.18, f32[512,128]{1,0:T(8,128)} %select_reduce_fusion.1, bf16[512,1024]{1,0:T(8,128)(2,1)S(1)} %bitcast.49), kind=kOutput, calls=%fused_computation.46 | convolution fusion | flops 806092672 | bytes 2359808 | tf_op jit(solution)/shard_map/dot_general | solution.py:178
  137.8 1.8 %multiply_convert_fusion = bf16[128,1024]{1,0:T(8,128)(2,1)} fusion(f32[1024]{0:T(1024)S(1)} %copy-done.6, f32[128]{0:T(128)S(1)} %add_rsqrt_fusion, f32[128,1024]{1,0:T(8,128)S(1)} %get-tuple-element.36, bf16[128,1024]{1,0:T(8,128)(2,1)} %collective-permute-done.5, bf16[128,1024]{1,0:T(8,128)(2,1)S(1)} %get-tuple-element.18), kind=kLoop, calls=%fused_computation.45 | loop fusion | flops 917504 | bytes 1315328 | tf_op jit(solution)/shard_map/convert_element_type | solution.py:191
  (38 shorter events, 1.0 us)
Async XLA Ops:
  0.0 86.1 %copy-start = (bf16[1,1024,1024]{2,1,0:T(8,128)(2,1)S(1)}, bf16[1,1024,1024]{2,1,0:T(8,128)(2,1)}, u32[]{:S(2)}) copy-start(bf16[1,1024,1024]{2,1,0:T(8,128)(2,1)} %param.21) | copy-start | bytes 6291460
  0.0 35.3 %copy-start.1 = (bf16[1024,512]{1,0:T(8,128)(2,1)S(1)}, bf16[1024,512]{1,0:T(8,128)(2,1)}, u32[]{:S(2)}) copy-start(bf16[1024,512]{1,0:T(8,128)(2,1)} %param.18) | copy-start | bytes 3145732
  0.0 35.3 %collective-permute-start = (bf16[128,1024]{1,0:T(8,128)(2,1)}, bf16[128,1024]{1,0:T(8,128)(2,1)}, u32[]{:S(2)}, u32[]{:S(2)}) collective-permute-start(bf16[128,1024]{1,0:T(8,128)(2,1)} %param.16), channel_id=1, source_target_pairs={{0,16},{16,0},{1,17},{17,1},{2,18},{18,2},{3,19},{19,3},{4,20},{20... | collective-permute-start | bytes 786440 | tf_op jit(solution)/shard_map/ppermute | solution.py:56
  4.8 42.0 %collective-permute-start.3 = (bf16[256,1024]{1,0:T(8,128)(2,1)}, bf16[256,1024]{1,0:T(8,128)(2,1)}, u32[]{:S(2)}, u32[]{:S(2)}) collective-permute-start(bf16[256,1024]{1,0:T(8,128)(2,1)} %pad_maximum_fusion.1), channel_id=1, source_target_pairs={{0,8},{8,0},{1,9},{9,1},{2,10},{10,2},{3,11},{11,3},{4,12},{12,4},... | collective-permute-start | bytes 1572872 | tf_op jit(solution)/shard_map/ppermute | solution.py:49
  15.2 16.1 %collective-permute-start.2 = (bf16[8,1024]{1,0:T(8,128)(2,1)}, bf16[8,1024]{1,0:T(8,128)(2,1)S(1)}, u32[]{:S(2)}, u32[]{:S(2)}) collective-permute-start(bf16[8,1024]{1,0:T(8,128)(2,1)} %reshape.66), channel_id=1, source_target_pairs={{0,8},{8,0},{1,9},{9,1},{2,10},{10,2},{3,11},{11,3},{4,12},{12,4},... | collective-permute-start | bytes 49160 | tf_op jit(solution)/shard_map/ppermute | solution.py:130
  15.5 15.7 %copy-start.3 = (f32[128,40]{0,1:T(8,128)}, f32[128,40]{0,1:T(8,128)S(1)}, u32[]{:S(2)}) copy-start(f32[128,40]{0,1:T(8,128)S(1)} %convert_element_type.103) | copy-start | bytes 61444
  36.6 8.9 %collective-permute-start.1 = (f32[128,512]{1,0:T(8,128)S(1)}, f32[128,512]{1,0:T(8,128)S(1)}, u32[]{:S(2)}, u32[]{:S(2)}) collective-permute-start(f32[128,512]{1,0:T(8,128)S(1)} %fusion.66), channel_id=1, source_target_pairs={{0,16},{8,24},{16,0},{24,8},{1,17},{9,25},{17,1},{25,9},{2,18},{10... | collective-permute-start | bytes 786440 | tf_op jit(solution)/shard_map/ppermute | solution.py:67
  38.2 14.7 %collective-permute-start.4 = (f32[128,512]{1,0:T(8,128)S(1)}, f32[128,512]{1,0:T(8,128)S(1)}, u32[]{:S(2)}, u32[]{:S(2)}) collective-permute-start(f32[128,512]{1,0:T(8,128)S(1)} %fusion.66), channel_id=1, source_target_pairs={{0,24},{8,16},{16,8},{24,0},{1,25},{9,17},{17,9},{25,1},{2,26},{10... | collective-permute-start | bytes 786440 | tf_op jit(solution)/shard_map/ppermute | solution.py:67
  46.8 7.4 %copy-start.5 = (f32[1024]{0:T(1024)S(1)}, f32[1024]{0:T(1024)}, u32[]{:S(2)}) copy-start(f32[1024]{0:T(1024)} %param.19) | copy-start | bytes 12292
  86.1 2.4 %copy-start.7 = (bf16[1,512,1024]{2,1,0:T(8,128)(2,1)S(1)}, bf16[1,512,1024]{2,1,0:T(8,128)(2,1)}, u32[]{:S(2)}) copy-start(bf16[1,512,1024]{2,1,0:T(8,128)(2,1)} %param.22) | copy-start | bytes 3145732
  90.9 23.3 %copy-start.2 = (f32[128,8]{1,0:T(8,128)S(1)}, f32[128,8]{1,0:T(8,128)}, u32[]{:S(2)}) copy-start(f32[128,8]{1,0:T(8,128)} %get-tuple-element.30) | copy-start | bytes 12292
  110.5 10.4 %copy-start.4 = (f32[128,40]{0,1:T(8,128)S(1)}, f32[128,40]{0,1:T(8,128)}, u32[]{:S(2)}) copy-start(f32[128,40]{0,1:T(8,128)} %copy-done.3) | copy-start | bytes 61444
  110.5 25.5 %all-to-all-start.1 = ((bf16[16,32,1024]{2,1,0:T(8,128)(2,1)}), bf16[16,32,1024]{2,1,0:T(8,128)(2,1)S(1)}, u32[]{:S(2)}, u32[]{:S(2)}) async-start(bf16[16,32,1024]{2,1,0:T(8,128)(2,1)} %get-tuple-element.25), calls=%async_computation.1 | async-start | bytes 2097152 | tf_op jit(solution)/shard_map/all_to_all | solution.py:174
  115.1 22.7 %copy-start.6 = (f32[1024]{0:T(1024)S(1)}, f32[1024]{0:T(1024)}, u32[]{:S(2)}) copy-start(f32[1024]{0:T(1024)} %param.20) | copy-start | bytes 12292
  117.7 18.3 %collective-permute-start.5 = (bf16[128,1024]{1,0:T(8,128)(2,1)}, bf16[128,1024]{1,0:T(8,128)(2,1)}, u32[]{:S(2)}, u32[]{:S(2)}) collective-permute-start(bf16[128,1024]{1,0:T(8,128)(2,1)} %convolution_convert_fusion.3), channel_id=1, source_target_pairs={{8,0},{0,8},{9,1},{1,9},{10,2},{2,10},{11,3},{3,11},{12,4},{4,12},... | collective-permute-start | bytes 786440 | tf_op jit(solution)/shard_map/ppermute | solution.py:186

commit v12 on v8

--- a/solution.py
+++ b/solution.py
@@ -124,9 +124,10 @@
         lax.ppermute(packed, "eh", [(i, (i + shift) % planes) for i in range(planes)])
         for shift in range(1, planes)
     ]
-    partials = []
+    hits = []
+    weights_in = []
+    buffers = []
     for shift, block in enumerate(received):
-        normed_s = block[:rows_here]
         meta_s = (
             block[rows_here:]
             .reshape(-1)[:meta_size]
@@ -135,36 +136,33 @@
         )
         code_s = meta_s[:, :picks_row] * 128 + meta_s[:, picks_row : 2 * picks_row]
         local = code_s.astype(jnp.int32) - my_plane * plane_slots
-        weights_s = (
-            meta_s[:, 2 * picks_row : 3 * picks_row] + meta_s[:, 3 * picks_row : 4 * picks_row]
-        ) + meta_s[:, 4 * picks_row :]
+        weights_in.append(
+            (meta_s[:, 2 * picks_row : 3 * picks_row] + meta_s[:, 3 * picks_row : 4 * picks_row])
+            + meta_s[:, 4 * picks_row :]
+        )
         hit = local[None, :, :] == slot_ids[:, None, None]
+        hits.append(hit)
         dispatch = jnp.any(hit, axis=2).astype(jnp.bfloat16)
-        buffer = jnp.dot(dispatch, normed_s, preferred_element_type=jnp.float32).astype(
-            jnp.bfloat16
-        )
-        arrived = lax.all_to_all(
-            buffer.reshape(groups * lanes, cap_size, features),
-            PLANE_AXES,
-            split_axis=0,
-            concat_axis=0,
-            tiled=True,
-        )
-        produced = expert(arrived.reshape(-1, features))
-        returned = lax.all_to_all(
-            produced.reshape(arrived.shape), PLANE_AXES, split_axis=0, concat_axis=0, tiled=True
-        )
-        combine = jnp.sum(jnp.where(hit, weights_s[None, :, :], 0.0), axis=2)
+        buffer = jnp.dot(dispatch, block[:rows_here], preferred_element_type=jnp.float32)
+        buffers.append(buffer.astype(jnp.bfloat16).reshape(groups * lanes, cap_size, features))
+    arrived = lax.all_to_all(
+        jnp.stack(buffers, axis=1), PLANE_AXES, split_axis=0, concat_axis=0, tiled=True
+    )
+    produced = expert(arrived.reshape(-1, features)).reshape(arrived.shape)
+    returned_all = lax.all_to_all(produced, PLANE_AXES, split_axis=0, concat_axis=0, tiled=True)
+    partials = [None] * planes
+    for shift in list(range(1, planes)) + [0]:
+        combine = jnp.sum(jnp.where(hits[shift], weights_in[shift][None, :, :], 0.0), axis=2)
         partial = jnp.dot(
             combine.T,
-            returned.reshape(plane_slots, features).astype(jnp.float32),
+            returned_all[:, shift].reshape(plane_slots, features).astype(jnp.float32),
             precision=lax.Precision.HIGHEST,
             preferred_element_type=jnp.float32,
         )
         if shift:
             back = [((i + shift) % planes, i) for i in range(planes)]
             partial = lax.ppermute(partial.astype(jnp.bfloat16), "eh", back).astype(jnp.float32)
-        partials.append(partial)
+        partials[shift] = partial
     mixture = partials[0]
     for partial in partials[1:]:
         mixture = mixture + partial

time: 131 us -> 126 us (0.962)
  blocking collectives: 0 us -> 30.2 us
  waiting for transfers between devices: 65.3 us -> 50.1 us
  starting transfers between devices: 24.6 us -> 15 us
  matrix products: 18.7 us -> 10.1 us
  other arithmetic: 13.2 us -> 11.7 us
    all_to_all x0 -> x1, blocking collectives: none -> 30.2 us  [on_device(): lax.all_to_all(jnp.stack(buffers, axis=1), PLANE_AXES, split_axis=0, conc...]
    all_to_all x4 -> x1, waiting for transfers between devices: 52.2 us -> 27.9 us  [on_device(): lax.all_to_all(produced, PLANE_AXES, split_axis=0, concat_axis=0, tiled=T...]
    all_to_all x4 -> x1, starting transfers between devices: 15.3 us -> 4.42 us  [on_device(): lax.all_to_all(produced, PLANE_AXES, split_axis=0, concat_axis=0, tiled=T...]
    ppermute x1, waiting for transfers between devices: 0.01 us -> 9.07 us  [on_device(): lax.ppermute(partial.astype(jnp.bfloat16), 'eh', back).astype(jnp.float32)]
    dot_general x4, matrix products: 7.22 us -> 2.3 us  [the longest x2 1.45 us: on_device(): jnp.dot(combine.T, returned_all[:, shift].reshape(plane_slots, features)....]
    dot_general x2 -> x1, matrix products: 5.12 us -> 2.35 us  [expert(): jnp.dot(rows_in, gate_up_local, preferred_element_type=jnp.float32)]
    unnamed x22 -> x16, local copies, waits for them, and re-layouts: 2.18 us -> 0.15 us
    slice x0 -> x1, local copies, waits for them, and re-layouts: none -> 1.71 us  [on_device(): returned_all[:, shift].reshape(plane_slots, features).astype(jnp.float32)]
  transfers between devices with their start and end apart: 8 -> 5, of which waited for: 6 -> 4; matrix products, arithmetic and copies ran while one was open for 18% -> 8% of each run, Pallas kernels for 0% -> 0%
where the time goes in v12:
time: 126 us; the launch traced here: 125 us
  waiting for transfers between devices  50.1 us (40%)
  blocking collectives  30.2 us (24%)
  starting transfers between devices  15 us (12%)
  other arithmetic  11.7 us (9%)
  matrix products  10.1 us (8%)
  between operations  4.02 us (3%)
  local copies, waits for them, and re-layouts  3.62 us (3%)
    all_to_all x1, blocking collectives, on_device(): lax.all_to_all(jnp.stack(buffers, axis=1), PLANE_AXES, split_axis=0, conc...  30.2 us
    all_to_all x1, waiting for transfers between devices, on_device(): lax.all_to_all(produced, PLANE_AXES, split_axis=0, concat_axis=0, tiled=T...  27.9 us
    ppermute x1, waiting for transfers between devices, on_device(): lax.ppermute(packed, 'eh', [(i, (i + shift) % planes) for i in range(plan...  11.5 us
    ppermute x1, waiting for transfers between devices, on_device(): lax.ppermute(partial.astype(jnp.bfloat16), 'eh', back).astype(jnp.float32)  9.07 us
    all_to_all x1, starting transfers between devices, on_device(): lax.all_to_all(produced, PLANE_AXES, split_axis=0, concat_axis=0, tiled=T...  4.42 us
    ppermute x1, starting transfers between devices, on_device(): lax.ppermute(partial.astype(jnp.bfloat16), 'eh', back).astype(jnp.float32)  3.43 us
    ppermute x1, starting transfers between devices, on_device(): visiting = lax.ppermute(attention, 'grp', ahead)  3.04 us
    ppermute x1, starting transfers between devices, on_device(): lax.ppermute(packed, 'eh', [(i, (i + shift) % planes) for i in range(plan...  2.65 us
  transfers between devices with their start and end apart: 5, of which 4 were waited for; matrix products, arithmetic and copies ran while one was open for 8% of the time, Pallas kernels for 0%

profile of v12, /device:TPU:0, one launch (start us, length us, event | category | flops | bytes accessed | tf_op | source)
XLA Modules:
  0.0 124.7 jit_solution(14391999557899971526)
XLA Ops:
  0.0 3.0 %collective-permute-start = (bf16[128,1024]{1,0:T(8,128)(2,1)}, bf16[128,1024]{1,0:T(8,128)(2,1)}, u32[]{:S(2)}, u32[]{:S(2)}) collective-permute-start(bf16[128,1024]{1,0:T(8,128)(2,1)} %param.16), channel_id=1, source_target_pairs={{0,16},{16,0},{1,17},{17,1},{2,18},{18,2},{3,19},{19,3},{4,20},{20... | collective-permute-start | bytes 786440 | tf_op jit(solution)/shard_map/ppermute | solution.py:52
  3.0 0.8 select_reduce_fusion.5
  3.8 0.8 select_reduce_fusion.4
  4.6 0.7 multiply_add_fusion
  5.3 0.7 multiply_add_fusion.1
  6.0 0.2 fusion.23
  6.2 0.8 broadcast_in_dim.88
  7.0 0.1 select_reduce_fusion.2
  7.1 0.7 constant_dynamic-update-slice_fusion.4
  7.8 0.7 constant_dynamic-update-slice_fusion.2
  8.5 0.7 constant_dynamic-update-slice_fusion.1
  9.2 0.7 constant_dynamic-update-slice_fusion
  9.9 0.0 collective-permute-done
  9.9 2.3 %fusion.50 = f32[128,512]{1,0:T(8,128)} fusion(bf16[128,1024]{1,0:T(8,128)(2,1)} %collective-permute-done, bf16[1024,512]{1,0:T(8,128)(2,1)} %param.18), kind=kOutput, calls=%fused_computation.113 | convolution fusion | flops 134217728 | bytes 1572864 | tf_op jit(solution)/shard_map/dot_general | solution.py:53
  12.3 1.5 %collective-permute-start.1 = (f32[128,512]{1,0:T(8,128)}, f32[128,512]{1,0:T(8,128)}, u32[]{:S(2)}, u32[]{:S(2)}) collective-permute-start(f32[128,512]{1,0:T(8,128)} %fusion.50), channel_id=1, source_target_pairs={{16,0},{0,16},{17,1},{1,17},{18,2},{2,18},{19,3},{3,19},{20,4},{4,... | collective-permute-start | bytes 786440 | tf_op jit(solution)/shard_map/ppermute | solution.py:54
  13.7 0.6 fusion.49
  18.1 0.1 copy.49
  18.2 0.1 reshape.51
  18.4 0.0 copy-start.3
  18.4 0.3 convolution_bitcast_fusion
  18.8 1.6 %collective-permute-done.1 = f32[128,512]{1,0:T(8,128)} collective-permute-done((f32[128,512]{1,0:T(8,128)}, f32[128,512]{1,0:T(8,128)}, u32[]{:S(2)}, u32[]{:S(2)}) %collective-permute-start.1) | collective-permute-done | bytes 262176 | tf_op jit(solution)/shard_map/ppermute | solution.py:54
  20.4 1.1 fusion.17
  21.4 0.2 fusion.8
  21.6 0.1 fusion.10
  21.8 2.7 %collective-permute-start.2 = (bf16[136,1024]{1,0:T(8,128)(2,1)S(1)}, bf16[136,1024]{1,0:T(8,128)(2,1)S(1)}, u32[]{:S(2)}, u32[]{:S(2)}) collective-permute-start(bf16[136,1024]{1,0:T(8,128)(2,1)S(1)} %pad_maximum_fusion.1), channel_id=1, source_target_pairs={{0,8},{8,0},{1,9},{9,1},{2,10},{10,2},{3,11},{11,3},{4,12},{12,4},... | collective-permute-start | bytes 835592 | tf_op jit(solution)/shard_map/ppermute | solution.py:124
  24.4 11.5 %collective-permute-done.2 = bf16[136,1024]{1,0:T(8,128)(2,1)S(1)} collective-permute-done((bf16[136,1024]{1,0:T(8,128)(2,1)S(1)}, bf16[136,1024]{1,0:T(8,128)(2,1)S(1)}, u32[]{:S(2)}, u32[]{:S(2)}) %collective-permute-start.2) | collective-permute-done | bytes 278560 | tf_op jit(solution)/shard_map/ppermute | solution.py:124
  36.0 0.1 reshape.94
  36.1 0.1 slice_add_fusion
  36.3 0.1 copy.56
  36.3 0.9 fusion.4
  37.3 0.4 convolution_convert_fusion.2
  37.7 0.9 fusion.3
  38.6 0.4 convolution_convert_fusion.1
  39.0 0.2 pad_maximum_fusion
  39.2 30.2 %all_to_all.10 = bf16[16,2,32,1024]{3,2,1,0:T(8,128)(2,1)S(1)} all-to-all(bf16[16,2,32,1024]{3,2,1,0:T(8,128)(2,1)S(1)} %pad_maximum_fusion), channel_id=1, replica_groups=mesh['grp'=2,'eh'=2,'el'=8] {'grp','el'}, dimensions={0} | all-to-all | bytes 4194304 | tf_op jit(solution)/shard_map/all_to_all | solution.py:148
  69.4 2.4 %fusion.1 = f32[1024,1024]{1,0:T(8,128)S(1)} fusion(bf16[1024,1024]{1,0:T(8,128)(2,1)S(1)} %bitcast.43, bf16[1,1024,1024]{2,1,0:T(8,128)(2,1)S(1)} %copy-done), kind=kOutput, calls=%fused_computation.3 | convolution fusion | flops 2147483648 | bytes 8388608 | tf_op jit(solution)/shard_map/dot_general | solution.py:115
  71.8 2.6 %convolution_convert_fusion = bf16[1024,1024]{1,0:T(8,128)(2,1)} fusion(f32[1024,1024]{1,0:T(8,128)S(1)} %fusion.1, bf16[1,512,1024]{2,1,0:T(8,128)(2,1)S(1)} %copy-done.6), kind=kOutput, calls=%fused_computation.11 | convolution fusion | flops 1077936128 | bytes 7340032 | tf_op jit(solution)/shard_map/dot_general | solution.py:119
  74.4 4.4 %all-to-all-start.1 = ((bf16[16,2,32,1024]{3,2,1,0:T(8,128)(2,1)}), bf16[16,2,32,1024]{3,2,1,0:T(8,128)(2,1)}, u32[]{:S(2)}, u32[]{:S(2)}) async-start(bf16[16,2,32,1024]{3,2,1,0:T(8,128)(2,1)} %bitcast.42), calls=%async_computation.1 | async-start | bytes 4194304 | tf_op jit(solution)/shard_map/all_to_all | solution.py:152
  78.8 0.7 select_reduce_fusion
  79.6 27.9 %all-to-all-done.1 = bf16[16,2,32,1024]{3,2,1,0:T(8,128)(2,1)} async-done(((bf16[16,2,32,1024]{3,2,1,0:T(8,128)(2,1)}), bf16[16,2,32,1024]{3,2,1,0:T(8,128)(2,1)}, u32[]{:S(2)}, u32[]{:S(2)}) %all-to-all-start.1) | async-done | bytes 2097184 | tf_op jit(solution)/shard_map/all_to_all | solution.py:152
  107.5 1.7 %fusion.48 = (bf16[16,1,32,1024]{3,2,1,0:T(8,128)(2,1)S(1)}, bf16[16,1,32,1024]{3,2,1,0:T(8,128)(2,1)S(1)}) fusion(bf16[16,2,32,1024]{3,2,1,0:T(8,128)(2,1)} %all-to-all-done.1), kind=kLoop, calls=%fused_computation.111 | loop fusion | bytes 4194304 | tf_op jit(solution)/shard_map/slice | solution.py:158
  109.2 0.0 copy-start.5
  109.2 0.7 convolution_convert_fusion.3
  109.9 3.4 %collective-permute-start.3 = (bf16[128,1024]{1,0:T(8,128)(2,1)S(1)}, bf16[128,1024]{1,0:T(8,128)(2,1)S(1)}, u32[]{:S(2)}, u32[]{:S(2)}) collective-permute-start(bf16[128,1024]{1,0:T(8,128)(2,1)S(1)} %convolution_convert_fusion.3), channel_id=1, source_target_pairs={{8,0},{0,8},{9,1},{1,9},{10,2},{2,10},{11,3},{3,11},{12,4},{4,12},... | collective-permute-start | bytes 786440 | tf_op jit(solution)/shard_map/ppermute | solution.py:164
  113.3 0.7 select_reduce_fusion.1
  114.0 9.1 %collective-permute-done.3 = bf16[128,1024]{1,0:T(8,128)(2,1)S(1)} collective-permute-done((bf16[128,1024]{1,0:T(8,128)(2,1)S(1)}, bf16[128,1024]{1,0:T(8,128)(2,1)S(1)}, u32[]{:S(2)}, u32[]{:S(2)}) %collective-permute-start.3) | collective-permute-done | bytes 262176 | tf_op jit(solution)/shard_map/ppermute | solution.py:164
  123.1 0.8 multiply_reduce_fusion
  123.9 0.8 multiply_convert_fusion
  (27 shorter events, 0.3 us)
Async XLA Ops:
  0.0 69.4 %copy-start = (bf16[1,1024,1024]{2,1,0:T(8,128)(2,1)S(1)}, bf16[1,1024,1024]{2,1,0:T(8,128)(2,1)}, u32[]{:S(2)}) copy-start(bf16[1,1024,1024]{2,1,0:T(8,128)(2,1)} %param.21) | copy-start | bytes 6291460
  0.0 18.4 %copy-start.2 = (bf16[128,1024]{1,0:T(8,128)(2,1)S(1)}, bf16[128,1024]{1,0:T(8,128)(2,1)}, u32[]{:S(2)}) copy-start(bf16[128,1024]{1,0:T(8,128)(2,1)} %param.16) | copy-start | bytes 786436
  0.0 18.4 %copy-start.1 = (bf16[1024,512]{1,0:T(8,128)(2,1)S(1)}, bf16[1024,512]{1,0:T(8,128)(2,1)}, u32[]{:S(2)}) copy-start(bf16[1024,512]{1,0:T(8,128)(2,1)} %param.18) | copy-start | bytes 3145732
  0.0 9.9 %collective-permute-start = (bf16[128,1024]{1,0:T(8,128)(2,1)}, bf16[128,1024]{1,0:T(8,128)(2,1)}, u32[]{:S(2)}, u32[]{:S(2)}) collective-permute-start(bf16[128,1024]{1,0:T(8,128)(2,1)} %param.16), channel_id=1, source_target_pairs={{0,16},{16,0},{1,17},{17,1},{2,18},{18,2},{3,19},{19,3},{4,20},{20... | collective-permute-start | bytes 786440 | tf_op jit(solution)/shard_map/ppermute | solution.py:52
  12.3 9.3 %copy-start.4 = (f32[1024]{0:T(1024)S(1)}, f32[1024]{0:T(1024)}, u32[]{:S(2)}) copy-start(f32[1024]{0:T(1024)} %param.19) | copy-start | bytes 12292
  12.3 8.1 %collective-permute-start.1 = (f32[128,512]{1,0:T(8,128)}, f32[128,512]{1,0:T(8,128)}, u32[]{:S(2)}, u32[]{:S(2)}) collective-permute-start(f32[128,512]{1,0:T(8,128)} %fusion.50), channel_id=1, source_target_pairs={{16,0},{0,16},{17,1},{1,17},{18,2},{2,18},{19,3},{3,19},{20,4},{4,... | collective-permute-start | bytes 786440 | tf_op jit(solution)/shard_map/ppermute | solution.py:54
  18.4 3.0 %copy-start.3 = (bf16[128,1024]{1,0:T(8,128)(2,1)S(1)}, bf16[128,1024]{1,0:T(8,128)(2,1)}, u32[]{:S(2)}) copy-start(bf16[128,1024]{1,0:T(8,128)(2,1)} %param.17) | copy-start | bytes 786436
  21.8 14.2 %collective-permute-start.2 = (bf16[136,1024]{1,0:T(8,128)(2,1)S(1)}, bf16[136,1024]{1,0:T(8,128)(2,1)S(1)}, u32[]{:S(2)}, u32[]{:S(2)}) collective-permute-start(bf16[136,1024]{1,0:T(8,128)(2,1)S(1)} %pad_maximum_fusion.1), channel_id=1, source_target_pairs={{0,8},{8,0},{1,9},{9,1},{2,10},{10,2},{3,11},{11,3},{4,12},{12,4},... | collective-permute-start | bytes 835592 | tf_op jit(solution)/shard_map/ppermute | solution.py:124
  69.4 2.4 %copy-start.6 = (bf16[1,512,1024]{2,1,0:T(8,128)(2,1)S(1)}, bf16[1,512,1024]{2,1,0:T(8,128)(2,1)}, u32[]{:S(2)}) copy-start(bf16[1,512,1024]{2,1,0:T(8,128)(2,1)} %param.22) | copy-start | bytes 3145732
  74.4 33.1 %all-to-all-start.1 = ((bf16[16,2,32,1024]{3,2,1,0:T(8,128)(2,1)}), bf16[16,2,32,1024]{3,2,1,0:T(8,128)(2,1)}, u32[]{:S(2)}, u32[]{:S(2)}) async-start(bf16[16,2,32,1024]{3,2,1,0:T(8,128)(2,1)} %bitcast.42), calls=%async_computation.1 | async-start | bytes 4194304 | tf_op jit(solution)/shard_map/all_to_all | solution.py:152
  109.2 14.7 %copy-start.5 = (f32[1024]{0:T(1024)S(1)}, f32[1024]{0:T(1024)}, u32[]{:S(2)}) copy-start(f32[1024]{0:T(1024)} %param.20) | copy-start | bytes 12292
  109.9 13.2 %collective-permute-start.3 = (bf16[128,1024]{1,0:T(8,128)(2,1)S(1)}, bf16[128,1024]{1,0:T(8,128)(2,1)S(1)}, u32[]{:S(2)}, u32[]{:S(2)}) collective-permute-start(bf16[128,1024]{1,0:T(8,128)(2,1)S(1)} %convolution_convert_fusion.3), channel_id=1, source_target_pairs={{8,0},{0,8},{9,1},{1,9},{10,2},{2,10},{11,3},{3,11},{12,4},{4,12},... | collective-permute-start | bytes 786440 | tf_op jit(solution)/shard_map/ppermute | solution.py:164

commit v13 on v12

--- a/solution.py
+++ b/solution.py
@@ -52,14 +52,25 @@
         visiting = lax.ppermute(attention, "grp", ahead)
         done = jnp.dot(visiting, out_proj, preferred_element_type=jnp.float32)
         blocks[shift] = lax.ppermute(done, "grp", back)
-    stacked = jnp.stack(blocks, axis=0)
     order_cols = (jnp.arange(groups, dtype=jnp.int32) - me_grp) % groups
-    attn_proj = jnp.concatenate(
-        [jnp.take(stacked, order_cols[j], axis=0) for j in range(groups)], axis=1
-    )
-    hidden_state = (residual.astype(jnp.float32) + attn_proj).astype(jnp.bfloat16)
+    width = features // groups
+    residual_cols = residual.reshape(rows_here, groups, width)
+    hidden_blocks = [
+        (
+            jnp.take(residual_cols, (me_grp + t) % groups, axis=1).astype(jnp.float32)
+            + blocks[t]
+        ).astype(jnp.bfloat16)
+        for t in range(groups)
+    ]
+
+    def in_column_order(parts):
+        stacked = jnp.stack(parts, axis=0)
+        return jnp.concatenate(
+            [jnp.take(stacked, order_cols[j], axis=0) for j in range(groups)], axis=1
+        )
+
+    hidden_state = in_column_order(hidden_blocks)
     normed = rms_scale(hidden_state.astype(jnp.float32), pre_gain).astype(jnp.bfloat16)
-
     experts_all = placement.shape[0]
     slot_table = jnp.arange(owners, dtype=jnp.int32)
     matches = (placement[None, :] == jnp.arange(experts_all, dtype=jnp.int32)[:, None]).astype(
@@ -105,7 +116,22 @@
     meta_size = rows_here * meta.shape[1]
     meta_rows = -(-meta_size // (8 * features)) * 8
     meta_block = jnp.pad(meta.reshape(-1), (0, meta_rows * features - meta_size))
-    packed = jnp.concatenate([normed, meta_block.reshape(meta_rows, features)], axis=0)
+    meta_block = meta_block.reshape(-1, width)
+    normed_in = [normed]
+    meta_in = [meta_block]
+    for shift in range(1, planes):
+        ring = [(i, (i + shift) % planes) for i in range(planes)]
+        first = lax.ppermute(
+            jnp.concatenate([hidden_blocks[0], meta_block], axis=0), "eh", ring
+        )
+        rest = [first[:rows_here]] + [
+            lax.ppermute(hidden_blocks[t], "eh", ring) for t in range(1, groups)
+        ]
+        meta_in.append(first[rows_here:])
+        hidden_s = in_column_order(rest)
+        normed_in.append(
+            rms_scale(hidden_s.astype(jnp.float32), pre_gain).astype(jnp.bfloat16)
+        )
     gate_up_local = slot_gate_up[0]
     down_local = slot_down[0]
     hidden_units = down_local.shape[0]
@@ -120,16 +146,12 @@
             jnp.bfloat16
         )
 
-    received = [packed] + [
-        lax.ppermute(packed, "eh", [(i, (i + shift) % planes) for i in range(planes)])
-        for shift in range(1, planes)
-    ]
     hits = []
     weights_in = []
     buffers = []
-    for shift, block in enumerate(received):
+    for shift in range(planes):
         meta_s = (
-            block[rows_here:]
+            meta_in[shift]
             .reshape(-1)[:meta_size]
             .reshape(rows_here, meta.shape[1])
             .astype(jnp.float32)
@@ -143,7 +165,7 @@
         hit = local[None, :, :] == slot_ids[:, None, None]
         hits.append(hit)
         dispatch = jnp.any(hit, axis=2).astype(jnp.bfloat16)
-        buffer = jnp.dot(dispatch, block[:rows_here], preferred_element_type=jnp.float32)
+        buffer = jnp.dot(dispatch, normed_in[shift], preferred_element_type=jnp.float32)
         buffers.append(buffer.astype(jnp.bfloat16).reshape(groups * lanes, cap_size, features))
     arrived = lax.all_to_all(
         jnp.stack(buffers, axis=1), PLANE_AXES, split_axis=0, concat_axis=0, tiled=True

time: 126 us -> 135 us (1.071)
  local copies, waits for them, and re-layouts: 3.62 us -> 10.3 us
  other arithmetic: 11.7 us -> 14.2 us
  starting transfers between devices: 15 us -> 12.6 us
    unnamed x16 -> x23, local copies, waits for them, and re-layouts: 0.15 us -> 4.38 us
    ppermute x1, waiting for transfers between devices: 1.6 us -> 4.8 us  [on_device(): blocks[shift] = lax.ppermute(done, 'grp', back)]
    ppermute x1 -> x2, waiting for transfers between devices: 11.5 us -> 8.57 us  [the longest x1 7.86 us: on_device(): lax.ppermute(hidden_blocks[t], 'eh', ring)]
    convert_element_type x3, other arithmetic: 0.14 us -> 2.07 us  [the longest x2 2.04 us: on_device(): meta_s = meta_in[shift].reshape(-1)[:meta_size].reshape(rows_here, meta.s...]
    ppermute x1, starting transfers between devices: 3.43 us -> 1.76 us  [on_device(): lax.ppermute(partial.astype(jnp.bfloat16), 'eh', back).astype(jnp.float32)]
    another operation x0 -> x2, local copies, waits for them, and re-layouts: none -> 1.59 us  [the longest x1 0.91 us: in_column_order(): stacked = jnp.stack(parts, axis=0)]
  transfers between devices with their start and end apart: 5 -> 6, of which waited for: 4 -> 5; matrix products, arithmetic and copies ran while one was open for 8% -> 18% of each run, Pallas kernels for 0% -> 0%
where the time goes in v13:
time: 135 us; the launch traced here: 133 us
  waiting for transfers between devices  51.2 us (38%)
  blocking collectives  30.2 us (22%)
  other arithmetic  14.2 us (11%)
  starting transfers between devices  12.6 us (9%)
  matrix products  10.5 us (8%)
  local copies, waits for them, and re-layouts  10.3 us (8%)
  between operations  4.26 us (3%)
    all_to_all x1, blocking collectives, on_device(): lax.all_to_all(jnp.stack(buffers, axis=1), PLANE_AXES, split_axis=0, conc...  30.2 us
    all_to_all x1, waiting for transfers between devices, on_device(): lax.all_to_all(produced, PLANE_AXES, split_axis=0, concat_axis=0, tiled=T...  27.8 us
    ppermute x1, waiting for transfers between devices, on_device(): lax.ppermute(partial.astype(jnp.bfloat16), 'eh', back).astype(jnp.float32)  10 us
    ppermute x1, waiting for transfers between devices, on_device(): lax.ppermute(hidden_blocks[t], 'eh', ring)  7.86 us
    ppermute x1, waiting for transfers between devices, on_device(): blocks[shift] = lax.ppermute(done, 'grp', back)  4.8 us
    all_to_all x1, starting transfers between devices, on_device(): lax.all_to_all(produced, PLANE_AXES, split_axis=0, concat_axis=0, tiled=T...  4.56 us
    unnamed x23, local copies, waits for them, and re-layouts  4.38 us
    ppermute x1, starting transfers between devices, on_device(): visiting = lax.ppermute(attention, 'grp', ahead)  2.97 us
  transfers between devices with their start and end apart: 6, of which 5 were waited for; matrix products, arithmetic and copies ran while one was open for 18% of the time, Pallas kernels for 0%

profile of v13, /device:TPU:0, one launch (start us, length us, event | category | flops | bytes accessed | tf_op | source)
XLA Modules:
  0.0 133.3 jit_solution(1335775139922107097)
XLA Ops:
  0.0 3.0 %collective-permute-start = (bf16[128,1024]{1,0:T(8,128)(2,1)}, bf16[128,1024]{1,0:T(8,128)(2,1)}, u32[]{:S(2)}, u32[]{:S(2)}) collective-permute-start(bf16[128,1024]{1,0:T(8,128)(2,1)} %param.18), channel_id=1, source_target_pairs={{0,16},{16,0},{1,17},{17,1},{2,18},{18,2},{3,19},{19,3},{4,20},{20... | collective-permute-start | bytes 786440 | tf_op jit(solution)/shard_map/ppermute | solution.py:52
  3.0 1.1 copy.58
  4.1 0.7 constant_dynamic-slice_fusion
  4.8 1.0 copy.67
  5.8 0.8 select_reduce_fusion.5
  6.6 0.8 select_reduce_fusion.4
  7.4 0.7 multiply_add_fusion
  8.1 0.7 multiply_add_fusion.1
  8.7 0.2 fusion.37
  9.0 0.8 broadcast_in_dim.99
  9.9 0.7 constant_dynamic-update-slice_fusion.4
  10.6 0.7 constant_dynamic-update-slice_fusion.2
  11.3 0.7 constant_dynamic-update-slice_fusion.1
  12.0 0.7 constant_dynamic-update-slice_fusion
  13.0 0.3 copy-done.5
  13.3 1.6 %fusion.5 = bf16[128,512]{1,0:T(8,128)(2,1)S(1)} fusion(bf16[128,1024]{1,0:T(8,128)(2,1)} %param.18, bf16[1024,512]{1,0:T(8,128)(2,1)} %param.20, bf16[128,1,512]{2,0,1:T(8,128)(2,1)S(1)} %copy.67, pred[]{:T(512)S(6)} %and.61), kind=kOutput, calls=%fused_computation.16 | convolution fusion | flops 134479872 | bytes 1572865 | tf_op jit(solution)/shard_map/dot_general | solution.py:48
  14.9 0.7 pad_maximum_fusion.4
  15.6 2.6 %collective-permute-start.2 = (bf16[144,512]{1,0:T(8,128)(2,1)}, bf16[144,512]{1,0:T(8,128)(2,1)}, u32[]{:S(2)}, u32[]{:S(2)}) collective-permute-start(bf16[144,512]{1,0:T(8,128)(2,1)} %pad_maximum_fusion.4), channel_id=1, source_target_pairs={{0,8},{8,0},{1,9},{9,1},{2,10},{10,2},{3,11},{11,3},{4,12},{12,4},... | collective-permute-start | bytes 442376 | tf_op jit(solution)/shard_map/ppermute | solution.py:124
  18.2 0.7 convert_element_type.105
  18.9 0.7 fusion.63
  23.7 0.9 fusion.4
  24.6 0.7 collective-permute-done.2
  25.3 1.3 %slice_convert_fusion = f32[10,512]{1,0:T(8,128)} fusion(bf16[144,512]{1,0:T(8,128)(2,1)} %collective-permute-done.2), kind=kLoop, calls=%fused_computation.76 | loop fusion | flops 5120 | bytes 30720 | tf_op jit(solution)/shard_map/convert_element_type | solution.py:157
  26.6 0.8 reshape.168
  27.5 0.8 slice_add_fusion
  28.2 0.9 copy.69
  29.1 0.9 copy.70
  30.1 1.3 fusion.64
  31.3 0.7 collective-permute-start.1
  32.0 0.9 fusion.3
  32.9 0.9 slice_bitcast_fusion
  33.8 4.8 %collective-permute-done.1 = f32[128,512]{1,0:T(8,128)S(1)} collective-permute-done((f32[128,512]{1,0:T(8,128)S(1)}, f32[128,512]{1,0:T(8,128)S(1)}, u32[]{:S(2)}, u32[]{:S(2)}) %collective-permute-start.1) | collective-permute-done | bytes 262176 | tf_op jit(solution)/shard_map/ppermute | solution.py:54
  39.0 0.5 convolution_convert_fusion.2
  39.5 7.9 %collective-permute-done.3 = bf16[128,512]{1,0:T(8,128)(2,1)S(1)} collective-permute-done((bf16[128,512]{1,0:T(8,128)(2,1)S(1)}, bf16[128,512]{1,0:T(8,128)(2,1)S(1)}, u32[]{:S(2)}, u32[]{:S(2)}) %collective-permute-start.3) | collective-permute-done | bytes 131104 | tf_op jit(solution)/shard_map/ppermute | solution.py:128
  47.6 0.5 convolution_convert_fusion.1
  48.4 30.2 %all_to_all.10 = bf16[16,2,32,1024]{3,2,1,0:T(8,128)(2,1)S(1)} all-to-all(bf16[16,2,32,1024]{3,2,1,0:T(8,128)(2,1)S(1)} %pad_maximum_fusion), channel_id=1, replica_groups=mesh['grp'=2,'eh'=2,'el'=8] {'grp','el'}, dimensions={0} | all-to-all | bytes 4194304 | tf_op jit(solution)/shard_map/all_to_all | solution.py:170
  78.5 2.4 %fusion.1 = f32[1024,1024]{1,0:T(8,128)S(1)} fusion(bf16[1024,1024]{1,0:T(8,128)(2,1)S(1)} %bitcast.53, bf16[1,1024,1024]{2,1,0:T(8,128)(2,1)S(1)} %copy-done), kind=kOutput, calls=%fused_computation.3 | convolution fusion | flops 2147483648 | bytes 8388608 | tf_op jit(solution)/shard_map/dot_general | solution.py:141
  80.9 2.6 %convolution_convert_fusion = bf16[1024,1024]{1,0:T(8,128)(2,1)} fusion(f32[1024,1024]{1,0:T(8,128)S(1)} %fusion.1, bf16[1,512,1024]{2,1,0:T(8,128)(2,1)S(1)} %copy-done.8), kind=kOutput, calls=%fused_computation.11 | convolution fusion | flops 1077936128 | bytes 7340032 | tf_op jit(solution)/shard_map/dot_general | solution.py:145
  83.5 4.6 %all-to-all-start.1 = ((bf16[16,2,32,1024]{3,2,1,0:T(8,128)(2,1)}), bf16[16,2,32,1024]{3,2,1,0:T(8,128)(2,1)}, u32[]{:S(2)}, u32[]{:S(2)}) async-start(bf16[16,2,32,1024]{3,2,1,0:T(8,128)(2,1)} %bitcast.52), calls=%async_computation.1 | async-start | bytes 4194304 | tf_op jit(solution)/shard_map/all_to_all | solution.py:174
  88.1 0.7 select_reduce_fusion
  88.9 27.8 %all-to-all-done.1 = bf16[16,2,32,1024]{3,2,1,0:T(8,128)(2,1)} async-done(((bf16[16,2,32,1024]{3,2,1,0:T(8,128)(2,1)}), bf16[16,2,32,1024]{3,2,1,0:T(8,128)(2,1)}, u32[]{:S(2)}, u32[]{:S(2)}) %all-to-all-start.1) | async-done | bytes 2097184 | tf_op jit(solution)/shard_map/all_to_all | solution.py:174
  116.7 1.7 %fusion.62 = (bf16[16,1,32,1024]{3,2,1,0:T(8,128)(2,1)S(1)}, bf16[16,1,32,1024]{3,2,1,0:T(8,128)(2,1)S(1)}) fusion(bf16[16,2,32,1024]{3,2,1,0:T(8,128)(2,1)} %all-to-all-done.1), kind=kLoop, calls=%fused_computation.136 | loop fusion | bytes 4194304 | tf_op jit(solution)/shard_map/slice | solution.py:180
  118.5 0.7 convolution_convert_fusion.3
  119.1 1.8 %collective-permute-start.4 = (bf16[128,1024]{1,0:T(8,128)(2,1)S(1)}, bf16[128,1024]{1,0:T(8,128)(2,1)S(1)}, u32[]{:S(2)}, u32[]{:S(2)}) collective-permute-start(bf16[128,1024]{1,0:T(8,128)(2,1)S(1)} %convolution_convert_fusion.3), channel_id=1, source_target_pairs={{8,0},{0,8},{9,1},{1,9},{10,2},{2,10},{11,3},{3,11},{12,4},{4,12},... | collective-permute-start | bytes 786440 | tf_op jit(solution)/shard_map/ppermute | solution.py:186
  120.9 0.7 select_reduce_fusion.1
  121.6 10.0 %collective-permute-done.4 = bf16[128,1024]{1,0:T(8,128)(2,1)S(1)} collective-permute-done((bf16[128,1024]{1,0:T(8,128)(2,1)S(1)}, bf16[128,1024]{1,0:T(8,128)(2,1)S(1)}, u32[]{:S(2)}, u32[]{:S(2)}) %collective-permute-start.4) | collective-permute-done | bytes 262176 | tf_op jit(solution)/shard_map/ppermute | solution.py:186
  131.7 0.8 multiply_reduce_fusion
  132.5 0.8 multiply_convert_fusion
  (42 shorter events, 1.5 us)
Async XLA Ops:
  0.0 78.5 %copy-start = (bf16[1,1024,1024]{2,1,0:T(8,128)(2,1)S(1)}, bf16[1,1024,1024]{2,1,0:T(8,128)(2,1)}, u32[]{:S(2)}) copy-start(bf16[1,1024,1024]{2,1,0:T(8,128)(2,1)} %param.23) | copy-start | bytes 6291460
  0.0 30.0 %collective-permute-start = (bf16[128,1024]{1,0:T(8,128)(2,1)}, bf16[128,1024]{1,0:T(8,128)(2,1)}, u32[]{:S(2)}, u32[]{:S(2)}) collective-permute-start(bf16[128,1024]{1,0:T(8,128)(2,1)} %param.18), channel_id=1, source_target_pairs={{0,16},{16,0},{1,17},{17,1},{2,18},{18,2},{3,19},{19,3},{4,20},{20... | collective-permute-start | bytes 786440 | tf_op jit(solution)/shard_map/ppermute | solution.py:52
  4.1 26.0 %copy-start.1 = (bf16[1024,512]{1,0:T(8,128)(2,1)S(1)}, bf16[1024,512]{1,0:T(8,128)(2,1)}, u32[]{:S(2)}) copy-start(bf16[1024,512]{1,0:T(8,128)(2,1)} %param.20) | copy-start | bytes 3145732
  12.7 0.6 copy-start.5
  15.6 9.7 %collective-permute-start.2 = (bf16[144,512]{1,0:T(8,128)(2,1)}, bf16[144,512]{1,0:T(8,128)(2,1)}, u32[]{:S(2)}, u32[]{:S(2)}) collective-permute-start(bf16[144,512]{1,0:T(8,128)(2,1)} %pad_maximum_fusion.4), channel_id=1, source_target_pairs={{0,8},{8,0},{1,9},{9,1},{2,10},{10,2},{3,11},{11,3},{4,12},{12,4},... | collective-permute-start | bytes 442376 | tf_op jit(solution)/shard_map/ppermute | solution.py:124
  18.9 4.6 %copy-start.3 = (f32[128,40]{0,1:T(8,128)}, f32[128,40]{0,1:T(8,128)S(1)}, u32[]{:S(2)}) copy-start(f32[128,40]{0,1:T(8,128)S(1)} %convert_element_type.105) | copy-start | bytes 61444
  23.7 15.3 %copy-start.6 = (f32[1024]{0:T(1024)S(1)}, f32[1024]{0:T(1024)}, u32[]{:S(2)}) copy-start(f32[1024]{0:T(1024)} %param.21) | copy-start | bytes 12292
  31.3 7.3 %collective-permute-start.1 = (f32[128,512]{1,0:T(8,128)S(1)}, f32[128,512]{1,0:T(8,128)S(1)}, u32[]{:S(2)}, u32[]{:S(2)}) collective-permute-start(f32[128,512]{1,0:T(8,128)S(1)} %fusion.64), channel_id=1, source_target_pairs={{16,0},{0,16},{17,1},{1,17},{18,2},{2,18},{19,3},{3,19},{20,4},{4,... | collective-permute-start | bytes 786440 | tf_op jit(solution)/shard_map/ppermute | solution.py:54
  38.6 8.7 %collective-permute-start.3 = (bf16[128,512]{1,0:T(8,128)(2,1)S(1)}, bf16[128,512]{1,0:T(8,128)(2,1)S(1)}, u32[]{:S(2)}, u32[]{:S(2)}) collective-permute-start(bf16[128,512]{1,0:T(8,128)(2,1)S(1)} %add_convert_fusion), channel_id=1, source_target_pairs={{0,8},{8,0},{1,9},{9,1},{2,10},{10,2},{3,11},{11,3},{4,12},{12,4},... | collective-permute-start | bytes 393224 | tf_op jit(solution)/shard_map/ppermute | solution.py:128
  78.5 2.4 %copy-start.8 = (bf16[1,512,1024]{2,1,0:T(8,128)(2,1)S(1)}, bf16[1,512,1024]{2,1,0:T(8,128)(2,1)}, u32[]{:S(2)}) copy-start(bf16[1,512,1024]{2,1,0:T(8,128)(2,1)} %param.24) | copy-start | bytes 3145732
  83.5 4.6 %copy-start.2 = (f32[128,8]{1,0:T(8,128)S(1)}, f32[128,8]{1,0:T(8,128)}, u32[]{:S(2)}) copy-start(f32[128,8]{1,0:T(8,128)} %get-tuple-element.40) | copy-start | bytes 12292
  83.5 33.2 %all-to-all-start.1 = ((bf16[16,2,32,1024]{3,2,1,0:T(8,128)(2,1)}), bf16[16,2,32,1024]{3,2,1,0:T(8,128)(2,1)}, u32[]{:S(2)}, u32[]{:S(2)}) async-start(bf16[16,2,32,1024]{3,2,1,0:T(8,128)(2,1)} %bitcast.52), calls=%async_computation.1 | async-start | bytes 4194304 | tf_op jit(solution)/shard_map/all_to_all | solution.py:174
  88.9 32.0 %copy-start.4 = (f32[128,40]{0,1:T(8,128)S(1)}, f32[128,40]{0,1:T(8,128)}, u32[]{:S(2)}) copy-start(f32[128,40]{0,1:T(8,128)} %copy-done.3) | copy-start | bytes 61444
  118.5 14.0 %copy-start.7 = (f32[1024]{0:T(1024)S(1)}, f32[1024]{0:T(1024)}, u32[]{:S(2)}) copy-start(f32[1024]{0:T(1024)} %param.22) | copy-start | bytes 12292
  119.1 12.5 %collective-permute-start.4 = (bf16[128,1024]{1,0:T(8,128)(2,1)S(1)}, bf16[128,1024]{1,0:T(8,128)(2,1)S(1)}, u32[]{:S(2)}, u32[]{:S(2)}) collective-permute-start(bf16[128,1024]{1,0:T(8,128)(2,1)S(1)} %convolution_convert_fusion.3), channel_id=1, source_target_pairs={{8,0},{0,8},{9,1},{1,9},{10,2},{2,10},{11,3},{3,11},{12,4},{4,12},... | collective-permute-start | bytes 786440 | tf_op jit(solution)/shard_map/ppermute | solution.py:186

commit v14 on v12

--- a/solution.py
+++ b/solution.py
@@ -120,9 +120,9 @@
             jnp.bfloat16
         )
 
+    gathered = lax.all_gather(packed, "eh", axis=0)
     received = [packed] + [
-        lax.ppermute(packed, "eh", [(i, (i + shift) % planes) for i in range(planes)])
-        for shift in range(1, planes)
+        jnp.take(gathered, (my_plane - shift) % planes, axis=0) for shift in range(1, planes)
     ]
     hits = []
     weights_in = []

time: 126 us -> 126 us (level)
  blocking collectives: 30.2 us -> 45 us
  waiting for transfers between devices: 50.1 us -> 38.5 us
  starting transfers between devices: 15 us -> 12.4 us
    all_gather x0 -> x1, blocking collectives: none -> 14.8 us  [on_device(): gathered = lax.all_gather(packed, 'eh', axis=0)]
    ppermute x1 -> x0, waiting for transfers between devices: 11.5 us -> none  [on_device(): lax.ppermute(packed, 'eh', [(i, (i + shift) % planes) for i in range(plan...]
    ppermute x1 -> x0, starting transfers between devices: 2.65 us -> none  [on_device(): lax.ppermute(packed, 'eh', [(i, (i + shift) % planes) for i in range(plan...]
  transfers between devices with their start and end apart: 5 -> 4, of which waited for: 4 -> 3; matrix products, arithmetic and copies ran while one was open for 8% -> 8% of each run, Pallas kernels for 0% -> 0%
where the time goes in v14:
time: 126 us; the launch traced here: 125 us
  blocking collectives  45 us (36%)
  waiting for transfers between devices  38.5 us (31%)
  starting transfers between devices  12.4 us (10%)
  other arithmetic  11.8 us (9%)
  matrix products  10.1 us (8%)
  between operations  4.07 us (3%)
  local copies, waits for them, and re-layouts  3.61 us (3%)
    all_to_all x1, blocking collectives, on_device(): lax.all_to_all(jnp.stack(buffers, axis=1), PLANE_AXES, split_axis=0, conc...  30.2 us
    all_to_all x1, waiting for transfers between devices, on_device(): lax.all_to_all(produced, PLANE_AXES, split_axis=0, concat_axis=0, tiled=T...  27.9 us
    all_gather x1, blocking collectives, on_device(): gathered = lax.all_gather(packed, 'eh', axis=0)  14.8 us
    ppermute x1, waiting for transfers between devices, on_device(): lax.ppermute(partial.astype(jnp.bfloat16), 'eh', back).astype(jnp.float32)  9.06 us
    all_to_all x1, starting transfers between devices, on_device(): lax.all_to_all(produced, PLANE_AXES, split_axis=0, concat_axis=0, tiled=T...  4.42 us
    ppermute x1, starting transfers between devices, on_device(): lax.ppermute(partial.astype(jnp.bfloat16), 'eh', back).astype(jnp.float32)  3.46 us
    ppermute x1, starting transfers between devices, on_device(): visiting = lax.ppermute(attention, 'grp', ahead)  3.04 us
    dot_general x1, matrix products, expert(): jnp.dot(expert_hidden, down_local, preferred_element_type=jnp.float32)  2.59 us
  transfers between devices with their start and end apart: 4, of which 3 were waited for; matrix products, arithmetic and copies ran while one was open for 8% of the time, Pallas kernels for 0%

profile of v14, /device:TPU:0, one launch (start us, length us, event | category | flops | bytes accessed | tf_op | source)
XLA Modules:
  0.0 125.4 jit_solution(18308495623665499165)
XLA Ops:
  0.0 3.0 %collective-permute-start = (bf16[128,1024]{1,0:T(8,128)(2,1)}, bf16[128,1024]{1,0:T(8,128)(2,1)}, u32[]{:S(2)}, u32[]{:S(2)}) collective-permute-start(bf16[128,1024]{1,0:T(8,128)(2,1)} %param.16), channel_id=1, source_target_pairs={{0,16},{16,0},{1,17},{17,1},{2,18},{18,2},{3,19},{19,3},{4,20},{20... | collective-permute-start | bytes 786440 | tf_op jit(solution)/shard_map/ppermute | solution.py:52
  3.0 0.8 select_reduce_fusion.5
  3.8 0.8 select_reduce_fusion.4
  4.6 0.7 multiply_add_fusion
  5.3 0.7 multiply_add_fusion.1
  6.0 0.2 fusion.22
  6.2 0.8 broadcast_in_dim.100
  7.0 0.1 select_reduce_fusion.2
  7.1 0.7 constant_dynamic-update-slice_fusion.4
  7.8 0.7 constant_dynamic-update-slice_fusion.2
  8.5 0.7 constant_dynamic-update-slice_fusion.1
  9.2 0.7 constant_dynamic-update-slice_fusion
  9.9 0.0 collective-permute-done
  9.9 2.3 %fusion.49 = f32[128,512]{1,0:T(8,128)} fusion(bf16[128,1024]{1,0:T(8,128)(2,1)} %collective-permute-done, bf16[1024,512]{1,0:T(8,128)(2,1)} %param.18), kind=kOutput, calls=%fused_computation.114 | convolution fusion | flops 134217728 | bytes 1572864 | tf_op jit(solution)/shard_map/dot_general | solution.py:53
  12.3 1.5 %collective-permute-start.1 = (f32[128,512]{1,0:T(8,128)}, f32[128,512]{1,0:T(8,128)}, u32[]{:S(2)}, u32[]{:S(2)}) collective-permute-start(f32[128,512]{1,0:T(8,128)} %fusion.49), channel_id=1, source_target_pairs={{16,0},{0,16},{17,1},{1,17},{18,2},{2,18},{19,3},{3,19},{20,4},{4,... | collective-permute-start | bytes 786440 | tf_op jit(solution)/shard_map/ppermute | solution.py:54
  13.7 0.6 fusion.48
  18.2 0.1 copy.48
  18.3 0.1 reshape.52
  18.5 0.0 copy-start.3
  18.5 0.3 convolution_bitcast_fusion
  18.8 1.6 %collective-permute-done.1 = f32[128,512]{1,0:T(8,128)} collective-permute-done((f32[128,512]{1,0:T(8,128)}, f32[128,512]{1,0:T(8,128)}, u32[]{:S(2)}, u32[]{:S(2)}) %collective-permute-start.1) | collective-permute-done | bytes 262176 | tf_op jit(solution)/shard_map/ppermute | solution.py:54
  20.4 1.1 fusion.17
  21.4 0.0 copy-done.3
  21.4 0.2 fusion.8
  21.6 0.1 fusion.10
  21.8 14.8 %all-gather = bf16[272,1024]{1,0:T(8,128)(2,1)S(1)} all-gather(bf16[136,1024]{1,0:T(8,128)(2,1)S(1)} %pad_maximum_fusion.1), channel_id=2, replica_groups=mesh['grp'=2,'eh'=2,'el'=8] {'eh'}, dimensions={0}, use_global_device_ids=true | all-gather | bytes 835584 | tf_op jit(solution)/shard_map/all_gather | solution.py:123
  36.6 0.1 reshape.124
  36.7 0.1 slice_add_fusion
  36.9 0.1 copy.55
  37.0 0.9 fusion.4
  37.9 0.4 convolution_convert_fusion.2
  38.3 0.9 fusion.3
  39.2 0.4 convolution_convert_fusion.1
  39.6 0.2 pad_maximum_fusion
  39.8 30.2 %all_to_all.10 = bf16[16,2,32,1024]{3,2,1,0:T(8,128)(2,1)S(1)} all-to-all(bf16[16,2,32,1024]{3,2,1,0:T(8,128)(2,1)S(1)} %pad_maximum_fusion), channel_id=1, replica_groups=mesh['grp'=2,'eh'=2,'el'=8] {'grp','el'}, dimensions={0} | all-to-all | bytes 4194304 | tf_op jit(solution)/shard_map/all_to_all | solution.py:148
  70.0 2.4 %fusion.1 = f32[1024,1024]{1,0:T(8,128)S(1)} fusion(bf16[1024,1024]{1,0:T(8,128)(2,1)S(1)} %bitcast.47, bf16[1,1024,1024]{2,1,0:T(8,128)(2,1)S(1)} %copy-done), kind=kOutput, calls=%fused_computation.3 | convolution fusion | flops 2147483648 | bytes 8388608 | tf_op jit(solution)/shard_map/dot_general | solution.py:115
  72.4 2.6 %convolution_convert_fusion = bf16[1024,1024]{1,0:T(8,128)(2,1)} fusion(f32[1024,1024]{1,0:T(8,128)S(1)} %fusion.1, bf16[1,512,1024]{2,1,0:T(8,128)(2,1)S(1)} %copy-done.6), kind=kOutput, calls=%fused_computation.11 | convolution fusion | flops 1077936128 | bytes 7340032 | tf_op jit(solution)/shard_map/dot_general | solution.py:119
  75.0 4.4 %all-to-all-start.1 = ((bf16[16,2,32,1024]{3,2,1,0:T(8,128)(2,1)}), bf16[16,2,32,1024]{3,2,1,0:T(8,128)(2,1)}, u32[]{:S(2)}, u32[]{:S(2)}) async-start(bf16[16,2,32,1024]{3,2,1,0:T(8,128)(2,1)} %bitcast.46), calls=%async_computation.1 | async-start | bytes 4194304 | tf_op jit(solution)/shard_map/all_to_all | solution.py:152
  79.5 0.7 select_reduce_fusion
  80.2 27.9 %all-to-all-done.1 = bf16[16,2,32,1024]{3,2,1,0:T(8,128)(2,1)} async-done(((bf16[16,2,32,1024]{3,2,1,0:T(8,128)(2,1)}), bf16[16,2,32,1024]{3,2,1,0:T(8,128)(2,1)}, u32[]{:S(2)}, u32[]{:S(2)}) %all-to-all-start.1) | async-done | bytes 2097184 | tf_op jit(solution)/shard_map/all_to_all | solution.py:152
  108.1 1.7 %fusion.47 = (bf16[16,1,32,1024]{3,2,1,0:T(8,128)(2,1)S(1)}, bf16[16,1,32,1024]{3,2,1,0:T(8,128)(2,1)S(1)}) fusion(bf16[16,2,32,1024]{3,2,1,0:T(8,128)(2,1)} %all-to-all-done.1), kind=kLoop, calls=%fused_computation.112 | loop fusion | bytes 4194304 | tf_op jit(solution)/shard_map/slice | solution.py:158
  109.8 0.0 copy-start.5
  109.8 0.7 convolution_convert_fusion.3
  110.5 3.5 %collective-permute-start.2 = (bf16[128,1024]{1,0:T(8,128)(2,1)S(1)}, bf16[128,1024]{1,0:T(8,128)(2,1)S(1)}, u32[]{:S(2)}, u32[]{:S(2)}) collective-permute-start(bf16[128,1024]{1,0:T(8,128)(2,1)S(1)} %convolution_convert_fusion.3), channel_id=1, source_target_pairs={{8,0},{0,8},{9,1},{1,9},{10,2},{2,10},{11,3},{3,11},{12,4},{4,12},... | collective-permute-start | bytes 786440 | tf_op jit(solution)/shard_map/ppermute | solution.py:164
  113.9 0.7 select_reduce_fusion.1
  114.7 9.1 %collective-permute-done.2 = bf16[128,1024]{1,0:T(8,128)(2,1)S(1)} collective-permute-done((bf16[128,1024]{1,0:T(8,128)(2,1)S(1)}, bf16[128,1024]{1,0:T(8,128)(2,1)S(1)}, u32[]{:S(2)}, u32[]{:S(2)}) %collective-permute-start.2) | collective-permute-done | bytes 262176 | tf_op jit(solution)/shard_map/ppermute | solution.py:164
  123.7 0.8 multiply_reduce_fusion
  124.5 0.8 multiply_convert_fusion
  (27 shorter events, 0.3 us)
Async XLA Ops:
  0.0 70.0 %copy-start = (bf16[1,1024,1024]{2,1,0:T(8,128)(2,1)S(1)}, bf16[1,1024,1024]{2,1,0:T(8,128)(2,1)}, u32[]{:S(2)}) copy-start(bf16[1,1024,1024]{2,1,0:T(8,128)(2,1)} %param.21) | copy-start | bytes 6291460
  0.0 18.4 %copy-start.2 = (bf16[128,1024]{1,0:T(8,128)(2,1)S(1)}, bf16[128,1024]{1,0:T(8,128)(2,1)}, u32[]{:S(2)}) copy-start(bf16[128,1024]{1,0:T(8,128)(2,1)} %param.16) | copy-start | bytes 786436
  0.0 18.5 %copy-start.1 = (bf16[1024,512]{1,0:T(8,128)(2,1)S(1)}, bf16[1024,512]{1,0:T(8,128)(2,1)}, u32[]{:S(2)}) copy-start(bf16[1024,512]{1,0:T(8,128)(2,1)} %param.18) | copy-start | bytes 3145732
  0.0 9.9 %collective-permute-start = (bf16[128,1024]{1,0:T(8,128)(2,1)}, bf16[128,1024]{1,0:T(8,128)(2,1)}, u32[]{:S(2)}, u32[]{:S(2)}) collective-permute-start(bf16[128,1024]{1,0:T(8,128)(2,1)} %param.16), channel_id=1, source_target_pairs={{0,16},{16,0},{1,17},{17,1},{2,18},{18,2},{3,19},{19,3},{4,20},{20... | collective-permute-start | bytes 786440 | tf_op jit(solution)/shard_map/ppermute | solution.py:52
  12.3 9.3 %copy-start.4 = (f32[1024]{0:T(1024)S(1)}, f32[1024]{0:T(1024)}, u32[]{:S(2)}) copy-start(f32[1024]{0:T(1024)} %param.19) | copy-start | bytes 12292
  12.3 8.1 %collective-permute-start.1 = (f32[128,512]{1,0:T(8,128)}, f32[128,512]{1,0:T(8,128)}, u32[]{:S(2)}, u32[]{:S(2)}) collective-permute-start(f32[128,512]{1,0:T(8,128)} %fusion.49), channel_id=1, source_target_pairs={{16,0},{0,16},{17,1},{1,17},{18,2},{2,18},{19,3},{3,19},{20,4},{4,... | collective-permute-start | bytes 786440 | tf_op jit(solution)/shard_map/ppermute | solution.py:54
  18.5 3.0 %copy-start.3 = (bf16[128,1024]{1,0:T(8,128)(2,1)S(1)}, bf16[128,1024]{1,0:T(8,128)(2,1)}, u32[]{:S(2)}) copy-start(bf16[128,1024]{1,0:T(8,128)(2,1)} %param.17) | copy-start | bytes 786436
  70.0 2.4 %copy-start.6 = (bf16[1,512,1024]{2,1,0:T(8,128)(2,1)S(1)}, bf16[1,512,1024]{2,1,0:T(8,128)(2,1)}, u32[]{:S(2)}) copy-start(bf16[1,512,1024]{2,1,0:T(8,128)(2,1)} %param.22) | copy-start | bytes 3145732
  75.0 33.1 %all-to-all-start.1 = ((bf16[16,2,32,1024]{3,2,1,0:T(8,128)(2,1)}), bf16[16,2,32,1024]{3,2,1,0:T(8,128)(2,1)}, u32[]{:S(2)}, u32[]{:S(2)}) async-start(bf16[16,2,32,1024]{3,2,1,0:T(8,128)(2,1)} %bitcast.46), calls=%async_computation.1 | async-start | bytes 4194304 | tf_op jit(solution)/shard_map/all_to_all | solution.py:152
  109.8 14.7 %copy-start.5 = (f32[1024]{0:T(1024)S(1)}, f32[1024]{0:T(1024)}, u32[]{:S(2)}) copy-start(f32[1024]{0:T(1024)} %param.20) | copy-start | bytes 12292
  110.5 13.3 %collective-permute-start.2 = (bf16[128,1024]{1,0:T(8,128)(2,1)S(1)}, bf16[128,1024]{1,0:T(8,128)(2,1)S(1)}, u32[]{:S(2)}, u32[]{:S(2)}) collective-permute-start(bf16[128,1024]{1,0:T(8,128)(2,1)S(1)} %convolution_convert_fusion.3), channel_id=1, source_target_pairs={{8,0},{0,8},{9,1},{1,9},{10,2},{2,10},{11,3},{3,11},{12,4},{4,12},... | collective-permute-start | bytes 786440 | tf_op jit(solution)/shard_map/ppermute | solution.py:164

commit v15 on v12

--- a/solution.py
+++ b/solution.py
@@ -149,13 +149,15 @@
         jnp.stack(buffers, axis=1), PLANE_AXES, split_axis=0, concat_axis=0, tiled=True
     )
     produced = expert(arrived.reshape(-1, features)).reshape(arrived.shape)
-    returned_all = lax.all_to_all(produced, PLANE_AXES, split_axis=0, concat_axis=0, tiled=True)
     partials = [None] * planes
     for shift in list(range(1, planes)) + [0]:
+        returned = lax.all_to_all(
+            produced[:, shift], PLANE_AXES, split_axis=0, concat_axis=0, tiled=True
+        )
         combine = jnp.sum(jnp.where(hits[shift], weights_in[shift][None, :, :], 0.0), axis=2)
         partial = jnp.dot(
             combine.T,
-            returned_all[:, shift].reshape(plane_slots, features).astype(jnp.float32),
+            returned.reshape(plane_slots, features).astype(jnp.float32),
             precision=lax.Precision.HIGHEST,
             preferred_element_type=jnp.float32,
         )

time: 126 us -> 123 us (0.976)
  waiting for transfers between devices: 50.1 us -> 26.6 us
  blocking collectives: 30.2 us -> 49.6 us
  other arithmetic: 11.7 us -> 13.4 us
  matrix products: 10.1 us -> 11.7 us
    all_to_all x0 -> x1, blocking collectives: none -> 19.4 us  [on_device(): lax.all_to_all(produced[:, shift], PLANE_AXES, split_axis=0, concat_axis=...]
    all_to_all x1, waiting for transfers between devices: 27.9 us -> 13.5 us  [on_device(): lax.all_to_all(produced[:, shift], PLANE_AXES, split_axis=0, concat_axis=...]
    ppermute x1, waiting for transfers between devices: 9.07 us -> 0.01 us  [on_device(): lax.ppermute(partial.astype(jnp.bfloat16), 'eh', back).astype(jnp.float32)]
    dot_general x2, matrix products: 1.45 us -> 4.39 us  [on_device(): jnp.dot(combine.T, returned.reshape(plane_slots, features).astype(jnp.flo...]
    slice x1 -> x0, local copies, waits for them, and re-layouts: 1.71 us -> none  [on_device(): returned_all[:, shift].reshape(plane_slots, features).astype(jnp.float32)]
    dot_general x1, matrix products: 2.6 us -> 1.32 us  [expert(): jnp.dot(expert_hidden, down_local, preferred_element_type=jnp.float32)]
  transfers between devices with their start and end apart: 5 -> 5, of which waited for: 4 -> 3; matrix products, arithmetic and copies ran while one was open for 8% -> 10% of each run, Pallas kernels for 0% -> 0%
where the time goes in v15:
time: 123 us
  blocking collectives  49.6 us (40%)
  waiting for transfers between devices  26.6 us (22%)
  starting transfers between devices  14.2 us (12%)
  other arithmetic  13.4 us (11%)
  matrix products  11.7 us (10%)
  between operations  4.02 us (3%)
  local copies, waits for them, and re-layouts  3.09 us (3%)
    all_to_all x1, blocking collectives, on_device(): lax.all_to_all(jnp.stack(buffers, axis=1), PLANE_AXES, split_axis=0, conc...  30.2 us
    all_to_all x1, blocking collectives, on_device(): lax.all_to_all(produced[:, shift], PLANE_AXES, split_axis=0, concat_axis=...  19.4 us
    all_to_all x1, waiting for transfers between devices, on_device(): lax.all_to_all(produced[:, shift], PLANE_AXES, split_axis=0, concat_axis=...  13.5 us
    ppermute x1, waiting for transfers between devices, on_device(): lax.ppermute(packed, 'eh', [(i, (i + shift) % planes) for i in range(plan...  11.5 us
    dot_general x2, matrix products, on_device(): jnp.dot(combine.T, returned.reshape(plane_slots, features).astype(jnp.flo...  4.39 us
    all_to_all x1, starting transfers between devices, on_device(): lax.all_to_all(produced[:, shift], PLANE_AXES, split_axis=0, concat_axis=...  3.65 us
    ppermute x1, starting transfers between devices, on_device(): lax.ppermute(partial.astype(jnp.bfloat16), 'eh', back).astype(jnp.float32)  3.37 us
    ppermute x1, starting transfers between devices, on_device(): visiting = lax.ppermute(attention, 'grp', ahead)  3.04 us
  transfers between devices with their start and end apart: 5, of which 3 were waited for; matrix products, arithmetic and copies ran while one was open for 10% of the time, Pallas kernels for 0%

profile of v15, /device:TPU:0, one launch (start us, length us, event | category | flops | bytes accessed | tf_op | source)
XLA Modules:
  0.0 122.7 jit_solution(9865875541126431654)
XLA Ops:
  0.0 3.0 %collective-permute-start = (bf16[128,1024]{1,0:T(8,128)(2,1)}, bf16[128,1024]{1,0:T(8,128)(2,1)}, u32[]{:S(2)}, u32[]{:S(2)}) collective-permute-start(bf16[128,1024]{1,0:T(8,128)(2,1)} %param.16), channel_id=1, source_target_pairs={{0,16},{16,0},{1,17},{17,1},{2,18},{18,2},{3,19},{19,3},{4,20},{20... | collective-permute-start | bytes 786440 | tf_op jit(solution)/shard_map/ppermute | solution.py:52
  3.0 0.8 select_reduce_fusion.5
  3.8 0.8 select_reduce_fusion.4
  4.6 0.7 multiply_add_fusion
  5.3 0.7 multiply_add_fusion.1
  6.0 0.2 fusion.23
  6.2 0.8 broadcast_in_dim.88
  7.0 0.1 select_reduce_fusion.2
  7.1 0.7 constant_dynamic-update-slice_fusion.4
  7.8 0.7 constant_dynamic-update-slice_fusion.2
  8.5 0.7 constant_dynamic-update-slice_fusion.1
  9.2 0.7 constant_dynamic-update-slice_fusion
  9.9 0.0 collective-permute-done
  9.9 2.3 %fusion.49 = f32[128,512]{1,0:T(8,128)} fusion(bf16[128,1024]{1,0:T(8,128)(2,1)} %collective-permute-done, bf16[1024,512]{1,0:T(8,128)(2,1)} %param.18), kind=kOutput, calls=%fused_computation.114 | convolution fusion | flops 134217728 | bytes 1572864 | tf_op jit(solution)/shard_map/dot_general | solution.py:53
  12.3 1.5 %collective-permute-start.1 = (f32[128,512]{1,0:T(8,128)}, f32[128,512]{1,0:T(8,128)}, u32[]{:S(2)}, u32[]{:S(2)}) collective-permute-start(f32[128,512]{1,0:T(8,128)} %fusion.49), channel_id=1, source_target_pairs={{16,0},{0,16},{17,1},{1,17},{18,2},{2,18},{19,3},{3,19},{20,4},{4,... | collective-permute-start | bytes 786440 | tf_op jit(solution)/shard_map/ppermute | solution.py:54
  13.7 0.6 fusion.48
  18.1 0.1 copy.49
  18.2 0.1 reshape.57
  18.4 0.0 copy-start.3
  18.4 0.3 convolution_bitcast_fusion
  18.8 1.6 %collective-permute-done.1 = f32[128,512]{1,0:T(8,128)} collective-permute-done((f32[128,512]{1,0:T(8,128)}, f32[128,512]{1,0:T(8,128)}, u32[]{:S(2)}, u32[]{:S(2)}) %collective-permute-start.1) | collective-permute-done | bytes 262176 | tf_op jit(solution)/shard_map/ppermute | solution.py:54
  20.4 1.1 fusion.17
  21.4 0.2 fusion.8
  21.6 0.1 fusion.10
  21.8 2.7 %collective-permute-start.2 = (bf16[136,1024]{1,0:T(8,128)(2,1)S(1)}, bf16[136,1024]{1,0:T(8,128)(2,1)S(1)}, u32[]{:S(2)}, u32[]{:S(2)}) collective-permute-start(bf16[136,1024]{1,0:T(8,128)(2,1)S(1)} %pad_maximum_fusion.1), channel_id=1, source_target_pairs={{0,8},{8,0},{1,9},{9,1},{2,10},{10,2},{3,11},{11,3},{4,12},{12,4},... | collective-permute-start | bytes 835592 | tf_op jit(solution)/shard_map/ppermute | solution.py:124
  24.4 11.5 %collective-permute-done.2 = bf16[136,1024]{1,0:T(8,128)(2,1)S(1)} collective-permute-done((bf16[136,1024]{1,0:T(8,128)(2,1)S(1)}, bf16[136,1024]{1,0:T(8,128)(2,1)S(1)}, u32[]{:S(2)}, u32[]{:S(2)}) %collective-permute-start.2) | collective-permute-done | bytes 278560 | tf_op jit(solution)/shard_map/ppermute | solution.py:124
  36.0 0.1 reshape.102
  36.1 0.1 slice_add_fusion
  36.3 0.1 copy.56
  36.3 0.9 fusion.4
  37.3 0.4 convolution_convert_fusion.2
  37.7 0.9 fusion.3
  38.6 0.4 convolution_convert_fusion.1
  39.0 0.2 pad_maximum_fusion
  39.2 30.2 %all_to_all.15 = bf16[16,2,32,1024]{3,2,1,0:T(8,128)(2,1)S(1)} all-to-all(bf16[16,2,32,1024]{3,2,1,0:T(8,128)(2,1)S(1)} %pad_maximum_fusion), channel_id=1, replica_groups=mesh['grp'=2,'eh'=2,'el'=8] {'grp','el'}, dimensions={0} | all-to-all | bytes 4194304 | tf_op jit(solution)/shard_map/all_to_all | solution.py:148
  69.4 2.4 %fusion.1 = f32[1024,1024]{1,0:T(8,128)S(1)} fusion(bf16[1024,1024]{1,0:T(8,128)(2,1)S(1)} %bitcast.47, bf16[1,1024,1024]{2,1,0:T(8,128)(2,1)S(1)} %copy-done), kind=kOutput, calls=%fused_computation.3 | convolution fusion | flops 2147483648 | bytes 8388608 | tf_op jit(solution)/shard_map/dot_general | solution.py:115
  71.8 1.3 %convolution_convert_fusion = bf16[1024,1024]{1,0:T(8,128)(2,1)S(1)} fusion(f32[1024,1024]{1,0:T(8,128)S(1)} %fusion.1, bf16[1,512,1024]{2,1,0:T(8,128)(2,1)S(1)} %copy-done.6), kind=kOutput, calls=%fused_computation.11 | convolution fusion | flops 1077936128 | bytes 7340032 | tf_op jit(solution)/shard_map/dot_general | solution.py:119
  73.1 1.2 slice_bitcast_fusion
  74.3 19.4 %all_to_all.16 = bf16[16,32,1024]{2,1,0:T(8,128)(2,1)} all-to-all(bf16[16,32,1024]{2,1,0:T(8,128)(2,1)S(1)} %get-tuple-element.22), channel_id=1, replica_groups=mesh['grp'=2,'eh'=2,'el'=8] {'grp','el'}, dimensions={0} | all-to-all | bytes 2097152 | tf_op jit(solution)/shard_map/all_to_all | solution.py:154
  93.7 3.7 %all-to-all-start.1 = ((bf16[16,32,1024]{2,1,0:T(8,128)(2,1)}), bf16[16,32,1024]{2,1,0:T(8,128)(2,1)S(1)}, u32[]{:S(2)}, u32[]{:S(2)}) async-start(bf16[16,32,1024]{2,1,0:T(8,128)(2,1)} %get-tuple-element.23), calls=%async_computation.1 | async-start | bytes 2097152 | tf_op jit(solution)/shard_map/all_to_all | solution.py:154
  97.4 0.7 select_reduce_fusion
  98.1 0.0 copy-start.5
  98.2 2.6 %convolution_convert_fusion.3 = bf16[128,1024]{1,0:T(8,128)(2,1)} fusion(f32[512,128]{1,0:T(8,128)S(1)} %select_reduce_fusion, bf16[512,1024]{1,0:T(8,128)(2,1)} %bitcast.43), kind=kOutput, calls=%fused_computation.14 | convolution fusion | flops 805437440 | bytes 1572864 | tf_op jit(solution)/shard_map/dot_general | solution.py:158
  100.7 3.4 %collective-permute-start.3 = (bf16[128,1024]{1,0:T(8,128)(2,1)}, bf16[128,1024]{1,0:T(8,128)(2,1)}, u32[]{:S(2)}, u32[]{:S(2)}) collective-permute-start(bf16[128,1024]{1,0:T(8,128)(2,1)} %convolution_convert_fusion.3), channel_id=1, source_target_pairs={{8,0},{0,8},{9,1},{1,9},{10,2},{2,10},{11,3},{3,11},{12,4},{4,12},... | collective-permute-start | bytes 786440 | tf_op jit(solution)/shard_map/ppermute | solution.py:166
  104.1 1.4 %select_reduce_fusion.1 = f32[512,128]{1,0:T(8,128)} fusion(f32[128,8]{0,1:T(8,128)S(1)} %slice_add_fusion.2, s32[128,8]{0,1:T(8,128)S(1)} %get-tuple-element.33), kind=kLoop, calls=%fused_computation.8 | loop fusion | flops 1507328 | bytes 270336 | tf_op jit(solution)/shard_map/reduce_sum | solution.py:157
  105.6 13.5 %all-to-all-done.1 = bf16[16,32,1024]{2,1,0:T(8,128)(2,1)S(1)} async-done(((bf16[16,32,1024]{2,1,0:T(8,128)(2,1)}), bf16[16,32,1024]{2,1,0:T(8,128)(2,1)S(1)}, u32[]{:S(2)}, u32[]{:S(2)}) %all-to-all-start.1) | async-done | bytes 1048608 | tf_op jit(solution)/shard_map/all_to_all | solution.py:154
  119.1 1.8 %multiply_reduce_fusion = (f32[128]{0:T(128)S(1)}, f32[128,1024]{1,0:T(8,128)S(1)}) fusion(bf16[128,1024]{1,0:T(8,128)(2,1)} %collective-permute-done.3, bf16[128,1024]{1,0:T(8,128)(2,1)S(1)} %get-tuple-element.18, f32[512,128]{1,0:T(8,128)} %select_reduce_fusion.1, bf16[512,1024]{1,0:T(8,128)(2,1)S(1)} %bitcast.42), kind=kOutput, calls=%fused_computation.33 | convolution fusion | flops 806092672 | bytes 2359808 | tf_op jit(solution)/shard_map/dot_general | solution.py:158
  120.9 1.8 %multiply_convert_fusion = bf16[128,1024]{1,0:T(8,128)(2,1)} fusion(f32[1024]{0:T(1024)S(1)} %copy-done.5, f32[128]{0:T(128)S(1)} %add_rsqrt_fusion, f32[128,1024]{1,0:T(8,128)S(1)} %get-tuple-element.32, bf16[128,1024]{1,0:T(8,128)(2,1)} %collective-permute-done.3, bf16[128,1024]{1,0:T(8,128)(2,1)S(1)} %get-tuple-element.18), kind=kLoop, calls=%fused_computation.32 | loop fusion | flops 917504 | bytes 1315328 | tf_op jit(solution)/shard_map/convert_element_type | solution.py:171
  (28 shorter events, 0.3 us)
Async XLA Ops:
  0.0 69.4 %copy-start = (bf16[1,1024,1024]{2,1,0:T(8,128)(2,1)S(1)}, bf16[1,1024,1024]{2,1,0:T(8,128)(2,1)}, u32[]{:S(2)}) copy-start(bf16[1,1024,1024]{2,1,0:T(8,128)(2,1)} %param.21) | copy-start | bytes 6291460
  0.0 18.4 %copy-start.2 = (bf16[128,1024]{1,0:T(8,128)(2,1)S(1)}, bf16[128,1024]{1,0:T(8,128)(2,1)}, u32[]{:S(2)}) copy-start(bf16[128,1024]{1,0:T(8,128)(2,1)} %param.16) | copy-start | bytes 786436
  0.0 18.4 %copy-start.1 = (bf16[1024,512]{1,0:T(8,128)(2,1)S(1)}, bf16[1024,512]{1,0:T(8,128)(2,1)}, u32[]{:S(2)}) copy-start(bf16[1024,512]{1,0:T(8,128)(2,1)} %param.18) | copy-start | bytes 3145732
  0.0 9.9 %collective-permute-start = (bf16[128,1024]{1,0:T(8,128)(2,1)}, bf16[128,1024]{1,0:T(8,128)(2,1)}, u32[]{:S(2)}, u32[]{:S(2)}) collective-permute-start(bf16[128,1024]{1,0:T(8,128)(2,1)} %param.16), channel_id=1, source_target_pairs={{0,16},{16,0},{1,17},{17,1},{2,18},{18,2},{3,19},{19,3},{4,20},{20... | collective-permute-start | bytes 786440 | tf_op jit(solution)/shard_map/ppermute | solution.py:52
  12.3 9.3 %copy-start.4 = (f32[1024]{0:T(1024)S(1)}, f32[1024]{0:T(1024)}, u32[]{:S(2)}) copy-start(f32[1024]{0:T(1024)} %param.19) | copy-start | bytes 12292
  12.3 8.1 %collective-permute-start.1 = (f32[128,512]{1,0:T(8,128)}, f32[128,512]{1,0:T(8,128)}, u32[]{:S(2)}, u32[]{:S(2)}) collective-permute-start(f32[128,512]{1,0:T(8,128)} %fusion.49), channel_id=1, source_target_pairs={{16,0},{0,16},{17,1},{1,17},{18,2},{2,18},{19,3},{3,19},{20,4},{4,... | collective-permute-start | bytes 786440 | tf_op jit(solution)/shard_map/ppermute | solution.py:54
  18.4 3.0 %copy-start.3 = (bf16[128,1024]{1,0:T(8,128)(2,1)S(1)}, bf16[128,1024]{1,0:T(8,128)(2,1)}, u32[]{:S(2)}) copy-start(bf16[128,1024]{1,0:T(8,128)(2,1)} %param.17) | copy-start | bytes 786436
  21.8 14.2 %collective-permute-start.2 = (bf16[136,1024]{1,0:T(8,128)(2,1)S(1)}, bf16[136,1024]{1,0:T(8,128)(2,1)S(1)}, u32[]{:S(2)}, u32[]{:S(2)}) collective-permute-start(bf16[136,1024]{1,0:T(8,128)(2,1)S(1)} %pad_maximum_fusion.1), channel_id=1, source_target_pairs={{0,8},{8,0},{1,9},{9,1},{2,10},{10,2},{3,11},{11,3},{4,12},{12,4},... | collective-permute-start | bytes 835592 | tf_op jit(solution)/shard_map/ppermute | solution.py:124
  69.4 2.4 %copy-start.6 = (bf16[1,512,1024]{2,1,0:T(8,128)(2,1)S(1)}, bf16[1,512,1024]{2,1,0:T(8,128)(2,1)}, u32[]{:S(2)}) copy-start(bf16[1,512,1024]{2,1,0:T(8,128)(2,1)} %param.22) | copy-start | bytes 3145732
  93.7 25.4 %all-to-all-start.1 = ((bf16[16,32,1024]{2,1,0:T(8,128)(2,1)}), bf16[16,32,1024]{2,1,0:T(8,128)(2,1)S(1)}, u32[]{:S(2)}, u32[]{:S(2)}) async-start(bf16[16,32,1024]{2,1,0:T(8,128)(2,1)} %get-tuple-element.23), calls=%async_computation.1 | async-start | bytes 2097152 | tf_op jit(solution)/shard_map/all_to_all | solution.py:154
  98.1 22.7 %copy-start.5 = (f32[1024]{0:T(1024)S(1)}, f32[1024]{0:T(1024)}, u32[]{:S(2)}) copy-start(f32[1024]{0:T(1024)} %param.20) | copy-start | bytes 12292
  100.7 18.3 %collective-permute-start.3 = (bf16[128,1024]{1,0:T(8,128)(2,1)}, bf16[128,1024]{1,0:T(8,128)(2,1)}, u32[]{:S(2)}, u32[]{:S(2)}) collective-permute-start(bf16[128,1024]{1,0:T(8,128)(2,1)} %convolution_convert_fusion.3), channel_id=1, source_target_pairs={{8,0},{0,8},{9,1},{1,9},{10,2},{2,10},{11,3},{3,11},{12,4},{4,12},... | collective-permute-start | bytes 786440 | tf_op jit(solution)/shard_map/ppermute | solution.py:166

commit v16 on v15

--- a/solution.py
+++ b/solution.py
@@ -146,13 +146,13 @@
         buffer = jnp.dot(dispatch, block[:rows_here], preferred_element_type=jnp.float32)
         buffers.append(buffer.astype(jnp.bfloat16).reshape(groups * lanes, cap_size, features))
     arrived = lax.all_to_all(
-        jnp.stack(buffers, axis=1), PLANE_AXES, split_axis=0, concat_axis=0, tiled=True
+        jnp.stack(buffers, axis=0), PLANE_AXES, split_axis=1, concat_axis=1, tiled=True
     )
     produced = expert(arrived.reshape(-1, features)).reshape(arrived.shape)
     partials = [None] * planes
     for shift in list(range(1, planes)) + [0]:
         returned = lax.all_to_all(
-            produced[:, shift], PLANE_AXES, split_axis=0, concat_axis=0, tiled=True
+            produced[shift], PLANE_AXES, split_axis=0, concat_axis=0, tiled=True
         )
         combine = jnp.sum(jnp.where(hits[shift], weights_in[shift][None, :, :], 0.0), axis=2)
         partial = jnp.dot(

time: 123 us -> 124 us (level)
  no operation moved by 1% of the time
where the time goes in v16:
time: 124 us; the launch traced here: 123 us
  blocking collectives  49.6 us (40%)
  waiting for transfers between devices  26.6 us (21%)
  starting transfers between devices  14.2 us (11%)
  other arithmetic  13.4 us (11%)
  matrix products  11.7 us (9%)
  between operations  4.04 us (3%)
  local copies, waits for them, and re-layouts  3.33 us (3%)
    all_to_all x1, blocking collectives, on_device(): lax.all_to_all(jnp.stack(buffers, axis=0), PLANE_AXES, split_axis=1, conc...  30.2 us
    all_to_all x1, blocking collectives, on_device(): lax.all_to_all(produced[shift], PLANE_AXES, split_axis=0, concat_axis=0,...  19.4 us
    all_to_all x1, waiting for transfers between devices, on_device(): lax.all_to_all(produced[shift], PLANE_AXES, split_axis=0, concat_axis=0,...  13.5 us
    ppermute x1, waiting for transfers between devices, on_device(): lax.ppermute(packed, 'eh', [(i, (i + shift) % planes) for i in range(plan...  11.5 us
    dot_general x2, matrix products, on_device(): jnp.dot(combine.T, returned.reshape(plane_slots, features).astype(jnp.flo...  4.38 us
    all_to_all x1, starting transfers between devices, on_device(): lax.all_to_all(produced[shift], PLANE_AXES, split_axis=0, concat_axis=0,...  3.65 us
    ppermute x1, starting transfers between devices, on_device(): lax.ppermute(partial.astype(jnp.bfloat16), 'eh', back).astype(jnp.float32)  3.38 us
    ppermute x1, starting transfers between devices, on_device(): visiting = lax.ppermute(attention, 'grp', ahead)  3.04 us
  transfers between devices with their start and end apart: 5, of which 3 were waited for; matrix products, arithmetic and copies ran while one was open for 10% of the time, Pallas kernels for 0%

profile of v16, /device:TPU:0, one launch (start us, length us, event | category | flops | bytes accessed | tf_op | source)
XLA Modules:
  0.0 122.9 jit_solution(17221960658275749202)
XLA Ops:
  0.0 3.0 %collective-permute-start = (bf16[128,1024]{1,0:T(8,128)(2,1)}, bf16[128,1024]{1,0:T(8,128)(2,1)}, u32[]{:S(2)}, u32[]{:S(2)}) collective-permute-start(bf16[128,1024]{1,0:T(8,128)(2,1)} %param.16), channel_id=1, source_target_pairs={{0,16},{16,0},{1,17},{17,1},{2,18},{18,2},{3,19},{19,3},{4,20},{20... | collective-permute-start | bytes 786440 | tf_op jit(solution)/shard_map/ppermute | solution.py:52
  3.0 0.8 select_reduce_fusion.5
  3.8 0.8 select_reduce_fusion.4
  4.6 0.7 multiply_add_fusion
  5.3 0.7 multiply_add_fusion.1
  6.0 0.2 fusion.23
  6.2 0.8 broadcast_in_dim.88
  7.0 0.1 select_reduce_fusion.2
  7.1 0.7 constant_dynamic-update-slice_fusion.4
  7.8 0.7 constant_dynamic-update-slice_fusion.2
  8.5 0.7 constant_dynamic-update-slice_fusion.1
  9.2 0.7 constant_dynamic-update-slice_fusion
  9.9 2.3 %fusion.50 = f32[128,512]{1,0:T(8,128)} fusion(bf16[128,1024]{1,0:T(8,128)(2,1)} %collective-permute-done, bf16[1024,512]{1,0:T(8,128)(2,1)} %param.18), kind=kOutput, calls=%fused_computation.113 | convolution fusion | flops 134217728 | bytes 1572864 | tf_op jit(solution)/shard_map/dot_general | solution.py:53
  12.3 1.5 %collective-permute-start.1 = (f32[128,512]{1,0:T(8,128)}, f32[128,512]{1,0:T(8,128)}, u32[]{:S(2)}, u32[]{:S(2)}) collective-permute-start(f32[128,512]{1,0:T(8,128)} %fusion.50), channel_id=1, source_target_pairs={{16,0},{0,16},{17,1},{1,17},{18,2},{2,18},{19,3},{3,19},{20,4},{4,... | collective-permute-start | bytes 786440 | tf_op jit(solution)/shard_map/ppermute | solution.py:54
  13.7 0.6 fusion.49
  18.1 0.1 copy.56
  18.2 0.1 reshape.59
  18.4 0.3 convolution_bitcast_fusion
  18.8 1.6 %collective-permute-done.1 = f32[128,512]{1,0:T(8,128)} collective-permute-done((f32[128,512]{1,0:T(8,128)}, f32[128,512]{1,0:T(8,128)}, u32[]{:S(2)}, u32[]{:S(2)}) %collective-permute-start.1) | collective-permute-done | bytes 262176 | tf_op jit(solution)/shard_map/ppermute | solution.py:54
  20.4 1.1 fusion.17
  21.4 0.2 fusion.8
  21.6 0.1 fusion.10
  21.8 2.7 %collective-permute-start.2 = (bf16[136,1024]{1,0:T(8,128)(2,1)S(1)}, bf16[136,1024]{1,0:T(8,128)(2,1)S(1)}, u32[]{:S(2)}, u32[]{:S(2)}) collective-permute-start(bf16[136,1024]{1,0:T(8,128)(2,1)S(1)} %pad_maximum_fusion.1), channel_id=1, source_target_pairs={{0,8},{8,0},{1,9},{9,1},{2,10},{10,2},{3,11},{11,3},{4,12},{12,4},... | collective-permute-start | bytes 835592 | tf_op jit(solution)/shard_map/ppermute | solution.py:124
  24.4 11.5 %collective-permute-done.2 = bf16[136,1024]{1,0:T(8,128)(2,1)S(1)} collective-permute-done((bf16[136,1024]{1,0:T(8,128)(2,1)S(1)}, bf16[136,1024]{1,0:T(8,128)(2,1)S(1)}, u32[]{:S(2)}, u32[]{:S(2)}) %collective-permute-start.2) | collective-permute-done | bytes 278560 | tf_op jit(solution)/shard_map/ppermute | solution.py:124
  36.0 0.1 reshape.103
  36.1 0.1 slice_add_fusion
  36.3 0.1 copy.64
  36.3 0.9 fusion.4
  37.3 0.4 convolution_convert_fusion.2
  37.7 0.9 fusion.3
  38.6 0.4 convolution_convert_fusion.1
  39.0 0.2 pad_maximum_fusion
  39.2 30.2 %all_to_all.15 = bf16[2,16,32,1024]{3,2,0,1:T(8,128)(2,1)S(1)} all-to-all(bf16[2,16,32,1024]{3,2,0,1:T(8,128)(2,1)S(1)} %pad_maximum_fusion), channel_id=1, replica_groups=mesh['grp'=2,'eh'=2,'el'=8] {'grp','el'}, dimensions={1} | all-to-all | bytes 4194304 | tf_op jit(solution)/shard_map/all_to_all | solution.py:148
  69.4 0.3 copy.61
  69.7 0.0 copy-start.6
  69.7 2.3 %fusion.1 = f32[1024,1024]{1,0:T(8,128)S(1)} fusion(bf16[1024,1024]{1,0:T(8,128)(2,1)S(1)} %bitcast.45, bf16[1,1024,1024]{2,1,0:T(8,128)(2,1)S(1)} %copy-done), kind=kOutput, calls=%fused_computation.3 | convolution fusion | flops 2147483648 | bytes 8388608 | tf_op jit(solution)/shard_map/dot_general | solution.py:115
  72.0 1.3 %convolution_convert_fusion = bf16[1024,1024]{1,0:T(8,128)(2,1)S(1)} fusion(f32[1024,1024]{1,0:T(8,128)S(1)} %fusion.1, bf16[1,512,1024]{2,1,0:T(8,128)(2,1)S(1)} %copy-done.6), kind=kOutput, calls=%fused_computation.11 | convolution fusion | flops 1077936128 | bytes 7340032 | tf_op jit(solution)/shard_map/dot_general | solution.py:119
  73.4 1.2 fusion.48
  74.5 19.4 %all_to_all.16 = bf16[16,32,1024]{2,1,0:T(8,128)(2,1)} all-to-all(bf16[16,32,1024]{2,1,0:T(8,128)(2,1)S(1)} %bitcast.44), channel_id=1, replica_groups=mesh['grp'=2,'eh'=2,'el'=8] {'grp','el'}, dimensions={0} | all-to-all | bytes 2097152 | tf_op jit(solution)/shard_map/all_to_all | solution.py:154
  93.9 3.7 %all-to-all-start.1 = ((bf16[16,32,1024]{2,1,0:T(8,128)(2,1)}), bf16[16,32,1024]{2,1,0:T(8,128)(2,1)S(1)}, u32[]{:S(2)}, u32[]{:S(2)}) async-start(bf16[16,32,1024]{2,1,0:T(8,128)(2,1)} %bitcast.41), calls=%async_computation.1 | async-start | bytes 2097152 | tf_op jit(solution)/shard_map/all_to_all | solution.py:154
  97.6 0.7 select_reduce_fusion
  98.4 0.0 copy-start.5
  98.4 2.6 %convolution_convert_fusion.3 = bf16[128,1024]{1,0:T(8,128)(2,1)} fusion(f32[512,128]{1,0:T(8,128)S(1)} %select_reduce_fusion, bf16[512,1024]{1,0:T(8,128)(2,1)} %bitcast.40), kind=kOutput, calls=%fused_computation.14 | convolution fusion | flops 805437440 | bytes 1572864 | tf_op jit(solution)/shard_map/dot_general | solution.py:158
  101.0 3.4 %collective-permute-start.3 = (bf16[128,1024]{1,0:T(8,128)(2,1)}, bf16[128,1024]{1,0:T(8,128)(2,1)}, u32[]{:S(2)}, u32[]{:S(2)}) collective-permute-start(bf16[128,1024]{1,0:T(8,128)(2,1)} %convolution_convert_fusion.3), channel_id=1, source_target_pairs={{8,0},{0,8},{9,1},{1,9},{10,2},{2,10},{11,3},{3,11},{12,4},{4,12},... | collective-permute-start | bytes 786440 | tf_op jit(solution)/shard_map/ppermute | solution.py:166
  104.4 1.4 %select_reduce_fusion.1 = f32[512,128]{1,0:T(8,128)} fusion(f32[128,8]{0,1:T(8,128)S(1)} %slice_add_fusion.2, s32[128,8]{0,1:T(8,128)S(1)} %get-tuple-element.33), kind=kLoop, calls=%fused_computation.8 | loop fusion | flops 1507328 | bytes 270336 | tf_op jit(solution)/shard_map/reduce_sum | solution.py:157
  105.8 13.5 %all-to-all-done.1 = bf16[16,32,1024]{2,1,0:T(8,128)(2,1)S(1)} async-done(((bf16[16,32,1024]{2,1,0:T(8,128)(2,1)}), bf16[16,32,1024]{2,1,0:T(8,128)(2,1)S(1)}, u32[]{:S(2)}, u32[]{:S(2)}) %all-to-all-start.1) | async-done | bytes 1048608 | tf_op jit(solution)/shard_map/all_to_all | solution.py:154
  119.3 1.8 %multiply_reduce_fusion = (f32[128]{0:T(128)S(1)}, f32[128,1024]{1,0:T(8,128)S(1)}) fusion(bf16[128,1024]{1,0:T(8,128)(2,1)} %collective-permute-done.3, bf16[128,1024]{1,0:T(8,128)(2,1)S(1)} %get-tuple-element.18, f32[512,128]{1,0:T(8,128)} %select_reduce_fusion.1, bf16[512,1024]{1,0:T(8,128)(2,1)S(1)} %bitcast.39), kind=kOutput, calls=%fused_computation.31 | convolution fusion | flops 806092672 | bytes 2359808 | tf_op jit(solution)/shard_map/dot_general | solution.py:158
  121.1 1.8 %multiply_convert_fusion = bf16[128,1024]{1,0:T(8,128)(2,1)} fusion(f32[1024]{0:T(1024)S(1)} %copy-done.5, f32[128]{0:T(128)S(1)} %add_rsqrt_fusion, f32[128,1024]{1,0:T(8,128)S(1)} %get-tuple-element.32, bf16[128,1024]{1,0:T(8,128)(2,1)} %collective-permute-done.3, bf16[128,1024]{1,0:T(8,128)(2,1)S(1)} %get-tuple-element.18), kind=kLoop, calls=%fused_computation.30 | loop fusion | flops 917504 | bytes 1315328 | tf_op jit(solution)/shard_map/convert_element_type | solution.py:171
  (29 shorter events, 0.3 us)
Async XLA Ops:
  0.0 69.7 %copy-start = (bf16[1,1024,1024]{2,1,0:T(8,128)(2,1)S(1)}, bf16[1,1024,1024]{2,1,0:T(8,128)(2,1)}, u32[]{:S(2)}) copy-start(bf16[1,1024,1024]{2,1,0:T(8,128)(2,1)} %param.21) | copy-start | bytes 6291460
  0.0 18.4 %copy-start.2 = (bf16[128,1024]{1,0:T(8,128)(2,1)S(1)}, bf16[128,1024]{1,0:T(8,128)(2,1)}, u32[]{:S(2)}) copy-start(bf16[128,1024]{1,0:T(8,128)(2,1)} %param.16) | copy-start | bytes 786436
  0.0 18.4 %copy-start.1 = (bf16[1024,512]{1,0:T(8,128)(2,1)S(1)}, bf16[1024,512]{1,0:T(8,128)(2,1)}, u32[]{:S(2)}) copy-start(bf16[1024,512]{1,0:T(8,128)(2,1)} %param.18) | copy-start | bytes 3145732
  0.0 9.9 %collective-permute-start = (bf16[128,1024]{1,0:T(8,128)(2,1)}, bf16[128,1024]{1,0:T(8,128)(2,1)}, u32[]{:S(2)}, u32[]{:S(2)}) collective-permute-start(bf16[128,1024]{1,0:T(8,128)(2,1)} %param.16), channel_id=1, source_target_pairs={{0,16},{16,0},{1,17},{17,1},{2,18},{18,2},{3,19},{19,3},{4,20},{20... | collective-permute-start | bytes 786440 | tf_op jit(solution)/shard_map/ppermute | solution.py:52
  12.3 9.3 %copy-start.4 = (f32[1024]{0:T(1024)S(1)}, f32[1024]{0:T(1024)}, u32[]{:S(2)}) copy-start(f32[1024]{0:T(1024)} %param.19) | copy-start | bytes 12292
  12.3 8.1 %collective-permute-start.1 = (f32[128,512]{1,0:T(8,128)}, f32[128,512]{1,0:T(8,128)}, u32[]{:S(2)}, u32[]{:S(2)}) collective-permute-start(f32[128,512]{1,0:T(8,128)} %fusion.50), channel_id=1, source_target_pairs={{16,0},{0,16},{17,1},{1,17},{18,2},{2,18},{19,3},{3,19},{20,4},{4,... | collective-permute-start | bytes 786440 | tf_op jit(solution)/shard_map/ppermute | solution.py:54
  18.4 3.0 %copy-start.3 = (bf16[128,1024]{1,0:T(8,128)(2,1)S(1)}, bf16[128,1024]{1,0:T(8,128)(2,1)}, u32[]{:S(2)}) copy-start(bf16[128,1024]{1,0:T(8,128)(2,1)} %param.17) | copy-start | bytes 786436
  21.8 14.2 %collective-permute-start.2 = (bf16[136,1024]{1,0:T(8,128)(2,1)S(1)}, bf16[136,1024]{1,0:T(8,128)(2,1)S(1)}, u32[]{:S(2)}, u32[]{:S(2)}) collective-permute-start(bf16[136,1024]{1,0:T(8,128)(2,1)S(1)} %pad_maximum_fusion.1), channel_id=1, source_target_pairs={{0,8},{8,0},{1,9},{9,1},{2,10},{10,2},{3,11},{11,3},{4,12},{12,4},... | collective-permute-start | bytes 835592 | tf_op jit(solution)/shard_map/ppermute | solution.py:124
  69.7 2.4 %copy-start.6 = (bf16[1,512,1024]{2,1,0:T(8,128)(2,1)S(1)}, bf16[1,512,1024]{2,1,0:T(8,128)(2,1)}, u32[]{:S(2)}) copy-start(bf16[1,512,1024]{2,1,0:T(8,128)(2,1)} %param.22) | copy-start | bytes 3145732
  93.9 25.4 %all-to-all-start.1 = ((bf16[16,32,1024]{2,1,0:T(8,128)(2,1)}), bf16[16,32,1024]{2,1,0:T(8,128)(2,1)S(1)}, u32[]{:S(2)}, u32[]{:S(2)}) async-start(bf16[16,32,1024]{2,1,0:T(8,128)(2,1)} %bitcast.41), calls=%async_computation.1 | async-start | bytes 2097152 | tf_op jit(solution)/shard_map/all_to_all | solution.py:154
  98.4 22.7 %copy-start.5 = (f32[1024]{0:T(1024)S(1)}, f32[1024]{0:T(1024)}, u32[]{:S(2)}) copy-start(f32[1024]{0:T(1024)} %param.20) | copy-start | bytes 12292
  101.0 18.3 %collective-permute-start.3 = (bf16[128,1024]{1,0:T(8,128)(2,1)}, bf16[128,1024]{1,0:T(8,128)(2,1)}, u32[]{:S(2)}, u32[]{:S(2)}) collective-permute-start(bf16[128,1024]{1,0:T(8,128)(2,1)} %convolution_convert_fusion.3), channel_id=1, source_target_pairs={{8,0},{0,8},{9,1},{1,9},{10,2},{2,10},{11,3},{3,11},{12,4},{4,12},... | collective-permute-start | bytes 786440 | tf_op jit(solution)/shard_map/ppermute | solution.py:166

commit v17 on v15

--- a/solution.py
+++ b/solution.py
@@ -158,7 +158,7 @@
         partial = jnp.dot(
             combine.T,
             returned.reshape(plane_slots, features).astype(jnp.float32),
-            precision=lax.Precision.HIGHEST,
+            precision=lax.Precision.HIGH,
             preferred_element_type=jnp.float32,
         )
         if shift:

time: 123 us -> 123 us (level)
  no operation moved by 1% of the time
where the time goes in v17:
time: 123 us
  blocking collectives  49.6 us (40%)
  waiting for transfers between devices  26.8 us (22%)
  starting transfers between devices  14.2 us (12%)
  other arithmetic  13.4 us (11%)
  matrix products  11.4 us (9%)
  between operations  4.02 us (3%)
  local copies, waits for them, and re-layouts  3.09 us (3%)
    all_to_all x1, blocking collectives, on_device(): lax.all_to_all(jnp.stack(buffers, axis=1), PLANE_AXES, split_axis=0, conc...  30.2 us
    all_to_all x1, blocking collectives, on_device(): lax.all_to_all(produced[:, shift], PLANE_AXES, split_axis=0, concat_axis=...  19.4 us
    all_to_all x1, waiting for transfers between devices, on_device(): lax.all_to_all(produced[:, shift], PLANE_AXES, split_axis=0, concat_axis=...  13.6 us
    ppermute x1, waiting for transfers between devices, on_device(): lax.ppermute(packed, 'eh', [(i, (i + shift) % planes) for i in range(plan...  11.5 us
    dot_general x2, matrix products, on_device(): jnp.dot(combine.T, returned.reshape(plane_slots, features).astype(jnp.flo...  4.09 us
    all_to_all x1, starting transfers between devices, on_device(): lax.all_to_all(produced[:, shift], PLANE_AXES, split_axis=0, concat_axis=...  3.65 us
    ppermute x1, starting transfers between devices, on_device(): lax.ppermute(partial.astype(jnp.bfloat16), 'eh', back).astype(jnp.float32)  3.37 us
    ppermute x1, starting transfers between devices, on_device(): visiting = lax.ppermute(attention, 'grp', ahead)  3.04 us
  transfers between devices with their start and end apart: 5, of which 3 were waited for; matrix products, arithmetic and copies ran while one was open for 10% of the time, Pallas kernels for 0%

profile of v17, /device:TPU:0, one launch (start us, length us, event | category | flops | bytes accessed | tf_op | source)
XLA Modules:
  0.0 122.5 jit_solution(18131621720874709334)
XLA Ops:
  0.0 3.0 %collective-permute-start = (bf16[128,1024]{1,0:T(8,128)(2,1)}, bf16[128,1024]{1,0:T(8,128)(2,1)}, u32[]{:S(2)}, u32[]{:S(2)}) collective-permute-start(bf16[128,1024]{1,0:T(8,128)(2,1)} %param.16), channel_id=1, source_target_pairs={{0,16},{16,0},{1,17},{17,1},{2,18},{18,2},{3,19},{19,3},{4,20},{20... | collective-permute-start | bytes 786440 | tf_op jit(solution)/shard_map/ppermute | solution.py:52
  3.0 0.8 select_reduce_fusion.5
  3.8 0.8 select_reduce_fusion.4
  4.6 0.7 multiply_add_fusion
  5.3 0.7 multiply_add_fusion.1
  6.0 0.2 fusion.23
  6.2 0.8 broadcast_in_dim.88
  7.0 0.1 select_reduce_fusion.2
  7.1 0.7 constant_dynamic-update-slice_fusion.4
  7.8 0.7 constant_dynamic-update-slice_fusion.2
  8.5 0.7 constant_dynamic-update-slice_fusion.1
  9.2 0.7 constant_dynamic-update-slice_fusion
  9.9 2.3 %fusion.49 = f32[128,512]{1,0:T(8,128)} fusion(bf16[128,1024]{1,0:T(8,128)(2,1)} %collective-permute-done, bf16[1024,512]{1,0:T(8,128)(2,1)} %param.18), kind=kOutput, calls=%fused_computation.114 | convolution fusion | flops 134217728 | bytes 1572864 | tf_op jit(solution)/shard_map/dot_general | solution.py:53
  12.3 1.5 %collective-permute-start.1 = (f32[128,512]{1,0:T(8,128)}, f32[128,512]{1,0:T(8,128)}, u32[]{:S(2)}, u32[]{:S(2)}) collective-permute-start(f32[128,512]{1,0:T(8,128)} %fusion.49), channel_id=1, source_target_pairs={{16,0},{0,16},{17,1},{1,17},{18,2},{2,18},{19,3},{3,19},{20,4},{4,... | collective-permute-start | bytes 786440 | tf_op jit(solution)/shard_map/ppermute | solution.py:54
  13.7 0.6 fusion.48
  18.1 0.1 copy.49
  18.2 0.1 reshape.57
  18.4 0.0 copy-start.3
  18.4 0.3 convolution_bitcast_fusion
  18.8 1.6 %collective-permute-done.1 = f32[128,512]{1,0:T(8,128)} collective-permute-done((f32[128,512]{1,0:T(8,128)}, f32[128,512]{1,0:T(8,128)}, u32[]{:S(2)}, u32[]{:S(2)}) %collective-permute-start.1) | collective-permute-done | bytes 262176 | tf_op jit(solution)/shard_map/ppermute | solution.py:54
  20.4 1.1 fusion.17
  21.4 0.2 fusion.8
  21.6 0.1 fusion.10
  21.8 2.7 %collective-permute-start.2 = (bf16[136,1024]{1,0:T(8,128)(2,1)S(1)}, bf16[136,1024]{1,0:T(8,128)(2,1)S(1)}, u32[]{:S(2)}, u32[]{:S(2)}) collective-permute-start(bf16[136,1024]{1,0:T(8,128)(2,1)S(1)} %pad_maximum_fusion.1), channel_id=1, source_target_pairs={{0,8},{8,0},{1,9},{9,1},{2,10},{10,2},{3,11},{11,3},{4,12},{12,4},... | collective-permute-start | bytes 835592 | tf_op jit(solution)/shard_map/ppermute | solution.py:124
  24.4 11.5 %collective-permute-done.2 = bf16[136,1024]{1,0:T(8,128)(2,1)S(1)} collective-permute-done((bf16[136,1024]{1,0:T(8,128)(2,1)S(1)}, bf16[136,1024]{1,0:T(8,128)(2,1)S(1)}, u32[]{:S(2)}, u32[]{:S(2)}) %collective-permute-start.2) | collective-permute-done | bytes 278560 | tf_op jit(solution)/shard_map/ppermute | solution.py:124
  36.0 0.1 reshape.102
  36.1 0.1 slice_add_fusion
  36.3 0.1 copy.56
  36.3 0.9 fusion.4
  37.3 0.4 convolution_convert_fusion.2
  37.7 0.9 fusion.3
  38.6 0.4 convolution_convert_fusion.1
  39.0 0.2 pad_maximum_fusion
  39.2 30.2 %all_to_all.15 = bf16[16,2,32,1024]{3,2,1,0:T(8,128)(2,1)S(1)} all-to-all(bf16[16,2,32,1024]{3,2,1,0:T(8,128)(2,1)S(1)} %pad_maximum_fusion), channel_id=1, replica_groups=mesh['grp'=2,'eh'=2,'el'=8] {'grp','el'}, dimensions={0} | all-to-all | bytes 4194304 | tf_op jit(solution)/shard_map/all_to_all | solution.py:148
  69.4 2.4 %fusion.1 = f32[1024,1024]{1,0:T(8,128)S(1)} fusion(bf16[1024,1024]{1,0:T(8,128)(2,1)S(1)} %bitcast.47, bf16[1,1024,1024]{2,1,0:T(8,128)(2,1)S(1)} %copy-done), kind=kOutput, calls=%fused_computation.3 | convolution fusion | flops 2147483648 | bytes 8388608 | tf_op jit(solution)/shard_map/dot_general | solution.py:115
  71.8 1.3 %convolution_convert_fusion = bf16[1024,1024]{1,0:T(8,128)(2,1)S(1)} fusion(f32[1024,1024]{1,0:T(8,128)S(1)} %fusion.1, bf16[1,512,1024]{2,1,0:T(8,128)(2,1)S(1)} %copy-done.6), kind=kOutput, calls=%fused_computation.11 | convolution fusion | flops 1077936128 | bytes 7340032 | tf_op jit(solution)/shard_map/dot_general | solution.py:119
  73.1 1.2 slice_bitcast_fusion
  74.3 19.4 %all_to_all.16 = bf16[16,32,1024]{2,1,0:T(8,128)(2,1)} all-to-all(bf16[16,32,1024]{2,1,0:T(8,128)(2,1)S(1)} %get-tuple-element.22), channel_id=1, replica_groups=mesh['grp'=2,'eh'=2,'el'=8] {'grp','el'}, dimensions={0} | all-to-all | bytes 2097152 | tf_op jit(solution)/shard_map/all_to_all | solution.py:154
  93.7 3.7 %all-to-all-start.1 = ((bf16[16,32,1024]{2,1,0:T(8,128)(2,1)}), bf16[16,32,1024]{2,1,0:T(8,128)(2,1)S(1)}, u32[]{:S(2)}, u32[]{:S(2)}) async-start(bf16[16,32,1024]{2,1,0:T(8,128)(2,1)} %get-tuple-element.23), calls=%async_computation.1 | async-start | bytes 2097152 | tf_op jit(solution)/shard_map/all_to_all | solution.py:154
  97.4 0.7 select_reduce_fusion
  98.1 0.0 copy-start.5
  98.2 2.4 %convolution_convert_fusion.3 = bf16[128,1024]{1,0:T(8,128)(2,1)} fusion(f32[512,128]{1,0:T(8,128)S(1)} %select_reduce_fusion, bf16[512,1024]{1,0:T(8,128)(2,1)} %bitcast.43), kind=kOutput, calls=%fused_computation.14 | convolution fusion | flops 402784256 | bytes 1572864 | tf_op jit(solution)/shard_map/dot_general | solution.py:158
  100.6 3.4 %collective-permute-start.3 = (bf16[128,1024]{1,0:T(8,128)(2,1)}, bf16[128,1024]{1,0:T(8,128)(2,1)}, u32[]{:S(2)}, u32[]{:S(2)}) collective-permute-start(bf16[128,1024]{1,0:T(8,128)(2,1)} %convolution_convert_fusion.3), channel_id=1, source_target_pairs={{8,0},{0,8},{9,1},{1,9},{10,2},{2,10},{11,3},{3,11},{12,4},{4,12},... | collective-permute-start | bytes 786440 | tf_op jit(solution)/shard_map/ppermute | solution.py:166
  104.0 1.4 %select_reduce_fusion.1 = f32[512,128]{1,0:T(8,128)} fusion(f32[128,8]{0,1:T(8,128)S(1)} %slice_add_fusion.2, s32[128,8]{0,1:T(8,128)S(1)} %get-tuple-element.33), kind=kLoop, calls=%fused_computation.8 | loop fusion | flops 1507328 | bytes 270336 | tf_op jit(solution)/shard_map/reduce_sum | solution.py:157
  105.4 13.6 %all-to-all-done.1 = bf16[16,32,1024]{2,1,0:T(8,128)(2,1)S(1)} async-done(((bf16[16,32,1024]{2,1,0:T(8,128)(2,1)}), bf16[16,32,1024]{2,1,0:T(8,128)(2,1)S(1)}, u32[]{:S(2)}, u32[]{:S(2)}) %all-to-all-start.1) | async-done | bytes 1048608 | tf_op jit(solution)/shard_map/all_to_all | solution.py:154
  119.1 0.0 collective-permute-done.3
  119.1 1.7 %multiply_reduce_fusion = (f32[128]{0:T(128)S(1)}, f32[128,1024]{1,0:T(8,128)S(1)}) fusion(bf16[128,1024]{1,0:T(8,128)(2,1)} %collective-permute-done.3, bf16[128,1024]{1,0:T(8,128)(2,1)S(1)} %get-tuple-element.18, f32[512,128]{1,0:T(8,128)} %select_reduce_fusion.1, bf16[512,1024]{1,0:T(8,128)(2,1)S(1)} %bitcast.42), kind=kOutput, calls=%fused_computation.33 | convolution fusion | flops 403439488 | bytes 2359808 | tf_op jit(solution)/shard_map/dot_general | solution.py:158
  120.7 1.8 %multiply_convert_fusion = bf16[128,1024]{1,0:T(8,128)(2,1)} fusion(f32[1024]{0:T(1024)S(1)} %copy-done.5, f32[128]{0:T(128)S(1)} %add_rsqrt_fusion, f32[128,1024]{1,0:T(8,128)S(1)} %get-tuple-element.32, bf16[128,1024]{1,0:T(8,128)(2,1)} %collective-permute-done.3, bf16[128,1024]{1,0:T(8,128)(2,1)S(1)} %get-tuple-element.18), kind=kLoop, calls=%fused_computation.32 | loop fusion | flops 917504 | bytes 1315328 | tf_op jit(solution)/shard_map/convert_element_type | solution.py:171
  (28 shorter events, 0.3 us)
Async XLA Ops:
  0.0 69.4 %copy-start = (bf16[1,1024,1024]{2,1,0:T(8,128)(2,1)S(1)}, bf16[1,1024,1024]{2,1,0:T(8,128)(2,1)}, u32[]{:S(2)}) copy-start(bf16[1,1024,1024]{2,1,0:T(8,128)(2,1)} %param.21) | copy-start | bytes 6291460
  0.0 18.4 %copy-start.2 = (bf16[128,1024]{1,0:T(8,128)(2,1)S(1)}, bf16[128,1024]{1,0:T(8,128)(2,1)}, u32[]{:S(2)}) copy-start(bf16[128,1024]{1,0:T(8,128)(2,1)} %param.16) | copy-start | bytes 786436
  0.0 18.4 %copy-start.1 = (bf16[1024,512]{1,0:T(8,128)(2,1)S(1)}, bf16[1024,512]{1,0:T(8,128)(2,1)}, u32[]{:S(2)}) copy-start(bf16[1024,512]{1,0:T(8,128)(2,1)} %param.18) | copy-start | bytes 3145732
  0.0 9.9 %collective-permute-start = (bf16[128,1024]{1,0:T(8,128)(2,1)}, bf16[128,1024]{1,0:T(8,128)(2,1)}, u32[]{:S(2)}, u32[]{:S(2)}) collective-permute-start(bf16[128,1024]{1,0:T(8,128)(2,1)} %param.16), channel_id=1, source_target_pairs={{0,16},{16,0},{1,17},{17,1},{2,18},{18,2},{3,19},{19,3},{4,20},{20... | collective-permute-start | bytes 786440 | tf_op jit(solution)/shard_map/ppermute | solution.py:52
  12.3 9.3 %copy-start.4 = (f32[1024]{0:T(1024)S(1)}, f32[1024]{0:T(1024)}, u32[]{:S(2)}) copy-start(f32[1024]{0:T(1024)} %param.19) | copy-start | bytes 12292
  12.3 8.1 %collective-permute-start.1 = (f32[128,512]{1,0:T(8,128)}, f32[128,512]{1,0:T(8,128)}, u32[]{:S(2)}, u32[]{:S(2)}) collective-permute-start(f32[128,512]{1,0:T(8,128)} %fusion.49), channel_id=1, source_target_pairs={{16,0},{0,16},{17,1},{1,17},{18,2},{2,18},{19,3},{3,19},{20,4},{4,... | collective-permute-start | bytes 786440 | tf_op jit(solution)/shard_map/ppermute | solution.py:54
  18.4 3.0 %copy-start.3 = (bf16[128,1024]{1,0:T(8,128)(2,1)S(1)}, bf16[128,1024]{1,0:T(8,128)(2,1)}, u32[]{:S(2)}) copy-start(bf16[128,1024]{1,0:T(8,128)(2,1)} %param.17) | copy-start | bytes 786436
  21.8 14.2 %collective-permute-start.2 = (bf16[136,1024]{1,0:T(8,128)(2,1)S(1)}, bf16[136,1024]{1,0:T(8,128)(2,1)S(1)}, u32[]{:S(2)}, u32[]{:S(2)}) collective-permute-start(bf16[136,1024]{1,0:T(8,128)(2,1)S(1)} %pad_maximum_fusion.1), channel_id=1, source_target_pairs={{0,8},{8,0},{1,9},{9,1},{2,10},{10,2},{3,11},{11,3},{4,12},{12,4},... | collective-permute-start | bytes 835592 | tf_op jit(solution)/shard_map/ppermute | solution.py:124
  69.4 2.4 %copy-start.6 = (bf16[1,512,1024]{2,1,0:T(8,128)(2,1)S(1)}, bf16[1,512,1024]{2,1,0:T(8,128)(2,1)}, u32[]{:S(2)}) copy-start(bf16[1,512,1024]{2,1,0:T(8,128)(2,1)} %param.22) | copy-start | bytes 3145732
  93.7 25.4 %all-to-all-start.1 = ((bf16[16,32,1024]{2,1,0:T(8,128)(2,1)}), bf16[16,32,1024]{2,1,0:T(8,128)(2,1)S(1)}, u32[]{:S(2)}, u32[]{:S(2)}) async-start(bf16[16,32,1024]{2,1,0:T(8,128)(2,1)} %get-tuple-element.23), calls=%async_computation.1 | async-start | bytes 2097152 | tf_op jit(solution)/shard_map/all_to_all | solution.py:154
  98.1 22.6 %copy-start.5 = (f32[1024]{0:T(1024)S(1)}, f32[1024]{0:T(1024)}, u32[]{:S(2)}) copy-start(f32[1024]{0:T(1024)} %param.20) | copy-start | bytes 12292
  100.6 18.5 %collective-permute-start.3 = (bf16[128,1024]{1,0:T(8,128)(2,1)}, bf16[128,1024]{1,0:T(8,128)(2,1)}, u32[]{:S(2)}, u32[]{:S(2)}) collective-permute-start(bf16[128,1024]{1,0:T(8,128)(2,1)} %convolution_convert_fusion.3), channel_id=1, source_target_pairs={{8,0},{0,8},{9,1},{1,9},{10,2},{2,10},{11,3},{3,11},{12,4},{4,12},... | collective-permute-start | bytes 786440 | tf_op jit(solution)/shard_map/ppermute | solution.py:166

commit v18 on v15

--- a/solution.py
+++ b/solution.py
@@ -44,20 +44,31 @@
     my_plane = lax.axis_index("eh")
 
     me_grp = lax.axis_index("grp")
-    blocks = [None] * groups
-    blocks[0] = jnp.dot(attention, out_proj, preferred_element_type=jnp.float32)
+    width = features // groups
+    residual_cols = residual.reshape(rows_here, groups, width)
+    hidden_blocks = [
+        (
+            jnp.take(residual_cols, me_grp, axis=1).astype(jnp.float32)
+            + jnp.dot(attention, out_proj, preferred_element_type=jnp.float32)
+        ).astype(jnp.bfloat16)
+    ]
     for shift in range(1, groups):
         ahead = [(g, (g + shift) % groups) for g in range(groups)]
         back = [(b, a) for a, b in ahead]
-        visiting = lax.ppermute(attention, "grp", ahead)
-        done = jnp.dot(visiting, out_proj, preferred_element_type=jnp.float32)
-        blocks[shift] = lax.ppermute(done, "grp", back)
-    stacked = jnp.stack(blocks, axis=0)
+        payload = jnp.concatenate(
+            [attention, jnp.take(residual_cols, (me_grp + shift) % groups, axis=1)], axis=1
+        )
+        visiting = lax.ppermute(payload, "grp", ahead)
+        done = (
+            visiting[:, features:].astype(jnp.float32)
+            + jnp.dot(visiting[:, :features], out_proj, preferred_element_type=jnp.float32)
+        ).astype(jnp.bfloat16)
+        hidden_blocks.append(lax.ppermute(done, "grp", back))
     order_cols = (jnp.arange(groups, dtype=jnp.int32) - me_grp) % groups
-    attn_proj = jnp.concatenate(
+    stacked = jnp.stack(hidden_blocks, axis=0)
+    hidden_state = jnp.concatenate(
         [jnp.take(stacked, order_cols[j], axis=0) for j in range(groups)], axis=1
     )
-    hidden_state = (residual.astype(jnp.float32) + attn_proj).astype(jnp.bfloat16)
     normed = rms_scale(hidden_state.astype(jnp.float32), pre_gain).astype(jnp.bfloat16)
 
     experts_all = placement.shape[0]

time: 123 us -> 132 us (1.073)
  local copies, waits for them, and re-layouts: 3.09 us -> 13.2 us
  other arithmetic: 13.4 us -> 11.9 us
  waiting for transfers between devices: 26.6 us -> 28 us
    unnamed x16 -> x33, local copies, waits for them, and re-layouts: 0.15 us -> 6.5 us
    ppermute x2, waiting for transfers between devices: 1.61 us -> 4.63 us  [the longest x1 4.62 us: on_device(): hidden_blocks.append(lax.ppermute(done, 'grp', back))]
    unnamed x4, other arithmetic: 2.13 us -> 0.07 us
    another operation x0 -> x1, local copies, waits for them, and re-layouts: none -> 1.73 us  [on_device(): jnp.take(residual_cols, (me_grp + shift) % groups, axis=1)]
    concatenate x0 -> x1, other arithmetic: none -> 1.71 us  [on_device(): jnp.concatenate([attention, jnp.take(residual_cols, (me_grp + shift) % gr...]
    ppermute x1, waiting for transfers between devices: 11.5 us -> 9.93 us  [on_device(): lax.ppermute(packed, 'eh', [(i, (i + shift) % planes) for i in range(plan...]
    ppermute x2, starting transfers between devices: 4.5 us -> 3.05 us  [the longest x1 2.98 us: on_device(): visiting = lax.ppermute(payload, 'grp', ahead)]
  transfers between devices with their start and end apart: 5 -> 5, of which waited for: 3 -> 3; matrix products, arithmetic and copies ran while one was open for 10% -> 11% of each run, Pallas kernels for 0% -> 0%
where the time goes in v18:
time: 132 us; the launch traced here: 131 us
  blocking collectives  49.6 us (38%)
  waiting for transfers between devices  28 us (21%)
  local copies, waits for them, and re-layouts  13.2 us (10%)
  starting transfers between devices  12.9 us (10%)
  other arithmetic  11.9 us (9%)
  matrix products  11.7 us (9%)
  between operations  4.11 us (3%)
    all_to_all x1, blocking collectives, on_device(): lax.all_to_all(jnp.stack(buffers, axis=1), PLANE_AXES, split_axis=0, conc...  30.2 us
    all_to_all x1, blocking collectives, on_device(): lax.all_to_all(produced[:, shift], PLANE_AXES, split_axis=0, concat_axis=...  19.4 us
    all_to_all x1, waiting for transfers between devices, on_device(): lax.all_to_all(produced[:, shift], PLANE_AXES, split_axis=0, concat_axis=...  13.5 us
    ppermute x1, waiting for transfers between devices, on_device(): lax.ppermute(packed, 'eh', [(i, (i + shift) % planes) for i in range(plan...  9.93 us
    unnamed x33, local copies, waits for them, and re-layouts  6.5 us
    ppermute x1, waiting for transfers between devices, on_device(): hidden_blocks.append(lax.ppermute(done, 'grp', back))  4.62 us
    dot_general x2, matrix products, on_device(): jnp.dot(combine.T, returned.reshape(plane_slots, features).astype(jnp.flo...  4.39 us
    all_to_all x1, starting transfers between devices, on_device(): lax.all_to_all(produced[:, shift], PLANE_AXES, split_axis=0, concat_axis=...  3.78 us
  transfers between devices with their start and end apart: 5, of which 3 were waited for; matrix products, arithmetic and copies ran while one was open for 11% of the time, Pallas kernels for 0%

profile of v18, /device:TPU:0, one launch (start us, length us, event | category | flops | bytes accessed | tf_op | source)
XLA Modules:
  0.0 131.4 jit_solution(7472922578305282688)
XLA Ops:
  0.1 1.9 %copy.58 = bf16[128,1024]{0,1:T(8,128)(2,1)} copy(bf16[128,1024]{1,0:T(8,128)(2,1)} %param.19) | data formatting | bytes 524288 | tf_op args[1]
  2.0 1.7 %constant_dynamic-slice_fusion = (bf16[128,1,512]{0,2,1:T(8,128)(2,1)}, bf16[128,1,512]{0,2,1:T(8,128)(2,1)}) fusion(bf16[128,2,512]{0,2,1:T(8,128)(2,1)} %bitcast.52, s32[]{:T(128)S(6)} %select_n.90, s32[]{:T(128)S(6)} %select_n.88), kind=kLoop, calls=%fused_computation.114 | loop fusion | bytes 524296 | tf_op jit(solution)/shard_map/jit(_take) | solution.py:59
  3.7 1.0 copy.68
  4.8 1.7 %pad_maximum_fusion.1 = bf16[128,1536]{1,0:T(8,128)(2,1)} fusion(bf16[128,512]{1,0:T(8,128)(2,1)S(1)} %select_bitcast_fusion, bf16[128,1024]{1,0:T(8,128)(2,1)} %param.18), kind=kLoop, calls=%fused_computation.30 | loop fusion | flops 786432 | bytes 786432 | tf_op jit(solution)/shard_map/concatenate | solution.py:58
  6.5 3.0 %collective-permute-start = (bf16[128,1536]{1,0:T(8,128)(2,1)}, bf16[128,1536]{1,0:T(8,128)(2,1)}, u32[]{:S(2)}, u32[]{:S(2)}) collective-permute-start(bf16[128,1536]{1,0:T(8,128)(2,1)} %pad_maximum_fusion.1), channel_id=1, source_target_pairs={{0,16},{16,0},{1,17},{17,1},{2,18},{18,2},{3,19},{19,3},{4,20},{20... | collective-permute-start | bytes 1179656 | tf_op jit(solution)/shard_map/ppermute | solution.py:61
  9.5 0.6 fusion.50
  13.9 0.8 select_reduce_fusion.5
  14.8 0.7 multiply_add_fusion.1
  15.4 0.2 fusion.26
  15.8 0.1 select_reduce_fusion.2
  16.0 0.7 copy.61
  16.7 0.6 convert_element_type.99
  17.3 1.0 copy.67
  18.3 0.9 reshape.62
  19.2 0.6 pad.4
  19.8 0.7 reshape.63
  20.6 0.7 fusion.40
  21.3 1.3 add_convert_fusion
  22.7 0.3 fusion.6
  23.0 4.6 %collective-permute-done.1 = bf16[128,512]{1,0:T(8,128)(2,1)S(1)} collective-permute-done((bf16[128,512]{1,0:T(8,128)(2,1)S(1)}, bf16[128,512]{1,0:T(8,128)(2,1)S(1)}, u32[]{:S(2)}, u32[]{:S(2)}) %collective-permute-start.1) | collective-permute-done | bytes 131104 | tf_op jit(solution)/shard_map/ppermute | solution.py:66
  27.6 0.1 fusion.21
  27.7 0.1 fusion.10
  27.9 0.1 fusion.12
  28.1 2.7 %collective-permute-start.2 = (bf16[136,1024]{1,0:T(8,128)(2,1)S(1)}, bf16[136,1024]{1,0:T(8,128)(2,1)S(1)}, u32[]{:S(2)}, u32[]{:S(2)}) collective-permute-start(bf16[136,1024]{1,0:T(8,128)(2,1)S(1)} %pad_maximum_fusion.2), channel_id=1, source_target_pairs={{0,8},{8,0},{1,9},{9,1},{2,10},{10,2},{3,11},{11,3},{4,12},{12,4},... | collective-permute-start | bytes 835592 | tf_op jit(solution)/shard_map/ppermute | solution.py:135
  30.7 0.9 fusion.4
  31.6 0.4 convolution_convert_fusion.2
  32.0 9.9 %collective-permute-done.2 = bf16[136,1024]{1,0:T(8,128)(2,1)S(1)} collective-permute-done((bf16[136,1024]{1,0:T(8,128)(2,1)S(1)}, bf16[136,1024]{1,0:T(8,128)(2,1)S(1)}, u32[]{:S(2)}, u32[]{:S(2)}) %collective-permute-start.2) | collective-permute-done | bytes 278560 | tf_op jit(solution)/shard_map/ppermute | solution.py:135
  42.0 0.7 copy-done.3
  42.7 0.1 reshape.148
  42.8 0.8 slice_add_fusion
  43.5 0.9 copy.69
  44.4 0.9 copy.70
  45.3 0.9 fusion.3
  46.2 1.4 %convolution_convert_fusion.1 = bf16[512,1024]{1,0:T(8,128)(2,1)S(1)} fusion(pred[512,128]{1,0:T(8,128)(4,1)S(1)} %fusion.3, bf16[136,1024]{1,0:T(8,128)(2,1)} %copy-done.3), kind=kOutput, calls=%fused_computation.12 | convolution fusion | flops 134742016 | bytes 1376256 | tf_op jit(solution)/shard_map/dot_general | solution.py:157
  47.6 0.2 pad_maximum_fusion
  47.8 30.2 %all_to_all.15 = bf16[16,2,32,1024]{3,2,1,0:T(8,128)(2,1)S(1)} all-to-all(bf16[16,2,32,1024]{3,2,1,0:T(8,128)(2,1)S(1)} %pad_maximum_fusion), channel_id=1, replica_groups=mesh['grp'=2,'eh'=2,'el'=8] {'grp','el'}, dimensions={0} | all-to-all | bytes 4194304 | tf_op jit(solution)/shard_map/all_to_all | solution.py:159
  78.0 2.4 %fusion.1 = f32[1024,1024]{1,0:T(8,128)S(1)} fusion(bf16[1024,1024]{1,0:T(8,128)(2,1)S(1)} %bitcast.51, bf16[1,1024,1024]{2,1,0:T(8,128)(2,1)S(1)} %copy-done), kind=kOutput, calls=%fused_computation.3 | convolution fusion | flops 2147483648 | bytes 8388608 | tf_op jit(solution)/shard_map/dot_general | solution.py:126
  80.4 1.3 convolution_convert_fusion
  81.7 1.2 slice_bitcast_fusion
  82.9 19.4 %all_to_all.16 = bf16[16,32,1024]{2,1,0:T(8,128)(2,1)} all-to-all(bf16[16,32,1024]{2,1,0:T(8,128)(2,1)S(1)} %get-tuple-element.32), channel_id=1, replica_groups=mesh['grp'=2,'eh'=2,'el'=8] {'grp','el'}, dimensions={0} | all-to-all | bytes 2097152 | tf_op jit(solution)/shard_map/all_to_all | solution.py:165
  102.3 3.8 %all-to-all-start.1 = ((bf16[16,32,1024]{2,1,0:T(8,128)(2,1)}), bf16[16,32,1024]{2,1,0:T(8,128)(2,1)S(1)}, u32[]{:S(2)}, u32[]{:S(2)}) async-start(bf16[16,32,1024]{2,1,0:T(8,128)(2,1)} %get-tuple-element.33), calls=%async_computation.1 | async-start | bytes 2097152 | tf_op jit(solution)/shard_map/all_to_all | solution.py:165
  106.1 0.7 select_reduce_fusion
  106.9 2.6 %convolution_convert_fusion.3 = bf16[128,1024]{1,0:T(8,128)(2,1)} fusion(f32[512,128]{1,0:T(8,128)S(1)} %select_reduce_fusion, bf16[512,1024]{1,0:T(8,128)(2,1)} %bitcast.47), kind=kOutput, calls=%fused_computation.14 | convolution fusion | flops 805437440 | bytes 1572864 | tf_op jit(solution)/shard_map/dot_general | solution.py:169
  109.5 3.4 %collective-permute-start.3 = (bf16[128,1024]{1,0:T(8,128)(2,1)}, bf16[128,1024]{1,0:T(8,128)(2,1)}, u32[]{:S(2)}, u32[]{:S(2)}) collective-permute-start(bf16[128,1024]{1,0:T(8,128)(2,1)} %convolution_convert_fusion.3), channel_id=1, source_target_pairs={{8,0},{0,8},{9,1},{1,9},{10,2},{2,10},{11,3},{3,11},{12,4},{4,12},... | collective-permute-start | bytes 786440 | tf_op jit(solution)/shard_map/ppermute | solution.py:177
  112.9 1.4 %select_reduce_fusion.1 = f32[512,128]{1,0:T(8,128)} fusion(f32[128,8]{0,1:T(8,128)S(1)} %slice_add_fusion.2, s32[128,8]{0,1:T(8,128)S(1)} %copy-done.6), kind=kLoop, calls=%fused_computation.8 | loop fusion | flops 1507328 | bytes 270336 | tf_op jit(solution)/shard_map/reduce_sum | solution.py:168
  114.3 13.5 %all-to-all-done.1 = bf16[16,32,1024]{2,1,0:T(8,128)(2,1)S(1)} async-done(((bf16[16,32,1024]{2,1,0:T(8,128)(2,1)}), bf16[16,32,1024]{2,1,0:T(8,128)(2,1)S(1)}, u32[]{:S(2)}, u32[]{:S(2)}) %all-to-all-start.1) | async-done | bytes 1048608 | tf_op jit(solution)/shard_map/all_to_all | solution.py:165
  127.8 1.8 %multiply_reduce_fusion = (f32[128]{0:T(128)S(1)}, f32[128,1024]{1,0:T(8,128)S(1)}) fusion(bf16[128,1024]{1,0:T(8,128)(2,1)} %collective-permute-done.3, bf16[128,512]{1,0:T(8,128)(2,1)S(1)} %get-tuple-element.35, bf16[128,512]{1,0:T(8,128)(2,1)S(1)} %get-tuple-element.34, f32[512,128]{1,0:T(8,128)} %select_reduce_fusion.1, bf16[512,1024]{1,0:T(8,128)(2,1)S(1)} %bitcast.46), kind=kOutput, calls=%fused_computation.29 | convolution fusion | flops 806485888 | bytes 2359808 | tf_op jit(solution)/shard_map/dot_general | solution.py:169
  129.6 1.8 %multiply_convert_fusion = bf16[128,1024]{1,0:T(8,128)(2,1)} fusion(f32[1024]{0:T(1024)S(1)} %copy-done.10, f32[128]{0:T(128)S(1)} %add_rsqrt_fusion, f32[128,1024]{1,0:T(8,128)S(1)} %get-tuple-element.44, bf16[128,1024]{1,0:T(8,128)(2,1)} %collective-permute-done.3, bf16[128,512]{1,0:T(8,128)(2,1)S(1)} %get-tuple-element.35, ...), kind=kLoop, calls=%fused_computation.28 | loop fusion | flops 1310720 | bytes 1315328 | tf_op jit(solution)/shard_map/convert_element_type | solution.py:182
  (49 shorter events, 0.6 us)
Async XLA Ops:
  0.0 78.0 %copy-start = (bf16[1,1024,1024]{2,1,0:T(8,128)(2,1)S(1)}, bf16[1,1024,1024]{2,1,0:T(8,128)(2,1)}, u32[]{:S(2)}) copy-start(bf16[1,1024,1024]{2,1,0:T(8,128)(2,1)} %param.23) | copy-start | bytes 6291460
  0.0 14.6 %copy-start.11 = (s32[128,8]{0,1:T(8,128)S(1)}, s32[128,8]{0,1:T(8,128)}, u32[]{:S(2)}) copy-start(s32[128,8]{0,1:T(8,128)} %param.25) | copy-start | bytes 12292
  0.0 14.7 %copy-start.8 = (s32[128,8]{0,1:T(8,128)S(1)}, s32[128,8]{0,1:T(8,128)}, u32[]{:S(2)}) copy-start(s32[128,8]{0,1:T(8,128)} %param.26) | copy-start | bytes 12292
  0.0 15.7 %copy-start.13 = (s32[2,16]{1,0:T(2,128)S(1)}, s32[2,16]{1,0:T(2,128)}, u32[]{:S(2)}) copy-start(s32[2,16]{1,0:T(2,128)} %param.30) | copy-start | bytes 388
  0.0 15.9 %copy-start.7 = (f32[128,8]{0,1:T(8,128)S(1)}, f32[128,8]{0,1:T(8,128)}, u32[]{:S(2)}) copy-start(f32[128,8]{0,1:T(8,128)} %param.31) | copy-start | bytes 12292
  0.0 21.3 %copy-start.1 = (bf16[1024,512]{1,0:T(8,128)(2,1)S(1)}, bf16[1024,512]{1,0:T(8,128)(2,1)}, u32[]{:S(2)}) copy-start(bf16[1024,512]{1,0:T(8,128)(2,1)} %param.20) | copy-start | bytes 3145732
  2.0 20.7 %copy-start.2 = (bf16[128,1024]{1,0:T(8,128)(2,1)S(1)}, bf16[128,1024]{1,0:T(8,128)(2,1)}, u32[]{:S(2)}) copy-start(bf16[128,1024]{1,0:T(8,128)(2,1)} %param.18) | copy-start | bytes 786436
  6.5 14.8 %collective-permute-start = (bf16[128,1536]{1,0:T(8,128)(2,1)}, bf16[128,1536]{1,0:T(8,128)(2,1)}, u32[]{:S(2)}, u32[]{:S(2)}) collective-permute-start(bf16[128,1536]{1,0:T(8,128)(2,1)} %pad_maximum_fusion.1), channel_id=1, source_target_pairs={{0,16},{16,0},{1,17},{17,1},{2,18},{18,2},{3,19},{19,3},{4,20},{20... | collective-permute-start | bytes 1179656 | tf_op jit(solution)/shard_map/ppermute | solution.py:61
  20.6 7.3 %copy-start.9 = (f32[1024]{0:T(1024)S(1)}, f32[1024]{0:T(1024)}, u32[]{:S(2)}) copy-start(f32[1024]{0:T(1024)} %param.21) | copy-start | bytes 12292
  21.3 9.4 %copy-start.5 = (s32[128,8]{0,1:T(8,128)}, s32[128,8]{0,1:T(8,128)S(1)}, u32[]{:S(2)}) copy-start(s32[128,8]{0,1:T(8,128)S(1)} %fusion.40) | copy-start | bytes 12292
  22.6 5.0 %collective-permute-start.1 = (bf16[128,512]{1,0:T(8,128)(2,1)S(1)}, bf16[128,512]{1,0:T(8,128)(2,1)S(1)}, u32[]{:S(2)}, u32[]{:S(2)}) collective-permute-start(bf16[128,512]{1,0:T(8,128)(2,1)S(1)} %add_convert_fusion), channel_id=1, source_target_pairs={{16,0},{0,16},{17,1},{1,17},{18,2},{2,18},{19,3},{3,19},{20,4},{4,... | collective-permute-start | bytes 393224 | tf_op jit(solution)/shard_map/ppermute | solution.py:66
  28.1 13.9 %collective-permute-start.2 = (bf16[136,1024]{1,0:T(8,128)(2,1)S(1)}, bf16[136,1024]{1,0:T(8,128)(2,1)S(1)}, u32[]{:S(2)}, u32[]{:S(2)}) collective-permute-start(bf16[136,1024]{1,0:T(8,128)(2,1)S(1)} %pad_maximum_fusion.2), channel_id=1, source_target_pairs={{0,8},{8,0},{1,9},{9,1},{2,10},{10,2},{3,11},{11,3},{4,12},{12,4},... | collective-permute-start | bytes 835592 | tf_op jit(solution)/shard_map/ppermute | solution.py:135
  42.0 0.7 copy-start.3
  78.0 2.4 %copy-start.12 = (bf16[1,512,1024]{2,1,0:T(8,128)(2,1)S(1)}, bf16[1,512,1024]{2,1,0:T(8,128)(2,1)}, u32[]{:S(2)}) copy-start(bf16[1,512,1024]{2,1,0:T(8,128)(2,1)} %param.24) | copy-start | bytes 3145732
  102.3 10.6 %copy-start.4 = (f32[128,40]{0,1:T(8,128)S(1)}, f32[128,40]{0,1:T(8,128)}, u32[]{:S(2)}) copy-start(f32[128,40]{0,1:T(8,128)} %convert_element_type.99) | copy-start | bytes 61444
  102.3 10.6 %copy-start.6 = (s32[128,8]{0,1:T(8,128)S(1)}, s32[128,8]{0,1:T(8,128)}, u32[]{:S(2)}) copy-start(s32[128,8]{0,1:T(8,128)} %copy-done.5) | copy-start | bytes 12292
  102.3 25.5 %all-to-all-start.1 = ((bf16[16,32,1024]{2,1,0:T(8,128)(2,1)}), bf16[16,32,1024]{2,1,0:T(8,128)(2,1)S(1)}, u32[]{:S(2)}, u32[]{:S(2)}) async-start(bf16[16,32,1024]{2,1,0:T(8,128)(2,1)} %get-tuple-element.33), calls=%async_computation.1 | async-start | bytes 2097152 | tf_op jit(solution)/shard_map/all_to_all | solution.py:165
  106.9 22.7 %copy-start.10 = (f32[1024]{0:T(1024)S(1)}, f32[1024]{0:T(1024)}, u32[]{:S(2)}) copy-start(f32[1024]{0:T(1024)} %param.22) | copy-start | bytes 12292
  109.5 18.3 %collective-permute-start.3 = (bf16[128,1024]{1,0:T(8,128)(2,1)}, bf16[128,1024]{1,0:T(8,128)(2,1)}, u32[]{:S(2)}, u32[]{:S(2)}) collective-permute-start(bf16[128,1024]{1,0:T(8,128)(2,1)} %convolution_convert_fusion.3), channel_id=1, source_target_pairs={{8,0},{0,8},{9,1},{1,9},{10,2},{2,10},{11,3},{3,11},{12,4},{4,12},... | collective-permute-start | bytes 786440 | tf_op jit(solution)/shard_map/ppermute | solution.py:177

commit v19 on v16

--- a/solution.py
+++ b/solution.py
@@ -148,12 +148,10 @@
     arrived = lax.all_to_all(
         jnp.stack(buffers, axis=0), PLANE_AXES, split_axis=1, concat_axis=1, tiled=True
     )
-    produced = expert(arrived.reshape(-1, features)).reshape(arrived.shape)
     partials = [None] * planes
     for shift in list(range(1, planes)) + [0]:
-        returned = lax.all_to_all(
-            produced[shift], PLANE_AXES, split_axis=0, concat_axis=0, tiled=True
-        )
+        produced = expert(arrived[shift].reshape(-1, features)).reshape(arrived.shape[1:])
+        returned = lax.all_to_all(produced, PLANE_AXES, split_axis=0, concat_axis=0, tiled=True)
         combine = jnp.sum(jnp.where(hits[shift], weights_in[shift][None, :, :], 0.0), axis=2)
         partial = jnp.dot(
             combine.T,

time: 124 us -> 124 us (level)
  blocking collectives: 49.6 us -> 30.2 us
  waiting for transfers between devices: 26.6 us -> 38.5 us
  matrix products: 11.7 us -> 15.4 us
  starting transfers between devices: 14.2 us -> 17.8 us
    all_to_all x1 -> x0, blocking collectives: 19.4 us -> none  [on_device(): lax.all_to_all(produced[shift], PLANE_AXES, split_axis=0, concat_axis=0,...]
    all_to_all x1 -> x2, waiting for transfers between devices: 13.5 us -> 25.3 us  [on_device(): lax.all_to_all(produced, PLANE_AXES, split_axis=0, concat_axis=0, tiled=T...]
    all_to_all x1 -> x2, starting transfers between devices: 3.65 us -> 7.31 us  [on_device(): lax.all_to_all(produced, PLANE_AXES, split_axis=0, concat_axis=0, tiled=T...]
    dot_general x1 -> x2, matrix products: 1.31 us -> 3.52 us  [expert(): jnp.dot(expert_hidden, down_local, preferred_element_type=jnp.float32)]
    dot_general x1 -> x2, matrix products: 2.34 us -> 3.82 us  [expert(): jnp.dot(rows_in, gate_up_local, preferred_element_type=jnp.float32)]
  transfers between devices with their start and end apart: 5 -> 6, of which waited for: 3 -> 4; matrix products, arithmetic and copies ran while one was open for 10% -> 14% of each run, Pallas kernels for 0% -> 0%
where the time goes in v19:
time: 124 us; the launch traced here: 123 us
  waiting for transfers between devices  38.5 us (31%)
  blocking collectives  30.2 us (24%)
  starting transfers between devices  17.8 us (14%)
  matrix products  15.4 us (12%)
  other arithmetic  13.4 us (11%)
  local copies, waits for them, and re-layouts  4.14 us (3%)
  between operations  4.04 us (3%)
    all_to_all x1, blocking collectives, on_device(): lax.all_to_all(jnp.stack(buffers, axis=0), PLANE_AXES, split_axis=1, conc...  30.2 us
    all_to_all x2, waiting for transfers between devices, on_device(): lax.all_to_all(produced, PLANE_AXES, split_axis=0, concat_axis=0, tiled=T...  25.3 us
    ppermute x1, waiting for transfers between devices, on_device(): lax.ppermute(packed, 'eh', [(i, (i + shift) % planes) for i in range(plan...  11.5 us
    all_to_all x2, starting transfers between devices, on_device(): lax.all_to_all(produced, PLANE_AXES, split_axis=0, concat_axis=0, tiled=T...  7.31 us
    dot_general x2, matrix products, on_device(): jnp.dot(combine.T, returned.reshape(plane_slots, features).astype(jnp.flo...  4.39 us
    dot_general x2, matrix products, expert(): jnp.dot(rows_in, gate_up_local, preferred_element_type=jnp.float32)  3.82 us
    dot_general x2, matrix products, expert(): jnp.dot(expert_hidden, down_local, preferred_element_type=jnp.float32)  3.52 us
    ppermute x1, starting transfers between devices, on_device(): lax.ppermute(partial.astype(jnp.bfloat16), 'eh', back).astype(jnp.float32)  3.38 us
  transfers between devices with their start and end apart: 6, of which 4 were waited for; matrix products, arithmetic and copies ran while one was open for 14% of the time, Pallas kernels for 0%

profile of v19, /device:TPU:0, one launch (start us, length us, event | category | flops | bytes accessed | tf_op | source)
XLA Modules:
  0.0 123.5 jit_solution(2017756934545845271)
XLA Ops:
  0.0 3.0 %collective-permute-start = (bf16[128,1024]{1,0:T(8,128)(2,1)}, bf16[128,1024]{1,0:T(8,128)(2,1)}, u32[]{:S(2)}, u32[]{:S(2)}) collective-permute-start(bf16[128,1024]{1,0:T(8,128)(2,1)} %param.16), channel_id=1, source_target_pairs={{0,16},{16,0},{1,17},{17,1},{2,18},{18,2},{3,19},{19,3},{4,20},{20... | collective-permute-start | bytes 786440 | tf_op jit(solution)/shard_map/ppermute | solution.py:52
  3.0 0.8 select_reduce_fusion.5
  3.8 0.8 select_reduce_fusion.4
  4.6 0.7 multiply_add_fusion
  5.3 0.7 multiply_add_fusion.1
  6.0 0.2 fusion.29
  6.2 0.8 broadcast_in_dim.88
  7.0 0.1 select_reduce_fusion.2
  7.1 0.7 constant_dynamic-update-slice_fusion.4
  7.8 0.7 constant_dynamic-update-slice_fusion.2
  8.5 0.7 constant_dynamic-update-slice_fusion.1
  9.2 0.7 constant_dynamic-update-slice_fusion
  9.9 2.3 %fusion.57 = f32[128,512]{1,0:T(8,128)} fusion(bf16[128,1024]{1,0:T(8,128)(2,1)} %collective-permute-done, bf16[1024,512]{1,0:T(8,128)(2,1)} %param.18), kind=kOutput, calls=%fused_computation.121 | convolution fusion | flops 134217728 | bytes 1572864 | tf_op jit(solution)/shard_map/dot_general | solution.py:53
  12.3 1.5 %collective-permute-start.1 = (f32[128,512]{1,0:T(8,128)}, f32[128,512]{1,0:T(8,128)}, u32[]{:S(2)}, u32[]{:S(2)}) collective-permute-start(f32[128,512]{1,0:T(8,128)} %fusion.57), channel_id=1, source_target_pairs={{16,0},{0,16},{17,1},{1,17},{18,2},{2,18},{19,3},{3,19},{20,4},{4,... | collective-permute-start | bytes 786440 | tf_op jit(solution)/shard_map/ppermute | solution.py:54
  13.7 0.6 fusion.56
  18.1 0.1 copy.47
  18.2 0.1 reshape.57
  18.4 0.3 convolution_bitcast_fusion
  18.8 1.6 %collective-permute-done.1 = f32[128,512]{1,0:T(8,128)} collective-permute-done((f32[128,512]{1,0:T(8,128)}, f32[128,512]{1,0:T(8,128)}, u32[]{:S(2)}, u32[]{:S(2)}) %collective-permute-start.1) | collective-permute-done | bytes 262176 | tf_op jit(solution)/shard_map/ppermute | solution.py:54
  20.4 1.1 fusion.23
  21.4 0.2 fusion.10
  21.6 0.1 fusion.12
  21.8 2.7 %collective-permute-start.2 = (bf16[136,1024]{1,0:T(8,128)(2,1)S(1)}, bf16[136,1024]{1,0:T(8,128)(2,1)S(1)}, u32[]{:S(2)}, u32[]{:S(2)}) collective-permute-start(bf16[136,1024]{1,0:T(8,128)(2,1)S(1)} %pad_maximum_fusion.1), channel_id=1, source_target_pairs={{0,8},{8,0},{1,9},{9,1},{2,10},{10,2},{3,11},{11,3},{4,12},{12,4},... | collective-permute-start | bytes 835592 | tf_op jit(solution)/shard_map/ppermute | solution.py:124
  24.4 11.5 %collective-permute-done.2 = bf16[136,1024]{1,0:T(8,128)(2,1)S(1)} collective-permute-done((bf16[136,1024]{1,0:T(8,128)(2,1)S(1)}, bf16[136,1024]{1,0:T(8,128)(2,1)S(1)}, u32[]{:S(2)}, u32[]{:S(2)}) %collective-permute-start.2) | collective-permute-done | bytes 278560 | tf_op jit(solution)/shard_map/ppermute | solution.py:124
  36.0 0.1 reshape.102
  36.1 0.1 slice_add_fusion
  36.3 0.9 fusion.5
  37.3 0.4 convolution_convert_fusion.1
  37.7 0.9 fusion.4
  38.6 0.4 convolution_convert_fusion
  39.0 0.2 pad_maximum_fusion
  39.2 30.2 %all_to_all.15 = bf16[2,16,32,1024]{3,2,0,1:T(8,128)(2,1)S(1)} all-to-all(bf16[2,16,32,1024]{3,2,0,1:T(8,128)(2,1)S(1)} %pad_maximum_fusion), channel_id=1, replica_groups=mesh['grp'=2,'eh'=2,'el'=8] {'grp','el'}, dimensions={1} | all-to-all | bytes 4194304 | tf_op jit(solution)/shard_map/all_to_all | solution.py:148
  69.4 1.2 fusion.55
  70.6 1.3 %fusion = f32[512,1024]{1,0:T(8,128)S(1)} fusion(bf16[512,1024]{1,0:T(8,128)(2,1)S(1)} %bitcast.52, bf16[1,1024,1024]{2,1,0:T(8,128)(2,1)S(1)} %copy-done), kind=kOutput, calls=%fused_computation.1 | convolution fusion | flops 1073741824 | bytes 5242880 | tf_op jit(solution)/shard_map/dot_general | solution.py:115
  71.9 1.8 %convolution_convert_fusion.2 = bf16[512,1024]{1,0:T(8,128)(2,1)} fusion(bf16[1,512,1024]{2,1,0:T(8,128)(2,1)S(1)} %copy-done.7, f32[512,1024]{1,0:T(8,128)S(1)} %fusion), kind=kOutput, calls=%fused_computation.13 | convolution fusion | flops 538968064 | bytes 4194304 | tf_op jit(solution)/shard_map/dot_general | solution.py:119
  73.6 3.7 %all-to-all-start.2 = ((bf16[16,32,1024]{2,1,0:T(8,128)(2,1)}), bf16[16,32,1024]{2,1,0:T(8,128)(2,1)S(1)}, u32[]{:S(2)}, u32[]{:S(2)}) async-start(bf16[16,32,1024]{2,1,0:T(8,128)(2,1)} %bitcast.50), calls=%async_computation.2 | async-start | bytes 2097152 | tf_op jit(solution)/shard_map/all_to_all | solution.py:154
  77.3 2.6 %fusion.2 = f32[512,1024]{1,0:T(8,128)S(1)} fusion(bf16[512,1024]{1,0:T(8,128)(2,1)} %bitcast.51, bf16[1,1024,1024]{2,1,0:T(8,128)(2,1)S(1)} %copy-done), kind=kOutput, calls=%fused_computation.3 | convolution fusion | flops 1073741824 | bytes 5242880 | tf_op jit(solution)/shard_map/dot_general | solution.py:115
  79.9 1.7 %convolution_convert_fusion.3 = bf16[512,1024]{1,0:T(8,128)(2,1)} fusion(bf16[1,512,1024]{2,1,0:T(8,128)(2,1)S(1)} %copy-done.8, f32[512,1024]{1,0:T(8,128)S(1)} %fusion.2), kind=kOutput, calls=%fused_computation.14 | convolution fusion | flops 538968064 | bytes 4194304 | tf_op jit(solution)/shard_map/dot_general | solution.py:119
  81.6 11.8 %all-to-all-done.2 = bf16[16,32,1024]{2,1,0:T(8,128)(2,1)S(1)} async-done(((bf16[16,32,1024]{2,1,0:T(8,128)(2,1)}), bf16[16,32,1024]{2,1,0:T(8,128)(2,1)S(1)}, u32[]{:S(2)}, u32[]{:S(2)}) %all-to-all-start.2) | async-done | bytes 1048608 | tf_op jit(solution)/shard_map/all_to_all | solution.py:154
  93.4 1.0 copy-done.2
  94.5 3.7 %all-to-all-start.1 = ((bf16[16,32,1024]{2,1,0:T(8,128)(2,1)}), bf16[16,32,1024]{2,1,0:T(8,128)(2,1)S(1)}, u32[]{:S(2)}, u32[]{:S(2)}) async-start(bf16[16,32,1024]{2,1,0:T(8,128)(2,1)} %bitcast.49), calls=%async_computation.1 | async-start | bytes 2097152 | tf_op jit(solution)/shard_map/all_to_all | solution.py:154
  98.2 0.7 select_reduce_fusion
  99.0 2.6 %convolution_convert_fusion.4 = bf16[128,1024]{1,0:T(8,128)(2,1)} fusion(f32[512,128]{1,0:T(8,128)S(1)} %select_reduce_fusion, bf16[512,1024]{1,0:T(8,128)(2,1)} %bitcast.46), kind=kOutput, calls=%fused_computation.15 | convolution fusion | flops 805437440 | bytes 1572864 | tf_op jit(solution)/shard_map/dot_general | solution.py:156
  101.5 3.4 %collective-permute-start.3 = (bf16[128,1024]{1,0:T(8,128)(2,1)}, bf16[128,1024]{1,0:T(8,128)(2,1)}, u32[]{:S(2)}, u32[]{:S(2)}) collective-permute-start(bf16[128,1024]{1,0:T(8,128)(2,1)} %convolution_convert_fusion.4), channel_id=1, source_target_pairs={{8,0},{0,8},{9,1},{1,9},{10,2},{2,10},{11,3},{3,11},{12,4},{4,12},... | collective-permute-start | bytes 786440 | tf_op jit(solution)/shard_map/ppermute | solution.py:164
  104.9 1.4 %select_reduce_fusion.1 = f32[512,128]{1,0:T(8,128)} fusion(f32[128,8]{0,1:T(8,128)S(1)} %slice_add_fusion.2, s32[128,8]{0,1:T(8,128)S(1)} %get-tuple-element.33), kind=kLoop, calls=%fused_computation.8 | loop fusion | flops 1507328 | bytes 270336 | tf_op jit(solution)/shard_map/reduce_sum | solution.py:155
  106.4 13.5 %all-to-all-done.1 = bf16[16,32,1024]{2,1,0:T(8,128)(2,1)S(1)} async-done(((bf16[16,32,1024]{2,1,0:T(8,128)(2,1)}), bf16[16,32,1024]{2,1,0:T(8,128)(2,1)S(1)}, u32[]{:S(2)}, u32[]{:S(2)}) %all-to-all-start.1) | async-done | bytes 1048608 | tf_op jit(solution)/shard_map/all_to_all | solution.py:154
  119.9 1.8 %multiply_reduce_fusion = (f32[128]{0:T(128)S(1)}, f32[128,1024]{1,0:T(8,128)S(1)}) fusion(bf16[128,1024]{1,0:T(8,128)(2,1)} %collective-permute-done.3, bf16[128,1024]{1,0:T(8,128)(2,1)S(1)} %get-tuple-element.18, f32[512,128]{1,0:T(8,128)} %select_reduce_fusion.1, bf16[512,1024]{1,0:T(8,128)(2,1)S(1)} %bitcast.45), kind=kOutput, calls=%fused_computation.36 | convolution fusion | flops 806092672 | bytes 2359808 | tf_op jit(solution)/shard_map/dot_general | solution.py:156
  121.7 1.8 %multiply_convert_fusion = bf16[128,1024]{1,0:T(8,128)(2,1)} fusion(f32[1024]{0:T(1024)S(1)} %copy-done.6, f32[128]{0:T(128)S(1)} %add_rsqrt_fusion, f32[128,1024]{1,0:T(8,128)S(1)} %get-tuple-element.32, bf16[128,1024]{1,0:T(8,128)(2,1)} %collective-permute-done.3, bf16[128,1024]{1,0:T(8,128)(2,1)S(1)} %get-tuple-element.18), kind=kLoop, calls=%fused_computation.35 | loop fusion | flops 917504 | bytes 1315328 | tf_op jit(solution)/shard_map/convert_element_type | solution.py:169
  (35 shorter events, 0.4 us)
Async XLA Ops:
  0.0 70.6 %copy-start = (bf16[1,1024,1024]{2,1,0:T(8,128)(2,1)S(1)}, bf16[1,1024,1024]{2,1,0:T(8,128)(2,1)}, u32[]{:S(2)}) copy-start(bf16[1,1024,1024]{2,1,0:T(8,128)(2,1)} %param.21) | copy-start | bytes 6291460
  0.0 18.4 %copy-start.3 = (bf16[128,1024]{1,0:T(8,128)(2,1)S(1)}, bf16[128,1024]{1,0:T(8,128)(2,1)}, u32[]{:S(2)}) copy-start(bf16[128,1024]{1,0:T(8,128)(2,1)} %param.16) | copy-start | bytes 786436
  0.0 18.4 %copy-start.1 = (bf16[1024,512]{1,0:T(8,128)(2,1)S(1)}, bf16[1024,512]{1,0:T(8,128)(2,1)}, u32[]{:S(2)}) copy-start(bf16[1024,512]{1,0:T(8,128)(2,1)} %param.18) | copy-start | bytes 3145732
  0.0 9.9 %collective-permute-start = (bf16[128,1024]{1,0:T(8,128)(2,1)}, bf16[128,1024]{1,0:T(8,128)(2,1)}, u32[]{:S(2)}, u32[]{:S(2)}) collective-permute-start(bf16[128,1024]{1,0:T(8,128)(2,1)} %param.16), channel_id=1, source_target_pairs={{0,16},{16,0},{1,17},{17,1},{2,18},{18,2},{3,19},{19,3},{4,20},{20... | collective-permute-start | bytes 786440 | tf_op jit(solution)/shard_map/ppermute | solution.py:52
  12.3 9.3 %copy-start.5 = (f32[1024]{0:T(1024)S(1)}, f32[1024]{0:T(1024)}, u32[]{:S(2)}) copy-start(f32[1024]{0:T(1024)} %param.19) | copy-start | bytes 12292
  12.3 8.1 %collective-permute-start.1 = (f32[128,512]{1,0:T(8,128)}, f32[128,512]{1,0:T(8,128)}, u32[]{:S(2)}, u32[]{:S(2)}) collective-permute-start(f32[128,512]{1,0:T(8,128)} %fusion.57), channel_id=1, source_target_pairs={{16,0},{0,16},{17,1},{1,17},{18,2},{2,18},{19,3},{3,19},{20,4},{4,... | collective-permute-start | bytes 786440 | tf_op jit(solution)/shard_map/ppermute | solution.py:54
  18.4 3.0 %copy-start.4 = (bf16[128,1024]{1,0:T(8,128)(2,1)S(1)}, bf16[128,1024]{1,0:T(8,128)(2,1)}, u32[]{:S(2)}) copy-start(bf16[128,1024]{1,0:T(8,128)(2,1)} %param.17) | copy-start | bytes 786436
  21.8 14.2 %collective-permute-start.2 = (bf16[136,1024]{1,0:T(8,128)(2,1)S(1)}, bf16[136,1024]{1,0:T(8,128)(2,1)S(1)}, u32[]{:S(2)}, u32[]{:S(2)}) collective-permute-start(bf16[136,1024]{1,0:T(8,128)(2,1)S(1)} %pad_maximum_fusion.1), channel_id=1, source_target_pairs={{0,8},{8,0},{1,9},{9,1},{2,10},{10,2},{3,11},{11,3},{4,12},{12,4},... | collective-permute-start | bytes 835592 | tf_op jit(solution)/shard_map/ppermute | solution.py:124
  70.6 1.3 %copy-start.7 = (bf16[1,512,1024]{2,1,0:T(8,128)(2,1)S(1)}, bf16[1,512,1024]{2,1,0:T(8,128)(2,1)}, u32[]{:S(2)}) copy-start(bf16[1,512,1024]{2,1,0:T(8,128)(2,1)} %param.22) | copy-start | bytes 3145732
  73.6 19.8 %all-to-all-start.2 = ((bf16[16,32,1024]{2,1,0:T(8,128)(2,1)}), bf16[16,32,1024]{2,1,0:T(8,128)(2,1)S(1)}, u32[]{:S(2)}, u32[]{:S(2)}) async-start(bf16[16,32,1024]{2,1,0:T(8,128)(2,1)} %bitcast.50), calls=%async_computation.2 | async-start | bytes 2097152 | tf_op jit(solution)/shard_map/all_to_all | solution.py:154
  77.3 2.6 %copy-start.8 = (bf16[1,512,1024]{2,1,0:T(8,128)(2,1)S(1)}, bf16[1,512,1024]{2,1,0:T(8,128)(2,1)}, u32[]{:S(2)}) copy-start(bf16[1,512,1024]{2,1,0:T(8,128)(2,1)} %param.22) | copy-start | bytes 3145732
  93.4 1.0 copy-start.2
  94.5 25.4 %all-to-all-start.1 = ((bf16[16,32,1024]{2,1,0:T(8,128)(2,1)}), bf16[16,32,1024]{2,1,0:T(8,128)(2,1)S(1)}, u32[]{:S(2)}, u32[]{:S(2)}) async-start(bf16[16,32,1024]{2,1,0:T(8,128)(2,1)} %bitcast.49), calls=%async_computation.1 | async-start | bytes 2097152 | tf_op jit(solution)/shard_map/all_to_all | solution.py:154
  98.9 22.7 %copy-start.6 = (f32[1024]{0:T(1024)S(1)}, f32[1024]{0:T(1024)}, u32[]{:S(2)}) copy-start(f32[1024]{0:T(1024)} %param.20) | copy-start | bytes 12292
  101.5 18.3 %collective-permute-start.3 = (bf16[128,1024]{1,0:T(8,128)(2,1)}, bf16[128,1024]{1,0:T(8,128)(2,1)}, u32[]{:S(2)}, u32[]{:S(2)}) collective-permute-start(bf16[128,1024]{1,0:T(8,128)(2,1)} %convolution_convert_fusion.4), channel_id=1, source_target_pairs={{8,0},{0,8},{9,1},{1,9},{10,2},{2,10},{11,3},{3,11},{12,4},{4,12},... | collective-permute-start | bytes 786440 | tf_op jit(solution)/shard_map/ppermute | solution.py:164

commit v20 on v15

--- a/solution.py
+++ b/solution.py
@@ -49,9 +49,13 @@
     for shift in range(1, groups):
         ahead = [(g, (g + shift) % groups) for g in range(groups)]
         back = [(b, a) for a, b in ahead]
-        visiting = lax.ppermute(attention, "grp", ahead)
-        done = jnp.dot(visiting, out_proj, preferred_element_type=jnp.float32)
-        blocks[shift] = lax.ppermute(done, "grp", back)
+        half = rows_here // 2
+        pieces = []
+        for lo in (0, half):
+            visiting = lax.ppermute(attention[lo : lo + half], "grp", ahead)
+            done = jnp.dot(visiting, out_proj, preferred_element_type=jnp.float32)
+            pieces.append(lax.ppermute(done, "grp", back))
+        blocks[shift] = jnp.concatenate(pieces, axis=0)
     stacked = jnp.stack(blocks, axis=0)
     order_cols = (jnp.arange(groups, dtype=jnp.int32) - me_grp) % groups
     attn_proj = jnp.concatenate(

time: 123 us -> 133 us (1.081)
  local copies, waits for them, and re-layouts: 3.09 us -> 8.87 us
  waiting for transfers between devices: 26.6 us -> 30.1 us
    ppermute x2 -> x4, waiting for transfers between devices: 1.61 us -> 5.05 us  [the longest x2 5.04 us: on_device(): pieces.append(lax.ppermute(done, 'grp', back))]
    slice x0 -> x1, local copies, waits for them, and re-layouts: none -> 1.83 us  [on_device(): visiting = lax.ppermute(attention[lo:lo + half], 'grp', ahead)]
    reshape x1, local copies, waits for them, and re-layouts: 0.12 us -> 1.46 us  [on_device(): meta.reshape(-1)]
    ppermute x2 -> x4, starting transfers between devices: 4.5 us -> 5.16 us  [the longest x2 3 us: on_device(): visiting = lax.ppermute(attention[lo:lo + half], 'grp', ahead)]
  transfers between devices with their start and end apart: 5 -> 7, of which waited for: 3 -> 4; matrix products, arithmetic and copies ran while one was open for 10% -> 15% of each run, Pallas kernels for 0% -> 0%
where the time goes in v20:
time: 133 us
  blocking collectives  50 us (38%)
  waiting for transfers between devices  30.1 us (23%)
  starting transfers between devices  15.3 us (12%)
  other arithmetic  13.1 us (10%)
  matrix products  11.3 us (8%)
  local copies, waits for them, and re-layouts  8.87 us (7%)
  between operations  4.03 us (3%)
    all_to_all x1, blocking collectives, on_device(): lax.all_to_all(jnp.stack(buffers, axis=1), PLANE_AXES, split_axis=0, conc...  30.6 us
    all_to_all x1, blocking collectives, on_device(): lax.all_to_all(produced[:, shift], PLANE_AXES, split_axis=0, concat_axis=...  19.4 us
    all_to_all x1, waiting for transfers between devices, on_device(): lax.all_to_all(produced[:, shift], PLANE_AXES, split_axis=0, concat_axis=...  13.5 us
    ppermute x1, waiting for transfers between devices, on_device(): lax.ppermute(packed, 'eh', [(i, (i + shift) % planes) for i in range(plan...  11.5 us
    ppermute x2, waiting for transfers between devices, on_device(): pieces.append(lax.ppermute(done, 'grp', back))  5.04 us
    dot_general x2, matrix products, on_device(): jnp.dot(combine.T, returned.reshape(plane_slots, features).astype(jnp.flo...  4.39 us
    all_to_all x1, starting transfers between devices, on_device(): lax.all_to_all(produced[:, shift], PLANE_AXES, split_axis=0, concat_axis=...  3.65 us
    ppermute x1, starting transfers between devices, on_device(): lax.ppermute(partial.astype(jnp.bfloat16), 'eh', back).astype(jnp.float32)  3.38 us
  transfers between devices with their start and end apart: 7, of which 4 were waited for; matrix products, arithmetic and copies ran while one was open for 15% of the time, Pallas kernels for 0%

profile of v20, /device:TPU:0, one launch (start us, length us, event | category | flops | bytes accessed | tf_op | source)
XLA Modules:
  0.0 132.7 jit_solution(13959925819484381166)
XLA Ops:
  0.0 1.8 %fusion.48 = (bf16[64,1024]{1,0:T(8,128)(2,1)}, bf16[64,1024]{1,0:T(8,128)(2,1)}) fusion(bf16[128,1024]{1,0:T(8,128)(2,1)} %param.16), kind=kLoop, calls=%fused_computation.114 | loop fusion | bytes 524288 | tf_op jit(solution)/shard_map/slice | solution.py:55
  1.8 3.0 %collective-permute-start = (bf16[64,1024]{1,0:T(8,128)(2,1)}, bf16[64,1024]{1,0:T(8,128)(2,1)}, u32[]{:S(2)}, u32[]{:S(2)}) collective-permute-start(bf16[64,1024]{1,0:T(8,128)(2,1)} %get-tuple-element.26), channel_id=1, source_target_pairs={{0,16},{16,0},{1,17},{17,1},{2,18},{18,2},{3,19},{19,3},{4,20},{20... | collective-permute-start | bytes 393224 | tf_op jit(solution)/shard_map/ppermute | solution.py:55
  4.8 0.6 fusion.49
  9.2 0.8 select_reduce_fusion.5
  10.0 0.8 select_reduce_fusion.4
  10.8 0.7 multiply_add_fusion
  11.5 0.7 multiply_add_fusion.1
  12.2 0.2 fusion.23
  12.4 0.6 select_reduce_fusion.3
  13.0 0.8 broadcast_in_dim.88
  13.9 0.7 constant_dynamic-update-slice_fusion.4
  14.6 0.7 constant_dynamic-update-slice_fusion.2
  15.3 0.7 constant_dynamic-update-slice_fusion.1
  16.0 0.7 constant_dynamic-update-slice_fusion
  16.7 0.7 copy.49
  17.4 1.5 %reshape.57 = bf16[5120]{0:T(1024)(128)(2,1)} reshape(bf16[128,40]{1,0:T(8,128)(2,1)} %copy.49) | data formatting | bytes 20480 | tf_op jit(solution)/shard_map/reshape | solution.py:111
  18.9 1.3 pad.4
  20.2 0.7 reshape.58
  20.9 1.6 %fusion.50 = f32[64,512]{1,0:T(8,128)S(1)} fusion(bf16[64,1024]{1,0:T(8,128)(2,1)} %collective-permute-done, bf16[1024,512]{1,0:T(8,128)(2,1)} %param.18), kind=kOutput, calls=%fused_computation.116 | convolution fusion | flops 67108864 | bytes 1310720 | tf_op jit(solution)/shard_map/dot_general | solution.py:56
  22.6 2.1 %collective-permute-start.1 = (f32[64,512]{1,0:T(8,128)S(1)}, f32[64,512]{1,0:T(8,128)S(1)}, u32[]{:S(2)}, u32[]{:S(2)}) collective-permute-start(f32[64,512]{1,0:T(8,128)S(1)} %fusion.50), channel_id=1, source_target_pairs={{16,0},{0,16},{17,1},{1,17},{18,2},{2,18},{19,3},{3,19},{20,4},{4,... | collective-permute-start | bytes 393224 | tf_op jit(solution)/shard_map/ppermute | solution.py:57
  24.6 0.3 fusion.51
  25.0 0.3 convolution_bitcast_fusion
  25.4 3.2 %collective-permute-done.1 = f32[64,512]{1,0:T(8,128)S(1)} collective-permute-done((f32[64,512]{1,0:T(8,128)S(1)}, f32[64,512]{1,0:T(8,128)S(1)}, u32[]{:S(2)}, u32[]{:S(2)}) %collective-permute-start.1) | collective-permute-done | bytes 131104 | tf_op jit(solution)/shard_map/ppermute | solution.py:57
  28.6 1.8 %collective-permute-done.3 = f32[64,512]{1,0:T(8,128)S(1)} collective-permute-done((f32[64,512]{1,0:T(8,128)S(1)}, f32[64,512]{1,0:T(8,128)S(1)}, u32[]{:S(2)}, u32[]{:S(2)}) %collective-permute-start.3) | collective-permute-done | bytes 131104 | tf_op jit(solution)/shard_map/ppermute | solution.py:57
  30.4 0.1 fusion.17
  30.6 0.2 fusion.8
  30.7 0.1 fusion.10
  30.9 3.1 %collective-permute-start.4 = (bf16[136,1024]{1,0:T(8,128)(2,1)S(1)}, bf16[136,1024]{1,0:T(8,128)(2,1)S(1)}, u32[]{:S(2)}, u32[]{:S(2)}) collective-permute-start(bf16[136,1024]{1,0:T(8,128)(2,1)S(1)} %pad_maximum_fusion.1), channel_id=1, source_target_pairs={{0,8},{8,0},{1,9},{9,1},{2,10},{10,2},{3,11},{11,3},{4,12},{12,4},... | collective-permute-start | bytes 835592 | tf_op jit(solution)/shard_map/ppermute | solution.py:128
  34.0 11.5 %collective-permute-done.4 = bf16[136,1024]{1,0:T(8,128)(2,1)S(1)} collective-permute-done((bf16[136,1024]{1,0:T(8,128)(2,1)S(1)}, bf16[136,1024]{1,0:T(8,128)(2,1)S(1)}, u32[]{:S(2)}, u32[]{:S(2)}) %collective-permute-start.4) | collective-permute-done | bytes 278560 | tf_op jit(solution)/shard_map/ppermute | solution.py:128
  45.6 0.1 slice_add_fusion
  45.9 0.9 fusion.4
  46.8 0.4 convolution_convert_fusion.2
  47.2 0.9 fusion.3
  48.1 0.4 convolution_convert_fusion.1
  48.5 0.2 pad_maximum_fusion
  48.8 30.6 %all_to_all.15 = bf16[16,2,32,1024]{3,2,1,0:T(8,128)(2,1)S(1)} all-to-all(bf16[16,2,32,1024]{3,2,1,0:T(8,128)(2,1)S(1)} %pad_maximum_fusion), channel_id=1, replica_groups=mesh['grp'=2,'eh'=2,'el'=8] {'grp','el'}, dimensions={0} | all-to-all | bytes 4194304 | tf_op jit(solution)/shard_map/all_to_all | solution.py:152
  79.4 2.4 %fusion.1 = f32[1024,1024]{1,0:T(8,128)S(1)} fusion(bf16[1024,1024]{1,0:T(8,128)(2,1)S(1)} %bitcast.50, bf16[1,1024,1024]{2,1,0:T(8,128)(2,1)S(1)} %copy-done), kind=kOutput, calls=%fused_computation.3 | convolution fusion | flops 2147483648 | bytes 8388608 | tf_op jit(solution)/shard_map/dot_general | solution.py:119
  81.7 1.3 convolution_convert_fusion
  83.1 1.2 slice_bitcast_fusion
  84.2 19.4 %all_to_all.16 = bf16[16,32,1024]{2,1,0:T(8,128)(2,1)} all-to-all(bf16[16,32,1024]{2,1,0:T(8,128)(2,1)S(1)} %get-tuple-element.22), channel_id=1, replica_groups=mesh['grp'=2,'eh'=2,'el'=8] {'grp','el'}, dimensions={0} | all-to-all | bytes 2097152 | tf_op jit(solution)/shard_map/all_to_all | solution.py:158
  103.7 3.7 %all-to-all-start.1 = ((bf16[16,32,1024]{2,1,0:T(8,128)(2,1)}), bf16[16,32,1024]{2,1,0:T(8,128)(2,1)S(1)}, u32[]{:S(2)}, u32[]{:S(2)}) async-start(bf16[16,32,1024]{2,1,0:T(8,128)(2,1)} %get-tuple-element.23), calls=%async_computation.1 | async-start | bytes 2097152 | tf_op jit(solution)/shard_map/all_to_all | solution.py:158
  107.4 0.7 select_reduce_fusion
  108.1 2.6 %convolution_convert_fusion.3 = bf16[128,1024]{1,0:T(8,128)(2,1)} fusion(f32[512,128]{1,0:T(8,128)S(1)} %select_reduce_fusion, bf16[512,1024]{1,0:T(8,128)(2,1)} %bitcast.46), kind=kOutput, calls=%fused_computation.14 | convolution fusion | flops 805437440 | bytes 1572864 | tf_op jit(solution)/shard_map/dot_general | solution.py:162
  110.7 3.4 %collective-permute-start.5 = (bf16[128,1024]{1,0:T(8,128)(2,1)}, bf16[128,1024]{1,0:T(8,128)(2,1)}, u32[]{:S(2)}, u32[]{:S(2)}) collective-permute-start(bf16[128,1024]{1,0:T(8,128)(2,1)} %convolution_convert_fusion.3), channel_id=1, source_target_pairs={{8,0},{0,8},{9,1},{1,9},{10,2},{2,10},{11,3},{3,11},{12,4},{4,12},... | collective-permute-start | bytes 786440 | tf_op jit(solution)/shard_map/ppermute | solution.py:170
  114.1 1.4 %select_reduce_fusion.1 = f32[512,128]{1,0:T(8,128)} fusion(f32[128,8]{0,1:T(8,128)S(1)} %slice_add_fusion.2, s32[128,8]{0,1:T(8,128)S(1)} %get-tuple-element.35), kind=kLoop, calls=%fused_computation.8 | loop fusion | flops 1507328 | bytes 270336 | tf_op jit(solution)/shard_map/reduce_sum | solution.py:161
  115.6 13.5 %all-to-all-done.1 = bf16[16,32,1024]{2,1,0:T(8,128)(2,1)S(1)} async-done(((bf16[16,32,1024]{2,1,0:T(8,128)(2,1)}), bf16[16,32,1024]{2,1,0:T(8,128)(2,1)S(1)}, u32[]{:S(2)}, u32[]{:S(2)}) %all-to-all-start.1) | async-done | bytes 1048608 | tf_op jit(solution)/shard_map/all_to_all | solution.py:158
  129.0 1.8 %multiply_reduce_fusion = (f32[128]{0:T(128)S(1)}, f32[128,1024]{1,0:T(8,128)S(1)}) fusion(bf16[128,1024]{1,0:T(8,128)(2,1)} %collective-permute-done.5, bf16[128,1024]{1,0:T(8,128)(2,1)S(1)} %get-tuple-element.18, f32[512,128]{1,0:T(8,128)} %select_reduce_fusion.1, bf16[512,1024]{1,0:T(8,128)(2,1)S(1)} %bitcast.45), kind=kOutput, calls=%fused_computation.33 | convolution fusion | flops 806092672 | bytes 2359808 | tf_op jit(solution)/shard_map/dot_general | solution.py:162
  130.9 1.8 %multiply_convert_fusion = bf16[128,1024]{1,0:T(8,128)(2,1)} fusion(f32[1024]{0:T(1024)S(1)} %copy-done.7, f32[128]{0:T(128)S(1)} %add_rsqrt_fusion, f32[128,1024]{1,0:T(8,128)S(1)} %get-tuple-element.34, bf16[128,1024]{1,0:T(8,128)(2,1)} %collective-permute-done.5, bf16[128,1024]{1,0:T(8,128)(2,1)S(1)} %get-tuple-element.18), kind=kLoop, calls=%fused_computation.32 | loop fusion | flops 917504 | bytes 1315328 | tf_op jit(solution)/shard_map/convert_element_type | solution.py:175
  (39 shorter events, 0.6 us)
Async XLA Ops:
  0.0 79.4 %copy-start = (bf16[1,1024,1024]{2,1,0:T(8,128)(2,1)S(1)}, bf16[1,1024,1024]{2,1,0:T(8,128)(2,1)}, u32[]{:S(2)}) copy-start(bf16[1,1024,1024]{2,1,0:T(8,128)(2,1)} %param.21) | copy-start | bytes 6291460
  0.0 25.0 %copy-start.2 = (bf16[128,1024]{1,0:T(8,128)(2,1)S(1)}, bf16[128,1024]{1,0:T(8,128)(2,1)}, u32[]{:S(2)}) copy-start(bf16[128,1024]{1,0:T(8,128)(2,1)} %param.16) | copy-start | bytes 786436
  0.0 24.6 %copy-start.1 = (bf16[1024,512]{1,0:T(8,128)(2,1)S(1)}, bf16[1024,512]{1,0:T(8,128)(2,1)}, u32[]{:S(2)}) copy-start(bf16[1024,512]{1,0:T(8,128)(2,1)} %param.18) | copy-start | bytes 3145732
  1.8 19.1 %collective-permute-start = (bf16[64,1024]{1,0:T(8,128)(2,1)}, bf16[64,1024]{1,0:T(8,128)(2,1)}, u32[]{:S(2)}, u32[]{:S(2)}) collective-permute-start(bf16[64,1024]{1,0:T(8,128)(2,1)} %get-tuple-element.26), channel_id=1, source_target_pairs={{0,16},{16,0},{1,17},{17,1},{2,18},{18,2},{3,19},{19,3},{4,20},{20... | collective-permute-start | bytes 393224 | tf_op jit(solution)/shard_map/ppermute | solution.py:55
  4.8 19.8 %collective-permute-start.2 = (bf16[64,1024]{1,0:T(8,128)(2,1)}, bf16[64,1024]{1,0:T(8,128)(2,1)S(1)}, u32[]{:S(2)}, u32[]{:S(2)}) collective-permute-start(bf16[64,1024]{1,0:T(8,128)(2,1)} %get-tuple-element.27), channel_id=1, source_target_pairs={{0,16},{16,0},{1,17},{17,1},{2,18},{18,2},{3,19},{19,3},{4,20},{20... | collective-permute-start | bytes 393224 | tf_op jit(solution)/shard_map/ppermute | solution.py:55
  16.7 2.2 %copy-start.4 = (bf16[128,40]{0,1:T(8,128)(2,1)}, bf16[128,40]{0,1:T(8,128)(2,1)S(1)}, u32[]{:S(2)}) copy-start(bf16[128,40]{0,1:T(8,128)(2,1)S(1)} %constant_dynamic-update-slice_fusion) | copy-start | bytes 30724
  22.5 8.0 %copy-start.3 = (bf16[128,1024]{1,0:T(8,128)(2,1)S(1)}, bf16[128,1024]{1,0:T(8,128)(2,1)}, u32[]{:S(2)}) copy-start(bf16[128,1024]{1,0:T(8,128)(2,1)} %param.17) | copy-start | bytes 786436
  22.6 6.0 %collective-permute-start.1 = (f32[64,512]{1,0:T(8,128)S(1)}, f32[64,512]{1,0:T(8,128)S(1)}, u32[]{:S(2)}, u32[]{:S(2)}) collective-permute-start(f32[64,512]{1,0:T(8,128)S(1)} %fusion.50), channel_id=1, source_target_pairs={{16,0},{0,16},{17,1},{1,17},{18,2},{2,18},{19,3},{3,19},{20,4},{4,... | collective-permute-start | bytes 393224 | tf_op jit(solution)/shard_map/ppermute | solution.py:57
  24.9 5.8 %copy-start.6 = (f32[1024]{0:T(1024)S(1)}, f32[1024]{0:T(1024)}, u32[]{:S(2)}) copy-start(f32[1024]{0:T(1024)} %param.19) | copy-start | bytes 12292
  24.9 5.5 %collective-permute-start.3 = (f32[64,512]{1,0:T(8,128)S(1)}, f32[64,512]{1,0:T(8,128)S(1)}, u32[]{:S(2)}, u32[]{:S(2)}) collective-permute-start(f32[64,512]{1,0:T(8,128)S(1)} %fusion.51), channel_id=1, source_target_pairs={{16,0},{0,16},{17,1},{1,17},{18,2},{2,18},{19,3},{3,19},{20,4},{4,... | collective-permute-start | bytes 393224 | tf_op jit(solution)/shard_map/ppermute | solution.py:57
  25.3 8.6 %copy-start.5 = (bf16[128,40]{0,1:T(8,128)(2,1)S(1)}, bf16[128,40]{0,1:T(8,128)(2,1)}, u32[]{:S(2)}) copy-start(bf16[128,40]{0,1:T(8,128)(2,1)} %copy-done.4) | copy-start | bytes 30724
  30.9 14.6 %collective-permute-start.4 = (bf16[136,1024]{1,0:T(8,128)(2,1)S(1)}, bf16[136,1024]{1,0:T(8,128)(2,1)S(1)}, u32[]{:S(2)}, u32[]{:S(2)}) collective-permute-start(bf16[136,1024]{1,0:T(8,128)(2,1)S(1)} %pad_maximum_fusion.1), channel_id=1, source_target_pairs={{0,8},{8,0},{1,9},{9,1},{2,10},{10,2},{3,11},{11,3},{4,12},{12,4},... | collective-permute-start | bytes 835592 | tf_op jit(solution)/shard_map/ppermute | solution.py:128
  79.4 2.4 %copy-start.8 = (bf16[1,512,1024]{2,1,0:T(8,128)(2,1)S(1)}, bf16[1,512,1024]{2,1,0:T(8,128)(2,1)}, u32[]{:S(2)}) copy-start(bf16[1,512,1024]{2,1,0:T(8,128)(2,1)} %param.22) | copy-start | bytes 3145732
  103.7 25.4 %all-to-all-start.1 = ((bf16[16,32,1024]{2,1,0:T(8,128)(2,1)}), bf16[16,32,1024]{2,1,0:T(8,128)(2,1)S(1)}, u32[]{:S(2)}, u32[]{:S(2)}) async-start(bf16[16,32,1024]{2,1,0:T(8,128)(2,1)} %get-tuple-element.23), calls=%async_computation.1 | async-start | bytes 2097152 | tf_op jit(solution)/shard_map/all_to_all | solution.py:158
  108.1 22.7 %copy-start.7 = (f32[1024]{0:T(1024)S(1)}, f32[1024]{0:T(1024)}, u32[]{:S(2)}) copy-start(f32[1024]{0:T(1024)} %param.20) | copy-start | bytes 12292
  110.7 18.3 %collective-permute-start.5 = (bf16[128,1024]{1,0:T(8,128)(2,1)}, bf16[128,1024]{1,0:T(8,128)(2,1)}, u32[]{:S(2)}, u32[]{:S(2)}) collective-permute-start(bf16[128,1024]{1,0:T(8,128)(2,1)} %convolution_convert_fusion.3), channel_id=1, source_target_pairs={{8,0},{0,8},{9,1},{1,9},{10,2},{2,10},{11,3},{3,11},{12,4},{4,12},... | collective-permute-start | bytes 786440 | tf_op jit(solution)/shard_map/ppermute | solution.py:170

commit v21 on v15

--- a/solution.py
+++ b/solution.py
@@ -140,6 +140,9 @@
             (meta_s[:, 2 * picks_row : 3 * picks_row] + meta_s[:, 3 * picks_row : 4 * picks_row])
             + meta_s[:, 4 * picks_row :]
         )
+        if shift == 0:
+            local = code - my_plane * plane_slots
+            weights_in[0] = weights_kept
         hit = local[None, :, :] == slot_ids[:, None, None]
         hits.append(hit)
         dispatch = jnp.any(hit, axis=2).astype(jnp.bfloat16)

time: 123 us -> 123 us (level)
  other arithmetic: 13.4 us -> 12 us
  transfers between devices with their start and end apart: 5 -> 5, of which waited for: 3 -> 4; matrix products, arithmetic and copies ran while one was open for 10% -> 9% of each run, Pallas kernels for 0% -> 0%
where the time goes in v21:
time: 123 us; the launch traced here: 122 us
  blocking collectives  50.2 us (41%)
  waiting for transfers between devices  26.9 us (22%)
  starting transfers between devices  14.4 us (12%)
  other arithmetic  12 us (10%)
  matrix products  11.7 us (10%)
  between operations  4.02 us (3%)
  local copies, waits for them, and re-layouts  3.09 us (3%)
    all_to_all x1, blocking collectives, on_device(): lax.all_to_all(jnp.stack(buffers, axis=1), PLANE_AXES, split_axis=0, conc...  30.8 us
    all_to_all x1, blocking collectives, on_device(): lax.all_to_all(produced[:, shift], PLANE_AXES, split_axis=0, concat_axis=...  19.4 us
    all_to_all x1, waiting for transfers between devices, on_device(): lax.all_to_all(produced[:, shift], PLANE_AXES, split_axis=0, concat_axis=...  13.5 us
    ppermute x1, waiting for transfers between devices, on_device(): lax.ppermute(packed, 'eh', [(i, (i + shift) % planes) for i in range(plan...  11.3 us
    dot_general x2, matrix products, on_device(): jnp.dot(combine.T, returned.reshape(plane_slots, features).astype(jnp.flo...  4.39 us
    all_to_all x1, starting transfers between devices, on_device(): lax.all_to_all(produced[:, shift], PLANE_AXES, split_axis=0, concat_axis=...  3.65 us
    ppermute x1, starting transfers between devices, on_device(): lax.ppermute(partial.astype(jnp.bfloat16), 'eh', back).astype(jnp.float32)  3.37 us
    ppermute x1, starting transfers between devices, on_device(): visiting = lax.ppermute(attention, 'grp', ahead)  3.04 us
  transfers between devices with their start and end apart: 5, of which 4 were waited for; matrix products, arithmetic and copies ran while one was open for 9% of the time, Pallas kernels for 0%

profile of v21, /device:TPU:0, one launch (start us, length us, event | category | flops | bytes accessed | tf_op | source)
XLA Modules:
  0.0 122.4 jit_solution(1720863318237102503)
XLA Ops:
  0.0 3.0 %collective-permute-start = (bf16[128,1024]{1,0:T(8,128)(2,1)}, bf16[128,1024]{1,0:T(8,128)(2,1)}, u32[]{:S(2)}, u32[]{:S(2)}) collective-permute-start(bf16[128,1024]{1,0:T(8,128)(2,1)} %param.16), channel_id=1, source_target_pairs={{0,16},{16,0},{1,17},{17,1},{2,18},{18,2},{3,19},{19,3},{4,20},{20... | collective-permute-start | bytes 786440 | tf_op jit(solution)/shard_map/ppermute | solution.py:52
  3.0 0.8 select_reduce_fusion.5
  3.8 0.8 select_reduce_fusion.4
  4.6 0.7 multiply_add_fusion
  5.3 0.7 multiply_add_fusion.1
  6.0 0.2 fusion.23
  6.2 0.8 broadcast_in_dim.88
  7.0 0.1 select_reduce_fusion.2
  7.1 0.7 constant_dynamic-update-slice_fusion.4
  7.8 0.7 constant_dynamic-update-slice_fusion.2
  8.6 1.1 collective-permute-done
  9.7 2.3 %fusion.47 = f32[128,512]{1,0:T(8,128)} fusion(bf16[128,1024]{1,0:T(8,128)(2,1)} %collective-permute-done, bf16[1024,512]{1,0:T(8,128)(2,1)} %param.18), kind=kOutput, calls=%fused_computation.110 | convolution fusion | flops 134217728 | bytes 1572864 | tf_op jit(solution)/shard_map/dot_general | solution.py:53
  12.0 1.7 %collective-permute-start.1 = (f32[128,512]{1,0:T(8,128)}, f32[128,512]{1,0:T(8,128)}, u32[]{:S(2)}, u32[]{:S(2)}) collective-permute-start(f32[128,512]{1,0:T(8,128)} %fusion.47), channel_id=1, source_target_pairs={{16,0},{0,16},{17,1},{1,17},{18,2},{2,18},{19,3},{3,19},{20,4},{4,... | collective-permute-start | bytes 786440 | tf_op jit(solution)/shard_map/ppermute | solution.py:54
  13.7 0.6 fusion.46
  18.1 0.1 copy.51
  18.2 0.1 reshape.55
  18.4 0.0 copy-start.3
  18.4 0.3 convolution_bitcast_fusion
  18.8 1.0 collective-permute-done.1
  19.8 1.1 fusion.17
  20.9 0.2 fusion.8
  21.0 0.1 fusion.10
  21.2 2.6 %collective-permute-start.2 = (bf16[136,1024]{1,0:T(8,128)(2,1)S(1)}, bf16[136,1024]{1,0:T(8,128)(2,1)S(1)}, u32[]{:S(2)}, u32[]{:S(2)}) collective-permute-start(bf16[136,1024]{1,0:T(8,128)(2,1)S(1)} %pad_maximum_fusion.1), channel_id=1, source_target_pairs={{0,8},{8,0},{1,9},{9,1},{2,10},{10,2},{3,11},{11,3},{4,12},{12,4},... | collective-permute-start | bytes 835592 | tf_op jit(solution)/shard_map/ppermute | solution.py:124
  23.8 11.3 %collective-permute-done.2 = bf16[136,1024]{1,0:T(8,128)(2,1)S(1)} collective-permute-done((bf16[136,1024]{1,0:T(8,128)(2,1)S(1)}, bf16[136,1024]{1,0:T(8,128)(2,1)S(1)}, u32[]{:S(2)}, u32[]{:S(2)}) %collective-permute-start.2) | collective-permute-done | bytes 278560 | tf_op jit(solution)/shard_map/ppermute | solution.py:124
  35.1 0.1 reshape.100
  35.2 0.1 slice_add_fusion
  35.4 0.1 copy.58
  35.5 0.9 fusion.4
  36.4 0.4 convolution_convert_fusion.2
  36.8 0.9 fusion.3
  37.7 0.4 convolution_convert_fusion.1
  38.1 0.2 pad_maximum_fusion
  38.3 30.8 %all_to_all.15 = bf16[16,2,32,1024]{3,2,1,0:T(8,128)(2,1)S(1)} all-to-all(bf16[16,2,32,1024]{3,2,1,0:T(8,128)(2,1)S(1)} %pad_maximum_fusion), channel_id=1, replica_groups=mesh['grp'=2,'eh'=2,'el'=8] {'grp','el'}, dimensions={0} | all-to-all | bytes 4194304 | tf_op jit(solution)/shard_map/all_to_all | solution.py:151
  69.1 2.4 %fusion.1 = f32[1024,1024]{1,0:T(8,128)S(1)} fusion(bf16[1024,1024]{1,0:T(8,128)(2,1)S(1)} %bitcast.47, bf16[1,1024,1024]{2,1,0:T(8,128)(2,1)S(1)} %copy-done), kind=kOutput, calls=%fused_computation.3 | convolution fusion | flops 2147483648 | bytes 8388608 | tf_op jit(solution)/shard_map/dot_general | solution.py:115
  71.5 0.0 copy-done.6
  71.5 1.3 %convolution_convert_fusion = bf16[1024,1024]{1,0:T(8,128)(2,1)S(1)} fusion(f32[1024,1024]{1,0:T(8,128)S(1)} %fusion.1, bf16[1,512,1024]{2,1,0:T(8,128)(2,1)S(1)} %copy-done.6), kind=kOutput, calls=%fused_computation.11 | convolution fusion | flops 1077936128 | bytes 7340032 | tf_op jit(solution)/shard_map/dot_general | solution.py:119
  72.8 1.2 slice_bitcast_fusion
  74.0 19.4 %all_to_all.16 = bf16[16,32,1024]{2,1,0:T(8,128)(2,1)} all-to-all(bf16[16,32,1024]{2,1,0:T(8,128)(2,1)S(1)} %get-tuple-element.24), channel_id=1, replica_groups=mesh['grp'=2,'eh'=2,'el'=8] {'grp','el'}, dimensions={0} | all-to-all | bytes 2097152 | tf_op jit(solution)/shard_map/all_to_all | solution.py:157
  93.4 3.7 %all-to-all-start.1 = ((bf16[16,32,1024]{2,1,0:T(8,128)(2,1)}), bf16[16,32,1024]{2,1,0:T(8,128)(2,1)S(1)}, u32[]{:S(2)}, u32[]{:S(2)}) async-start(bf16[16,32,1024]{2,1,0:T(8,128)(2,1)} %get-tuple-element.25), calls=%async_computation.1 | async-start | bytes 2097152 | tf_op jit(solution)/shard_map/all_to_all | solution.py:157
  97.1 0.7 select_reduce_fusion
  97.9 0.0 copy-start.5
  97.9 2.6 %convolution_convert_fusion.3 = bf16[128,1024]{1,0:T(8,128)(2,1)} fusion(f32[512,128]{1,0:T(8,128)S(1)} %select_reduce_fusion, bf16[512,1024]{1,0:T(8,128)(2,1)} %bitcast.43), kind=kOutput, calls=%fused_computation.14 | convolution fusion | flops 805437440 | bytes 1572864 | tf_op jit(solution)/shard_map/dot_general | solution.py:161
  100.5 3.4 %collective-permute-start.3 = (bf16[128,1024]{1,0:T(8,128)(2,1)}, bf16[128,1024]{1,0:T(8,128)(2,1)}, u32[]{:S(2)}, u32[]{:S(2)}) collective-permute-start(bf16[128,1024]{1,0:T(8,128)(2,1)} %convolution_convert_fusion.3), channel_id=1, source_target_pairs={{8,0},{0,8},{9,1},{1,9},{10,2},{2,10},{11,3},{3,11},{12,4},{4,12},... | collective-permute-start | bytes 786440 | tf_op jit(solution)/shard_map/ppermute | solution.py:169
  103.9 1.4 %select_reduce_fusion.1 = f32[512,128]{1,0:T(8,128)} fusion(f32[128,8]{0,1:T(8,128)S(1)} %get-tuple-element.20, s32[128,8]{0,1:T(8,128)S(1)} %get-tuple-element.36), kind=kLoop, calls=%fused_computation.8 | loop fusion | flops 1507328 | bytes 270336 | tf_op jit(solution)/shard_map/reduce_sum | solution.py:160
  105.3 13.5 %all-to-all-done.1 = bf16[16,32,1024]{2,1,0:T(8,128)(2,1)S(1)} async-done(((bf16[16,32,1024]{2,1,0:T(8,128)(2,1)}), bf16[16,32,1024]{2,1,0:T(8,128)(2,1)S(1)}, u32[]{:S(2)}, u32[]{:S(2)}) %all-to-all-start.1) | async-done | bytes 1048608 | tf_op jit(solution)/shard_map/all_to_all | solution.py:157
  118.8 0.0 collective-permute-done.3
  118.8 1.8 %multiply_reduce_fusion = (f32[128]{0:T(128)S(1)}, f32[128,1024]{1,0:T(8,128)S(1)}) fusion(bf16[128,1024]{1,0:T(8,128)(2,1)} %collective-permute-done.3, bf16[128,1024]{1,0:T(8,128)(2,1)S(1)} %get-tuple-element.18, f32[512,128]{1,0:T(8,128)} %select_reduce_fusion.1, bf16[512,1024]{1,0:T(8,128)(2,1)S(1)} %bitcast.42), kind=kOutput, calls=%fused_computation.33 | convolution fusion | flops 806092672 | bytes 2359808 | tf_op jit(solution)/shard_map/dot_general | solution.py:161
  120.6 1.8 %multiply_convert_fusion = bf16[128,1024]{1,0:T(8,128)(2,1)} fusion(f32[1024]{0:T(1024)S(1)} %copy-done.5, f32[128]{0:T(128)S(1)} %add_rsqrt_fusion, f32[128,1024]{1,0:T(8,128)S(1)} %get-tuple-element.34, bf16[128,1024]{1,0:T(8,128)(2,1)} %collective-permute-done.3, bf16[128,1024]{1,0:T(8,128)(2,1)S(1)} %get-tuple-element.18), kind=kLoop, calls=%fused_computation.32 | loop fusion | flops 917504 | bytes 1315328 | tf_op jit(solution)/shard_map/convert_element_type | solution.py:174
  (26 shorter events, 0.3 us)
Async XLA Ops:
  0.0 69.1 %copy-start = (bf16[1,1024,1024]{2,1,0:T(8,128)(2,1)S(1)}, bf16[1,1024,1024]{2,1,0:T(8,128)(2,1)}, u32[]{:S(2)}) copy-start(bf16[1,1024,1024]{2,1,0:T(8,128)(2,1)} %param.21) | copy-start | bytes 6291460
  0.0 18.4 %copy-start.2 = (bf16[128,1024]{1,0:T(8,128)(2,1)S(1)}, bf16[128,1024]{1,0:T(8,128)(2,1)}, u32[]{:S(2)}) copy-start(bf16[128,1024]{1,0:T(8,128)(2,1)} %param.16) | copy-start | bytes 786436
  0.0 18.4 %copy-start.1 = (bf16[1024,512]{1,0:T(8,128)(2,1)S(1)}, bf16[1024,512]{1,0:T(8,128)(2,1)}, u32[]{:S(2)}) copy-start(bf16[1024,512]{1,0:T(8,128)(2,1)} %param.18) | copy-start | bytes 3145732
  0.0 9.7 %collective-permute-start = (bf16[128,1024]{1,0:T(8,128)(2,1)}, bf16[128,1024]{1,0:T(8,128)(2,1)}, u32[]{:S(2)}, u32[]{:S(2)}) collective-permute-start(bf16[128,1024]{1,0:T(8,128)(2,1)} %param.16), channel_id=1, source_target_pairs={{0,16},{16,0},{1,17},{17,1},{2,18},{18,2},{3,19},{19,3},{4,20},{20... | collective-permute-start | bytes 786440 | tf_op jit(solution)/shard_map/ppermute | solution.py:52
  12.0 9.0 %copy-start.4 = (f32[1024]{0:T(1024)S(1)}, f32[1024]{0:T(1024)}, u32[]{:S(2)}) copy-start(f32[1024]{0:T(1024)} %param.19) | copy-start | bytes 12292
  12.0 7.8 %collective-permute-start.1 = (f32[128,512]{1,0:T(8,128)}, f32[128,512]{1,0:T(8,128)}, u32[]{:S(2)}, u32[]{:S(2)}) collective-permute-start(f32[128,512]{1,0:T(8,128)} %fusion.47), channel_id=1, source_target_pairs={{16,0},{0,16},{17,1},{1,17},{18,2},{2,18},{19,3},{3,19},{20,4},{4,... | collective-permute-start | bytes 786440 | tf_op jit(solution)/shard_map/ppermute | solution.py:54
  18.4 2.4 %copy-start.3 = (bf16[128,1024]{1,0:T(8,128)(2,1)S(1)}, bf16[128,1024]{1,0:T(8,128)(2,1)}, u32[]{:S(2)}) copy-start(bf16[128,1024]{1,0:T(8,128)(2,1)} %param.17) | copy-start | bytes 786436
  21.2 13.9 %collective-permute-start.2 = (bf16[136,1024]{1,0:T(8,128)(2,1)S(1)}, bf16[136,1024]{1,0:T(8,128)(2,1)S(1)}, u32[]{:S(2)}, u32[]{:S(2)}) collective-permute-start(bf16[136,1024]{1,0:T(8,128)(2,1)S(1)} %pad_maximum_fusion.1), channel_id=1, source_target_pairs={{0,8},{8,0},{1,9},{9,1},{2,10},{10,2},{3,11},{11,3},{4,12},{12,4},... | collective-permute-start | bytes 835592 | tf_op jit(solution)/shard_map/ppermute | solution.py:124
  69.1 2.4 %copy-start.6 = (bf16[1,512,1024]{2,1,0:T(8,128)(2,1)S(1)}, bf16[1,512,1024]{2,1,0:T(8,128)(2,1)}, u32[]{:S(2)}) copy-start(bf16[1,512,1024]{2,1,0:T(8,128)(2,1)} %param.22) | copy-start | bytes 3145732
  93.4 25.4 %all-to-all-start.1 = ((bf16[16,32,1024]{2,1,0:T(8,128)(2,1)}), bf16[16,32,1024]{2,1,0:T(8,128)(2,1)S(1)}, u32[]{:S(2)}, u32[]{:S(2)}) async-start(bf16[16,32,1024]{2,1,0:T(8,128)(2,1)} %get-tuple-element.25), calls=%async_computation.1 | async-start | bytes 2097152 | tf_op jit(solution)/shard_map/all_to_all | solution.py:157
  97.9 22.7 %copy-start.5 = (f32[1024]{0:T(1024)S(1)}, f32[1024]{0:T(1024)}, u32[]{:S(2)}) copy-start(f32[1024]{0:T(1024)} %param.20) | copy-start | bytes 12292
  100.5 18.3 %collective-permute-start.3 = (bf16[128,1024]{1,0:T(8,128)(2,1)}, bf16[128,1024]{1,0:T(8,128)(2,1)}, u32[]{:S(2)}, u32[]{:S(2)}) collective-permute-start(bf16[128,1024]{1,0:T(8,128)(2,1)} %convolution_convert_fusion.3), channel_id=1, source_target_pairs={{8,0},{0,8},{9,1},{1,9},{10,2},{2,10},{11,3},{3,11},{12,4},{4,12},... | collective-permute-start | bytes 786440 | tf_op jit(solution)/shard_map/ppermute | solution.py:169
